TPU v7x, 32 devices: a whole 2x2x4 slice. The times are simulated.
32 devices in a mesh: group: 4 (over y, x), dom: 8 (over z, core).
Axes of the slice: x: 2, y: 2, z: 4, core: 2. Of those that a mesh axis runs over, the one named last changes fastest.
Arguments:
- pin_feats: bfloat16 [32768, 256], P(('group', 'dom')), may hold values from -6 to 6
- w_self: bfloat16 [256, 256], replicated, may hold values from -0.375 to 0.375
- w_edge: bfloat16 [4, 256, 256], replicated, may hold values from -0.375 to 0.375
- w_head: bfloat16 [256, 1024], replicated, may hold values from -0.375 to 0.375
- w_out: bfloat16 [1024], replicated, may hold values from -0.1875 to 0.1875
- send_rows: int32 [32, 512], P(('group', 'dom')), may hold values from 0 to 1023
- edge_src: int32 [32, 4, 1024], P(('group', 'dom')), may hold values from 0 to 1535
- edge_dst: int32 [32, 4, 1024], P(('group', 'dom')), may hold values from 0 to 1023
- pin_owner: int32 [32768, 1], P(('group', 'dom')), may hold values from 0 to 31; in each aligned block of 1024 rows (0 to 1023, 1024 to 2047, ...) at most 64 rows name the same one
- pin_net: int32 [32768], P(('group', 'dom')), may hold values from 0 to 255
- net_target: float32 [8192], P(('group', 'dom')), may hold values from -6 to 6
Outputs:
- prediction: float32 [8192], P(('group', 'dom'))
- grad_feats: bfloat16 [32768, 256], P(('group', 'dom'))
- grad_self: float32 [256, 256], replicated
- grad_edge: float32 [4, 256, 256], replicated
- grad_head: float32 [256, 1024], replicated
- grad_out: float32 [1024], replicated
Inputs may be any that keep to these rules, and one draw needn't show every extreme that they name: `pin_owner`: among the pins of one device at most 64 name one owner, and in every draw some device sends exactly 64 pins to some owner.
All inputs are finite; a program needn't handle non-finite values.
Results may differ from a plain program's by a relative error of at most 0.0094.
Values may be sent and summed in bfloat16 or wider, within the bound.
No kernel may reach another device: no remote copies, remote signals or barrier semaphores. Data moves between devices by JAX's collectives and lax.ppermute only.
A program may use at most 64 MiB of HBM per device.

v0:
```python
import math

import jax
import jax.numpy as jnp
from jax import lax
from jax.sharding import PartitionSpec as P


F32 = jnp.float32
BF16 = jnp.bfloat16


def extended(block, sides, width):
    for axis, dim in sides:
        count = lax.axis_size(axis)
        forward = [(i, i + 1) for i in range(count - 1)]
        backward = [(target, source) for source, target in forward]
        low = lax.ppermute(
            lax.slice_in_dim(block, block.shape[dim] - width, None, axis=dim), axis, forward
        )
        high = lax.ppermute(lax.slice_in_dim(block, 0, width, axis=dim), axis, backward)
        block = jnp.concatenate([low, block, high], axis=dim)
    return block


def silu_slope(values):
    sigma_val = jax.nn.sigmoid(values)
    return sigma_val * (1.0 + values * (1.0 - sigma_val))


def one_hot(index, count):
    return (index[..., None] == jnp.arange(count, dtype=index.dtype)).astype(BF16)


def split_dot(spec, left, right):
    return jnp.einsum(
        spec, left, right.astype(F32), precision=lax.Precision.HIGHEST, preferred_element_type=F32
    )


def all_sum(rows, owners):
    count, width = rows.shape
    unit = owners * 16
    length = -(-count // unit) * unit
    rows = jnp.pad(rows, ((0, length - count), (0, 0)))
    axes = ("group", "dom")
    mine = lax.all_to_all(
        rows.astype(BF16).reshape(owners, -1, width), axes, split_axis=0, concat_axis=0, tiled=True
    )
    mine = jnp.sum(mine.astype(F32), axis=0).astype(BF16)
    spread = jnp.broadcast_to(mine[None], (owners,) + mine.shape)
    gathered = lax.all_to_all(spread, axes, split_axis=0, concat_axis=0, tiled=True)
    return gathered.reshape(length, width)[:count].astype(F32)


def on_device(
    pin_feats,
    w_self,
    w_edge,
    w_head,
    w_out,
    send_rows,
    edge_src,
    edge_dst,
    pin_owner,
    pin_net,
    net_target,
):
    pin_count, feat_width = pin_feats.shape
    send_list = send_rows[0]
    halo_span = send_list.shape[0] // 2
    send_hot = one_hot(send_list, pin_count)
    outgoing = jnp.dot(send_hot, pin_feats, preferred_element_type=F32).astype(BF16)
    padded = extended(outgoing, (("dom", 0),), halo_span)
    node_table = jnp.concatenate([pin_feats, padded[:halo_span], padded[3 * halo_span :]], 0)
    table_rows = node_table.shape[0]
    sources = edge_src[0]
    endpoints = edge_dst[0]
    src_hot = one_hot(sources, table_rows)
    dst_hot = one_hot(endpoints, pin_count)
    gathered = jnp.einsum(
        "ter,rd->ted", src_hot, node_table, preferred_element_type=F32
    ).astype(BF16)
    edge_in = jnp.einsum("tep,ted->tpd", dst_hot, gathered, preferred_element_type=F32)
    summed = split_dot("tpk,tkd->pd", edge_in, w_edge)
    degree = jnp.sum(dst_hot.astype(F32), axis=(0, 1))
    inverse = 1.0 / (1.0 + degree)
    preact = (
        jnp.dot(pin_feats, w_self, preferred_element_type=F32) + summed * inverse[:, None]
    )
    hidden = jax.nn.silu(preact).astype(BF16)
    groups = lax.axis_size("group")
    domains = lax.axis_size("dom")
    owners = groups * domains
    capacity = max(2, 2 * pin_count // owners)
    net_count = net_target.shape[0]
    owner_ids = pin_owner[:, 0]
    owner_hot = one_hot(owner_ids, owners)
    earlier = (
        jnp.arange(pin_count, dtype=jnp.int32)[None, :]
        < jnp.arange(pin_count, dtype=jnp.int32)[:, None]
    ).astype(BF16)
    before = jnp.dot(earlier, owner_hot, preferred_element_type=F32)
    slot_rank = jnp.sum(before * owner_hot.astype(F32), axis=1).astype(jnp.int32)
    pin_slot = owner_ids * capacity + slot_rank
    slot_hot = one_hot(pin_slot, owners * capacity)
    net_code = (pin_net + 1).astype(BF16)[:, None]
    slot_nets = jnp.dot(slot_hot.T, net_code, preferred_element_type=F32)[:, 0] - 1.0
    outbound = jnp.dot(slot_hot.T, hidden, preferred_element_type=F32).astype(BF16)
    id_rows = -(-capacity // feat_width)
    id_block = jnp.pad(
        slot_nets.reshape(owners, capacity), ((0, 0), (0, id_rows * feat_width - capacity))
    ).astype(BF16)
    packet = jnp.concatenate(
        [
            outbound.reshape(owners, capacity, feat_width),
            id_block.reshape(owners, id_rows, feat_width),
        ],
        1,
    )
    packet_in = lax.all_to_all(packet, ("group", "dom"), split_axis=0, concat_axis=0, tiled=True)
    inbound = packet_in[:, :capacity].reshape(-1, feat_width)
    slot_nets_in = (
        packet_in[:, capacity:].reshape(owners, -1)[:, :capacity].astype(F32).astype(jnp.int32)
    ).reshape(-1)
    net_hot = one_hot(slot_nets_in, net_count)
    pooled = jnp.einsum("sn,sd->nd", net_hot, inbound, preferred_element_type=F32)
    pooled_b = pooled.astype(BF16)
    head_pre = jnp.dot(pooled_b, w_head, preferred_element_type=F32)
    activated = jax.nn.silu(head_pre).astype(BF16)
    predicted = jnp.dot(activated, w_out, preferred_element_type=F32)
    misfit = predicted - net_target
    head_grad = (
        misfit[:, None] * w_out.astype(F32)[None, :] * silu_slope(head_pre)
    ).astype(BF16)
    head_sum_t = jnp.einsum("nh,nd->hd", head_grad, pooled_b, preferred_element_type=F32)
    out_sum = jnp.dot(misfit, activated.astype(F32), precision=lax.Precision.HIGHEST)
    net_grad = jnp.einsum(
        "nh,dh->nd", head_grad, w_head, preferred_element_type=F32
    ).astype(BF16)
    returned = jnp.dot(net_hot, net_grad, preferred_element_type=F32).astype(BF16)
    arrived = lax.all_to_all(
        returned.reshape(owners, capacity, feat_width),
        ("group", "dom"),
        split_axis=0,
        concat_axis=0,
        tiled=True,
    ).reshape(-1, feat_width)
    pin_grad = jnp.dot(slot_hot, arrived, preferred_element_type=F32)
    preact_grad = (pin_grad * silu_slope(preact)).astype(BF16)
    self_sum = jnp.einsum("pk,pd->kd", pin_feats, preact_grad, preferred_element_type=F32)
    agg_grad = (preact_grad.astype(F32) * inverse[:, None]).astype(BF16)
    edge_rows = jnp.einsum(
        "tep,pd->ted", dst_hot, agg_grad, preferred_element_type=F32
    ).astype(BF16)
    edge_sum = jnp.einsum("tek,ted->tkd", gathered, edge_rows, preferred_element_type=F32)
    row_in = jnp.einsum("ter,ted->trd", src_hot, edge_rows, preferred_element_type=F32)
    table_grad = split_dot("trd,tkd->rk", row_in, w_edge)
    local_grad = (
        jnp.einsum("pd,kd->pk", preact_grad, w_self, preferred_element_type=F32)
        + table_grad[:pin_count]
    )
    halo_grad = table_grad[pin_count:].astype(BF16)
    back_padded = extended(halo_grad, (("dom", 0),), halo_span)
    received = jnp.concatenate([back_padded[:halo_span], back_padded[3 * halo_span :]], 0)
    grad_feats = (
        local_grad + jnp.einsum("sp,sd->pd", send_hot, received, preferred_element_type=F32)
    ).astype(BF16)
    head_width = head_sum_t.shape[0]
    pieces = (
        self_sum,
        edge_sum.reshape(-1, feat_width),
        head_sum_t,
        out_sum.reshape(-1, feat_width),
    )
    totals = all_sum(jnp.concatenate(pieces, 0), owners)
    grad_scale = 1.0 / math.sqrt(pin_count * owners)
    outs = []
    offset = 0
    for piece in pieces:
        outs.append(totals[offset : offset + piece.shape[0]] * grad_scale)
        offset += piece.shape[0]
    return (
        predicted,
        grad_feats,
        outs[0],
        outs[1].reshape(edge_sum.shape),
        outs[2].T,
        outs[3].reshape(head_width),
    )


def solution(mesh):
    in_specs = (
        P(("group", "dom"), None),
        P(),
        P(),
        P(),
        P(),
        P(("group", "dom"), None),
        P(("group", "dom"), None, None),
        P(("group", "dom"), None, None),
        P(("group", "dom"), None),
        P(("group", "dom")),
        P(("group", "dom")),
    )
    out_specs = (P(("group", "dom")), P(("group", "dom"), None), P(), P(), P(), P())
    return jax.shard_map(
        on_device, mesh=mesh, in_specs=in_specs, out_specs=out_specs, check_vma=False
    )
```

profile of v0, /device:TPU:1, one launch (start us, length us, event | category | flops | bytes accessed | tf_op | source)
XLA Modules:
  0.0 188.1 jit_solution(12452435584735663364)
XLA Ops:
  0.6 0.0 copy-start
  0.7 1.6 fusion.35
  2.3 4.6 %collective-permute-start = (bf16[256,256]{1,0:T(8,128)(2,1)S(1)}, bf16[256,256]{1,0:T(8,128)(2,1)S(1)}, u32[]{:S(2)}, u32[]{:S(2)}) collective-permute-start(bf16[256,256]{1,0:T(8,128)(2,1)S(1)} %get-tuple-element.34), channel_id=1, source_target_pairs={{0,1},{1,2},{2,3},{3,4},{4,5},{5,6},{6,7},{8,9},{9,10},{10,11},{11... | collective-permute-start | bytes 393224 | tf_op jit(solution)/shard_map/ppermute | solution.py:18
  6.9 1.9 %collective-permute-start.1 = (bf16[256,256]{1,0:T(8,128)(2,1)S(1)}, bf16[256,256]{1,0:T(8,128)(2,1)S(1)}, u32[]{:S(2)}, u32[]{:S(2)}) collective-permute-start(bf16[256,256]{1,0:T(8,128)(2,1)S(1)} %get-tuple-element.35), channel_id=1, source_target_pairs={{1,0},{2,1},{3,2},{4,3},{5,4},{6,5},{7,6},{9,8},{10,9},{11,10},{12... | collective-permute-start | bytes 393224 | tf_op jit(solution)/shard_map/ppermute | solution.py:21
  8.9 0.0 copy-done.11
  8.9 0.0 copy-done.13
  8.9 1.9 %convert_reduce_fusion = f32[1024]{0:T(1024)S(1)} fusion(s32[4,1024]{1,0:T(4,128)S(1)} %bitcast.91), kind=kLoop, calls=%fused_computation.3 | loop fusion | flops 16776192 | bytes 20480 | tf_op jit(solution)/shard_map/reduce_sum | solution.py:86
  10.9 0.5 fusion.39
  11.4 0.0 copy-start.5
  11.4 0.0 copy-start.7
  11.5 0.0 copy-start.14
  11.5 1.5 fusion.10
  12.9 0.1 sub.16
  13.1 0.0 copy-done.5
  13.1 0.3 fusion.65
  13.4 0.0 collective-permute-done
  13.4 0.0 collective-permute-done.1
  13.4 6.9 %fusion.24 = bf16[4,1024,256]{2,1,0:T(8,128)(2,1)S(1)} fusion(s32[4,1024]{1,0:T(4,128)S(1)} %bitcast.94, bf16[256,256]{1,0:T(8,128)(2,1)S(1)} %collective-permute-done.1, bf16[256,256]{1,0:T(8,128)(2,1)S(1)} %collective-permute-done, bf16[1024,256]{1,0:T(8,128)(2,1)S(1)} %copy-done.5), kind=kOutput, calls=%fused_computation.34 | convolution fusion | flops 3230924800 | bytes 2899968 | tf_op jit(solution)/shard_map/ter,rd->ted/dot_general | solution.py:81
  20.4 0.0 copy-start.1
  20.4 5.8 %fusion.4 = f32[4,1024,256]{2,1,0:T(8,128)S(1)} fusion(bf16[4,1024,256]{2,1,0:T(8,128)(2,1)S(1)} %fusion.24, s32[4,1024]{1,0:T(4,128)S(1)} %bitcast.92), kind=kOutput, calls=%fused_computation.7 | convolution fusion | flops 2151677952 | bytes 6307840 | tf_op jit(solution)/shard_map/tep,ted->tpd/dot_general | solution.py:84
  26.2 2.1 %fusion.28 = f32[1024,256]{1,0:T(8,128)S(1)} fusion(f32[1024,256]{1,0:T(8,128)S(1)} %fusion.65, f32[4,1024,256]{2,1,0:T(8,128)S(1)} %fusion.4, bf16[4,256,256]{2,1,0:T(8,128)(2,1)S(1)} %copy-done.1, f32[1024]{0:T(1024)S(1)} %add_divide_fusion.2), kind=kOutput, calls=%fused_computation.40 | convolution fusion | flops 3221749760 | bytes 6819840 | tf_op jit(solution)/shard_map/tpk,tkd->pd/dot_general | solution.py:36
  28.3 0.0 copy-start.6
  28.3 2.5 %fusion.20 = bf16[2048,256]{1,0:T(8,128)(2,1)S(1)} fusion(s32[1024]{0:T(1024)S(1)} %bitcast.88, f32[1024,256]{1,0:T(8,128)S(1)} %fusion.28), kind=kOutput, calls=%fused_computation.27 | convolution fusion | flops 1077673984 | bytes 2101248 | tf_op jit(solution)/shard_map/dot_general | solution.py:109
  30.9 0.0 copy-start.8
  30.9 1.1 pad_maximum_fusion
  32.0 6.1 %all-to-all-start = ((bf16[32,65,256]{2,1,0:T(8,128)(2,1)}), bf16[32,65,256]{2,1,0:T(8,128)(2,1)S(1)}, u32[]{:S(2)}, u32[]{:S(2)}) async-start(bf16[32,65,256]{2,1,0:T(8,128)(2,1)} %pad_maximum_fusion), calls=%async_computation | async-start | bytes 2359296 | tf_op jit(solution)/shard_map/all_to_all | solution.py:121
  38.2 29.8 %all-to-all-done = bf16[32,65,256]{2,1,0:T(8,128)(2,1)S(1)} async-done(((bf16[32,65,256]{2,1,0:T(8,128)(2,1)}), bf16[32,65,256]{2,1,0:T(8,128)(2,1)S(1)}, u32[]{:S(2)}, u32[]{:S(2)}) %all-to-all-start) | async-done | bytes 1064992 | tf_op jit(solution)/shard_map/all_to_all | solution.py:121
  68.0 0.1 eq.110
  68.1 0.1 slice.60
  68.2 1.1 fusion.36
  69.3 0.0 copy-start.12
  69.3 0.5 multiply_convert_fusion.2
  69.7 0.2 fusion.66
  70.0 0.4 multiply_convert_fusion.1
  70.4 2.0 %convolution_convert_fusion = bf16[2048,256]{1,0:T(8,128)(2,1)} fusion(bf16[256,1024]{1,0:T(8,128)(2,1)S(1)} %multiply_convert_fusion.1, bf16[256,1024]{1,0:T(8,128)(2,1)S(1)} %copy-done, s32[2048]{0:T(1024)S(1)} %eq.110), kind=kOutput, calls=%fused_computation.28 | convolution fusion | flops 403767296 | bytes 2105344 | tf_op jit(solution)/shard_map/dot_general | solution.py:141
  72.4 3.7 %all-to-all-start.1 = ((bf16[32,64,256]{2,1,0:T(8,128)(2,1)}), bf16[32,64,256]{2,1,0:T(8,128)(2,1)}, u32[]{:S(2)}, u32[]{:S(2)}) async-start(bf16[32,64,256]{2,1,0:T(8,128)(2,1)} %bitcast.75), calls=%async_computation.1 | async-start | bytes 2097152 | tf_op jit(solution)/shard_map/all_to_all | solution.py:142
  76.1 0.3 fusion.67
  76.5 0.4 convolution_convert_fusion.1
  76.8 26.5 %all-to-all-done.1 = bf16[32,64,256]{2,1,0:T(8,128)(2,1)} async-done(((bf16[32,64,256]{2,1,0:T(8,128)(2,1)}), bf16[32,64,256]{2,1,0:T(8,128)(2,1)}, u32[]{:S(2)}, u32[]{:S(2)}) %all-to-all-start.1) | async-done | bytes 1048608 | tf_op jit(solution)/shard_map/all_to_all | solution.py:142
  103.3 3.3 %fusion.33 = bf16[1024,256]{1,0:T(8,128)(2,1)S(1)} fusion(bf16[2048,256]{1,0:T(8,128)(2,1)} %bitcast.15, s32[1024]{0:T(1024)S(1)} %bitcast.89, f32[1024,256]{1,0:T(8,128)} %copy-done.6), kind=kOutput, calls=%fused_computation.45 | convolution fusion | flops 1078198272 | bytes 2625536 | tf_op jit(solution)/shard_map/dot_general | solution.py:149
  106.6 0.3 fusion.37
  107.0 3.3 %fusion.25 = bf16[4,1024,256]{2,1,0:T(8,128)(2,1)S(1)} fusion(s32[4,1024]{1,0:T(4,128)S(1)} %bitcast.93, bf16[1024,256]{1,0:T(8,128)(2,1)S(1)} %fusion.33, f32[1024]{0:T(1024)S(1)} %add_divide_fusion.2), kind=kOutput, calls=%fused_computation.35 | convolution fusion | flops 2153512960 | bytes 2641920 | tf_op jit(solution)/shard_map/tep,pd->ted/dot_general | solution.py:153
  110.3 0.9 convolution_convert_fusion.2
  111.2 0.4 copy-done.4
  111.6 0.1 fusion.32
  111.7 35.6 %all_to_all.20 = bf16[32,80,256]{2,1,0:T(8,128)(2,1)S(1)} all-to-all(bf16[32,80,256]{2,1,0:T(8,128)(2,1)S(1)} %bitcast.72), channel_id=1, replica_groups=mesh['group'=4,'dom'=8] {'group','dom'}, dimensions={0} | all-to-all | bytes 2621440 | tf_op jit(solution)/shard_map/all_to_all | solution.py:47
  147.3 0.2 reduce_sum.32
  147.5 1.2 broadcast_in_dim.2
  148.7 2.7 %all-to-all-start.3 = ((bf16[32,80,256]{2,1,0:T(8,128)(2,1)}), bf16[32,80,256]{2,1,0:T(8,128)(2,1)S(1)}, u32[]{:S(2)}, u32[]{:S(2)}) async-start(bf16[32,80,256]{2,1,0:T(8,128)(2,1)} %broadcast_in_dim.2), calls=%async_computation.3 | async-start | bytes 2621440 | tf_op jit(solution)/shard_map/all_to_all | solution.py:52
  151.3 5.9 %fusion = f32[4,1536,256]{2,1,0:T(8,128)S(1)} fusion(bf16[4,1024,256]{2,1,0:T(8,128)(2,1)} %copy-done.4, s32[4,1024]{1,0:T(4,128)S(1)} %bitcast.95), kind=kOutput, calls=%fused_computation.1 | convolution fusion | flops 3227516928 | bytes 8404992 | tf_op jit(solution)/shard_map/ter,ted->trd/dot_general | solution.py:157
  157.2 3.1 %fusion.64 = (bf16[1536,256]{1,0:T(8,128)(2,1)S(1)}, f32[1536,256]{1,0:T(8,128)S(1)}) fusion(f32[4,1536,256]{2,1,0:T(8,128)S(1)} %fusion, bf16[4,256,256]{2,1,0:T(8,128)(2,1)S(1)} %copy-done.1), kind=kOutput, calls=%fused_computation.100 | convolution fusion | flops 4832231424 | bytes 9175040 | tf_op jit(solution)/shard_map/trd,tkd->rk/dot_general | solution.py:36
  160.3 0.0 copy-start.16
  160.3 3.6 %collective-permute-start.2 = (bf16[256,256]{1,0:T(8,128)(2,1)S(1)}, bf16[256,256]{1,0:T(8,128)(2,1)S(1)}, u32[]{:S(2)}, u32[]{:S(2)}) collective-permute-start(bf16[256,256]{1,0:T(8,128)(2,1)S(1)} %get-tuple-element.32), channel_id=1, source_target_pairs={{0,1},{1,2},{2,3},{3,4},{4,5},{5,6},{6,7},{8,9},{9,10},{10,11},{11... | collective-permute-start | bytes 393224 | tf_op jit(solution)/shard_map/ppermute | solution.py:18
  163.9 1.9 %collective-permute-start.3 = (bf16[256,256]{1,0:T(8,128)(2,1)S(1)}, bf16[256,256]{1,0:T(8,128)(2,1)S(1)}, u32[]{:S(2)}, u32[]{:S(2)}) collective-permute-start(bf16[256,256]{1,0:T(8,128)(2,1)S(1)} %get-tuple-element.33), channel_id=1, source_target_pairs={{1,0},{2,1},{3,2},{4,3},{5,4},{6,5},{7,6},{9,8},{10,9},{11,10},{12... | collective-permute-start | bytes 393224 | tf_op jit(solution)/shard_map/ppermute | solution.py:21
  165.9 0.3 convolution_add_fusion
  166.2 8.2 %collective-permute-done.2 = bf16[256,256]{1,0:T(8,128)(2,1)S(1)} collective-permute-done((bf16[256,256]{1,0:T(8,128)(2,1)S(1)}, bf16[256,256]{1,0:T(8,128)(2,1)S(1)}, u32[]{:S(2)}, u32[]{:S(2)}) %collective-permute-start.2) | collective-permute-done | bytes 131104 | tf_op jit(solution)/shard_map/ppermute | solution.py:18
  174.4 0.0 collective-permute-done.3
  174.4 1.6 fusion.34
  176.0 8.0 %all-to-all-done.3 = bf16[32,80,256]{2,1,0:T(8,128)(2,1)S(1)} async-done(((bf16[32,80,256]{2,1,0:T(8,128)(2,1)}), bf16[32,80,256]{2,1,0:T(8,128)(2,1)S(1)}, u32[]{:S(2)}, u32[]{:S(2)}) %all-to-all-start.3) | async-done | bytes 1310752 | tf_op jit(solution)/shard_map/all_to_all | solution.py:52
  184.1 0.2 slice_convert_fusion
  184.3 0.7 slice_multiply_fusion.2
  185.0 1.2 fusion.40
  186.2 0.6 copy.38
  186.8 1.3 copy.33
  (40 shorter events, 0.2 us)
Async XLA Ops:
  0.6 68.6 %copy-start = (bf16[256,1024]{1,0:T(8,128)(2,1)S(1)}, bf16[256,1024]{1,0:T(8,128)(2,1)}, u32[]{:S(2)}) copy-start(bf16[256,1024]{1,0:T(8,128)(2,1)} %param.14) | copy-start | bytes 1572868
  0.6 8.2 %copy-start.11 = (s32[1024]{0:T(1024)S(1)}, s32[1024]{0:T(1024)}, u32[]{:S(2)}) copy-start(s32[1024]{0:T(1024)} %param.20) | copy-start | bytes 12292
  0.7 8.2 %copy-start.13 = (s32[1,4,1024]{2,1,0:T(4,128)S(1)}, s32[1,4,1024]{2,1,0:T(4,128)}, u32[]{:S(2)}) copy-start(s32[1,4,1024]{2,1,0:T(4,128)} %param.18) | copy-start | bytes 49156
  0.7 10.2 %copy-start.10 = (s32[1024,1]{0,1:T(1,128)S(1)}, s32[1024,1]{0,1:T(1,128)}, u32[]{:S(2)}) copy-start(s32[1024,1]{0,1:T(1,128)} %param.19) | copy-start | bytes 12292
  2.3 11.1 %collective-permute-start = (bf16[256,256]{1,0:T(8,128)(2,1)S(1)}, bf16[256,256]{1,0:T(8,128)(2,1)S(1)}, u32[]{:S(2)}, u32[]{:S(2)}) collective-permute-start(bf16[256,256]{1,0:T(8,128)(2,1)S(1)} %get-tuple-element.34), channel_id=1, source_target_pairs={{0,1},{1,2},{2,3},{3,4},{4,5},{5,6},{6,7},{8,9},{9,10},{10,11},{11... | collective-permute-start | bytes 393224 | tf_op jit(solution)/shard_map/ppermute | solution.py:18
  6.9 6.5 %collective-permute-start.1 = (bf16[256,256]{1,0:T(8,128)(2,1)S(1)}, bf16[256,256]{1,0:T(8,128)(2,1)S(1)}, u32[]{:S(2)}, u32[]{:S(2)}) collective-permute-start(bf16[256,256]{1,0:T(8,128)(2,1)S(1)} %get-tuple-element.35), channel_id=1, source_target_pairs={{1,0},{2,1},{3,2},{4,3},{5,4},{6,5},{7,6},{9,8},{10,9},{11,10},{12... | collective-permute-start | bytes 393224 | tf_op jit(solution)/shard_map/ppermute | solution.py:21
  11.4 1.7 copy-start.5
  11.4 1.7 copy-start.7
  11.5 2.0 %copy-start.14 = (s32[1,4,1024]{2,1,0:T(4,128)S(1)}, s32[1,4,1024]{2,1,0:T(4,128)}, u32[]{:S(2)}) copy-start(s32[1,4,1024]{2,1,0:T(4,128)} %param.17) | copy-start | bytes 49156
  20.4 5.8 %copy-start.2 = (bf16[4,1024,256]{2,1,0:T(8,128)(2,1)}, bf16[4,1024,256]{2,1,0:T(8,128)(2,1)S(1)}, u32[]{:S(2)}) copy-start(bf16[4,1024,256]{2,1,0:T(8,128)(2,1)S(1)} %fusion.24) | copy-start | bytes 6291460
  20.4 5.8 %copy-start.1 = (bf16[4,256,256]{2,1,0:T(8,128)(2,1)S(1)}, bf16[4,256,256]{2,1,0:T(8,128)(2,1)}, u32[]{:S(2)}) copy-start(bf16[4,256,256]{2,1,0:T(8,128)(2,1)} %param.13) | copy-start | bytes 1572868
  28.3 2.6 %copy-start.6 = (f32[1024,256]{1,0:T(8,128)}, f32[1024,256]{1,0:T(8,128)S(1)}, u32[]{:S(2)}) copy-start(f32[1024,256]{1,0:T(8,128)S(1)} %fusion.28) | copy-start | bytes 3145732
  30.9 7.3 %copy-start.8 = (bf16[1024]{0:T(1024)(128)(2,1)S(1)}, bf16[1024]{0:T(1024)(128)(2,1)}, u32[]{:S(2)}) copy-start(bf16[1024]{0:T(1024)(128)(2,1)} %param.15) | copy-start | bytes 6148
  32.0 36.0 %all-to-all-start = ((bf16[32,65,256]{2,1,0:T(8,128)(2,1)}), bf16[32,65,256]{2,1,0:T(8,128)(2,1)S(1)}, u32[]{:S(2)}, u32[]{:S(2)}) async-start(bf16[32,65,256]{2,1,0:T(8,128)(2,1)} %pad_maximum_fusion), calls=%async_computation | async-start | bytes 2359296 | tf_op jit(solution)/shard_map/all_to_all | solution.py:121
  69.3 0.7 copy-start.12
  70.0 2.4 %copy-start.9 = (f32[1,256]{1,0:T(1,128)}, f32[1,256]{1,0:T(1,128)S(1)}, u32[]{:S(2)}) copy-start(f32[1,256]{1,0:T(1,128)S(1)} %fusion.66) | copy-start | bytes 3076
  72.4 30.9 %all-to-all-start.1 = ((bf16[32,64,256]{2,1,0:T(8,128)(2,1)}), bf16[32,64,256]{2,1,0:T(8,128)(2,1)}, u32[]{:S(2)}, u32[]{:S(2)}) async-start(bf16[32,64,256]{2,1,0:T(8,128)(2,1)} %bitcast.75), calls=%async_computation.1 | async-start | bytes 2097152 | tf_op jit(solution)/shard_map/all_to_all | solution.py:142
  107.0 3.3 %copy-start.3 = (bf16[4,1024,256]{2,1,0:T(8,128)(2,1)S(1)}, bf16[4,1024,256]{2,1,0:T(8,128)(2,1)}, u32[]{:S(2)}) copy-start(bf16[4,1024,256]{2,1,0:T(8,128)(2,1)} %copy-done.2) | copy-start | bytes 6291460
  110.3 1.3 copy-start.4
  147.5 3.8 %copy-start.15 = (s32[1,4,1024]{2,1,0:T(4,128)S(1)}, s32[1,4,1024]{2,1,0:T(4,128)}, u32[]{:S(2)}) copy-start(s32[1,4,1024]{2,1,0:T(4,128)} %param.17) | copy-start | bytes 49156
  148.7 35.4 %all-to-all-start.3 = ((bf16[32,80,256]{2,1,0:T(8,128)(2,1)}), bf16[32,80,256]{2,1,0:T(8,128)(2,1)S(1)}, u32[]{:S(2)}, u32[]{:S(2)}) async-start(bf16[32,80,256]{2,1,0:T(8,128)(2,1)} %broadcast_in_dim.2), calls=%async_computation.3 | async-start | bytes 2621440 | tf_op jit(solution)/shard_map/all_to_all | solution.py:52
  160.3 14.1 %copy-start.16 = (s32[1,512]{1,0:T(1,128)S(1)}, s32[1,512]{1,0:T(1,128)}, u32[]{:S(2)}) copy-start(s32[1,512]{1,0:T(1,128)} %param.16) | copy-start | bytes 6148
  160.3 14.1 %collective-permute-start.2 = (bf16[256,256]{1,0:T(8,128)(2,1)S(1)}, bf16[256,256]{1,0:T(8,128)(2,1)S(1)}, u32[]{:S(2)}, u32[]{:S(2)}) collective-permute-start(bf16[256,256]{1,0:T(8,128)(2,1)S(1)} %get-tuple-element.32), channel_id=1, source_target_pairs={{0,1},{1,2},{2,3},{3,4},{4,5},{5,6},{6,7},{8,9},{9,10},{10,11},{11... | collective-permute-start | bytes 393224 | tf_op jit(solution)/shard_map/ppermute | solution.py:18
  163.9 10.5 %collective-permute-start.3 = (bf16[256,256]{1,0:T(8,128)(2,1)S(1)}, bf16[256,256]{1,0:T(8,128)(2,1)S(1)}, u32[]{:S(2)}, u32[]{:S(2)}) collective-permute-start(bf16[256,256]{1,0:T(8,128)(2,1)S(1)} %get-tuple-element.33), channel_id=1, source_target_pairs={{1,0},{2,1},{3,2},{4,3},{5,4},{6,5},{7,6},{9,8},{10,9},{11,10},{12... | collective-permute-start | bytes 393224 | tf_op jit(solution)/shard_map/ppermute | solution.py:21
where the time goes:
time: 189 us; the launch traced here: 188 us
  waiting for transfers between devices  72.5 us (38%)
  matrix products  44.3 us (23%)
  blocking collectives  35.6 us (19%)
  starting transfers between devices  24.6 us (13%)
  other arithmetic  5.9 us (3%)
  local copies, waits for them, and re-layouts  3.97 us (2%)
    all_to_all x1, blocking collectives, all_sum(): lax.all_to_all(rows.astype(BF16).reshape(owners, -1, width), axes, split_...  35.6 us
    all_to_all x1, waiting for transfers between devices, on_device(): lax.all_to_all(packet, ('group', 'dom'), split_axis=0, concat_axis=0, til...  29.8 us
    all_to_all x1, waiting for transfers between devices, on_device(): lax.all_to_all(returned.reshape(owners, capacity, feat_width), ('group',...  26.5 us
    ppermute x2, starting transfers between devices, extended(): lax.ppermute(lax.slice_in_dim(block, block.shape[dim] - width, None, axis...  8.19 us
    ppermute x2, waiting for transfers between devices, extended(): lax.ppermute(lax.slice_in_dim(block, block.shape[dim] - width, None, axis...  8.19 us
    all_to_all x1, waiting for transfers between devices, all_sum(): lax.all_to_all(spread, axes, split_axis=0, concat_axis=0, tiled=True)  8.05 us
    dot_general x1, matrix products, on_device(): jnp.einsum('ter,rd->ted', src_hot, node_table, preferred_element_type=F32)  6.93 us
    all_to_all x1, starting transfers between devices, on_device(): lax.all_to_all(packet, ('group', 'dom'), split_axis=0, concat_axis=0, til...  6.14 us
  transfers between devices with their start and end apart: 7, of which 4 were waited for; matrix products, arithmetic and copies ran while one was open for 9% of the time, Pallas kernels for 0%

commit v1 on v0

--- a/solution.py
+++ b/solution.py
@@ -47,7 +47,9 @@
     mine = lax.all_to_all(
         rows.astype(BF16).reshape(owners, -1, width), axes, split_axis=0, concat_axis=0, tiled=True
     )
-    mine = jnp.sum(mine.astype(F32), axis=0).astype(BF16)
+    mine = jnp.einsum(
+        "o,orw->rw", jnp.ones((owners,), BF16), mine, preferred_element_type=F32
+    ).astype(BF16)
     spread = jnp.broadcast_to(mine[None], (owners,) + mine.shape)
     gathered = lax.all_to_all(spread, axes, split_axis=0, concat_axis=0, tiled=True)
     return gathered.reshape(length, width)[:count].astype(F32)
@@ -135,6 +137,10 @@
     ).astype(BF16)
     head_sum_t = jnp.einsum("nh,nd->hd", head_grad, pooled_b, preferred_element_type=F32)
     out_sum = jnp.dot(misfit, activated.astype(F32), precision=lax.Precision.HIGHEST)
+    head_width = head_sum_t.shape[0]
+    head_totals = all_sum(
+        jnp.concatenate([head_sum_t, out_sum.reshape(-1, feat_width)], 0), owners
+    )
     net_grad = jnp.einsum(
         "nh,dh->nd", head_grad, w_head, preferred_element_type=F32
     ).astype(BF16)
@@ -166,27 +172,15 @@
     grad_feats = (
         local_grad + jnp.einsum("sp,sd->pd", send_hot, received, preferred_element_type=F32)
     ).astype(BF16)
-    head_width = head_sum_t.shape[0]
-    pieces = (
-        self_sum,
-        edge_sum.reshape(-1, feat_width),
-        head_sum_t,
-        out_sum.reshape(-1, feat_width),
-    )
-    totals = all_sum(jnp.concatenate(pieces, 0), owners)
+    tail_totals = all_sum(jnp.concatenate([self_sum, edge_sum.reshape(-1, feat_width)], 0), owners)
     grad_scale = 1.0 / math.sqrt(pin_count * owners)
-    outs = []
-    offset = 0
-    for piece in pieces:
-        outs.append(totals[offset : offset + piece.shape[0]] * grad_scale)
-        offset += piece.shape[0]
     return (
         predicted,
         grad_feats,
-        outs[0],
-        outs[1].reshape(edge_sum.shape),
-        outs[2].T,
-        outs[3].reshape(head_width),
+        tail_totals[:feat_width] * grad_scale,
+        tail_totals[feat_width:].reshape(edge_sum.shape) * grad_scale,
+        head_totals[:head_width].T * grad_scale,
+        head_totals[head_width:].reshape(head_width) * grad_scale,
     )
 
 

time: 189 us -> 208 us (1.10)
  waiting for transfers between devices: 72.5 us -> 109 us
  blocking collectives: 35.6 us -> 0 us
  starting transfers between devices: 24.6 us -> 35.1 us
  matrix products: 44.3 us -> 47 us
  other arithmetic: 5.9 us -> 8.53 us
    all_to_all x1 -> x0, blocking collectives: 35.6 us -> none  [all_sum(): lax.all_to_all(rows.astype(BF16).reshape(owners, -1, width), axes, split_...]
    all_to_all x0 -> x2, waiting for transfers between devices: none -> 33.4 us  [all_sum(): lax.all_to_all(rows.astype(BF16).reshape(owners, -1, width), axes, split_...]
    all_to_all x1 -> x2, waiting for transfers between devices: 8.05 us -> 20.4 us  [all_sum(): lax.all_to_all(spread, axes, split_axis=0, concat_axis=0, tiled=True)]
    ppermute x2, waiting for transfers between devices: 8.19 us -> 0.01 us  [extended(): lax.ppermute(lax.slice_in_dim(block, block.shape[dim] - width, None, axis...]
    all_to_all x0 -> x2, starting transfers between devices: none -> 6.16 us  [all_sum(): lax.all_to_all(rows.astype(BF16).reshape(owners, -1, width), axes, split_...]
    all_to_all x1 -> x2, starting transfers between devices: 2.67 us -> 7.05 us  [all_sum(): lax.all_to_all(spread, axes, split_axis=0, concat_axis=0, tiled=True)]
  transfers between devices with their start and end apart: 7 -> 10, of which waited for: 4 -> 6; matrix products, arithmetic and copies ran while one was open for 9% -> 16% of each run, Pallas kernels for 0% -> 0%
where the time goes in v1:
time: 208 us; the launch traced here: 206 us
  waiting for transfers between devices  109 us (52%)
  matrix products  47 us (23%)
  starting transfers between devices  35.1 us (17%)
  other arithmetic  8.53 us (4%)
  local copies, waits for them, and re-layouts  5.41 us (3%)
    all_to_all x2, waiting for transfers between devices, all_sum(): lax.all_to_all(rows.astype(BF16).reshape(owners, -1, width), axes, split_...  33.4 us
    all_to_all x1, waiting for transfers between devices, on_device(): lax.all_to_all(packet, ('group', 'dom'), split_axis=0, concat_axis=0, til...  29.8 us
    all_to_all x1, waiting for transfers between devices, on_device(): lax.all_to_all(returned.reshape(owners, capacity, feat_width), ('group',...  25.5 us
    all_to_all x2, waiting for transfers between devices, all_sum(): lax.all_to_all(spread, axes, split_axis=0, concat_axis=0, tiled=True)  20.4 us
    ppermute x2, starting transfers between devices, extended(): lax.ppermute(lax.slice_in_dim(block, block.shape[dim] - width, None, axis...  8.18 us
    all_to_all x2, starting transfers between devices, all_sum(): lax.all_to_all(spread, axes, split_axis=0, concat_axis=0, tiled=True)  7.05 us
    dot_general x1, matrix products, on_device(): jnp.einsum('ter,rd->ted', src_hot, node_table, preferred_element_type=F32)  6.93 us
    all_to_all x2, starting transfers between devices, all_sum(): lax.all_to_all(rows.astype(BF16).reshape(owners, -1, width), axes, split_...  6.16 us
  transfers between devices with their start and end apart: 10, of which 6 were waited for; matrix products, arithmetic and copies ran while one was open for 16% of the time, Pallas kernels for 0%

profile of v1, /device:TPU:1, one launch (start us, length us, event | category | flops | bytes accessed | tf_op | source)
XLA Modules:
  0.0 206.4 jit_solution(4410033123487112262)
XLA Ops:
  0.6 0.0 copy-start
  0.7 1.6 fusion.32
  2.3 4.6 %collective-permute-start = (bf16[256,256]{1,0:T(8,128)(2,1)S(1)}, bf16[256,256]{1,0:T(8,128)(2,1)S(1)}, u32[]{:S(2)}, u32[]{:S(2)}) collective-permute-start(bf16[256,256]{1,0:T(8,128)(2,1)S(1)} %get-tuple-element.32), channel_id=1, source_target_pairs={{0,1},{1,2},{2,3},{3,4},{4,5},{5,6},{6,7},{8,9},{9,10},{10,11},{11... | collective-permute-start | bytes 393224 | tf_op jit(solution)/shard_map/ppermute | solution.py:18
  6.9 1.9 collective-permute-start.1
  8.9 1.9 convert_reduce_fusion
  10.9 0.5 fusion.36
  11.4 0.0 copy-start.5
  11.4 0.0 copy-start.8
  11.5 0.0 copy-start.15
  11.5 1.5 fusion.10
  12.9 0.1 sub.16
  13.1 0.3 fusion.72
  13.4 6.9 %fusion.20 = bf16[4,1024,256]{2,1,0:T(8,128)(2,1)S(1)} fusion(s32[4,1024]{1,0:T(4,128)S(1)} %bitcast.103, bf16[256,256]{1,0:T(8,128)(2,1)S(1)} %collective-permute-done.1, bf16[256,256]{1,0:T(8,128)(2,1)S(1)} %collective-permute-done, bf16[1024,256]{1,0:T(8,128)(2,1)S(1)} %copy-done.5), kind=kOutput, calls=%fused_computation.29 | convolution fusion | flops 3230924800 | bytes 2899968 | tf_op jit(solution)/shard_map/ter,rd->ted/dot_general | solution.py:83
  20.4 5.8 %fusion.4 = f32[4,1024,256]{2,1,0:T(8,128)S(1)} fusion(bf16[4,1024,256]{2,1,0:T(8,128)(2,1)S(1)} %fusion.20, s32[4,1024]{1,0:T(4,128)S(1)} %bitcast.101), kind=kOutput, calls=%fused_computation.7 | convolution fusion | flops 2151677952 | bytes 6307840 | tf_op jit(solution)/shard_map/tep,ted->tpd/dot_general | solution.py:86
  26.2 2.1 %fusion.28 = f32[1024,256]{1,0:T(8,128)S(1)} fusion(f32[1024,256]{1,0:T(8,128)S(1)} %fusion.72, f32[4,1024,256]{2,1,0:T(8,128)S(1)} %fusion.4, bf16[4,256,256]{2,1,0:T(8,128)(2,1)S(1)} %copy-done.1, f32[1024]{0:T(1024)S(1)} %add_divide_fusion.2), kind=kOutput, calls=%fused_computation.41 | convolution fusion | flops 3221749760 | bytes 6819840 | tf_op jit(solution)/shard_map/tpk,tkd->pd/dot_general | solution.py:36
  28.3 0.0 copy-start.7
  28.3 2.5 %fusion.16 = bf16[2048,256]{1,0:T(8,128)(2,1)S(1)} fusion(s32[1024]{0:T(1024)S(1)} %bitcast.97, f32[1024,256]{1,0:T(8,128)S(1)} %fusion.28), kind=kOutput, calls=%fused_computation.22 | convolution fusion | flops 1077673984 | bytes 2101248 | tf_op jit(solution)/shard_map/dot_general | solution.py:111
  30.9 1.1 pad_maximum_fusion
  32.0 6.1 %all-to-all-start = ((bf16[32,65,256]{2,1,0:T(8,128)(2,1)}), bf16[32,65,256]{2,1,0:T(8,128)(2,1)S(1)}, u32[]{:S(2)}, u32[]{:S(2)}) async-start(bf16[32,65,256]{2,1,0:T(8,128)(2,1)} %pad_maximum_fusion), calls=%async_computation | async-start | bytes 2359296 | tf_op jit(solution)/shard_map/all_to_all | solution.py:123
  38.2 29.8 %all-to-all-done = bf16[32,65,256]{2,1,0:T(8,128)(2,1)S(1)} async-done(((bf16[32,65,256]{2,1,0:T(8,128)(2,1)}), bf16[32,65,256]{2,1,0:T(8,128)(2,1)S(1)}, u32[]{:S(2)}, u32[]{:S(2)}) %all-to-all-start) | async-done | bytes 1064992 | tf_op jit(solution)/shard_map/all_to_all | solution.py:123
  68.0 0.1 eq.110
  68.1 0.1 slice.64
  68.2 1.1 fusion.33
  69.3 0.5 multiply_convert_fusion.2
  69.7 0.2 fusion.73
  70.0 0.4 multiply_convert_fusion.1
  70.4 2.0 convolution_convert_fusion
  72.4 3.7 %all-to-all-start.1 = ((bf16[32,64,256]{2,1,0:T(8,128)(2,1)}), bf16[32,64,256]{2,1,0:T(8,128)(2,1)}, u32[]{:S(2)}, u32[]{:S(2)}) async-start(bf16[32,64,256]{2,1,0:T(8,128)(2,1)} %bitcast.82), calls=%async_computation.1 | async-start | bytes 2097152 | tf_op jit(solution)/shard_map/all_to_all | solution.py:148
  76.1 0.3 fusion.74
  76.5 0.4 convolution_convert_fusion.1
  76.8 0.9 fusion.43
  77.8 25.5 %all-to-all-done.1 = bf16[32,64,256]{2,1,0:T(8,128)(2,1)} async-done(((bf16[32,64,256]{2,1,0:T(8,128)(2,1)}), bf16[32,64,256]{2,1,0:T(8,128)(2,1)}, u32[]{:S(2)}, u32[]{:S(2)}) %all-to-all-start.1) | async-done | bytes 1048608 | tf_op jit(solution)/shard_map/all_to_all | solution.py:148
  103.3 3.1 %all-to-all-start.4 = ((bf16[32,48,256]{2,1,0:T(8,128)(2,1)}), bf16[32,48,256]{2,1,0:T(8,128)(2,1)S(1)}, u32[]{:S(2)}, u32[]{:S(2)}) async-start(bf16[32,48,256]{2,1,0:T(8,128)(2,1)} %bitcast.26), calls=%async_computation.4 | async-start | bytes 1572864 | tf_op jit(solution)/shard_map/all_to_all | solution.py:47
  106.4 3.3 %fusion.30 = bf16[1024,256]{1,0:T(8,128)(2,1)S(1)} fusion(bf16[2048,256]{1,0:T(8,128)(2,1)} %bitcast.15, s32[1024]{0:T(1024)S(1)} %bitcast.98, f32[1024,256]{1,0:T(8,128)} %copy-done.7), kind=kOutput, calls=%fused_computation.43 | convolution fusion | flops 1078198272 | bytes 2625536 | tf_op jit(solution)/shard_map/dot_general | solution.py:155
  109.7 0.4 fusion.34
  110.1 3.3 %fusion.21 = bf16[4,1024,256]{2,1,0:T(8,128)(2,1)S(1)} fusion(s32[4,1024]{1,0:T(4,128)S(1)} %bitcast.102, bf16[1024,256]{1,0:T(8,128)(2,1)S(1)} %fusion.30, f32[1024]{0:T(1024)S(1)} %add_divide_fusion.2), kind=kOutput, calls=%fused_computation.30 | convolution fusion | flops 2153512960 | bytes 2641920 | tf_op jit(solution)/shard_map/tep,pd->ted/dot_general | solution.py:159
  113.4 0.9 convolution_convert_fusion.2
  114.3 0.4 copy-done.4
  114.8 0.9 fusion.42
  115.7 12.2 %all-to-all-done.4 = bf16[32,48,256]{2,1,0:T(8,128)(2,1)S(1)} async-done(((bf16[32,48,256]{2,1,0:T(8,128)(2,1)}), bf16[32,48,256]{2,1,0:T(8,128)(2,1)S(1)}, u32[]{:S(2)}, u32[]{:S(2)}) %all-to-all-start.4) | async-done | bytes 786464 | tf_op jit(solution)/shard_map/all_to_all | solution.py:47
  127.9 3.1 %all-to-all-start.2 = ((bf16[32,48,256]{2,1,0:T(8,128)(2,1)}), bf16[32,48,256]{2,1,0:T(8,128)(2,1)S(1)}, u32[]{:S(2)}, u32[]{:S(2)}) async-start(bf16[32,48,256]{2,1,0:T(8,128)(2,1)} %bitcast.20), calls=%async_computation.2 | async-start | bytes 1572864 | tf_op jit(solution)/shard_map/all_to_all | solution.py:47
  131.0 0.3 fusion.48
  131.3 21.2 %all-to-all-done.2 = bf16[32,48,256]{2,1,0:T(8,128)(2,1)S(1)} async-done(((bf16[32,48,256]{2,1,0:T(8,128)(2,1)}), bf16[32,48,256]{2,1,0:T(8,128)(2,1)S(1)}, u32[]{:S(2)}, u32[]{:S(2)}) %all-to-all-start.2) | async-done | bytes 786464 | tf_op jit(solution)/shard_map/all_to_all | solution.py:47
  152.5 0.9 broadcast_in_dim.5
  153.5 3.7 %all-to-all-start.5 = ((bf16[32,48,256]{2,1,0:T(8,128)(2,1)}), bf16[32,48,256]{2,1,0:T(8,128)(2,1)}, u32[]{:S(2)}, u32[]{:S(2)}) async-start(bf16[32,48,256]{2,1,0:T(8,128)(2,1)} %broadcast_in_dim.5), calls=%async_computation.5 | async-start | bytes 1572864 | tf_op jit(solution)/shard_map/all_to_all | solution.py:54
  157.2 5.9 %fusion = f32[4,1536,256]{2,1,0:T(8,128)S(1)} fusion(bf16[4,1024,256]{2,1,0:T(8,128)(2,1)} %copy-done.4, s32[4,1024]{1,0:T(4,128)S(1)} %bitcast.104), kind=kOutput, calls=%fused_computation.1 | convolution fusion | flops 3227516928 | bytes 8404992 | tf_op jit(solution)/shard_map/ter,ted->trd/dot_general | solution.py:163
  163.1 3.1 %fusion.71 = (bf16[1536,256]{1,0:T(8,128)(2,1)S(1)}, f32[1536,256]{1,0:T(8,128)S(1)}) fusion(f32[4,1536,256]{2,1,0:T(8,128)S(1)} %fusion, bf16[4,256,256]{2,1,0:T(8,128)(2,1)S(1)} %copy-done.1), kind=kOutput, calls=%fused_computation.111 | convolution fusion | flops 4832231424 | bytes 9175040 | tf_op jit(solution)/shard_map/trd,tkd->rk/dot_general | solution.py:36
  166.2 0.7 fusion.69
  166.9 3.6 %collective-permute-start.2 = (bf16[256,256]{1,0:T(8,128)(2,1)}, bf16[256,256]{1,0:T(8,128)(2,1)}, u32[]{:S(2)}, u32[]{:S(2)}) collective-permute-start(bf16[256,256]{1,0:T(8,128)(2,1)} %get-tuple-element.30), channel_id=1, source_target_pairs={{0,1},{1,2},{2,3},{3,4},{4,5},{5,6},{6,7},{8,9},{9,10},{10,11},{11... | collective-permute-start | bytes 393224 | tf_op jit(solution)/shard_map/ppermute | solution.py:18
  170.5 1.9 collective-permute-start.3
  172.4 0.3 fusion.50
  172.7 6.0 %all-to-all-done.5 = bf16[32,48,256]{2,1,0:T(8,128)(2,1)} async-done(((bf16[32,48,256]{2,1,0:T(8,128)(2,1)}), bf16[32,48,256]{2,1,0:T(8,128)(2,1)}, u32[]{:S(2)}, u32[]{:S(2)}) %all-to-all-start.5) | async-done | bytes 786464 | tf_op jit(solution)/shard_map/all_to_all | solution.py:54
  178.8 0.9 broadcast_in_dim.4
  179.7 3.3 %all-to-all-start.3 = ((bf16[32,48,256]{2,1,0:T(8,128)(2,1)}), bf16[32,48,256]{2,1,0:T(8,128)(2,1)S(1)}, u32[]{:S(2)}, u32[]{:S(2)}) async-start(bf16[32,48,256]{2,1,0:T(8,128)(2,1)} %broadcast_in_dim.4), calls=%async_computation.3 | async-start | bytes 1572864 | tf_op jit(solution)/shard_map/all_to_all | solution.py:54
  183.0 1.4 convolution_add_fusion
  184.4 2.6 %fusion.31 = bf16[1024,256]{1,0:T(8,128)(2,1)} fusion(f32[1024,256]{1,0:T(8,128)S(1)} %convolution_add_fusion, s32[512]{0:T(512)S(1)} %bitcast.106, bf16[256,256]{1,0:T(8,128)(2,1)} %collective-permute-done.3, bf16[256,256]{1,0:T(8,128)(2,1)} %collective-permute-done.2), kind=kOutput, calls=%fused_computation.45 | convolution fusion | flops 270008320 | bytes 1837056 | tf_op jit(solution)/shard_map/sp,sd->pd/dot_general | solution.py:173
  187.0 1.1 slice_convert_fusion.1
  188.2 0.1 fusion.37
  188.3 1.3 copy.33
  189.6 0.6 copy.42
  190.2 14.4 %all-to-all-done.3 = bf16[32,48,256]{2,1,0:T(8,128)(2,1)S(1)} async-done(((bf16[32,48,256]{2,1,0:T(8,128)(2,1)}), bf16[32,48,256]{2,1,0:T(8,128)(2,1)S(1)}, u32[]{:S(2)}, u32[]{:S(2)}) %all-to-all-start.3) | async-done | bytes 786464 | tf_op jit(solution)/shard_map/all_to_all | solution.py:54
  204.5 0.1 slice_convert_fusion
  204.6 0.7 slice_multiply_fusion.2
  205.4 1.1 slice_multiply_fusion.1
  (52 shorter events, 0.3 us)
Async XLA Ops:
  0.6 68.6 %copy-start = (bf16[256,1024]{1,0:T(8,128)(2,1)S(1)}, bf16[256,1024]{1,0:T(8,128)(2,1)}, u32[]{:S(2)}) copy-start(bf16[256,1024]{1,0:T(8,128)(2,1)} %param.14) | copy-start | bytes 1572868
  0.6 8.2 %copy-start.12 = (s32[1024]{0:T(1024)S(1)}, s32[1024]{0:T(1024)}, u32[]{:S(2)}) copy-start(s32[1024]{0:T(1024)} %param.20) | copy-start | bytes 12292
  0.7 8.2 %copy-start.14 = (s32[1,4,1024]{2,1,0:T(4,128)S(1)}, s32[1,4,1024]{2,1,0:T(4,128)}, u32[]{:S(2)}) copy-start(s32[1,4,1024]{2,1,0:T(4,128)} %param.18) | copy-start | bytes 49156
  0.7 10.2 %copy-start.11 = (s32[1024,1]{0,1:T(1,128)S(1)}, s32[1024,1]{0,1:T(1,128)}, u32[]{:S(2)}) copy-start(s32[1024,1]{0,1:T(1,128)} %param.19) | copy-start | bytes 12292
  2.3 11.1 %collective-permute-start = (bf16[256,256]{1,0:T(8,128)(2,1)S(1)}, bf16[256,256]{1,0:T(8,128)(2,1)S(1)}, u32[]{:S(2)}, u32[]{:S(2)}) collective-permute-start(bf16[256,256]{1,0:T(8,128)(2,1)S(1)} %get-tuple-element.32), channel_id=1, source_target_pairs={{0,1},{1,2},{2,3},{3,4},{4,5},{5,6},{6,7},{8,9},{9,10},{10,11},{11... | collective-permute-start | bytes 393224 | tf_op jit(solution)/shard_map/ppermute | solution.py:18
  6.9 6.5 %collective-permute-start.1 = (bf16[256,256]{1,0:T(8,128)(2,1)S(1)}, bf16[256,256]{1,0:T(8,128)(2,1)S(1)}, u32[]{:S(2)}, u32[]{:S(2)}) collective-permute-start(bf16[256,256]{1,0:T(8,128)(2,1)S(1)} %get-tuple-element.33), channel_id=1, source_target_pairs={{1,0},{2,1},{3,2},{4,3},{5,4},{6,5},{7,6},{9,8},{10,9},{11,10},{12... | collective-permute-start | bytes 393224 | tf_op jit(solution)/shard_map/ppermute | solution.py:21
  11.4 1.7 copy-start.5
  11.4 1.7 copy-start.8
  11.5 2.0 copy-start.15
  20.4 5.8 %copy-start.2 = (bf16[4,1024,256]{2,1,0:T(8,128)(2,1)}, bf16[4,1024,256]{2,1,0:T(8,128)(2,1)S(1)}, u32[]{:S(2)}) copy-start(bf16[4,1024,256]{2,1,0:T(8,128)(2,1)S(1)} %fusion.20) | copy-start | bytes 6291460
  20.4 5.8 %copy-start.1 = (bf16[4,256,256]{2,1,0:T(8,128)(2,1)S(1)}, bf16[4,256,256]{2,1,0:T(8,128)(2,1)}, u32[]{:S(2)}) copy-start(bf16[4,256,256]{2,1,0:T(8,128)(2,1)} %param.13) | copy-start | bytes 1572868
  28.3 2.6 %copy-start.7 = (f32[1024,256]{1,0:T(8,128)}, f32[1024,256]{1,0:T(8,128)S(1)}, u32[]{:S(2)}) copy-start(f32[1024,256]{1,0:T(8,128)S(1)} %fusion.28) | copy-start | bytes 3145732
  30.8 7.3 %copy-start.9 = (bf16[1024]{0:T(1024)(128)(2,1)S(1)}, bf16[1024]{0:T(1024)(128)(2,1)}, u32[]{:S(2)}) copy-start(bf16[1024]{0:T(1024)(128)(2,1)} %param.15) | copy-start | bytes 6148
  32.0 36.0 %all-to-all-start = ((bf16[32,65,256]{2,1,0:T(8,128)(2,1)}), bf16[32,65,256]{2,1,0:T(8,128)(2,1)S(1)}, u32[]{:S(2)}, u32[]{:S(2)}) async-start(bf16[32,65,256]{2,1,0:T(8,128)(2,1)} %pad_maximum_fusion), calls=%async_computation | async-start | bytes 2359296 | tf_op jit(solution)/shard_map/all_to_all | solution.py:123
  69.3 0.7 copy-start.13
  70.0 2.4 %copy-start.10 = (f32[1,256]{1,0:T(1,128)}, f32[1,256]{1,0:T(1,128)S(1)}, u32[]{:S(2)}) copy-start(f32[1,256]{1,0:T(1,128)S(1)} %fusion.73) | copy-start | bytes 3076
  72.4 30.9 %all-to-all-start.1 = ((bf16[32,64,256]{2,1,0:T(8,128)(2,1)}), bf16[32,64,256]{2,1,0:T(8,128)(2,1)}, u32[]{:S(2)}, u32[]{:S(2)}) async-start(bf16[32,64,256]{2,1,0:T(8,128)(2,1)} %bitcast.82), calls=%async_computation.1 | async-start | bytes 2097152 | tf_op jit(solution)/shard_map/all_to_all | solution.py:148
  103.3 24.6 %all-to-all-start.4 = ((bf16[32,48,256]{2,1,0:T(8,128)(2,1)}), bf16[32,48,256]{2,1,0:T(8,128)(2,1)S(1)}, u32[]{:S(2)}, u32[]{:S(2)}) async-start(bf16[32,48,256]{2,1,0:T(8,128)(2,1)} %bitcast.26), calls=%async_computation.4 | async-start | bytes 1572864 | tf_op jit(solution)/shard_map/all_to_all | solution.py:47
  109.7 3.7 %copy-start.6 = (bf16[1024,256]{1,0:T(8,128)(2,1)}, bf16[1024,256]{1,0:T(8,128)(2,1)S(1)}, u32[]{:S(2)}) copy-start(bf16[1024,256]{1,0:T(8,128)(2,1)S(1)} %fusion.30) | copy-start | bytes 1572868
  110.1 3.3 %copy-start.3 = (bf16[4,1024,256]{2,1,0:T(8,128)(2,1)S(1)}, bf16[4,1024,256]{2,1,0:T(8,128)(2,1)}, u32[]{:S(2)}) copy-start(bf16[4,1024,256]{2,1,0:T(8,128)(2,1)} %copy-done.2) | copy-start | bytes 6291460
  113.4 1.3 copy-start.4
  127.9 24.6 %all-to-all-start.2 = ((bf16[32,48,256]{2,1,0:T(8,128)(2,1)}), bf16[32,48,256]{2,1,0:T(8,128)(2,1)S(1)}, u32[]{:S(2)}, u32[]{:S(2)}) async-start(bf16[32,48,256]{2,1,0:T(8,128)(2,1)} %bitcast.20), calls=%async_computation.2 | async-start | bytes 1572864 | tf_op jit(solution)/shard_map/all_to_all | solution.py:47
  153.5 25.3 %all-to-all-start.5 = ((bf16[32,48,256]{2,1,0:T(8,128)(2,1)}), bf16[32,48,256]{2,1,0:T(8,128)(2,1)}, u32[]{:S(2)}, u32[]{:S(2)}) async-start(bf16[32,48,256]{2,1,0:T(8,128)(2,1)} %broadcast_in_dim.5), calls=%async_computation.5 | async-start | bytes 1572864 | tf_op jit(solution)/shard_map/all_to_all | solution.py:54
  166.9 17.5 %collective-permute-start.2 = (bf16[256,256]{1,0:T(8,128)(2,1)}, bf16[256,256]{1,0:T(8,128)(2,1)}, u32[]{:S(2)}, u32[]{:S(2)}) collective-permute-start(bf16[256,256]{1,0:T(8,128)(2,1)} %get-tuple-element.30), channel_id=1, source_target_pairs={{0,1},{1,2},{2,3},{3,4},{4,5},{5,6},{6,7},{8,9},{9,10},{10,11},{11... | collective-permute-start | bytes 393224 | tf_op jit(solution)/shard_map/ppermute | solution.py:18
  170.5 13.9 %collective-permute-start.3 = (bf16[256,256]{1,0:T(8,128)(2,1)}, bf16[256,256]{1,0:T(8,128)(2,1)}, u32[]{:S(2)}, u32[]{:S(2)}) collective-permute-start(bf16[256,256]{1,0:T(8,128)(2,1)} %get-tuple-element.31), channel_id=1, source_target_pairs={{1,0},{2,1},{3,2},{4,3},{5,4},{6,5},{7,6},{9,8},{10,9},{11,10},{12... | collective-permute-start | bytes 393224 | tf_op jit(solution)/shard_map/ppermute | solution.py:21
  179.7 4.7 %copy-start.16 = (s32[1,512]{1,0:T(1,128)S(1)}, s32[1,512]{1,0:T(1,128)}, u32[]{:S(2)}) copy-start(s32[1,512]{1,0:T(1,128)} %param.16) | copy-start | bytes 6148
  179.7 24.8 %all-to-all-start.3 = ((bf16[32,48,256]{2,1,0:T(8,128)(2,1)}), bf16[32,48,256]{2,1,0:T(8,128)(2,1)S(1)}, u32[]{:S(2)}, u32[]{:S(2)}) async-start(bf16[32,48,256]{2,1,0:T(8,128)(2,1)} %broadcast_in_dim.4), calls=%async_computation.3 | async-start | bytes 1572864 | tf_op jit(solution)/shard_map/all_to_all | solution.py:54

commit v2 on v0

--- a/solution.py
+++ b/solution.py
@@ -47,7 +47,9 @@
     mine = lax.all_to_all(
         rows.astype(BF16).reshape(owners, -1, width), axes, split_axis=0, concat_axis=0, tiled=True
     )
-    mine = jnp.sum(mine.astype(F32), axis=0).astype(BF16)
+    mine = jnp.einsum(
+        "o,orw->rw", jnp.ones((owners,), BF16), mine, preferred_element_type=F32
+    ).astype(BF16)
     spread = jnp.broadcast_to(mine[None], (owners,) + mine.shape)
     gathered = lax.all_to_all(spread, axes, split_axis=0, concat_axis=0, tiled=True)
     return gathered.reshape(length, width)[:count].astype(F32)

time: 189 us -> 190 us (level)
  no operation moved by 1% of the time
where the time goes in v2:
time: 190 us; the launch traced here: 188 us
  waiting for transfers between devices  72.5 us (38%)
  matrix products  44.8 us (24%)
  blocking collectives  35.6 us (19%)
  starting transfers between devices  24.6 us (13%)
  other arithmetic  5.71 us (3%)
  local copies, waits for them, and re-layouts  4 us (2%)
    all_to_all x1, blocking collectives, all_sum(): lax.all_to_all(rows.astype(BF16).reshape(owners, -1, width), axes, split_...  35.6 us
    all_to_all x1, waiting for transfers between devices, on_device(): lax.all_to_all(packet, ('group', 'dom'), split_axis=0, concat_axis=0, til...  29.8 us
    all_to_all x1, waiting for transfers between devices, on_device(): lax.all_to_all(returned.reshape(owners, capacity, feat_width), ('group',...  26.5 us
    ppermute x2, waiting for transfers between devices, extended(): lax.ppermute(lax.slice_in_dim(block, block.shape[dim] - width, None, axis...  8.2 us
    ppermute x2, starting transfers between devices, extended(): lax.ppermute(lax.slice_in_dim(block, block.shape[dim] - width, None, axis...  8.19 us
    all_to_all x1, waiting for transfers between devices, all_sum(): lax.all_to_all(spread, axes, split_axis=0, concat_axis=0, tiled=True)  8.05 us
    dot_general x1, matrix products, on_device(): jnp.einsum('ter,rd->ted', src_hot, node_table, preferred_element_type=F32)  6.93 us
    all_to_all x1, starting transfers between devices, on_device(): lax.all_to_all(packet, ('group', 'dom'), split_axis=0, concat_axis=0, til...  6.14 us
  transfers between devices with their start and end apart: 7, of which 4 were waited for; matrix products, arithmetic and copies ran while one was open for 9% of the time, Pallas kernels for 0%

profile of v2, /device:TPU:1, one launch (start us, length us, event | category | flops | bytes accessed | tf_op | source)
XLA Modules:
  0.0 188.4 jit_solution(13762378819026697280)
XLA Ops:
  0.6 0.0 copy-start
  0.6 0.0 copy-start.11
  0.7 0.0 copy-start.13
  0.7 0.0 copy-start.10
  0.7 1.6 fusion.37
  2.3 4.6 %collective-permute-start = (bf16[256,256]{1,0:T(8,128)(2,1)S(1)}, bf16[256,256]{1,0:T(8,128)(2,1)S(1)}, u32[]{:S(2)}, u32[]{:S(2)}) collective-permute-start(bf16[256,256]{1,0:T(8,128)(2,1)S(1)} %get-tuple-element.34), channel_id=1, source_target_pairs={{0,1},{1,2},{2,3},{3,4},{4,5},{5,6},{6,7},{8,9},{9,10},{10,11},{11... | collective-permute-start | bytes 393224 | tf_op jit(solution)/shard_map/ppermute | solution.py:18
  6.9 1.9 %collective-permute-start.1 = (bf16[256,256]{1,0:T(8,128)(2,1)S(1)}, bf16[256,256]{1,0:T(8,128)(2,1)S(1)}, u32[]{:S(2)}, u32[]{:S(2)}) collective-permute-start(bf16[256,256]{1,0:T(8,128)(2,1)S(1)} %get-tuple-element.35), channel_id=1, source_target_pairs={{1,0},{2,1},{3,2},{4,3},{5,4},{6,5},{7,6},{9,8},{10,9},{11,10},{12... | collective-permute-start | bytes 393224 | tf_op jit(solution)/shard_map/ppermute | solution.py:21
  8.9 1.9 %convert_reduce_fusion = f32[1024]{0:T(1024)S(1)} fusion(s32[4,1024]{1,0:T(4,128)S(1)} %bitcast.95), kind=kLoop, calls=%fused_computation.3 | loop fusion | flops 16776192 | bytes 20480 | tf_op jit(solution)/shard_map/reduce_sum | solution.py:88
  10.9 0.5 fusion.41
  11.4 0.0 copy-start.5
  11.4 0.0 copy-start.7
  11.5 0.0 copy-start.14
  11.5 1.5 fusion.10
  12.9 0.1 sub.16
  13.1 0.3 fusion.69
  13.4 0.0 collective-permute-done
  13.4 0.0 collective-permute-done.1
  13.4 6.9 %fusion.24 = bf16[4,1024,256]{2,1,0:T(8,128)(2,1)S(1)} fusion(s32[4,1024]{1,0:T(4,128)S(1)} %bitcast.98, bf16[256,256]{1,0:T(8,128)(2,1)S(1)} %collective-permute-done.1, bf16[256,256]{1,0:T(8,128)(2,1)S(1)} %collective-permute-done, bf16[1024,256]{1,0:T(8,128)(2,1)S(1)} %copy-done.5), kind=kOutput, calls=%fused_computation.34 | convolution fusion | flops 3230924800 | bytes 2899968 | tf_op jit(solution)/shard_map/ter,rd->ted/dot_general | solution.py:83
  20.4 0.0 copy-start.1
  20.4 5.8 %fusion.4 = f32[4,1024,256]{2,1,0:T(8,128)S(1)} fusion(bf16[4,1024,256]{2,1,0:T(8,128)(2,1)S(1)} %fusion.24, s32[4,1024]{1,0:T(4,128)S(1)} %bitcast.96), kind=kOutput, calls=%fused_computation.7 | convolution fusion | flops 2151677952 | bytes 6307840 | tf_op jit(solution)/shard_map/tep,ted->tpd/dot_general | solution.py:86
  26.2 2.1 %fusion.28 = f32[1024,256]{1,0:T(8,128)S(1)} fusion(f32[1024,256]{1,0:T(8,128)S(1)} %fusion.69, f32[4,1024,256]{2,1,0:T(8,128)S(1)} %fusion.4, bf16[4,256,256]{2,1,0:T(8,128)(2,1)S(1)} %copy-done.1, f32[1024]{0:T(1024)S(1)} %add_divide_fusion.2), kind=kOutput, calls=%fused_computation.40 | convolution fusion | flops 3221749760 | bytes 6819840 | tf_op jit(solution)/shard_map/tpk,tkd->pd/dot_general | solution.py:36
  28.3 0.0 copy-start.6
  28.3 2.5 %fusion.20 = bf16[2048,256]{1,0:T(8,128)(2,1)S(1)} fusion(s32[1024]{0:T(1024)S(1)} %bitcast.92, f32[1024,256]{1,0:T(8,128)S(1)} %fusion.28), kind=kOutput, calls=%fused_computation.27 | convolution fusion | flops 1077673984 | bytes 2101248 | tf_op jit(solution)/shard_map/dot_general | solution.py:111
  30.9 0.0 copy-start.8
  30.9 1.1 pad_maximum_fusion
  32.0 6.1 %all-to-all-start = ((bf16[32,65,256]{2,1,0:T(8,128)(2,1)}), bf16[32,65,256]{2,1,0:T(8,128)(2,1)S(1)}, u32[]{:S(2)}, u32[]{:S(2)}) async-start(bf16[32,65,256]{2,1,0:T(8,128)(2,1)} %pad_maximum_fusion), calls=%async_computation | async-start | bytes 2359296 | tf_op jit(solution)/shard_map/all_to_all | solution.py:123
  38.2 29.8 %all-to-all-done = bf16[32,65,256]{2,1,0:T(8,128)(2,1)S(1)} async-done(((bf16[32,65,256]{2,1,0:T(8,128)(2,1)}), bf16[32,65,256]{2,1,0:T(8,128)(2,1)S(1)}, u32[]{:S(2)}, u32[]{:S(2)}) %all-to-all-start) | async-done | bytes 1064992 | tf_op jit(solution)/shard_map/all_to_all | solution.py:123
  68.0 0.1 eq.110
  68.1 0.1 slice.60
  68.2 1.1 fusion.38
  69.3 0.0 copy-start.12
  69.3 0.5 multiply_convert_fusion.2
  69.7 0.2 fusion.70
  70.0 0.4 multiply_convert_fusion.1
  70.4 2.0 %convolution_convert_fusion = bf16[2048,256]{1,0:T(8,128)(2,1)} fusion(bf16[256,1024]{1,0:T(8,128)(2,1)S(1)} %multiply_convert_fusion.1, bf16[256,1024]{1,0:T(8,128)(2,1)S(1)} %copy-done, s32[2048]{0:T(1024)S(1)} %eq.110), kind=kOutput, calls=%fused_computation.28 | convolution fusion | flops 403767296 | bytes 2105344 | tf_op jit(solution)/shard_map/dot_general | solution.py:143
  72.4 3.8 %all-to-all-start.1 = ((bf16[32,64,256]{2,1,0:T(8,128)(2,1)}), bf16[32,64,256]{2,1,0:T(8,128)(2,1)}, u32[]{:S(2)}, u32[]{:S(2)}) async-start(bf16[32,64,256]{2,1,0:T(8,128)(2,1)} %bitcast.78), calls=%async_computation.1 | async-start | bytes 2097152 | tf_op jit(solution)/shard_map/all_to_all | solution.py:144
  76.2 0.3 fusion.71
  76.5 0.4 convolution_convert_fusion.1
  76.9 26.5 %all-to-all-done.1 = bf16[32,64,256]{2,1,0:T(8,128)(2,1)} async-done(((bf16[32,64,256]{2,1,0:T(8,128)(2,1)}), bf16[32,64,256]{2,1,0:T(8,128)(2,1)}, u32[]{:S(2)}, u32[]{:S(2)}) %all-to-all-start.1) | async-done | bytes 1048608 | tf_op jit(solution)/shard_map/all_to_all | solution.py:144
  103.3 3.3 %fusion.35 = bf16[1024,256]{1,0:T(8,128)(2,1)S(1)} fusion(bf16[2048,256]{1,0:T(8,128)(2,1)} %bitcast.15, s32[1024]{0:T(1024)S(1)} %bitcast.93, f32[1024,256]{1,0:T(8,128)} %copy-done.6), kind=kOutput, calls=%fused_computation.47 | convolution fusion | flops 1078198272 | bytes 2625536 | tf_op jit(solution)/shard_map/dot_general | solution.py:151
  106.6 0.4 fusion.39
  107.0 3.3 %fusion.25 = bf16[4,1024,256]{2,1,0:T(8,128)(2,1)S(1)} fusion(s32[4,1024]{1,0:T(4,128)S(1)} %bitcast.97, bf16[1024,256]{1,0:T(8,128)(2,1)S(1)} %fusion.35, f32[1024]{0:T(1024)S(1)} %add_divide_fusion.2), kind=kOutput, calls=%fused_computation.35 | convolution fusion | flops 2153512960 | bytes 2641920 | tf_op jit(solution)/shard_map/tep,pd->ted/dot_general | solution.py:155
  110.3 0.9 convolution_convert_fusion.2
  111.2 0.4 copy-done.4
  111.7 0.1 fusion.32
  111.7 35.6 %all_to_all.20 = bf16[32,80,256]{2,1,0:T(8,128)(2,1)S(1)} all-to-all(bf16[32,80,256]{2,1,0:T(8,128)(2,1)S(1)} %bitcast.75), channel_id=1, replica_groups=mesh['group'=4,'dom'=8] {'group','dom'}, dimensions={0} | all-to-all | bytes 2621440 | tf_op jit(solution)/shard_map/all_to_all | solution.py:47
  147.3 0.5 fusion.33
  147.8 1.2 broadcast_in_dim.5
  149.0 2.7 %all-to-all-start.3 = ((bf16[32,80,256]{2,1,0:T(8,128)(2,1)}), bf16[32,80,256]{2,1,0:T(8,128)(2,1)S(1)}, u32[]{:S(2)}, u32[]{:S(2)}) async-start(bf16[32,80,256]{2,1,0:T(8,128)(2,1)} %broadcast_in_dim.5), calls=%async_computation.3 | async-start | bytes 2621440 | tf_op jit(solution)/shard_map/all_to_all | solution.py:54
  151.7 5.9 %fusion = f32[4,1536,256]{2,1,0:T(8,128)S(1)} fusion(bf16[4,1024,256]{2,1,0:T(8,128)(2,1)} %copy-done.4, s32[4,1024]{1,0:T(4,128)S(1)} %bitcast.99), kind=kOutput, calls=%fused_computation.1 | convolution fusion | flops 3227516928 | bytes 8404992 | tf_op jit(solution)/shard_map/ter,ted->trd/dot_general | solution.py:159
  157.5 3.1 %fusion.68 = (bf16[1536,256]{1,0:T(8,128)(2,1)S(1)}, f32[1536,256]{1,0:T(8,128)S(1)}) fusion(f32[4,1536,256]{2,1,0:T(8,128)S(1)} %fusion, bf16[4,256,256]{2,1,0:T(8,128)(2,1)S(1)} %copy-done.1), kind=kOutput, calls=%fused_computation.105 | convolution fusion | flops 4832231424 | bytes 9175040 | tf_op jit(solution)/shard_map/trd,tkd->rk/dot_general | solution.py:36
  160.6 0.0 copy-start.16
  160.7 3.6 %collective-permute-start.2 = (bf16[256,256]{1,0:T(8,128)(2,1)S(1)}, bf16[256,256]{1,0:T(8,128)(2,1)S(1)}, u32[]{:S(2)}, u32[]{:S(2)}) collective-permute-start(bf16[256,256]{1,0:T(8,128)(2,1)S(1)} %get-tuple-element.32), channel_id=1, source_target_pairs={{0,1},{1,2},{2,3},{3,4},{4,5},{5,6},{6,7},{8,9},{9,10},{10,11},{11... | collective-permute-start | bytes 393224 | tf_op jit(solution)/shard_map/ppermute | solution.py:18
  164.3 1.9 %collective-permute-start.3 = (bf16[256,256]{1,0:T(8,128)(2,1)S(1)}, bf16[256,256]{1,0:T(8,128)(2,1)S(1)}, u32[]{:S(2)}, u32[]{:S(2)}) collective-permute-start(bf16[256,256]{1,0:T(8,128)(2,1)S(1)} %get-tuple-element.33), channel_id=1, source_target_pairs={{1,0},{2,1},{3,2},{4,3},{5,4},{6,5},{7,6},{9,8},{10,9},{11,10},{12... | collective-permute-start | bytes 393224 | tf_op jit(solution)/shard_map/ppermute | solution.py:21
  166.2 0.3 convolution_add_fusion
  166.5 8.2 %collective-permute-done.2 = bf16[256,256]{1,0:T(8,128)(2,1)S(1)} collective-permute-done((bf16[256,256]{1,0:T(8,128)(2,1)S(1)}, bf16[256,256]{1,0:T(8,128)(2,1)S(1)}, u32[]{:S(2)}, u32[]{:S(2)}) %collective-permute-start.2) | collective-permute-done | bytes 131104 | tf_op jit(solution)/shard_map/ppermute | solution.py:18
  174.7 0.0 collective-permute-done.3
  174.8 1.6 fusion.36
  176.4 8.0 %all-to-all-done.3 = bf16[32,80,256]{2,1,0:T(8,128)(2,1)S(1)} async-done(((bf16[32,80,256]{2,1,0:T(8,128)(2,1)}), bf16[32,80,256]{2,1,0:T(8,128)(2,1)S(1)}, u32[]{:S(2)}, u32[]{:S(2)}) %all-to-all-start.3) | async-done | bytes 1310752 | tf_op jit(solution)/shard_map/all_to_all | solution.py:54
  184.4 0.2 slice_convert_fusion
  184.6 0.7 slice_multiply_fusion.2
  185.4 1.2 fusion.42
  186.5 0.6 copy.40
  187.1 1.3 copy.33
  (41 shorter events, 0.2 us)
Async XLA Ops:
  0.6 68.6 %copy-start = (bf16[256,1024]{1,0:T(8,128)(2,1)S(1)}, bf16[256,1024]{1,0:T(8,128)(2,1)}, u32[]{:S(2)}) copy-start(bf16[256,1024]{1,0:T(8,128)(2,1)} %param.14) | copy-start | bytes 1572868
  0.6 8.2 %copy-start.11 = (s32[1024]{0:T(1024)S(1)}, s32[1024]{0:T(1024)}, u32[]{:S(2)}) copy-start(s32[1024]{0:T(1024)} %param.20) | copy-start | bytes 12292
  0.7 8.2 %copy-start.13 = (s32[1,4,1024]{2,1,0:T(4,128)S(1)}, s32[1,4,1024]{2,1,0:T(4,128)}, u32[]{:S(2)}) copy-start(s32[1,4,1024]{2,1,0:T(4,128)} %param.18) | copy-start | bytes 49156
  0.7 10.2 %copy-start.10 = (s32[1024,1]{0,1:T(1,128)S(1)}, s32[1024,1]{0,1:T(1,128)}, u32[]{:S(2)}) copy-start(s32[1024,1]{0,1:T(1,128)} %param.19) | copy-start | bytes 12292
  2.3 11.1 %collective-permute-start = (bf16[256,256]{1,0:T(8,128)(2,1)S(1)}, bf16[256,256]{1,0:T(8,128)(2,1)S(1)}, u32[]{:S(2)}, u32[]{:S(2)}) collective-permute-start(bf16[256,256]{1,0:T(8,128)(2,1)S(1)} %get-tuple-element.34), channel_id=1, source_target_pairs={{0,1},{1,2},{2,3},{3,4},{4,5},{5,6},{6,7},{8,9},{9,10},{10,11},{11... | collective-permute-start | bytes 393224 | tf_op jit(solution)/shard_map/ppermute | solution.py:18
  6.9 6.5 %collective-permute-start.1 = (bf16[256,256]{1,0:T(8,128)(2,1)S(1)}, bf16[256,256]{1,0:T(8,128)(2,1)S(1)}, u32[]{:S(2)}, u32[]{:S(2)}) collective-permute-start(bf16[256,256]{1,0:T(8,128)(2,1)S(1)} %get-tuple-element.35), channel_id=1, source_target_pairs={{1,0},{2,1},{3,2},{4,3},{5,4},{6,5},{7,6},{9,8},{10,9},{11,10},{12... | collective-permute-start | bytes 393224 | tf_op jit(solution)/shard_map/ppermute | solution.py:21
  11.4 1.7 copy-start.5
  11.4 1.7 copy-start.7
  11.5 2.0 %copy-start.14 = (s32[1,4,1024]{2,1,0:T(4,128)S(1)}, s32[1,4,1024]{2,1,0:T(4,128)}, u32[]{:S(2)}) copy-start(s32[1,4,1024]{2,1,0:T(4,128)} %param.17) | copy-start | bytes 49156
  20.4 5.8 %copy-start.2 = (bf16[4,1024,256]{2,1,0:T(8,128)(2,1)}, bf16[4,1024,256]{2,1,0:T(8,128)(2,1)S(1)}, u32[]{:S(2)}) copy-start(bf16[4,1024,256]{2,1,0:T(8,128)(2,1)S(1)} %fusion.24) | copy-start | bytes 6291460
  20.4 5.8 %copy-start.1 = (bf16[4,256,256]{2,1,0:T(8,128)(2,1)S(1)}, bf16[4,256,256]{2,1,0:T(8,128)(2,1)}, u32[]{:S(2)}) copy-start(bf16[4,256,256]{2,1,0:T(8,128)(2,1)} %param.13) | copy-start | bytes 1572868
  28.3 2.6 %copy-start.6 = (f32[1024,256]{1,0:T(8,128)}, f32[1024,256]{1,0:T(8,128)S(1)}, u32[]{:S(2)}) copy-start(f32[1024,256]{1,0:T(8,128)S(1)} %fusion.28) | copy-start | bytes 3145732
  30.9 7.3 %copy-start.8 = (bf16[1024]{0:T(1024)(128)(2,1)S(1)}, bf16[1024]{0:T(1024)(128)(2,1)}, u32[]{:S(2)}) copy-start(bf16[1024]{0:T(1024)(128)(2,1)} %param.15) | copy-start | bytes 6148
  32.0 36.0 %all-to-all-start = ((bf16[32,65,256]{2,1,0:T(8,128)(2,1)}), bf16[32,65,256]{2,1,0:T(8,128)(2,1)S(1)}, u32[]{:S(2)}, u32[]{:S(2)}) async-start(bf16[32,65,256]{2,1,0:T(8,128)(2,1)} %pad_maximum_fusion), calls=%async_computation | async-start | bytes 2359296 | tf_op jit(solution)/shard_map/all_to_all | solution.py:123
  69.3 0.7 copy-start.12
  70.0 2.4 %copy-start.9 = (f32[1,256]{1,0:T(1,128)}, f32[1,256]{1,0:T(1,128)S(1)}, u32[]{:S(2)}) copy-start(f32[1,256]{1,0:T(1,128)S(1)} %fusion.70) | copy-start | bytes 3076
  72.4 31.0 %all-to-all-start.1 = ((bf16[32,64,256]{2,1,0:T(8,128)(2,1)}), bf16[32,64,256]{2,1,0:T(8,128)(2,1)}, u32[]{:S(2)}, u32[]{:S(2)}) async-start(bf16[32,64,256]{2,1,0:T(8,128)(2,1)} %bitcast.78), calls=%async_computation.1 | async-start | bytes 2097152 | tf_op jit(solution)/shard_map/all_to_all | solution.py:144
  107.0 3.3 %copy-start.3 = (bf16[4,1024,256]{2,1,0:T(8,128)(2,1)S(1)}, bf16[4,1024,256]{2,1,0:T(8,128)(2,1)}, u32[]{:S(2)}) copy-start(bf16[4,1024,256]{2,1,0:T(8,128)(2,1)} %copy-done.2) | copy-start | bytes 6291460
  110.3 1.3 copy-start.4
  147.8 3.9 %copy-start.15 = (s32[1,4,1024]{2,1,0:T(4,128)S(1)}, s32[1,4,1024]{2,1,0:T(4,128)}, u32[]{:S(2)}) copy-start(s32[1,4,1024]{2,1,0:T(4,128)} %param.17) | copy-start | bytes 49156
  149.0 35.4 %all-to-all-start.3 = ((bf16[32,80,256]{2,1,0:T(8,128)(2,1)}), bf16[32,80,256]{2,1,0:T(8,128)(2,1)S(1)}, u32[]{:S(2)}, u32[]{:S(2)}) async-start(bf16[32,80,256]{2,1,0:T(8,128)(2,1)} %broadcast_in_dim.5), calls=%async_computation.3 | async-start | bytes 2621440 | tf_op jit(solution)/shard_map/all_to_all | solution.py:54
  160.6 14.1 %copy-start.16 = (s32[1,512]{1,0:T(1,128)S(1)}, s32[1,512]{1,0:T(1,128)}, u32[]{:S(2)}) copy-start(s32[1,512]{1,0:T(1,128)} %param.16) | copy-start | bytes 6148
  160.7 14.1 %collective-permute-start.2 = (bf16[256,256]{1,0:T(8,128)(2,1)S(1)}, bf16[256,256]{1,0:T(8,128)(2,1)S(1)}, u32[]{:S(2)}, u32[]{:S(2)}) collective-permute-start(bf16[256,256]{1,0:T(8,128)(2,1)S(1)} %get-tuple-element.32), channel_id=1, source_target_pairs={{0,1},{1,2},{2,3},{3,4},{4,5},{5,6},{6,7},{8,9},{9,10},{10,11},{11... | collective-permute-start | bytes 393224 | tf_op jit(solution)/shard_map/ppermute | solution.py:18
  164.3 10.5 %collective-permute-start.3 = (bf16[256,256]{1,0:T(8,128)(2,1)S(1)}, bf16[256,256]{1,0:T(8,128)(2,1)S(1)}, u32[]{:S(2)}, u32[]{:S(2)}) collective-permute-start(bf16[256,256]{1,0:T(8,128)(2,1)S(1)} %get-tuple-element.33), channel_id=1, source_target_pairs={{1,0},{2,1},{3,2},{4,3},{5,4},{6,5},{7,6},{9,8},{10,9},{11,10},{12... | collective-permute-start | bytes 393224 | tf_op jit(solution)/shard_map/ppermute | solution.py:21

commit v3 on v2

--- a/solution.py
+++ b/solution.py
@@ -109,22 +109,20 @@
     net_code = (pin_net + 1).astype(BF16)[:, None]
     slot_nets = jnp.dot(slot_hot.T, net_code, preferred_element_type=F32)[:, 0] - 1.0
     outbound = jnp.dot(slot_hot.T, hidden, preferred_element_type=F32).astype(BF16)
-    id_rows = -(-capacity // feat_width)
-    id_block = jnp.pad(
-        slot_nets.reshape(owners, capacity), ((0, 0), (0, id_rows * feat_width - capacity))
-    ).astype(BF16)
-    packet = jnp.concatenate(
-        [
-            outbound.reshape(owners, capacity, feat_width),
-            id_block.reshape(owners, id_rows, feat_width),
-        ],
-        1,
-    )
-    packet_in = lax.all_to_all(packet, ("group", "dom"), split_axis=0, concat_axis=0, tiled=True)
-    inbound = packet_in[:, :capacity].reshape(-1, feat_width)
-    slot_nets_in = (
-        packet_in[:, capacity:].reshape(owners, -1)[:, :capacity].astype(F32).astype(jnp.int32)
+    slot_nets_in = lax.all_to_all(
+        slot_nets.astype(jnp.int32).reshape(owners, capacity),
+        ("group", "dom"),
+        split_axis=0,
+        concat_axis=0,
+        tiled=True,
     ).reshape(-1)
+    inbound = lax.all_to_all(
+        outbound.reshape(owners, capacity, feat_width),
+        ("group", "dom"),
+        split_axis=0,
+        concat_axis=0,
+        tiled=True,
+    ).reshape(-1, feat_width)
     net_hot = one_hot(slot_nets_in, net_count)
     pooled = jnp.einsum("sn,sd->nd", net_hot, inbound, preferred_element_type=F32)
     pooled_b = pooled.astype(BF16)

time: 190 us -> 193 us (1.016)
  waiting for transfers between devices: 72.5 us -> 67.3 us
  starting transfers between devices: 24.6 us -> 29 us
    all_to_all x1 -> x2, starting transfers between devices: 6.14 us -> 11.6 us  [the longest x1 7.09 us: on_device(): lax.all_to_all(slot_nets.astype(jnp.int32).reshape(owners, capacity), ('g...]
    all_to_all x1 -> x2, waiting for transfers between devices: 29.8 us -> 25.7 us  [the longest x1 25.7 us: on_device(): lax.all_to_all(outbound.reshape(owners, capacity, feat_width), ('group',...]
    ppermute x2, waiting for transfers between devices: 0.01 us -> 3.67 us  [extended(): lax.ppermute(lax.slice_in_dim(block, 0, width, axis=dim), axis, backward)]
    ppermute x2, waiting for transfers between devices: 8.2 us -> 5.04 us  [extended(): lax.ppermute(lax.slice_in_dim(block, block.shape[dim] - width, None, axis...]
    dot_general x1, matrix products: 5.85 us -> 9 us  [on_device(): jnp.einsum('ter,ted->trd', src_hot, edge_rows, preferred_element_type=F32)]
    dot_general x1, matrix products: 6.93 us -> 4.83 us  [on_device(): jnp.einsum('ter,rd->ted', src_hot, node_table, preferred_element_type=F32)]
  transfers between devices with their start and end apart: 7 -> 8, of which waited for: 4 -> 6; matrix products, arithmetic and copies ran while one was open for 9% -> 18% of each run, Pallas kernels for 0% -> 0%
where the time goes in v3:
time: 193 us; the launch traced here: 192 us
  waiting for transfers between devices  67.3 us (35%)
  matrix products  46.5 us (24%)
  blocking collectives  35.6 us (18%)
  starting transfers between devices  29 us (15%)
  other arithmetic  6.73 us (3%)
  local copies, waits for them, and re-layouts  5.86 us (3%)
    all_to_all x1, blocking collectives, all_sum(): lax.all_to_all(rows.astype(BF16).reshape(owners, -1, width), axes, split_...  35.6 us
    all_to_all x1, waiting for transfers between devices, on_device(): lax.all_to_all(returned.reshape(owners, capacity, feat_width), ('group',...  26.5 us
    all_to_all x1, waiting for transfers between devices, on_device(): lax.all_to_all(outbound.reshape(owners, capacity, feat_width), ('group',...  25.7 us
    dot_general x1, matrix products, on_device(): jnp.einsum('ter,ted->trd', src_hot, edge_rows, preferred_element_type=F32)  9 us
    ppermute x2, starting transfers between devices, extended(): lax.ppermute(lax.slice_in_dim(block, block.shape[dim] - width, None, axis...  7.14 us
    all_to_all x1, starting transfers between devices, on_device(): lax.all_to_all(slot_nets.astype(jnp.int32).reshape(owners, capacity), ('g...  7.09 us
    all_to_all x1, waiting for transfers between devices, all_sum(): lax.all_to_all(spread, axes, split_axis=0, concat_axis=0, tiled=True)  6.43 us
    dot_general x1, matrix products, on_device(): jnp.einsum('tep,ted->tpd', dst_hot, gathered, preferred_element_type=F32)  5.76 us
  transfers between devices with their start and end apart: 8, of which 6 were waited for; matrix products, arithmetic and copies ran while one was open for 18% of the time, Pallas kernels for 0%

profile of v3, /device:TPU:1, one launch (start us, length us, event | category | flops | bytes accessed | tf_op | source)
XLA Modules:
  0.0 192.0 jit_solution(7292342949467862917)
XLA Ops:
  0.6 0.0 copy-start
  0.6 0.7 add_convert_fusion.1
  1.4 1.3 fusion.41
  2.7 0.0 copy-start.5
  2.7 0.0 copy-start.14
  2.7 0.7 multiply_add_fusion
  3.5 1.5 fusion.11
  5.0 0.7 convert_element_type.111
  5.7 7.1 %all-to-all-start = ((s32[32,1,64]{2,1,0:T(1,128)}), s32[32,1,64]{2,1,0:T(1,128)S(1)}, u32[]{:S(2)}, u32[]{:S(2)}) async-start(s32[32,1,64]{2,1,0:T(1,128)} %convert_element_type.111), calls=%async_computation | async-start | bytes 32768 | tf_op jit(solution)/shard_map/all_to_all | solution.py:112
  12.8 0.5 fusion.37
  13.3 3.5 %collective-permute-start = (bf16[256,256]{1,0:T(8,128)(2,1)S(1)}, bf16[256,256]{1,0:T(8,128)(2,1)S(1)}, u32[]{:S(2)}, u32[]{:S(2)}) collective-permute-start(bf16[256,256]{1,0:T(8,128)(2,1)S(1)} %get-tuple-element.22), channel_id=1, source_target_pairs={{0,1},{1,2},{2,3},{3,4},{4,5},{5,6},{6,7},{8,9},{9,10},{10,11},{11... | collective-permute-start | bytes 393224 | tf_op jit(solution)/shard_map/ppermute | solution.py:18
  16.9 1.9 %collective-permute-start.1 = (bf16[256,256]{1,0:T(8,128)(2,1)S(1)}, bf16[256,256]{1,0:T(8,128)(2,1)S(1)}, u32[]{:S(2)}, u32[]{:S(2)}) collective-permute-start(bf16[256,256]{1,0:T(8,128)(2,1)S(1)} %get-tuple-element.23), channel_id=1, source_target_pairs={{1,0},{2,1},{3,2},{4,3},{5,4},{6,5},{7,6},{9,8},{10,9},{11,10},{12... | collective-permute-start | bytes 393224 | tf_op jit(solution)/shard_map/ppermute | solution.py:21
  18.8 1.9 %convert_reduce_fusion = f32[1024]{0:T(1024)S(1)} fusion(s32[4,1024]{1,0:T(4,128)S(1)} %bitcast.88), kind=kLoop, calls=%fused_computation.3 | loop fusion | flops 16776192 | bytes 20480 | tf_op jit(solution)/shard_map/reduce_sum | solution.py:88
  20.8 0.3 fusion.69
  21.1 0.0 collective-permute-done
  21.1 2.1 %collective-permute-done.1 = bf16[256,256]{1,0:T(8,128)(2,1)S(1)} collective-permute-done((bf16[256,256]{1,0:T(8,128)(2,1)S(1)}, bf16[256,256]{1,0:T(8,128)(2,1)S(1)}, u32[]{:S(2)}, u32[]{:S(2)}) %collective-permute-start.1) | collective-permute-done | bytes 131104 | tf_op jit(solution)/shard_map/ppermute | solution.py:21
  23.2 4.8 %fusion.24 = bf16[4,1024,256]{2,1,0:T(8,128)(2,1)S(1)} fusion(s32[4,1024]{1,0:T(4,128)S(1)} %bitcast.91, bf16[256,256]{1,0:T(8,128)(2,1)S(1)} %collective-permute-done.1, bf16[256,256]{1,0:T(8,128)(2,1)S(1)} %collective-permute-done, bf16[1024,256]{1,0:T(8,128)(2,1)S(1)} %copy-done.5), kind=kOutput, calls=%fused_computation.34 | convolution fusion | flops 3230924800 | bytes 2899968 | tf_op jit(solution)/shard_map/ter,rd->ted/dot_general | solution.py:83
  28.0 0.0 copy-start.2
  28.0 0.0 copy-start.1
  28.0 5.8 %fusion.4 = f32[4,1024,256]{2,1,0:T(8,128)S(1)} fusion(bf16[4,1024,256]{2,1,0:T(8,128)(2,1)S(1)} %fusion.24, s32[4,1024]{1,0:T(4,128)S(1)} %bitcast.89), kind=kOutput, calls=%fused_computation.7 | convolution fusion | flops 2151677952 | bytes 6307840 | tf_op jit(solution)/shard_map/tep,ted->tpd/dot_general | solution.py:86
  33.8 2.1 %fusion.28 = f32[1024,256]{1,0:T(8,128)S(1)} fusion(f32[1024,256]{1,0:T(8,128)S(1)} %fusion.69, f32[4,1024,256]{2,1,0:T(8,128)S(1)} %fusion.4, bf16[4,256,256]{2,1,0:T(8,128)(2,1)S(1)} %copy-done.1, f32[1024]{0:T(1024)S(1)} %add_divide_fusion.2), kind=kOutput, calls=%fused_computation.40 | convolution fusion | flops 3221749760 | bytes 6819840 | tf_op jit(solution)/shard_map/tpk,tkd->pd/dot_general | solution.py:36
  35.9 0.0 copy-start.6
  35.9 1.0 copy-done.6
  36.9 3.5 %fusion.20 = bf16[2048,256]{1,0:T(8,128)(2,1)} fusion(s32[1024]{0:T(1024)S(1)} %bitcast.85, f32[1024,256]{1,0:T(8,128)S(1)} %fusion.28), kind=kOutput, calls=%fused_computation.27 | convolution fusion | flops 1077673984 | bytes 2101248 | tf_op jit(solution)/shard_map/dot_general | solution.py:111
  40.4 0.0 all-to-all-done
  40.4 4.5 %all-to-all-start.1 = ((bf16[32,64,256]{2,1,0:T(8,128)(2,1)}), bf16[32,64,256]{2,1,0:T(8,128)(2,1)S(1)}, u32[]{:S(2)}, u32[]{:S(2)}) async-start(bf16[32,64,256]{2,1,0:T(8,128)(2,1)} %bitcast.9), calls=%async_computation.1 | async-start | bytes 2097152 | tf_op jit(solution)/shard_map/all_to_all | solution.py:119
  44.9 0.5 broadcast.63
  45.4 0.7 reduce.3
  46.1 0.1 eq.98
  46.2 25.7 %all-to-all-done.1 = bf16[32,64,256]{2,1,0:T(8,128)(2,1)S(1)} async-done(((bf16[32,64,256]{2,1,0:T(8,128)(2,1)}), bf16[32,64,256]{2,1,0:T(8,128)(2,1)S(1)}, u32[]{:S(2)}, u32[]{:S(2)}) %all-to-all-start.1) | async-done | bytes 1048608 | tf_op jit(solution)/shard_map/all_to_all | solution.py:119
  71.9 1.0 fusion.38
  73.0 0.0 copy-start.10
  73.0 0.5 multiply_convert_fusion.2
  73.4 0.2 fusion.70
  73.7 0.4 multiply_convert_fusion.1
  74.1 2.0 %convolution_convert_fusion = bf16[2048,256]{1,0:T(8,128)(2,1)} fusion(bf16[256,1024]{1,0:T(8,128)(2,1)S(1)} %multiply_convert_fusion.1, bf16[256,1024]{1,0:T(8,128)(2,1)S(1)} %copy-done, s32[2048]{0:T(1024)S(1)} %eq.98), kind=kOutput, calls=%fused_computation.28 | convolution fusion | flops 403767296 | bytes 2105344 | tf_op jit(solution)/shard_map/dot_general | solution.py:141
  76.1 3.7 %all-to-all-start.2 = ((bf16[32,64,256]{2,1,0:T(8,128)(2,1)}), bf16[32,64,256]{2,1,0:T(8,128)(2,1)}, u32[]{:S(2)}, u32[]{:S(2)}) async-start(bf16[32,64,256]{2,1,0:T(8,128)(2,1)} %bitcast.74), calls=%async_computation.2 | async-start | bytes 2097152 | tf_op jit(solution)/shard_map/all_to_all | solution.py:142
  79.8 0.3 fusion.71
  80.2 0.4 convolution_convert_fusion.1
  80.5 26.5 %all-to-all-done.2 = bf16[32,64,256]{2,1,0:T(8,128)(2,1)} async-done(((bf16[32,64,256]{2,1,0:T(8,128)(2,1)}), bf16[32,64,256]{2,1,0:T(8,128)(2,1)}, u32[]{:S(2)}, u32[]{:S(2)}) %all-to-all-start.2) | async-done | bytes 1048608 | tf_op jit(solution)/shard_map/all_to_all | solution.py:142
  107.0 3.3 %fusion.35 = bf16[1024,256]{1,0:T(8,128)(2,1)S(1)} fusion(bf16[2048,256]{1,0:T(8,128)(2,1)} %bitcast.13, s32[1024]{0:T(1024)S(1)} %bitcast.86, f32[1024,256]{1,0:T(8,128)} %copy-done.6), kind=kOutput, calls=%fused_computation.47 | convolution fusion | flops 1078198272 | bytes 2625536 | tf_op jit(solution)/shard_map/dot_general | solution.py:149
  110.3 0.4 fusion.39
  110.7 3.3 %fusion.25 = bf16[4,1024,256]{2,1,0:T(8,128)(2,1)S(1)} fusion(s32[4,1024]{1,0:T(4,128)S(1)} %bitcast.90, bf16[1024,256]{1,0:T(8,128)(2,1)S(1)} %fusion.35, f32[1024]{0:T(1024)S(1)} %add_divide_fusion.2), kind=kOutput, calls=%fused_computation.35 | convolution fusion | flops 2153512960 | bytes 2641920 | tf_op jit(solution)/shard_map/tep,pd->ted/dot_general | solution.py:153
  114.0 0.9 convolution_convert_fusion.2
  114.9 0.4 copy-done.4
  115.3 0.1 fusion.32
  115.4 35.6 %all_to_all.26 = bf16[32,80,256]{2,1,0:T(8,128)(2,1)S(1)} all-to-all(bf16[32,80,256]{2,1,0:T(8,128)(2,1)S(1)} %bitcast.70), channel_id=1, replica_groups=mesh['group'=4,'dom'=8] {'group','dom'}, dimensions={0} | all-to-all | bytes 2621440 | tf_op jit(solution)/shard_map/all_to_all | solution.py:47
  151.0 0.5 fusion.33
  151.5 1.2 broadcast_in_dim.5
  152.6 2.7 %all-to-all-start.4 = ((bf16[32,80,256]{2,1,0:T(8,128)(2,1)}), bf16[32,80,256]{2,1,0:T(8,128)(2,1)S(1)}, u32[]{:S(2)}, u32[]{:S(2)}) async-start(bf16[32,80,256]{2,1,0:T(8,128)(2,1)} %broadcast_in_dim.5), calls=%async_computation.4 | async-start | bytes 2621440 | tf_op jit(solution)/shard_map/all_to_all | solution.py:54
  155.3 9.0 %fusion = f32[4,1536,256]{2,1,0:T(8,128)S(1)} fusion(bf16[4,1024,256]{2,1,0:T(8,128)(2,1)} %copy-done.4, s32[4,1024]{1,0:T(4,128)S(1)} %bitcast.92), kind=kOutput, calls=%fused_computation.1 | convolution fusion | flops 3227516928 | bytes 8404992 | tf_op jit(solution)/shard_map/ter,ted->trd/dot_general | solution.py:157
  164.3 3.1 %fusion.68 = (bf16[1536,256]{1,0:T(8,128)(2,1)S(1)}, f32[1536,256]{1,0:T(8,128)S(1)}) fusion(f32[4,1536,256]{2,1,0:T(8,128)S(1)} %fusion, bf16[4,256,256]{2,1,0:T(8,128)(2,1)S(1)} %copy-done.1), kind=kOutput, calls=%fused_computation.101 | convolution fusion | flops 4832231424 | bytes 9175040 | tf_op jit(solution)/shard_map/trd,tkd->rk/dot_general | solution.py:36
  167.5 3.6 %collective-permute-start.2 = (bf16[256,256]{1,0:T(8,128)(2,1)S(1)}, bf16[256,256]{1,0:T(8,128)(2,1)S(1)}, u32[]{:S(2)}, u32[]{:S(2)}) collective-permute-start(bf16[256,256]{1,0:T(8,128)(2,1)S(1)} %get-tuple-element.20), channel_id=1, source_target_pairs={{0,1},{1,2},{2,3},{3,4},{4,5},{5,6},{6,7},{8,9},{9,10},{10,11},{11... | collective-permute-start | bytes 393224 | tf_op jit(solution)/shard_map/ppermute | solution.py:18
  171.1 1.9 %collective-permute-start.3 = (bf16[256,256]{1,0:T(8,128)(2,1)S(1)}, bf16[256,256]{1,0:T(8,128)(2,1)S(1)}, u32[]{:S(2)}, u32[]{:S(2)}) collective-permute-start(bf16[256,256]{1,0:T(8,128)(2,1)S(1)} %get-tuple-element.21), channel_id=1, source_target_pairs={{1,0},{2,1},{3,2},{4,3},{5,4},{6,5},{7,6},{9,8},{10,9},{11,10},{12... | collective-permute-start | bytes 393224 | tf_op jit(solution)/shard_map/ppermute | solution.py:21
  173.0 0.3 convolution_add_fusion
  173.3 5.0 %collective-permute-done.2 = bf16[256,256]{1,0:T(8,128)(2,1)S(1)} collective-permute-done((bf16[256,256]{1,0:T(8,128)(2,1)S(1)}, bf16[256,256]{1,0:T(8,128)(2,1)S(1)}, u32[]{:S(2)}, u32[]{:S(2)}) %collective-permute-start.2) | collective-permute-done | bytes 131104 | tf_op jit(solution)/shard_map/ppermute | solution.py:18
  178.4 1.6 collective-permute-done.3
  180.0 1.6 fusion.36
  181.6 6.4 %all-to-all-done.4 = bf16[32,80,256]{2,1,0:T(8,128)(2,1)S(1)} async-done(((bf16[32,80,256]{2,1,0:T(8,128)(2,1)}), bf16[32,80,256]{2,1,0:T(8,128)(2,1)S(1)}, u32[]{:S(2)}, u32[]{:S(2)}) %all-to-all-start.4) | async-done | bytes 1310752 | tf_op jit(solution)/shard_map/all_to_all | solution.py:54
  188.1 0.2 slice_convert_fusion
  188.3 0.7 slice_multiply_fusion.2
  189.0 1.2 fusion.42
  190.1 0.6 copy.24
  190.7 1.3 copy.20
  (34 shorter events, 0.2 us)
Async XLA Ops:
  0.6 72.3 %copy-start = (bf16[256,1024]{1,0:T(8,128)(2,1)S(1)}, bf16[256,1024]{1,0:T(8,128)(2,1)}, u32[]{:S(2)}) copy-start(bf16[256,1024]{1,0:T(8,128)(2,1)} %param.14) | copy-start | bytes 1572868
  2.7 10.1 %copy-start.5 = (bf16[1024,256]{1,0:T(8,128)(2,1)S(1)}, bf16[1024,256]{1,0:T(8,128)(2,1)}, u32[]{:S(2)}) copy-start(bf16[1024,256]{1,0:T(8,128)(2,1)} %param.11) | copy-start | bytes 1572868
  2.7 10.1 %copy-start.14 = (s32[1,512]{1,0:T(1,128)S(1)}, s32[1,512]{1,0:T(1,128)}, u32[]{:S(2)}) copy-start(s32[1,512]{1,0:T(1,128)} %param.16) | copy-start | bytes 6148
  3.5 15.3 %copy-start.11 = (s32[1,4,1024]{2,1,0:T(4,128)S(1)}, s32[1,4,1024]{2,1,0:T(4,128)}, u32[]{:S(2)}) copy-start(s32[1,4,1024]{2,1,0:T(4,128)} %param.18) | copy-start | bytes 49156
  3.5 17.3 %copy-start.7 = (bf16[256,256]{1,0:T(8,128)(2,1)S(1)}, bf16[256,256]{1,0:T(8,128)(2,1)}, u32[]{:S(2)}) copy-start(bf16[256,256]{1,0:T(8,128)(2,1)} %param.12) | copy-start | bytes 393220
  5.0 18.2 %copy-start.12 = (s32[1,4,1024]{2,1,0:T(4,128)S(1)}, s32[1,4,1024]{2,1,0:T(4,128)}, u32[]{:S(2)}) copy-start(s32[1,4,1024]{2,1,0:T(4,128)} %param.17) | copy-start | bytes 49156
  5.7 34.7 %all-to-all-start = ((s32[32,1,64]{2,1,0:T(1,128)}), s32[32,1,64]{2,1,0:T(1,128)S(1)}, u32[]{:S(2)}, u32[]{:S(2)}) async-start(s32[32,1,64]{2,1,0:T(1,128)} %convert_element_type.111), calls=%async_computation | async-start | bytes 32768 | tf_op jit(solution)/shard_map/all_to_all | solution.py:112
  13.3 7.8 %collective-permute-start = (bf16[256,256]{1,0:T(8,128)(2,1)S(1)}, bf16[256,256]{1,0:T(8,128)(2,1)S(1)}, u32[]{:S(2)}, u32[]{:S(2)}) collective-permute-start(bf16[256,256]{1,0:T(8,128)(2,1)S(1)} %get-tuple-element.22), channel_id=1, source_target_pairs={{0,1},{1,2},{2,3},{3,4},{4,5},{5,6},{6,7},{8,9},{9,10},{10,11},{11... | collective-permute-start | bytes 393224 | tf_op jit(solution)/shard_map/ppermute | solution.py:18
  16.9 6.3 %collective-permute-start.1 = (bf16[256,256]{1,0:T(8,128)(2,1)S(1)}, bf16[256,256]{1,0:T(8,128)(2,1)S(1)}, u32[]{:S(2)}, u32[]{:S(2)}) collective-permute-start(bf16[256,256]{1,0:T(8,128)(2,1)S(1)} %get-tuple-element.23), channel_id=1, source_target_pairs={{1,0},{2,1},{3,2},{4,3},{5,4},{6,5},{7,6},{9,8},{10,9},{11,10},{12... | collective-permute-start | bytes 393224 | tf_op jit(solution)/shard_map/ppermute | solution.py:21
  28.0 5.8 %copy-start.2 = (bf16[4,1024,256]{2,1,0:T(8,128)(2,1)}, bf16[4,1024,256]{2,1,0:T(8,128)(2,1)S(1)}, u32[]{:S(2)}) copy-start(bf16[4,1024,256]{2,1,0:T(8,128)(2,1)S(1)} %fusion.24) | copy-start | bytes 6291460
  28.0 5.8 %copy-start.1 = (bf16[4,256,256]{2,1,0:T(8,128)(2,1)S(1)}, bf16[4,256,256]{2,1,0:T(8,128)(2,1)}, u32[]{:S(2)}) copy-start(bf16[4,256,256]{2,1,0:T(8,128)(2,1)} %param.13) | copy-start | bytes 1572868
  35.9 1.0 copy-start.6
  40.4 4.5 %copy-start.8 = (bf16[1024]{0:T(1024)(128)(2,1)S(1)}, bf16[1024]{0:T(1024)(128)(2,1)}, u32[]{:S(2)}) copy-start(bf16[1024]{0:T(1024)(128)(2,1)} %param.15) | copy-start | bytes 6148
  40.4 31.5 %all-to-all-start.1 = ((bf16[32,64,256]{2,1,0:T(8,128)(2,1)}), bf16[32,64,256]{2,1,0:T(8,128)(2,1)S(1)}, u32[]{:S(2)}, u32[]{:S(2)}) async-start(bf16[32,64,256]{2,1,0:T(8,128)(2,1)} %bitcast.9), calls=%async_computation.1 | async-start | bytes 2097152 | tf_op jit(solution)/shard_map/all_to_all | solution.py:119
  73.0 0.7 copy-start.10
  73.7 2.4 %copy-start.9 = (f32[1,256]{1,0:T(1,128)}, f32[1,256]{1,0:T(1,128)S(1)}, u32[]{:S(2)}) copy-start(f32[1,256]{1,0:T(1,128)S(1)} %fusion.70) | copy-start | bytes 3076
  76.1 30.9 %all-to-all-start.2 = ((bf16[32,64,256]{2,1,0:T(8,128)(2,1)}), bf16[32,64,256]{2,1,0:T(8,128)(2,1)}, u32[]{:S(2)}, u32[]{:S(2)}) async-start(bf16[32,64,256]{2,1,0:T(8,128)(2,1)} %bitcast.74), calls=%async_computation.2 | async-start | bytes 2097152 | tf_op jit(solution)/shard_map/all_to_all | solution.py:142
  110.7 3.3 %copy-start.3 = (bf16[4,1024,256]{2,1,0:T(8,128)(2,1)S(1)}, bf16[4,1024,256]{2,1,0:T(8,128)(2,1)}, u32[]{:S(2)}) copy-start(bf16[4,1024,256]{2,1,0:T(8,128)(2,1)} %copy-done.2) | copy-start | bytes 6291460
  114.0 1.3 copy-start.4
  151.5 3.9 %copy-start.13 = (s32[1,4,1024]{2,1,0:T(4,128)S(1)}, s32[1,4,1024]{2,1,0:T(4,128)}, u32[]{:S(2)}) copy-start(s32[1,4,1024]{2,1,0:T(4,128)} %param.17) | copy-start | bytes 49156
  152.6 35.4 %all-to-all-start.4 = ((bf16[32,80,256]{2,1,0:T(8,128)(2,1)}), bf16[32,80,256]{2,1,0:T(8,128)(2,1)S(1)}, u32[]{:S(2)}, u32[]{:S(2)}) async-start(bf16[32,80,256]{2,1,0:T(8,128)(2,1)} %broadcast_in_dim.5), calls=%async_computation.4 | async-start | bytes 2621440 | tf_op jit(solution)/shard_map/all_to_all | solution.py:54
  167.5 10.9 %collective-permute-start.2 = (bf16[256,256]{1,0:T(8,128)(2,1)S(1)}, bf16[256,256]{1,0:T(8,128)(2,1)S(1)}, u32[]{:S(2)}, u32[]{:S(2)}) collective-permute-start(bf16[256,256]{1,0:T(8,128)(2,1)S(1)} %get-tuple-element.20), channel_id=1, source_target_pairs={{0,1},{1,2},{2,3},{3,4},{4,5},{5,6},{6,7},{8,9},{9,10},{10,11},{11... | collective-permute-start | bytes 393224 | tf_op jit(solution)/shard_map/ppermute | solution.py:18
  171.1 8.9 %collective-permute-start.3 = (bf16[256,256]{1,0:T(8,128)(2,1)S(1)}, bf16[256,256]{1,0:T(8,128)(2,1)S(1)}, u32[]{:S(2)}, u32[]{:S(2)}) collective-permute-start(bf16[256,256]{1,0:T(8,128)(2,1)S(1)} %get-tuple-element.21), channel_id=1, source_target_pairs={{1,0},{2,1},{3,2},{4,3},{5,4},{6,5},{7,6},{9,8},{10,9},{11,10},{12... | collective-permute-start | bytes 393224 | tf_op jit(solution)/shard_map/ppermute | solution.py:21

commit v4 on v2

--- a/solution.py
+++ b/solution.py
@@ -109,7 +109,7 @@
     net_code = (pin_net + 1).astype(BF16)[:, None]
     slot_nets = jnp.dot(slot_hot.T, net_code, preferred_element_type=F32)[:, 0] - 1.0
     outbound = jnp.dot(slot_hot.T, hidden, preferred_element_type=F32).astype(BF16)
-    id_rows = -(-capacity // feat_width)
+    id_rows = -(-capacity // (8 * feat_width)) * 8
     id_block = jnp.pad(
         slot_nets.reshape(owners, capacity), ((0, 0), (0, id_rows * feat_width - capacity))
     ).astype(BF16)

time: 190 us -> 188 us (0.989)
  waiting for transfers between devices: 72.5 us -> 69.3 us
    ppermute x2, waiting for transfers between devices: 8.2 us -> 5.04 us  [extended(): lax.ppermute(lax.slice_in_dim(block, block.shape[dim] - width, None, axis...]
    dot_general x1, matrix products: 5.85 us -> 9 us  [on_device(): jnp.einsum('ter,ted->trd', src_hot, edge_rows, preferred_element_type=F32)]
    dot_general x1, matrix products: 6.93 us -> 4.85 us  [on_device(): jnp.einsum('ter,rd->ted', src_hot, node_table, preferred_element_type=F32)]
  transfers between devices with their start and end apart: 7 -> 7, of which waited for: 4 -> 5; matrix products, arithmetic and copies ran while one was open for 9% -> 10% of each run, Pallas kernels for 0% -> 0%
where the time goes in v4:
time: 188 us; the launch traced here: 186 us
  waiting for transfers between devices  69.3 us (37%)
  matrix products  45.9 us (24%)
  blocking collectives  35.6 us (19%)
  starting transfers between devices  24.6 us (13%)
  other arithmetic  5.69 us (3%)
  local copies, waits for them, and re-layouts  4.01 us (2%)
    all_to_all x1, blocking collectives, all_sum(): lax.all_to_all(rows.astype(BF16).reshape(owners, -1, width), axes, split_...  35.6 us
    all_to_all x1, waiting for transfers between devices, on_device(): lax.all_to_all(packet, ('group', 'dom'), split_axis=0, concat_axis=0, til...  29.8 us
    all_to_all x1, waiting for transfers between devices, on_device(): lax.all_to_all(returned.reshape(owners, capacity, feat_width), ('group',...  26.5 us
    dot_general x1, matrix products, on_device(): jnp.einsum('ter,ted->trd', src_hot, edge_rows, preferred_element_type=F32)  9 us
    ppermute x2, starting transfers between devices, extended(): lax.ppermute(lax.slice_in_dim(block, block.shape[dim] - width, None, axis...  8.2 us
    all_to_all x1, waiting for transfers between devices, all_sum(): lax.all_to_all(spread, axes, split_axis=0, concat_axis=0, tiled=True)  6.42 us
    all_to_all x1, starting transfers between devices, on_device(): lax.all_to_all(packet, ('group', 'dom'), split_axis=0, concat_axis=0, til...  6.15 us
    dot_general x1, matrix products, on_device(): jnp.einsum('tep,ted->tpd', dst_hot, gathered, preferred_element_type=F32)  5.76 us
  transfers between devices with their start and end apart: 7, of which 5 were waited for; matrix products, arithmetic and copies ran while one was open for 10% of the time, Pallas kernels for 0%

profile of v4, /device:TPU:1, one launch (start us, length us, event | category | flops | bytes accessed | tf_op | source)
XLA Modules:
  0.0 186.3 jit_solution(17331707062312330720)
XLA Ops:
  0.6 0.0 copy-start
  0.7 1.6 fusion.37
  2.3 4.6 %collective-permute-start = (bf16[256,256]{1,0:T(8,128)(2,1)S(1)}, bf16[256,256]{1,0:T(8,128)(2,1)S(1)}, u32[]{:S(2)}, u32[]{:S(2)}) collective-permute-start(bf16[256,256]{1,0:T(8,128)(2,1)S(1)} %get-tuple-element.22), channel_id=1, source_target_pairs={{0,1},{1,2},{2,3},{3,4},{4,5},{5,6},{6,7},{8,9},{9,10},{10,11},{11... | collective-permute-start | bytes 393224 | tf_op jit(solution)/shard_map/ppermute | solution.py:18
  6.9 1.9 %collective-permute-start.1 = (bf16[256,256]{1,0:T(8,128)(2,1)S(1)}, bf16[256,256]{1,0:T(8,128)(2,1)S(1)}, u32[]{:S(2)}, u32[]{:S(2)}) collective-permute-start(bf16[256,256]{1,0:T(8,128)(2,1)S(1)} %get-tuple-element.23), channel_id=1, source_target_pairs={{1,0},{2,1},{3,2},{4,3},{5,4},{6,5},{7,6},{9,8},{10,9},{11,10},{12... | collective-permute-start | bytes 393224 | tf_op jit(solution)/shard_map/ppermute | solution.py:21
  8.9 1.9 %convert_reduce_fusion = f32[1024]{0:T(1024)S(1)} fusion(s32[4,1024]{1,0:T(4,128)S(1)} %bitcast.97), kind=kLoop, calls=%fused_computation.3 | loop fusion | flops 16776192 | bytes 20480 | tf_op jit(solution)/shard_map/reduce_sum | solution.py:88
  10.9 0.5 fusion.41
  11.4 0.0 copy-start.5
  11.4 0.0 copy-start.7
  11.5 0.0 copy-start.14
  11.5 1.5 fusion.10
  12.9 0.1 sub.16
  13.1 0.3 fusion.69
  13.4 0.0 collective-permute-done
  13.4 0.0 collective-permute-done.1
  13.5 4.8 %fusion.24 = bf16[4,1024,256]{2,1,0:T(8,128)(2,1)S(1)} fusion(s32[4,1024]{1,0:T(4,128)S(1)} %bitcast.100, bf16[256,256]{1,0:T(8,128)(2,1)S(1)} %collective-permute-done.1, bf16[256,256]{1,0:T(8,128)(2,1)S(1)} %collective-permute-done, bf16[1024,256]{1,0:T(8,128)(2,1)S(1)} %copy-done.5), kind=kOutput, calls=%fused_computation.34 | convolution fusion | flops 3230924800 | bytes 2899968 | tf_op jit(solution)/shard_map/ter,rd->ted/dot_general | solution.py:83
  18.3 0.0 copy-start.1
  18.3 5.8 %fusion.4 = f32[4,1024,256]{2,1,0:T(8,128)S(1)} fusion(bf16[4,1024,256]{2,1,0:T(8,128)(2,1)S(1)} %fusion.24, s32[4,1024]{1,0:T(4,128)S(1)} %bitcast.98), kind=kOutput, calls=%fused_computation.7 | convolution fusion | flops 2151677952 | bytes 6307840 | tf_op jit(solution)/shard_map/tep,ted->tpd/dot_general | solution.py:86
  24.1 2.1 %fusion.28 = f32[1024,256]{1,0:T(8,128)S(1)} fusion(f32[1024,256]{1,0:T(8,128)S(1)} %fusion.69, f32[4,1024,256]{2,1,0:T(8,128)S(1)} %fusion.4, bf16[4,256,256]{2,1,0:T(8,128)(2,1)S(1)} %copy-done.1, f32[1024]{0:T(1024)S(1)} %add_divide_fusion.2), kind=kOutput, calls=%fused_computation.40 | convolution fusion | flops 3221749760 | bytes 6819840 | tf_op jit(solution)/shard_map/tpk,tkd->pd/dot_general | solution.py:36
  26.2 0.0 copy-start.6
  26.2 2.5 %fusion.20 = bf16[2048,256]{1,0:T(8,128)(2,1)S(1)} fusion(s32[1024]{0:T(1024)S(1)} %bitcast.94, f32[1024,256]{1,0:T(8,128)S(1)} %fusion.28), kind=kOutput, calls=%fused_computation.27 | convolution fusion | flops 1077673984 | bytes 2101248 | tf_op jit(solution)/shard_map/dot_general | solution.py:111
  28.8 0.0 copy-start.8
  28.8 1.1 pad_maximum_fusion
  29.9 6.1 %all-to-all-start = ((bf16[32,72,256]{2,1,0:T(8,128)(2,1)}), bf16[32,72,256]{2,1,0:T(8,128)(2,1)S(1)}, u32[]{:S(2)}, u32[]{:S(2)}) async-start(bf16[32,72,256]{2,1,0:T(8,128)(2,1)} %pad_maximum_fusion), calls=%async_computation | async-start | bytes 2359296 | tf_op jit(solution)/shard_map/all_to_all | solution.py:123
  36.1 29.8 %all-to-all-done = bf16[32,72,256]{2,1,0:T(8,128)(2,1)S(1)} async-done(((bf16[32,72,256]{2,1,0:T(8,128)(2,1)}), bf16[32,72,256]{2,1,0:T(8,128)(2,1)S(1)}, u32[]{:S(2)}, u32[]{:S(2)}) %all-to-all-start) | async-done | bytes 1179680 | tf_op jit(solution)/shard_map/all_to_all | solution.py:123
  65.9 0.1 eq.110
  66.0 0.1 slice.60
  66.1 1.1 fusion.38
  67.2 0.0 copy-done
  67.2 0.0 copy-start.12
  67.2 0.4 multiply_convert_fusion.2
  67.7 0.2 fusion.70
  67.9 0.0 copy-done.12
  67.9 0.4 multiply_convert_fusion.1
  68.3 2.0 %convolution_convert_fusion = bf16[2048,256]{1,0:T(8,128)(2,1)} fusion(bf16[256,1024]{1,0:T(8,128)(2,1)S(1)} %multiply_convert_fusion.1, bf16[256,1024]{1,0:T(8,128)(2,1)S(1)} %copy-done, s32[2048]{0:T(1024)S(1)} %eq.110), kind=kOutput, calls=%fused_computation.28 | convolution fusion | flops 403767296 | bytes 2105344 | tf_op jit(solution)/shard_map/dot_general | solution.py:143
  70.3 0.0 copy-done.9
  70.3 3.8 %all-to-all-start.1 = ((bf16[32,64,256]{2,1,0:T(8,128)(2,1)}), bf16[32,64,256]{2,1,0:T(8,128)(2,1)}, u32[]{:S(2)}, u32[]{:S(2)}) async-start(bf16[32,64,256]{2,1,0:T(8,128)(2,1)} %bitcast.77), calls=%async_computation.1 | async-start | bytes 2097152 | tf_op jit(solution)/shard_map/all_to_all | solution.py:144
  74.1 0.3 fusion.71
  74.4 0.4 convolution_convert_fusion.1
  74.8 26.5 %all-to-all-done.1 = bf16[32,64,256]{2,1,0:T(8,128)(2,1)} async-done(((bf16[32,64,256]{2,1,0:T(8,128)(2,1)}), bf16[32,64,256]{2,1,0:T(8,128)(2,1)}, u32[]{:S(2)}, u32[]{:S(2)}) %all-to-all-start.1) | async-done | bytes 1048608 | tf_op jit(solution)/shard_map/all_to_all | solution.py:144
  101.3 3.3 %fusion.35 = bf16[1024,256]{1,0:T(8,128)(2,1)S(1)} fusion(bf16[2048,256]{1,0:T(8,128)(2,1)} %bitcast.13, s32[1024]{0:T(1024)S(1)} %bitcast.95, f32[1024,256]{1,0:T(8,128)} %copy-done.6), kind=kOutput, calls=%fused_computation.47 | convolution fusion | flops 1078198272 | bytes 2625536 | tf_op jit(solution)/shard_map/dot_general | solution.py:151
  104.5 0.3 fusion.39
  104.9 3.3 %fusion.25 = bf16[4,1024,256]{2,1,0:T(8,128)(2,1)S(1)} fusion(s32[4,1024]{1,0:T(4,128)S(1)} %bitcast.99, bf16[1024,256]{1,0:T(8,128)(2,1)S(1)} %fusion.35, f32[1024]{0:T(1024)S(1)} %add_divide_fusion.2), kind=kOutput, calls=%fused_computation.35 | convolution fusion | flops 2153512960 | bytes 2641920 | tf_op jit(solution)/shard_map/tep,pd->ted/dot_general | solution.py:155
  108.2 0.9 convolution_convert_fusion.2
  109.1 0.4 copy-done.4
  109.6 0.1 fusion.32
  109.6 35.6 %all_to_all.20 = bf16[32,80,256]{2,1,0:T(8,128)(2,1)S(1)} all-to-all(bf16[32,80,256]{2,1,0:T(8,128)(2,1)S(1)} %bitcast.74), channel_id=1, replica_groups=mesh['group'=4,'dom'=8] {'group','dom'}, dimensions={0} | all-to-all | bytes 2621440 | tf_op jit(solution)/shard_map/all_to_all | solution.py:47
  145.2 0.5 fusion.33
  145.7 1.2 broadcast_in_dim.5
  146.9 2.7 %all-to-all-start.3 = ((bf16[32,80,256]{2,1,0:T(8,128)(2,1)}), bf16[32,80,256]{2,1,0:T(8,128)(2,1)S(1)}, u32[]{:S(2)}, u32[]{:S(2)}) async-start(bf16[32,80,256]{2,1,0:T(8,128)(2,1)} %broadcast_in_dim.5), calls=%async_computation.3 | async-start | bytes 2621440 | tf_op jit(solution)/shard_map/all_to_all | solution.py:54
  149.6 9.0 %fusion = f32[4,1536,256]{2,1,0:T(8,128)S(1)} fusion(bf16[4,1024,256]{2,1,0:T(8,128)(2,1)} %copy-done.4, s32[4,1024]{1,0:T(4,128)S(1)} %bitcast.101), kind=kOutput, calls=%fused_computation.1 | convolution fusion | flops 3227516928 | bytes 8404992 | tf_op jit(solution)/shard_map/ter,ted->trd/dot_general | solution.py:159
  158.6 3.1 %fusion.68 = (bf16[1536,256]{1,0:T(8,128)(2,1)S(1)}, f32[1536,256]{1,0:T(8,128)S(1)}) fusion(f32[4,1536,256]{2,1,0:T(8,128)S(1)} %fusion, bf16[4,256,256]{2,1,0:T(8,128)(2,1)S(1)} %copy-done.1), kind=kOutput, calls=%fused_computation.103 | convolution fusion | flops 4832231424 | bytes 9175040 | tf_op jit(solution)/shard_map/trd,tkd->rk/dot_general | solution.py:36
  161.7 0.0 copy-start.16
  161.8 3.6 %collective-permute-start.2 = (bf16[256,256]{1,0:T(8,128)(2,1)S(1)}, bf16[256,256]{1,0:T(8,128)(2,1)S(1)}, u32[]{:S(2)}, u32[]{:S(2)}) collective-permute-start(bf16[256,256]{1,0:T(8,128)(2,1)S(1)} %get-tuple-element.20), channel_id=1, source_target_pairs={{0,1},{1,2},{2,3},{3,4},{4,5},{5,6},{6,7},{8,9},{9,10},{10,11},{11... | collective-permute-start | bytes 393224 | tf_op jit(solution)/shard_map/ppermute | solution.py:18
  165.4 1.9 %collective-permute-start.3 = (bf16[256,256]{1,0:T(8,128)(2,1)S(1)}, bf16[256,256]{1,0:T(8,128)(2,1)S(1)}, u32[]{:S(2)}, u32[]{:S(2)}) collective-permute-start(bf16[256,256]{1,0:T(8,128)(2,1)S(1)} %get-tuple-element.21), channel_id=1, source_target_pairs={{1,0},{2,1},{3,2},{4,3},{5,4},{6,5},{7,6},{9,8},{10,9},{11,10},{12... | collective-permute-start | bytes 393224 | tf_op jit(solution)/shard_map/ppermute | solution.py:21
  167.3 0.3 convolution_add_fusion
  167.6 5.0 %collective-permute-done.2 = bf16[256,256]{1,0:T(8,128)(2,1)S(1)} collective-permute-done((bf16[256,256]{1,0:T(8,128)(2,1)S(1)}, bf16[256,256]{1,0:T(8,128)(2,1)S(1)}, u32[]{:S(2)}, u32[]{:S(2)}) %collective-permute-start.2) | collective-permute-done | bytes 131104 | tf_op jit(solution)/shard_map/ppermute | solution.py:18
  172.7 1.6 collective-permute-done.3
  174.3 1.6 fusion.36
  175.9 6.4 %all-to-all-done.3 = bf16[32,80,256]{2,1,0:T(8,128)(2,1)S(1)} async-done(((bf16[32,80,256]{2,1,0:T(8,128)(2,1)}), bf16[32,80,256]{2,1,0:T(8,128)(2,1)S(1)}, u32[]{:S(2)}, u32[]{:S(2)}) %all-to-all-start.3) | async-done | bytes 1310752 | tf_op jit(solution)/shard_map/all_to_all | solution.py:54
  182.3 0.2 slice_convert_fusion
  182.5 0.7 slice_multiply_fusion.2
  183.3 1.2 fusion.42
  184.4 0.6 copy.26
  185.0 1.3 copy.20
  (41 shorter events, 0.3 us)
Async XLA Ops:
  0.6 66.5 %copy-start = (bf16[256,1024]{1,0:T(8,128)(2,1)S(1)}, bf16[256,1024]{1,0:T(8,128)(2,1)}, u32[]{:S(2)}) copy-start(bf16[256,1024]{1,0:T(8,128)(2,1)} %param.14) | copy-start | bytes 1572868
  0.6 8.2 %copy-start.11 = (s32[1024]{0:T(1024)S(1)}, s32[1024]{0:T(1024)}, u32[]{:S(2)}) copy-start(s32[1024]{0:T(1024)} %param.20) | copy-start | bytes 12292
  0.7 8.2 %copy-start.13 = (s32[1,4,1024]{2,1,0:T(4,128)S(1)}, s32[1,4,1024]{2,1,0:T(4,128)}, u32[]{:S(2)}) copy-start(s32[1,4,1024]{2,1,0:T(4,128)} %param.18) | copy-start | bytes 49156
  0.7 10.2 %copy-start.10 = (s32[1024,1]{0,1:T(1,128)S(1)}, s32[1024,1]{0,1:T(1,128)}, u32[]{:S(2)}) copy-start(s32[1024,1]{0,1:T(1,128)} %param.19) | copy-start | bytes 12292
  2.3 11.1 %collective-permute-start = (bf16[256,256]{1,0:T(8,128)(2,1)S(1)}, bf16[256,256]{1,0:T(8,128)(2,1)S(1)}, u32[]{:S(2)}, u32[]{:S(2)}) collective-permute-start(bf16[256,256]{1,0:T(8,128)(2,1)S(1)} %get-tuple-element.22), channel_id=1, source_target_pairs={{0,1},{1,2},{2,3},{3,4},{4,5},{5,6},{6,7},{8,9},{9,10},{10,11},{11... | collective-permute-start | bytes 393224 | tf_op jit(solution)/shard_map/ppermute | solution.py:18
  6.9 6.5 %collective-permute-start.1 = (bf16[256,256]{1,0:T(8,128)(2,1)S(1)}, bf16[256,256]{1,0:T(8,128)(2,1)S(1)}, u32[]{:S(2)}, u32[]{:S(2)}) collective-permute-start(bf16[256,256]{1,0:T(8,128)(2,1)S(1)} %get-tuple-element.23), channel_id=1, source_target_pairs={{1,0},{2,1},{3,2},{4,3},{5,4},{6,5},{7,6},{9,8},{10,9},{11,10},{12... | collective-permute-start | bytes 393224 | tf_op jit(solution)/shard_map/ppermute | solution.py:21
  11.4 1.7 copy-start.5
  11.4 1.7 copy-start.7
  11.5 2.0 %copy-start.14 = (s32[1,4,1024]{2,1,0:T(4,128)S(1)}, s32[1,4,1024]{2,1,0:T(4,128)}, u32[]{:S(2)}) copy-start(s32[1,4,1024]{2,1,0:T(4,128)} %param.17) | copy-start | bytes 49156
  18.3 5.8 %copy-start.2 = (bf16[4,1024,256]{2,1,0:T(8,128)(2,1)}, bf16[4,1024,256]{2,1,0:T(8,128)(2,1)S(1)}, u32[]{:S(2)}) copy-start(bf16[4,1024,256]{2,1,0:T(8,128)(2,1)S(1)} %fusion.24) | copy-start | bytes 6291460
  18.3 5.8 %copy-start.1 = (bf16[4,256,256]{2,1,0:T(8,128)(2,1)S(1)}, bf16[4,256,256]{2,1,0:T(8,128)(2,1)}, u32[]{:S(2)}) copy-start(bf16[4,256,256]{2,1,0:T(8,128)(2,1)} %param.13) | copy-start | bytes 1572868
  26.2 2.6 %copy-start.6 = (f32[1024,256]{1,0:T(8,128)}, f32[1024,256]{1,0:T(8,128)S(1)}, u32[]{:S(2)}) copy-start(f32[1024,256]{1,0:T(8,128)S(1)} %fusion.28) | copy-start | bytes 3145732
  28.8 7.3 %copy-start.8 = (bf16[1024]{0:T(1024)(128)(2,1)S(1)}, bf16[1024]{0:T(1024)(128)(2,1)}, u32[]{:S(2)}) copy-start(bf16[1024]{0:T(1024)(128)(2,1)} %param.15) | copy-start | bytes 6148
  29.9 36.0 %all-to-all-start = ((bf16[32,72,256]{2,1,0:T(8,128)(2,1)}), bf16[32,72,256]{2,1,0:T(8,128)(2,1)S(1)}, u32[]{:S(2)}, u32[]{:S(2)}) async-start(bf16[32,72,256]{2,1,0:T(8,128)(2,1)} %pad_maximum_fusion), calls=%async_computation | async-start | bytes 2359296 | tf_op jit(solution)/shard_map/all_to_all | solution.py:123
  67.2 0.7 copy-start.12
  67.9 2.4 %copy-start.9 = (f32[1,256]{1,0:T(1,128)}, f32[1,256]{1,0:T(1,128)S(1)}, u32[]{:S(2)}) copy-start(f32[1,256]{1,0:T(1,128)S(1)} %fusion.70) | copy-start | bytes 3076
  70.3 31.0 %all-to-all-start.1 = ((bf16[32,64,256]{2,1,0:T(8,128)(2,1)}), bf16[32,64,256]{2,1,0:T(8,128)(2,1)}, u32[]{:S(2)}, u32[]{:S(2)}) async-start(bf16[32,64,256]{2,1,0:T(8,128)(2,1)} %bitcast.77), calls=%async_computation.1 | async-start | bytes 2097152 | tf_op jit(solution)/shard_map/all_to_all | solution.py:144
  104.9 3.3 %copy-start.3 = (bf16[4,1024,256]{2,1,0:T(8,128)(2,1)S(1)}, bf16[4,1024,256]{2,1,0:T(8,128)(2,1)}, u32[]{:S(2)}) copy-start(bf16[4,1024,256]{2,1,0:T(8,128)(2,1)} %copy-done.2) | copy-start | bytes 6291460
  108.2 1.3 copy-start.4
  145.7 3.9 %copy-start.15 = (s32[1,4,1024]{2,1,0:T(4,128)S(1)}, s32[1,4,1024]{2,1,0:T(4,128)}, u32[]{:S(2)}) copy-start(s32[1,4,1024]{2,1,0:T(4,128)} %param.17) | copy-start | bytes 49156
  146.9 35.4 %all-to-all-start.3 = ((bf16[32,80,256]{2,1,0:T(8,128)(2,1)}), bf16[32,80,256]{2,1,0:T(8,128)(2,1)S(1)}, u32[]{:S(2)}, u32[]{:S(2)}) async-start(bf16[32,80,256]{2,1,0:T(8,128)(2,1)} %broadcast_in_dim.5), calls=%async_computation.3 | async-start | bytes 2621440 | tf_op jit(solution)/shard_map/all_to_all | solution.py:54
  161.7 12.6 %copy-start.16 = (s32[1,512]{1,0:T(1,128)S(1)}, s32[1,512]{1,0:T(1,128)}, u32[]{:S(2)}) copy-start(s32[1,512]{1,0:T(1,128)} %param.16) | copy-start | bytes 6148
  161.8 10.9 %collective-permute-start.2 = (bf16[256,256]{1,0:T(8,128)(2,1)S(1)}, bf16[256,256]{1,0:T(8,128)(2,1)S(1)}, u32[]{:S(2)}, u32[]{:S(2)}) collective-permute-start(bf16[256,256]{1,0:T(8,128)(2,1)S(1)} %get-tuple-element.20), channel_id=1, source_target_pairs={{0,1},{1,2},{2,3},{3,4},{4,5},{5,6},{6,7},{8,9},{9,10},{10,11},{11... | collective-permute-start | bytes 393224 | tf_op jit(solution)/shard_map/ppermute | solution.py:18
  165.4 8.9 %collective-permute-start.3 = (bf16[256,256]{1,0:T(8,128)(2,1)S(1)}, bf16[256,256]{1,0:T(8,128)(2,1)S(1)}, u32[]{:S(2)}, u32[]{:S(2)}) collective-permute-start(bf16[256,256]{1,0:T(8,128)(2,1)S(1)} %get-tuple-element.21), channel_id=1, source_target_pairs={{1,0},{2,1},{3,2},{4,3},{5,4},{6,5},{7,6},{9,8},{10,9},{11,10},{12... | collective-permute-start | bytes 393224 | tf_op jit(solution)/shard_map/ppermute | solution.py:21

commit v5 on v4

--- a/solution.py
+++ b/solution.py
@@ -40,7 +40,7 @@
 
 def all_sum(rows, owners):
     count, width = rows.shape
-    unit = owners * 16
+    unit = owners * 8
     length = -(-count // unit) * unit
     rows = jnp.pad(rows, ((0, length - count), (0, 0)))
     axes = ("group", "dom")
@@ -141,13 +141,28 @@
         "nh,dh->nd", head_grad, w_head, preferred_element_type=F32
     ).astype(BF16)
     returned = jnp.dot(net_hot, net_grad, preferred_element_type=F32).astype(BF16)
-    arrived = lax.all_to_all(
-        returned.reshape(owners, capacity, feat_width),
-        ("group", "dom"),
-        split_axis=0,
-        concat_axis=0,
-        tiled=True,
-    ).reshape(-1, feat_width)
+    out_rows = out_sum.reshape(-1, feat_width).astype(BF16)
+    back_rows = -(-(capacity + out_rows.shape[0]) // 8) * 8
+    back_packet = jnp.concatenate(
+        [
+            returned.reshape(owners, capacity, feat_width),
+            jnp.broadcast_to(out_rows[None], (owners,) + out_rows.shape),
+            jnp.zeros(
+                (owners, back_rows - capacity - out_rows.shape[0], feat_width), BF16
+            ),
+        ],
+        1,
+    )
+    back_in = lax.all_to_all(
+        back_packet, ("group", "dom"), split_axis=0, concat_axis=0, tiled=True
+    )
+    arrived = back_in[:, :capacity].reshape(-1, feat_width)
+    out_total = jnp.einsum(
+        "o,orw->rw",
+        jnp.ones((owners,), BF16),
+        back_in[:, capacity : capacity + out_rows.shape[0]],
+        preferred_element_type=F32,
+    ).reshape(-1)
     pin_grad = jnp.dot(slot_hot, arrived, preferred_element_type=F32)
     preact_grad = (pin_grad * silu_slope(preact)).astype(BF16)
     self_sum = jnp.einsum("pk,pd->kd", pin_feats, preact_grad, preferred_element_type=F32)
@@ -168,13 +183,7 @@
     grad_feats = (
         local_grad + jnp.einsum("sp,sd->pd", send_hot, received, preferred_element_type=F32)
     ).astype(BF16)
-    head_width = head_sum_t.shape[0]
-    pieces = (
-        self_sum,
-        edge_sum.reshape(-1, feat_width),
-        head_sum_t,
-        out_sum.reshape(-1, feat_width),
-    )
+    pieces = (self_sum, edge_sum.reshape(-1, feat_width), head_sum_t)
     totals = all_sum(jnp.concatenate(pieces, 0), owners)
     grad_scale = 1.0 / math.sqrt(pin_count * owners)
     outs = []
@@ -188,7 +197,7 @@
         outs[0],
         outs[1].reshape(edge_sum.shape),
         outs[2].T,
-        outs[3].reshape(head_width),
+        out_total * grad_scale,
     )
 
 

time: 188 us -> 187 us (level)
  blocking collectives: 35.6 us -> 0 us
  waiting for transfers between devices: 69.3 us -> 96.7 us
  other arithmetic: 5.69 us -> 8.96 us
  starting transfers between devices: 24.6 us -> 27.5 us
  local copies, waits for them, and re-layouts: 4.01 us -> 6.53 us
    all_to_all x1 -> x0, blocking collectives: 35.6 us -> none  [all_sum(): lax.all_to_all(rows.astype(BF16).reshape(owners, -1, width), axes, split_...]
    all_to_all x1 -> x2, waiting for transfers between devices: 26.5 us -> 58.1 us  [the longest x1 29.3 us: all_sum(): lax.all_to_all(rows.astype(BF16).reshape(owners, -1, width), axes, split_...]
    ppermute x2, waiting for transfers between devices: 5.04 us -> 2.22 us  [extended(): lax.ppermute(lax.slice_in_dim(block, block.shape[dim] - width, None, axis...]
    all_to_all x1, waiting for transfers between devices: 6.42 us -> 3.89 us  [all_sum(): lax.all_to_all(spread, axes, split_axis=0, concat_axis=0, tiled=True)]
    all_to_all x1 -> x2, starting transfers between devices: 3.77 us -> 6.21 us  [the longest x1 3.11 us: all_sum(): lax.all_to_all(rows.astype(BF16).reshape(owners, -1, width), axes, split_...]
    unnamed x39 -> x57, local copies, waits for them, and re-layouts: 2.47 us -> 4.29 us
  transfers between devices with their start and end apart: 7 -> 8, of which waited for: 5 -> 6; matrix products, arithmetic and copies ran while one was open for 10% -> 12% of each run, Pallas kernels for 0% -> 0%
where the time goes in v5:
time: 187 us; the launch traced here: 185 us
  waiting for transfers between devices  96.7 us (52%)
  matrix products  44.1 us (24%)
  starting transfers between devices  27.5 us (15%)
  other arithmetic  8.96 us (5%)
  local copies, waits for them, and re-layouts  6.53 us (3%)
    all_to_all x1, waiting for transfers between devices, all_sum(): lax.all_to_all(rows.astype(BF16).reshape(owners, -1, width), axes, split_...  29.3 us
    all_to_all x1, waiting for transfers between devices, on_device(): lax.all_to_all(packet, ('group', 'dom'), split_axis=0, concat_axis=0, til...  29.2 us
    all_to_all x1, waiting for transfers between devices, on_device(): lax.all_to_all(back_packet, ('group', 'dom'), split_axis=0, concat_axis=0...  28.8 us
    dot_general x1, matrix products, on_device(): jnp.einsum('ter,ted->trd', src_hot, edge_rows, preferred_element_type=F32)  9 us
    ppermute x2, starting transfers between devices, extended(): lax.ppermute(lax.slice_in_dim(block, block.shape[dim] - width, None, axis...  8.19 us
    all_to_all x1, starting transfers between devices, on_device(): lax.all_to_all(packet, ('group', 'dom'), split_axis=0, concat_axis=0, til...  6.15 us
    dot_general x1, matrix products, on_device(): jnp.einsum('tep,ted->tpd', dst_hot, gathered, preferred_element_type=F32)  5.76 us
    dot_general x2, matrix products, split_dot(): jnp.einsum(spec, left, right.astype(F32), precision=lax.Precision.HIGHEST...  5.19 us
  transfers between devices with their start and end apart: 8, of which 6 were waited for; matrix products, arithmetic and copies ran while one was open for 12% of the time, Pallas kernels for 0%

profile of v5, /device:TPU:1, one launch (start us, length us, event | category | flops | bytes accessed | tf_op | source)
XLA Modules:
  0.0 185.2 jit_solution(487537347089348462)
XLA Ops:
  0.6 0.0 copy-start
  0.7 1.6 fusion.28
  2.3 4.6 %collective-permute-start = (bf16[256,256]{1,0:T(8,128)(2,1)S(1)}, bf16[256,256]{1,0:T(8,128)(2,1)S(1)}, u32[]{:S(2)}, u32[]{:S(2)}) collective-permute-start(bf16[256,256]{1,0:T(8,128)(2,1)S(1)} %get-tuple-element.22), channel_id=1, source_target_pairs={{0,1},{1,2},{2,3},{3,4},{4,5},{5,6},{6,7},{8,9},{9,10},{10,11},{11... | collective-permute-start | bytes 393224 | tf_op jit(solution)/shard_map/ppermute | solution.py:18
  6.9 1.9 %collective-permute-start.1 = (bf16[256,256]{1,0:T(8,128)(2,1)S(1)}, bf16[256,256]{1,0:T(8,128)(2,1)S(1)}, u32[]{:S(2)}, u32[]{:S(2)}) collective-permute-start(bf16[256,256]{1,0:T(8,128)(2,1)S(1)} %get-tuple-element.23), channel_id=1, source_target_pairs={{1,0},{2,1},{3,2},{4,3},{5,4},{6,5},{7,6},{9,8},{10,9},{11,10},{12... | collective-permute-start | bytes 393224 | tf_op jit(solution)/shard_map/ppermute | solution.py:21
  8.9 1.9 %convert_reduce_fusion = f32[1024]{0:T(1024)S(1)} fusion(s32[4,1024]{1,0:T(4,128)S(1)} %bitcast.104), kind=kLoop, calls=%fused_computation.3 | loop fusion | flops 16776192 | bytes 20480 | tf_op jit(solution)/shard_map/reduce_sum | solution.py:88
  10.9 0.5 fusion.34
  11.4 0.0 copy-start.5
  11.5 0.0 copy-start.16
  11.5 1.5 fusion.10
  13.0 0.1 sub.16
  13.1 0.3 fusion.64
  13.5 4.8 %fusion.20 = bf16[4,1024,256]{2,1,0:T(8,128)(2,1)S(1)} fusion(s32[4,1024]{1,0:T(4,128)S(1)} %bitcast.107, bf16[256,256]{1,0:T(8,128)(2,1)S(1)} %collective-permute-done.1, bf16[256,256]{1,0:T(8,128)(2,1)S(1)} %collective-permute-done, bf16[1024,256]{1,0:T(8,128)(2,1)S(1)} %copy-done.5), kind=kOutput, calls=%fused_computation.29 | convolution fusion | flops 3230924800 | bytes 2899968 | tf_op jit(solution)/shard_map/ter,rd->ted/dot_general | solution.py:83
  18.3 5.8 %fusion.4 = f32[4,1024,256]{2,1,0:T(8,128)S(1)} fusion(bf16[4,1024,256]{2,1,0:T(8,128)(2,1)S(1)} %fusion.20, s32[4,1024]{1,0:T(4,128)S(1)} %bitcast.105), kind=kOutput, calls=%fused_computation.7 | convolution fusion | flops 2151677952 | bytes 6307840 | tf_op jit(solution)/shard_map/tep,ted->tpd/dot_general | solution.py:86
  24.1 2.1 %fusion.24 = f32[1024,256]{1,0:T(8,128)S(1)} fusion(f32[1024,256]{1,0:T(8,128)S(1)} %fusion.64, f32[4,1024,256]{2,1,0:T(8,128)S(1)} %fusion.4, bf16[4,256,256]{2,1,0:T(8,128)(2,1)S(1)} %copy-done.1, f32[1024]{0:T(1024)S(1)} %add_divide_fusion.2), kind=kOutput, calls=%fused_computation.35 | convolution fusion | flops 3221749760 | bytes 6819840 | tf_op jit(solution)/shard_map/tpk,tkd->pd/dot_general | solution.py:36
  26.2 2.5 %fusion.16 = bf16[2048,256]{1,0:T(8,128)(2,1)S(1)} fusion(s32[1024]{0:T(1024)S(1)} %bitcast.102, f32[1024,256]{1,0:T(8,128)S(1)} %fusion.24), kind=kOutput, calls=%fused_computation.22 | convolution fusion | flops 1077673984 | bytes 2101248 | tf_op jit(solution)/shard_map/dot_general | solution.py:111
  28.8 0.0 copy-start.13
  28.8 1.1 pad_maximum_fusion
  29.9 6.1 %all-to-all-start = ((bf16[32,72,256]{2,1,0:T(8,128)(2,1)}), bf16[32,72,256]{2,1,0:T(8,128)(2,1)S(1)}, u32[]{:S(2)}, u32[]{:S(2)}) async-start(bf16[32,72,256]{2,1,0:T(8,128)(2,1)} %pad_maximum_fusion), calls=%async_computation | async-start | bytes 2359296 | tf_op jit(solution)/shard_map/all_to_all | solution.py:123
  36.1 0.6 pad.13.clone
  36.7 29.2 %all-to-all-done = bf16[32,72,256]{2,1,0:T(8,128)(2,1)S(1)} async-done(((bf16[32,72,256]{2,1,0:T(8,128)(2,1)}), bf16[32,72,256]{2,1,0:T(8,128)(2,1)S(1)}, u32[]{:S(2)}, u32[]{:S(2)}) %all-to-all-start) | async-done | bytes 1179680 | tf_op jit(solution)/shard_map/all_to_all | solution.py:123
  66.0 0.1 eq.110
  66.0 0.1 slice.60
  66.2 1.1 fusion.31
  67.2 0.5 multiply_convert_fusion.2
  67.7 0.2 fusion.65
  68.0 0.6 copy-done.14
  68.5 0.3 fusion.66
  68.8 0.4 multiply_convert_fusion.1
  69.3 1.0 convolution_convert_fusion
  70.3 1.6 maximum_maximum_fusion
  71.8 3.1 %all-to-all-start.1 = ((bf16[32,72,256]{2,1,0:T(8,128)(2,1)}), bf16[32,72,256]{2,1,0:T(8,128)(2,1)S(1)}, u32[]{:S(2)}, u32[]{:S(2)}) async-start(bf16[32,72,256]{2,1,0:T(8,128)(2,1)} %maximum_maximum_fusion), calls=%async_computation.1 | async-start | bytes 2359296 | tf_op jit(solution)/shard_map/all_to_all | solution.py:156
  75.0 1.1 convolution_convert_fusion.1
  76.1 28.8 %all-to-all-done.1 = bf16[32,72,256]{2,1,0:T(8,128)(2,1)S(1)} async-done(((bf16[32,72,256]{2,1,0:T(8,128)(2,1)}), bf16[32,72,256]{2,1,0:T(8,128)(2,1)S(1)}, u32[]{:S(2)}, u32[]{:S(2)}) %all-to-all-start.1) | async-done | bytes 1179680 | tf_op jit(solution)/shard_map/all_to_all | solution.py:156
  104.9 0.1 slice.61
  105.0 1.1 copy-done.10
  106.1 1.8 fusion.26
  107.9 0.0 copy-start.6
  107.9 0.4 fusion.32
  108.3 3.3 %fusion.21 = bf16[4,1024,256]{2,1,0:T(8,128)(2,1)S(1)} fusion(s32[4,1024]{1,0:T(4,128)S(1)} %bitcast.106, bf16[1024,256]{1,0:T(8,128)(2,1)S(1)} %fusion.26, f32[1024]{0:T(1024)S(1)} %add_divide_fusion.2), kind=kOutput, calls=%fused_computation.30 | convolution fusion | flops 2153512960 | bytes 2641920 | tf_op jit(solution)/shard_map/tep,pd->ted/dot_general | solution.py:170
  111.6 0.9 convolution_convert_fusion.2
  112.5 0.4 copy-done.4
  113.0 0.1 copy-done.8
  113.0 1.1 pad_maximum_fusion.1
  114.2 3.1 %all-to-all-start.2 = ((bf16[32,72,256]{2,1,0:T(8,128)(2,1)}), bf16[32,72,256]{2,1,0:T(8,128)(2,1)S(1)}, u32[]{:S(2)}, u32[]{:S(2)}) async-start(bf16[32,72,256]{2,1,0:T(8,128)(2,1)} %bitcast.20), calls=%async_computation.2 | async-start | bytes 2359296 | tf_op jit(solution)/shard_map/all_to_all | solution.py:47
  117.3 0.6 copy.26
  118.0 29.3 %all-to-all-done.2 = bf16[32,72,256]{2,1,0:T(8,128)(2,1)S(1)} async-done(((bf16[32,72,256]{2,1,0:T(8,128)(2,1)}), bf16[32,72,256]{2,1,0:T(8,128)(2,1)S(1)}, u32[]{:S(2)}, u32[]{:S(2)}) %all-to-all-start.2) | async-done | bytes 1179680 | tf_op jit(solution)/shard_map/all_to_all | solution.py:47
  147.2 0.3 fusion.29
  147.5 1.1 broadcast_in_dim.8
  148.7 3.1 %all-to-all-start.3 = ((bf16[32,72,256]{2,1,0:T(8,128)(2,1)}), bf16[32,72,256]{2,1,0:T(8,128)(2,1)S(1)}, u32[]{:S(2)}, u32[]{:S(2)}) async-start(bf16[32,72,256]{2,1,0:T(8,128)(2,1)} %broadcast_in_dim.8), calls=%async_computation.3 | async-start | bytes 2359296 | tf_op jit(solution)/shard_map/all_to_all | solution.py:54
  151.8 9.0 %fusion = f32[4,1536,256]{2,1,0:T(8,128)S(1)} fusion(bf16[4,1024,256]{2,1,0:T(8,128)(2,1)} %copy-done.4, s32[4,1024]{1,0:T(4,128)S(1)} %bitcast.108), kind=kOutput, calls=%fused_computation.1 | convolution fusion | flops 3227516928 | bytes 8404992 | tf_op jit(solution)/shard_map/ter,ted->trd/dot_general | solution.py:174
  160.8 3.1 %fusion.63 = (bf16[1536,256]{1,0:T(8,128)(2,1)S(1)}, f32[1536,256]{1,0:T(8,128)S(1)}) fusion(f32[4,1536,256]{2,1,0:T(8,128)S(1)} %fusion, bf16[4,256,256]{2,1,0:T(8,128)(2,1)S(1)} %copy-done.1), kind=kOutput, calls=%fused_computation.99 | convolution fusion | flops 4832231424 | bytes 9175040 | tf_op jit(solution)/shard_map/trd,tkd->rk/dot_general | solution.py:36
  164.0 3.6 %collective-permute-start.2 = (bf16[256,256]{1,0:T(8,128)(2,1)S(1)}, bf16[256,256]{1,0:T(8,128)(2,1)S(1)}, u32[]{:S(2)}, u32[]{:S(2)}) collective-permute-start(bf16[256,256]{1,0:T(8,128)(2,1)S(1)} %get-tuple-element.20), channel_id=1, source_target_pairs={{0,1},{1,2},{2,3},{3,4},{4,5},{5,6},{6,7},{8,9},{9,10},{10,11},{11... | collective-permute-start | bytes 393224 | tf_op jit(solution)/shard_map/ppermute | solution.py:18
  167.6 1.9 %collective-permute-start.3 = (bf16[256,256]{1,0:T(8,128)(2,1)S(1)}, bf16[256,256]{1,0:T(8,128)(2,1)S(1)}, u32[]{:S(2)}, u32[]{:S(2)}) collective-permute-start(bf16[256,256]{1,0:T(8,128)(2,1)S(1)} %get-tuple-element.21), channel_id=1, source_target_pairs={{1,0},{2,1},{3,2},{4,3},{5,4},{6,5},{7,6},{9,8},{10,9},{11,10},{12... | collective-permute-start | bytes 393224 | tf_op jit(solution)/shard_map/ppermute | solution.py:21
  169.5 0.1 fusion.53
  169.7 0.3 convolution_add_fusion
  170.0 0.6 broadcast_multiply_fusion
  170.6 2.2 %collective-permute-done.2 = bf16[256,256]{1,0:T(8,128)(2,1)S(1)} collective-permute-done((bf16[256,256]{1,0:T(8,128)(2,1)S(1)}, bf16[256,256]{1,0:T(8,128)(2,1)S(1)}, u32[]{:S(2)}, u32[]{:S(2)}) %collective-permute-start.2) | collective-permute-done | bytes 131104 | tf_op jit(solution)/shard_map/ppermute | solution.py:18
  172.8 3.4 %collective-permute-done.3 = bf16[256,256]{1,0:T(8,128)(2,1)S(1)} collective-permute-done((bf16[256,256]{1,0:T(8,128)(2,1)S(1)}, bf16[256,256]{1,0:T(8,128)(2,1)S(1)}, u32[]{:S(2)}, u32[]{:S(2)}) %collective-permute-start.3) | collective-permute-done | bytes 131104 | tf_op jit(solution)/shard_map/ppermute | solution.py:21
  176.2 1.6 fusion.27
  177.8 3.9 %all-to-all-done.3 = bf16[32,72,256]{2,1,0:T(8,128)(2,1)S(1)} async-done(((bf16[32,72,256]{2,1,0:T(8,128)(2,1)}), bf16[32,72,256]{2,1,0:T(8,128)(2,1)S(1)}, u32[]{:S(2)}, u32[]{:S(2)}) %all-to-all-start.3) | async-done | bytes 1179680 | tf_op jit(solution)/shard_map/all_to_all | solution.py:54
  181.7 0.3 bitcast_convert_fusion
  182.0 0.7 slice_multiply_fusion.2
  182.7 1.2 fusion.35
  183.9 1.3 copy.20
  (67 shorter events, 0.4 us)
Async XLA Ops:
  0.6 66.6 %copy-start = (bf16[256,1024]{1,0:T(8,128)(2,1)S(1)}, bf16[256,1024]{1,0:T(8,128)(2,1)}, u32[]{:S(2)}) copy-start(bf16[256,1024]{1,0:T(8,128)(2,1)} %param.14) | copy-start | bytes 1572868
  0.6 8.2 %copy-start.18 = (s32[1024]{0:T(1024)S(1)}, s32[1024]{0:T(1024)}, u32[]{:S(2)}) copy-start(s32[1024]{0:T(1024)} %param.20) | copy-start | bytes 12292
  0.7 8.2 %copy-start.21 = (s32[1,4,1024]{2,1,0:T(4,128)S(1)}, s32[1,4,1024]{2,1,0:T(4,128)}, u32[]{:S(2)}) copy-start(s32[1,4,1024]{2,1,0:T(4,128)} %param.18) | copy-start | bytes 49156
  0.7 10.2 %copy-start.15 = (s32[1024,1]{0,1:T(1,128)S(1)}, s32[1024,1]{0,1:T(1,128)}, u32[]{:S(2)}) copy-start(s32[1024,1]{0,1:T(1,128)} %param.19) | copy-start | bytes 12292
  2.3 11.1 %collective-permute-start = (bf16[256,256]{1,0:T(8,128)(2,1)S(1)}, bf16[256,256]{1,0:T(8,128)(2,1)S(1)}, u32[]{:S(2)}, u32[]{:S(2)}) collective-permute-start(bf16[256,256]{1,0:T(8,128)(2,1)S(1)} %get-tuple-element.22), channel_id=1, source_target_pairs={{0,1},{1,2},{2,3},{3,4},{4,5},{5,6},{6,7},{8,9},{9,10},{10,11},{11... | collective-permute-start | bytes 393224 | tf_op jit(solution)/shard_map/ppermute | solution.py:18
  6.9 6.5 %collective-permute-start.1 = (bf16[256,256]{1,0:T(8,128)(2,1)S(1)}, bf16[256,256]{1,0:T(8,128)(2,1)S(1)}, u32[]{:S(2)}, u32[]{:S(2)}) collective-permute-start(bf16[256,256]{1,0:T(8,128)(2,1)S(1)} %get-tuple-element.23), channel_id=1, source_target_pairs={{1,0},{2,1},{3,2},{4,3},{5,4},{6,5},{7,6},{9,8},{10,9},{11,10},{12... | collective-permute-start | bytes 393224 | tf_op jit(solution)/shard_map/ppermute | solution.py:21
  11.4 1.7 copy-start.5
  11.4 1.7 copy-start.11
  11.5 14.8 %copy-start.16 = (s32[1024,1]{0,1:T(1,128)}, s32[1024,1]{0,1:T(1,128)S(1)}, u32[]{:S(2)}) copy-start(s32[1024,1]{0,1:T(1,128)S(1)} %multiply_add_fusion) | copy-start | bytes 12292
  11.5 2.0 %copy-start.23 = (s32[1,4,1024]{2,1,0:T(4,128)S(1)}, s32[1,4,1024]{2,1,0:T(4,128)}, u32[]{:S(2)}) copy-start(s32[1,4,1024]{2,1,0:T(4,128)} %param.17) | copy-start | bytes 49156
  18.3 5.8 %copy-start.2 = (bf16[4,1024,256]{2,1,0:T(8,128)(2,1)}, bf16[4,1024,256]{2,1,0:T(8,128)(2,1)S(1)}, u32[]{:S(2)}) copy-start(bf16[4,1024,256]{2,1,0:T(8,128)(2,1)S(1)} %fusion.20) | copy-start | bytes 6291460
  18.3 5.8 %copy-start.1 = (bf16[4,256,256]{2,1,0:T(8,128)(2,1)S(1)}, bf16[4,256,256]{2,1,0:T(8,128)(2,1)}, u32[]{:S(2)}) copy-start(bf16[4,256,256]{2,1,0:T(8,128)(2,1)} %param.13) | copy-start | bytes 1572868
  26.2 2.6 %copy-start.9 = (f32[1024,256]{1,0:T(8,128)}, f32[1024,256]{1,0:T(8,128)S(1)}, u32[]{:S(2)}) copy-start(f32[1024,256]{1,0:T(8,128)S(1)} %fusion.24) | copy-start | bytes 3145732
  28.8 7.3 %copy-start.13 = (bf16[1024]{0:T(1024)(128)(2,1)S(1)}, bf16[1024]{0:T(1024)(128)(2,1)}, u32[]{:S(2)}) copy-start(bf16[1024]{0:T(1024)(128)(2,1)} %param.15) | copy-start | bytes 6148
  29.9 36.0 %all-to-all-start = ((bf16[32,72,256]{2,1,0:T(8,128)(2,1)}), bf16[32,72,256]{2,1,0:T(8,128)(2,1)S(1)}, u32[]{:S(2)}, u32[]{:S(2)}) async-start(bf16[32,72,256]{2,1,0:T(8,128)(2,1)} %pad_maximum_fusion), calls=%async_computation | async-start | bytes 2359296 | tf_op jit(solution)/shard_map/all_to_all | solution.py:123
  67.2 0.7 copy-start.19
  67.9 0.6 copy-start.14
  68.8 1.5 copy-start.20
  71.8 33.1 %all-to-all-start.1 = ((bf16[32,72,256]{2,1,0:T(8,128)(2,1)}), bf16[32,72,256]{2,1,0:T(8,128)(2,1)S(1)}, u32[]{:S(2)}, u32[]{:S(2)}) async-start(bf16[32,72,256]{2,1,0:T(8,128)(2,1)} %maximum_maximum_fusion), calls=%async_computation.1 | async-start | bytes 2359296 | tf_op jit(solution)/shard_map/all_to_all | solution.py:156
  75.0 30.1 %copy-start.17 = (s32[1024,1]{0,1:T(1,128)S(1)}, s32[1024,1]{0,1:T(1,128)}, u32[]{:S(2)}) copy-start(s32[1024,1]{0,1:T(1,128)} %copy-done.16) | copy-start | bytes 12292
  104.9 1.2 copy-start.10
  106.1 2.2 %copy-start.22 = (s32[1,4,1024]{2,1,0:T(4,128)S(1)}, s32[1,4,1024]{2,1,0:T(4,128)}, u32[]{:S(2)}) copy-start(s32[1,4,1024]{2,1,0:T(4,128)} %param.18) | copy-start | bytes 49156
  107.9 3.7 %copy-start.6 = (bf16[1024,256]{1,0:T(8,128)(2,1)}, bf16[1024,256]{1,0:T(8,128)(2,1)S(1)}, u32[]{:S(2)}) copy-start(bf16[1024,256]{1,0:T(8,128)(2,1)S(1)} %fusion.26) | copy-start | bytes 1572868
  108.3 3.3 %copy-start.3 = (bf16[4,1024,256]{2,1,0:T(8,128)(2,1)S(1)}, bf16[4,1024,256]{2,1,0:T(8,128)(2,1)}, u32[]{:S(2)}) copy-start(bf16[4,1024,256]{2,1,0:T(8,128)(2,1)} %copy-done.2) | copy-start | bytes 6291460
  111.6 1.4 copy-start.4
  111.6 1.4 copy-start.8
  114.2 33.1 %all-to-all-start.2 = ((bf16[32,72,256]{2,1,0:T(8,128)(2,1)}), bf16[32,72,256]{2,1,0:T(8,128)(2,1)S(1)}, u32[]{:S(2)}, u32[]{:S(2)}) async-start(bf16[32,72,256]{2,1,0:T(8,128)(2,1)} %bitcast.20), calls=%async_computation.2 | async-start | bytes 2359296 | tf_op jit(solution)/shard_map/all_to_all | solution.py:47
  147.5 4.3 %copy-start.24 = (s32[1,4,1024]{2,1,0:T(4,128)S(1)}, s32[1,4,1024]{2,1,0:T(4,128)}, u32[]{:S(2)}) copy-start(s32[1,4,1024]{2,1,0:T(4,128)} %param.17) | copy-start | bytes 49156
  148.7 33.1 %all-to-all-start.3 = ((bf16[32,72,256]{2,1,0:T(8,128)(2,1)}), bf16[32,72,256]{2,1,0:T(8,128)(2,1)S(1)}, u32[]{:S(2)}, u32[]{:S(2)}) async-start(bf16[32,72,256]{2,1,0:T(8,128)(2,1)} %broadcast_in_dim.8), calls=%async_computation.3 | async-start | bytes 2359296 | tf_op jit(solution)/shard_map/all_to_all | solution.py:54
  160.8 8.7 %copy-start.12 = (bf16[4,8,4,256]{3,1,2,0:T(8,128)(2,1)S(1)}, bf16[4,8,4,256]{3,1,2,0:T(8,128)(2,1)}, u32[]{:S(2)}) copy-start(bf16[4,8,4,256]{3,1,2,0:T(8,128)(2,1)} %copy.26) | copy-start | bytes 196612
  160.8 8.8 %copy-start.7 = (bf16[1024,256]{1,0:T(8,128)(2,1)S(1)}, bf16[1024,256]{1,0:T(8,128)(2,1)}, u32[]{:S(2)}) copy-start(bf16[1024,256]{1,0:T(8,128)(2,1)} %copy-done.6) | copy-start | bytes 1572868
  163.9 12.3 %copy-start.25 = (s32[1,512]{1,0:T(1,128)S(1)}, s32[1,512]{1,0:T(1,128)}, u32[]{:S(2)}) copy-start(s32[1,512]{1,0:T(1,128)} %param.16) | copy-start | bytes 6148
  164.0 8.8 %collective-permute-start.2 = (bf16[256,256]{1,0:T(8,128)(2,1)S(1)}, bf16[256,256]{1,0:T(8,128)(2,1)S(1)}, u32[]{:S(2)}, u32[]{:S(2)}) collective-permute-start(bf16[256,256]{1,0:T(8,128)(2,1)S(1)} %get-tuple-element.20), channel_id=1, source_target_pairs={{0,1},{1,2},{2,3},{3,4},{4,5},{5,6},{6,7},{8,9},{9,10},{10,11},{11... | collective-permute-start | bytes 393224 | tf_op jit(solution)/shard_map/ppermute | solution.py:18
  167.6 8.6 %collective-permute-start.3 = (bf16[256,256]{1,0:T(8,128)(2,1)S(1)}, bf16[256,256]{1,0:T(8,128)(2,1)S(1)}, u32[]{:S(2)}, u32[]{:S(2)}) collective-permute-start(bf16[256,256]{1,0:T(8,128)(2,1)S(1)} %get-tuple-element.21), channel_id=1, source_target_pairs={{1,0},{2,1},{3,2},{4,3},{5,4},{6,5},{7,6},{9,8},{10,9},{11,10},{12... | collective-permute-start | bytes 393224 | tf_op jit(solution)/shard_map/ppermute | solution.py:21

commit v6 on v5

--- a/solution.py
+++ b/solution.py
@@ -10,9 +10,18 @@
 BF16 = jnp.bfloat16
 
 
+DOM = ("zdom", "core")
+ALL = ("group",) + DOM
+CHIP = ("group", "zdom")
+
+
+def size_of(axes):
+    return math.prod(lax.axis_size(axis) for axis in axes)
+
+
 def extended(block, sides, width):
     for axis, dim in sides:
-        count = lax.axis_size(axis)
+        count = size_of(axis)
         forward = [(i, i + 1) for i in range(count - 1)]
         backward = [(target, source) for source, target in forward]
         low = lax.ppermute(
@@ -40,19 +49,30 @@
 
 def all_sum(rows, owners):
     count, width = rows.shape
-    unit = owners * 8
+    chips = size_of(CHIP)
+    cores = lax.axis_size("core")
+    unit = chips * cores * 8
     length = -(-count // unit) * unit
-    rows = jnp.pad(rows, ((0, length - count), (0, 0)))
-    axes = ("group", "dom")
+    rows = jnp.pad(rows, ((0, length - count), (0, 0))).reshape(cores, length // cores, width)
+    core = lax.axis_index("core")
+    swap = [(i, (i + 1) % cores) for i in range(cores)]
+    kept = lax.dynamic_index_in_dim(rows, core, 0, keepdims=False)
+    given = lax.dynamic_index_in_dim(rows, (core + 1) % cores, 0, keepdims=False)
+    half = kept + lax.ppermute(given, "core", swap)
     mine = lax.all_to_all(
-        rows.astype(BF16).reshape(owners, -1, width), axes, split_axis=0, concat_axis=0, tiled=True
+        half.astype(BF16).reshape(chips, -1, width), CHIP, split_axis=0, concat_axis=0, tiled=True
     )
     mine = jnp.einsum(
-        "o,orw->rw", jnp.ones((owners,), BF16), mine, preferred_element_type=F32
-    ).astype(BF16)
-    spread = jnp.broadcast_to(mine[None], (owners,) + mine.shape)
-    gathered = lax.all_to_all(spread, axes, split_axis=0, concat_axis=0, tiled=True)
-    return gathered.reshape(length, width)[:count].astype(F32)
+        "o,orw->rw", jnp.ones((chips,), BF16), mine, preferred_element_type=F32
+    ).astype(BF16)
+    spread = jnp.broadcast_to(mine[None], (chips,) + mine.shape)
+    own_half = lax.all_to_all(spread, CHIP, split_axis=0, concat_axis=0, tiled=True).reshape(
+        -1, width
+    )
+    other_half = lax.ppermute(own_half, "core", swap)
+    first = jnp.where(core == 0, own_half, other_half)
+    second = jnp.where(core == 0, other_half, own_half)
+    return jnp.concatenate([first, second], 0)[:count].astype(F32)
 
 
 def on_device(
@@ -73,7 +93,7 @@
     halo_span = send_list.shape[0] // 2
     send_hot = one_hot(send_list, pin_count)
     outgoing = jnp.dot(send_hot, pin_feats, preferred_element_type=F32).astype(BF16)
-    padded = extended(outgoing, (("dom", 0),), halo_span)
+    padded = extended(outgoing, ((DOM, 0),), halo_span)
     node_table = jnp.concatenate([pin_feats, padded[:halo_span], padded[3 * halo_span :]], 0)
     table_rows = node_table.shape[0]
     sources = edge_src[0]
@@ -92,7 +112,7 @@
     )
     hidden = jax.nn.silu(preact).astype(BF16)
     groups = lax.axis_size("group")
-    domains = lax.axis_size("dom")
+    domains = size_of(DOM)
     owners = groups * domains
     capacity = max(2, 2 * pin_count // owners)
     net_count = net_target.shape[0]
@@ -120,7 +140,7 @@
         ],
         1,
     )
-    packet_in = lax.all_to_all(packet, ("group", "dom"), split_axis=0, concat_axis=0, tiled=True)
+    packet_in = lax.all_to_all(packet, ALL, split_axis=0, concat_axis=0, tiled=True)
     inbound = packet_in[:, :capacity].reshape(-1, feat_width)
     slot_nets_in = (
         packet_in[:, capacity:].reshape(owners, -1)[:, :capacity].astype(F32).astype(jnp.int32)
@@ -154,7 +174,7 @@
         1,
     )
     back_in = lax.all_to_all(
-        back_packet, ("group", "dom"), split_axis=0, concat_axis=0, tiled=True
+        back_packet, ALL, split_axis=0, concat_axis=0, tiled=True
     )
     arrived = back_in[:, :capacity].reshape(-1, feat_width)
     out_total = jnp.einsum(
@@ -178,7 +198,7 @@
         + table_grad[:pin_count]
     )
     halo_grad = table_grad[pin_count:].astype(BF16)
-    back_padded = extended(halo_grad, (("dom", 0),), halo_span)
+    back_padded = extended(halo_grad, ((DOM, 0),), halo_span)
     received = jnp.concatenate([back_padded[:halo_span], back_padded[3 * halo_span :]], 0)
     grad_feats = (
         local_grad + jnp.einsum("sp,sd->pd", send_hot, received, preferred_element_type=F32)
@@ -203,19 +223,24 @@
 
 def solution(mesh):
     in_specs = (
-        P(("group", "dom"), None),
-        P(),
-        P(),
-        P(),
-        P(),
-        P(("group", "dom"), None),
-        P(("group", "dom"), None, None),
-        P(("group", "dom"), None, None),
-        P(("group", "dom"), None),
-        P(("group", "dom")),
-        P(("group", "dom")),
-    )
-    out_specs = (P(("group", "dom")), P(("group", "dom"), None), P(), P(), P(), P())
+        P(ALL, None),
+        P(),
+        P(),
+        P(),
+        P(),
+        P(ALL, None),
+        P(ALL, None, None),
+        P(ALL, None, None),
+        P(ALL, None),
+        P(ALL),
+        P(ALL),
+    )
+    out_specs = (P(ALL), P(ALL, None), P(), P(), P(), P())
+    shape = mesh.devices.shape
+    cores = 2
+    chip_mesh = jax.sharding.Mesh(
+        mesh.devices.reshape(shape[0], shape[1] // cores, cores), ("group", "zdom", "core")
+    )
     return jax.shard_map(
-        on_device, mesh=mesh, in_specs=in_specs, out_specs=out_specs, check_vma=False
-    )
+        on_device, mesh=chip_mesh, in_specs=in_specs, out_specs=out_specs, check_vma=False
+    )

time: 187 us -> 180 us (0.963)
  waiting for transfers between devices: 96.7 us -> 80.8 us
  starting transfers between devices: 27.5 us -> 30.7 us
  other arithmetic: 8.96 us -> 11.6 us
  matrix products: 44.1 us -> 46.5 us
    all_to_all x4, waiting for transfers between devices: 91.1 us -> 74.8 us  [the longest x1 29.2 us: on_device(): lax.all_to_all(packet, ALL, split_axis=0, concat_axis=0, tiled=True)]
    ppermute x0 -> x2, waiting for transfers between devices: none -> 2.82 us  [the longest x1 2.82 us: all_sum(): half = kept + lax.ppermute(given, 'core', swap)]
    ppermute x2, waiting for transfers between devices: 2.22 us -> 0.01 us  [extended(): lax.ppermute(lax.slice_in_dim(block, block.shape[dim] - width, None, axis...]
    convert_element_type x1, other arithmetic: 0.25 us -> 2.2 us  [all_sum(): half.astype(BF16).reshape(chips, -1, width)]
    unnamed x57 -> x53, local copies, waits for them, and re-layouts: 4.29 us -> 4.1 us
  transfers between devices with their start and end apart: 8 -> 10, of which waited for: 6 -> 5; matrix products, arithmetic and copies ran while one was open for 12% -> 14% of each run, Pallas kernels for 0% -> 0%
where the time goes in v6:
time: 180 us; the launch traced here: 179 us
  waiting for transfers between devices  80.8 us (45%)
  matrix products  46.5 us (26%)
  starting transfers between devices  30.7 us (17%)
  other arithmetic  11.6 us (6%)
  local copies, waits for them, and re-layouts  8.08 us (4%)
    all_to_all x1, waiting for transfers between devices, on_device(): lax.all_to_all(packet, ALL, split_axis=0, concat_axis=0, tiled=True)  29.2 us
    all_to_all x1, waiting for transfers between devices, on_device(): lax.all_to_all(back_packet, ALL, split_axis=0, concat_axis=0, tiled=True)  28.6 us
    all_to_all x1, waiting for transfers between devices, all_sum(): lax.all_to_all(half.astype(BF16).reshape(chips, -1, width), CHIP, split_a...  17 us
    ppermute x2, starting transfers between devices, extended(): lax.ppermute(lax.slice_in_dim(block, block.shape[dim] - width, None, axis...  9.17 us
    dot_general x1, matrix products, on_device(): jnp.einsum('ter,ted->trd', src_hot, edge_rows, preferred_element_type=F32)  9 us
    all_to_all x1, starting transfers between devices, on_device(): lax.all_to_all(packet, ALL, split_axis=0, concat_axis=0, tiled=True)  6.15 us
    dot_general x1, matrix products, on_device(): jnp.einsum('tep,ted->tpd', dst_hot, gathered, preferred_element_type=F32)  5.76 us
    dot_general x2, matrix products, split_dot(): jnp.einsum(spec, left, right.astype(F32), precision=lax.Precision.HIGHEST...  5.19 us
  transfers between devices with their start and end apart: 10, of which 5 were waited for; matrix products, arithmetic and copies ran while one was open for 14% of the time, Pallas kernels for 0%

profile of v6, /device:TPU:1, one launch (start us, length us, event | category | flops | bytes accessed | tf_op | source)
XLA Modules:
  0.0 179.1 jit_solution(1589773370556388376)
XLA Ops:
  0.7 1.6 fusion.28
  2.3 4.6 %collective-permute-start = (bf16[256,256]{1,0:T(8,128)(2,1)S(1)}, bf16[256,256]{1,0:T(8,128)(2,1)S(1)}, u32[]{:S(2)}, u32[]{:S(2)}) collective-permute-start(bf16[256,256]{1,0:T(8,128)(2,1)S(1)} %get-tuple-element.24), channel_id=1, source_target_pairs={{0,1},{1,2},{2,3},{3,4},{4,5},{5,6},{6,7},{8,9},{9,10},{10,11},{11... | collective-permute-start | bytes 393224 | tf_op jit(solution)/shard_map/ppermute | solution.py:27
  6.9 1.9 %collective-permute-start.1 = (bf16[256,256]{1,0:T(8,128)(2,1)S(1)}, bf16[256,256]{1,0:T(8,128)(2,1)S(1)}, u32[]{:S(2)}, u32[]{:S(2)}) collective-permute-start(bf16[256,256]{1,0:T(8,128)(2,1)S(1)} %get-tuple-element.25), channel_id=1, source_target_pairs={{1,0},{2,1},{3,2},{4,3},{5,4},{6,5},{7,6},{9,8},{10,9},{11,10},{12... | collective-permute-start | bytes 393224 | tf_op jit(solution)/shard_map/ppermute | solution.py:30
  8.8 0.7 add_convert_fusion.1
  9.6 2.8 %convert_reduce_fusion = f32[1024]{0:T(1024)S(1)} fusion(s32[4,1024]{1,0:T(4,128)} %bitcast.114), kind=kLoop, calls=%fused_computation.3 | loop fusion | flops 16776192 | bytes 20480 | tf_op jit(solution)/shard_map/reduce_sum | solution.py:108
  12.4 1.3 fusion.32
  13.8 1.5 fusion.10
  15.3 0.1 sub.16
  15.4 0.3 fusion.63
  15.8 4.8 %fusion.20 = bf16[4,1024,256]{2,1,0:T(8,128)(2,1)S(1)} fusion(s32[4,1024]{1,0:T(4,128)S(1)} %bitcast.117, bf16[256,256]{1,0:T(8,128)(2,1)S(1)} %collective-permute-done.1, bf16[256,256]{1,0:T(8,128)(2,1)S(1)} %collective-permute-done, bf16[1024,256]{1,0:T(8,128)(2,1)S(1)} %copy-done.7), kind=kOutput, calls=%fused_computation.30 | convolution fusion | flops 3230924800 | bytes 2899968 | tf_op jit(solution)/shard_map/ter,rd->ted/dot_general | solution.py:103
  20.7 5.8 %fusion.4 = f32[4,1024,256]{2,1,0:T(8,128)S(1)} fusion(bf16[4,1024,256]{2,1,0:T(8,128)(2,1)S(1)} %fusion.20, s32[4,1024]{1,0:T(4,128)S(1)} %bitcast.115), kind=kOutput, calls=%fused_computation.7 | convolution fusion | flops 2151677952 | bytes 6307840 | tf_op jit(solution)/shard_map/tep,ted->tpd/dot_general | solution.py:106
  26.5 2.1 %fusion.24 = f32[1024,256]{1,0:T(8,128)S(1)} fusion(f32[1024,256]{1,0:T(8,128)S(1)} %fusion.63, f32[4,1024,256]{2,1,0:T(8,128)S(1)} %fusion.4, bf16[4,256,256]{2,1,0:T(8,128)(2,1)S(1)} %copy-done.3, f32[1024]{0:T(1024)S(1)} %add_divide_fusion.2), kind=kOutput, calls=%fused_computation.36 | convolution fusion | flops 3221749760 | bytes 6819840 | tf_op jit(solution)/shard_map/tpk,tkd->pd/dot_general | solution.py:45
  28.6 1.0 copy-done.10
  29.5 2.5 %fusion.16 = bf16[2048,256]{1,0:T(8,128)(2,1)S(1)} fusion(s32[1024]{0:T(1024)S(1)} %bitcast.112, f32[1024,256]{1,0:T(8,128)S(1)} %fusion.24), kind=kOutput, calls=%fused_computation.22 | convolution fusion | flops 1077673984 | bytes 2101248 | tf_op jit(solution)/shard_map/dot_general | solution.py:131
  32.1 1.1 pad_maximum_fusion.1
  33.2 6.2 %all-to-all-start = ((bf16[32,72,256]{2,1,0:T(8,128)(2,1)}), bf16[32,72,256]{2,1,0:T(8,128)(2,1)S(1)}, u32[]{:S(2)}, u32[]{:S(2)}) async-start(bf16[32,72,256]{2,1,0:T(8,128)(2,1)} %pad_maximum_fusion.1), calls=%async_computation | async-start | bytes 2359296 | tf_op jit(solution)/shard_map/all_to_all | solution.py:143
  39.4 0.6 pad.15.clone
  40.0 29.2 %all-to-all-done = bf16[32,72,256]{2,1,0:T(8,128)(2,1)S(1)} async-done(((bf16[32,72,256]{2,1,0:T(8,128)(2,1)}), bf16[32,72,256]{2,1,0:T(8,128)(2,1)S(1)}, u32[]{:S(2)}, u32[]{:S(2)}) %all-to-all-start) | async-done | bytes 1179680 | tf_op jit(solution)/shard_map/all_to_all | solution.py:143
  69.2 0.1 eq.116
  69.3 0.1 slice.60
  69.4 1.1 fusion.30
  70.5 0.5 multiply_convert_fusion.2
  71.0 0.2 fusion.64
  71.2 0.0 copy-done.17
  71.2 0.5 copy-done.13
  71.8 0.3 fusion.65
  72.1 0.4 multiply_convert_fusion.1
  72.5 1.0 convolution_convert_fusion
  73.6 1.5 maximum_maximum_fusion
  75.1 3.1 %all-to-all-start.1 = ((bf16[32,72,256]{2,1,0:T(8,128)(2,1)}), bf16[32,72,256]{2,1,0:T(8,128)(2,1)S(1)}, u32[]{:S(2)}, u32[]{:S(2)}) async-start(bf16[32,72,256]{2,1,0:T(8,128)(2,1)} %maximum_maximum_fusion), calls=%async_computation.1 | async-start | bytes 2359296 | tf_op jit(solution)/shard_map/all_to_all | solution.py:176
  78.2 1.3 fusion.67
  79.6 28.6 %all-to-all-done.1 = bf16[32,72,256]{2,1,0:T(8,128)(2,1)S(1)} async-done(((bf16[32,72,256]{2,1,0:T(8,128)(2,1)}), bf16[32,72,256]{2,1,0:T(8,128)(2,1)S(1)}, u32[]{:S(2)}, u32[]{:S(2)}) %all-to-all-start.1) | async-done | bytes 1179680 | tf_op jit(solution)/shard_map/all_to_all | solution.py:176
  108.2 0.1 slice.61
  108.3 3.3 %fusion.26 = bf16[1024,256]{1,0:T(8,128)(2,1)S(1)} fusion(bf16[2048,256]{1,0:T(8,128)(2,1)S(1)} %bitcast.93, s32[1024]{0:T(1024)S(1)} %bitcast.113, f32[1024,256]{1,0:T(8,128)} %copy-done.10), kind=kOutput, calls=%fused_computation.38 | convolution fusion | flops 1078198272 | bytes 2625536 | tf_op jit(solution)/shard_map/dot_general | solution.py:186
  111.6 0.3 convolution_bitcast_fusion.2
  112.0 3.3 %fusion.21 = bf16[4,1024,256]{2,1,0:T(8,128)(2,1)S(1)} fusion(s32[4,1024]{1,0:T(4,128)S(1)} %bitcast.116, bf16[1024,256]{1,0:T(8,128)(2,1)S(1)} %fusion.26, f32[1024]{0:T(1024)S(1)} %add_divide_fusion.2), kind=kOutput, calls=%fused_computation.31 | convolution fusion | flops 2153512960 | bytes 2641920 | tf_op jit(solution)/shard_map/tep,pd->ted/dot_general | solution.py:190
  115.3 0.9 fusion.66
  116.2 0.5 copy-done.6
  116.7 0.6 copy-done.2
  117.3 0.2 pad_maximum_fusion
  117.5 1.1 dynamic-slice_bitcast_fusion
  118.6 0.9 collective-permute-start.4
  119.4 2.8 %collective-permute-done.4 = f32[1152,256]{1,0:T(8,128)} collective-permute-done((f32[1152,256]{1,0:T(8,128)}, f32[1152,256]{1,0:T(8,128)}, u32[]{:S(2)}, u32[]{:S(2)}) %collective-permute-start.4) | collective-permute-done | bytes 1179680 | tf_op jit(solution)/shard_map/ppermute | solution.py:61
  122.2 2.2 %fusion.29 = bf16[1152,256]{1,0:T(8,128)(2,1)} fusion(f32[1152,256]{1,0:T(8,128)} %collective-permute-done.4, f32[2,1152,256]{2,1,0:T(8,128)S(1)} %bitcast.88, s32[]{:T(128)S(6)} %select_n.27), kind=kLoop, calls=%fused_computation.44 | loop fusion | flops 589824 | bytes 2949124 | tf_op jit(solution)/shard_map/convert_element_type | solution.py:63
  124.4 3.7 %all-to-all-start.2 = ((bf16[16,72,256]{2,1,0:T(8,128)(2,1)}), bf16[16,72,256]{2,1,0:T(8,128)(2,1)S(1)}, u32[]{:S(2)}, u32[]{:S(2)}) async-start(bf16[16,72,256]{2,1,0:T(8,128)(2,1)} %bitcast.23), calls=%async_computation.2 | async-start | bytes 1179648 | tf_op jit(solution)/shard_map/all_to_all | solution.py:62
  128.2 17.0 %all-to-all-done.2 = bf16[16,72,256]{2,1,0:T(8,128)(2,1)S(1)} async-done(((bf16[16,72,256]{2,1,0:T(8,128)(2,1)}), bf16[16,72,256]{2,1,0:T(8,128)(2,1)S(1)}, u32[]{:S(2)}, u32[]{:S(2)}) %all-to-all-start.2) | async-done | bytes 589856 | tf_op jit(solution)/shard_map/all_to_all | solution.py:62
  145.2 0.2 fusion.41
  145.4 0.9 broadcast_in_dim.10
  146.3 3.8 %all-to-all-start.3 = ((bf16[16,72,256]{2,1,0:T(8,128)(2,1)}), bf16[16,72,256]{2,1,0:T(8,128)(2,1)S(1)}, u32[]{:S(2)}, u32[]{:S(2)}) async-start(bf16[16,72,256]{2,1,0:T(8,128)(2,1)} %broadcast_in_dim.10), calls=%async_computation.3 | async-start | bytes 1179648 | tf_op jit(solution)/shard_map/all_to_all | solution.py:69
  150.1 9.0 %fusion = f32[4,1536,256]{2,1,0:T(8,128)S(1)} fusion(bf16[4,1024,256]{2,1,0:T(8,128)(2,1)} %copy-done.6, s32[4,1024]{1,0:T(4,128)S(1)} %bitcast.118), kind=kOutput, calls=%fused_computation.1 | convolution fusion | flops 3227516928 | bytes 8404992 | tf_op jit(solution)/shard_map/ter,ted->trd/dot_general | solution.py:194
  159.1 0.9 slice.65
  160.1 3.1 %fusion.62 = (bf16[1536,256]{1,0:T(8,128)(2,1)S(1)}, f32[1536,256]{1,0:T(8,128)S(1)}) fusion(f32[4,1536,256]{2,1,0:T(8,128)S(1)} %fusion, bf16[4,256,256]{2,1,0:T(8,128)(2,1)S(1)} %copy-done.3), kind=kOutput, calls=%fused_computation.100 | convolution fusion | flops 4832231424 | bytes 9175040 | tf_op jit(solution)/shard_map/trd,tkd->rk/dot_general | solution.py:45
  163.2 4.6 %collective-permute-start.2 = (bf16[256,256]{1,0:T(8,128)(2,1)S(1)}, bf16[256,256]{1,0:T(8,128)(2,1)S(1)}, u32[]{:S(2)}, u32[]{:S(2)}) collective-permute-start(bf16[256,256]{1,0:T(8,128)(2,1)S(1)} %get-tuple-element.22), channel_id=1, source_target_pairs={{0,1},{1,2},{2,3},{3,4},{4,5},{5,6},{6,7},{8,9},{9,10},{10,11},{11... | collective-permute-start | bytes 393224 | tf_op jit(solution)/shard_map/ppermute | solution.py:27
  167.8 1.9 %collective-permute-start.3 = (bf16[256,256]{1,0:T(8,128)(2,1)S(1)}, bf16[256,256]{1,0:T(8,128)(2,1)S(1)}, u32[]{:S(2)}, u32[]{:S(2)}) collective-permute-start(bf16[256,256]{1,0:T(8,128)(2,1)S(1)} %get-tuple-element.23), channel_id=1, source_target_pairs={{1,0},{2,1},{3,2},{4,3},{5,4},{6,5},{7,6},{9,8},{10,9},{11,10},{12... | collective-permute-start | bytes 393224 | tf_op jit(solution)/shard_map/ppermute | solution.py:30
  169.8 0.3 convolution_add_fusion
  170.1 0.1 collective-permute-start.5
  170.2 0.1 fusion.52
  170.3 0.6 broadcast_multiply_fusion
  170.9 3.2 %collective-permute-done.3 = bf16[256,256]{1,0:T(8,128)(2,1)S(1)} collective-permute-done((bf16[256,256]{1,0:T(8,128)(2,1)S(1)}, bf16[256,256]{1,0:T(8,128)(2,1)S(1)}, u32[]{:S(2)}, u32[]{:S(2)}) %collective-permute-start.3) | collective-permute-done | bytes 131104 | tf_op jit(solution)/shard_map/ppermute | solution.py:30
  174.1 1.6 fusion.27
  175.7 0.1 broadcast_select_fusion.1
  175.9 0.7 convert_multiply_fusion.1
  176.6 1.2 multiply_bitcast_fusion
  177.7 1.3 copy.20
  (69 shorter events, 0.4 us)
Async XLA Ops:
  0.6 69.8 %copy-start = (bf16[256,1024]{1,0:T(8,128)(2,1)S(1)}, bf16[256,1024]{1,0:T(8,128)(2,1)}, u32[]{:S(2)}) copy-start(bf16[256,1024]{1,0:T(8,128)(2,1)} %param.14) | copy-start | bytes 1572868
  0.6 13.1 %copy-start.14 = (s32[1024,1]{0,1:T(1,128)S(1)}, s32[1024,1]{0,1:T(1,128)}, u32[]{:S(2)}) copy-start(s32[1024,1]{0,1:T(1,128)} %param.19) | copy-start | bytes 12292
  2.3 13.4 %collective-permute-start = (bf16[256,256]{1,0:T(8,128)(2,1)S(1)}, bf16[256,256]{1,0:T(8,128)(2,1)S(1)}, u32[]{:S(2)}, u32[]{:S(2)}) collective-permute-start(bf16[256,256]{1,0:T(8,128)(2,1)S(1)} %get-tuple-element.24), channel_id=1, source_target_pairs={{0,1},{1,2},{2,3},{3,4},{4,5},{5,6},{6,7},{8,9},{9,10},{10,11},{11... | collective-permute-start | bytes 393224 | tf_op jit(solution)/shard_map/ppermute | solution.py:27
  6.9 8.8 %collective-permute-start.1 = (bf16[256,256]{1,0:T(8,128)(2,1)S(1)}, bf16[256,256]{1,0:T(8,128)(2,1)S(1)}, u32[]{:S(2)}, u32[]{:S(2)}) collective-permute-start(bf16[256,256]{1,0:T(8,128)(2,1)S(1)} %get-tuple-element.25), channel_id=1, source_target_pairs={{1,0},{2,1},{3,2},{4,3},{5,4},{6,5},{7,6},{9,8},{10,9},{11,10},{12... | collective-permute-start | bytes 393224 | tf_op jit(solution)/shard_map/ppermute | solution.py:30
  12.4 3.0 %copy-start.7 = (bf16[1024,256]{1,0:T(8,128)(2,1)S(1)}, bf16[1024,256]{1,0:T(8,128)(2,1)}, u32[]{:S(2)}) copy-start(bf16[1024,256]{1,0:T(8,128)(2,1)} %param.11) | copy-start | bytes 1572868
  12.4 3.0 %copy-start.11 = (bf16[256,256]{1,0:T(8,128)(2,1)S(1)}, bf16[256,256]{1,0:T(8,128)(2,1)}, u32[]{:S(2)}) copy-start(bf16[256,256]{1,0:T(8,128)(2,1)} %param.12) | copy-start | bytes 393220
  13.8 14.8 %copy-start.15 = (s32[1024,1]{0,1:T(1,128)}, s32[1024,1]{0,1:T(1,128)S(1)}, u32[]{:S(2)}) copy-start(s32[1024,1]{0,1:T(1,128)S(1)} %multiply_add_fusion) | copy-start | bytes 12292
  13.8 2.0 %copy-start.21 = (s32[1,4,1024]{2,1,0:T(4,128)S(1)}, s32[1,4,1024]{2,1,0:T(4,128)}, u32[]{:S(2)}) copy-start(s32[1,4,1024]{2,1,0:T(4,128)} %param.17) | copy-start | bytes 49156
  15.8 4.9 %copy-start.19 = (s32[1,4,1024]{2,1,0:T(4,128)S(1)}, s32[1,4,1024]{2,1,0:T(4,128)}, u32[]{:S(2)}) copy-start(s32[1,4,1024]{2,1,0:T(4,128)} %param.18) | copy-start | bytes 49156
  20.6 5.8 %copy-start.4 = (bf16[4,1024,256]{2,1,0:T(8,128)(2,1)}, bf16[4,1024,256]{2,1,0:T(8,128)(2,1)S(1)}, u32[]{:S(2)}) copy-start(bf16[4,1024,256]{2,1,0:T(8,128)(2,1)S(1)} %fusion.20) | copy-start | bytes 6291460
  20.6 5.8 %copy-start.3 = (bf16[4,256,256]{2,1,0:T(8,128)(2,1)S(1)}, bf16[4,256,256]{2,1,0:T(8,128)(2,1)}, u32[]{:S(2)}) copy-start(bf16[4,256,256]{2,1,0:T(8,128)(2,1)} %param.13) | copy-start | bytes 1572868
  28.5 1.0 copy-start.10
  32.1 7.3 %copy-start.12 = (bf16[1024]{0:T(1024)(128)(2,1)S(1)}, bf16[1024]{0:T(1024)(128)(2,1)}, u32[]{:S(2)}) copy-start(bf16[1024]{0:T(1024)(128)(2,1)} %param.15) | copy-start | bytes 6148
  33.2 36.0 %all-to-all-start = ((bf16[32,72,256]{2,1,0:T(8,128)(2,1)}), bf16[32,72,256]{2,1,0:T(8,128)(2,1)S(1)}, u32[]{:S(2)}, u32[]{:S(2)}) async-start(bf16[32,72,256]{2,1,0:T(8,128)(2,1)} %pad_maximum_fusion.1), calls=%async_computation | async-start | bytes 2359296 | tf_op jit(solution)/shard_map/all_to_all | solution.py:143
  70.5 0.7 copy-start.17
  71.2 0.6 copy-start.13
  71.2 2.4 %copy-start.18 = (bf16[72]{0:T(256)(128)(2,1)S(1)}, bf16[72]{0:T(256)(128)(2,1)}, u32[]{:S(2)}) copy-start(bf16[72]{0:T(256)(128)(2,1)} %pad.15.clone) | copy-start | bytes 436
  75.1 33.1 %all-to-all-start.1 = ((bf16[32,72,256]{2,1,0:T(8,128)(2,1)}), bf16[32,72,256]{2,1,0:T(8,128)(2,1)S(1)}, u32[]{:S(2)}, u32[]{:S(2)}) async-start(bf16[32,72,256]{2,1,0:T(8,128)(2,1)} %maximum_maximum_fusion), calls=%async_computation.1 | async-start | bytes 2359296 | tf_op jit(solution)/shard_map/all_to_all | solution.py:176
  78.2 30.1 %copy-start.16 = (s32[1024,1]{0,1:T(1,128)S(1)}, s32[1024,1]{0,1:T(1,128)}, u32[]{:S(2)}) copy-start(s32[1024,1]{0,1:T(1,128)} %copy-done.15) | copy-start | bytes 12292
  108.1 3.4 %copy-start.1 = (bf16[32,72,256]{2,1,0:T(8,128)(2,1)}, bf16[32,72,256]{2,1,0:T(8,128)(2,1)S(1)}, u32[]{:S(2)}) copy-start(bf16[32,72,256]{2,1,0:T(8,128)(2,1)S(1)} %all-to-all-done.1) | copy-start | bytes 3538948
  108.3 3.7 %copy-start.20 = (s32[1,4,1024]{2,1,0:T(4,128)S(1)}, s32[1,4,1024]{2,1,0:T(4,128)}, u32[]{:S(2)}) copy-start(s32[1,4,1024]{2,1,0:T(4,128)} %param.18) | copy-start | bytes 49156
  111.6 3.7 %copy-start.8 = (bf16[1024,256]{1,0:T(8,128)(2,1)}, bf16[1024,256]{1,0:T(8,128)(2,1)S(1)}, u32[]{:S(2)}) copy-start(bf16[1024,256]{1,0:T(8,128)(2,1)S(1)} %fusion.26) | copy-start | bytes 1572868
  112.0 3.3 %copy-start.5 = (bf16[4,1024,256]{2,1,0:T(8,128)(2,1)S(1)}, bf16[4,1024,256]{2,1,0:T(8,128)(2,1)}, u32[]{:S(2)}) copy-start(bf16[4,1024,256]{2,1,0:T(8,128)(2,1)} %copy-done.4) | copy-start | bytes 6291460
  115.3 1.4 copy-start.6
  115.3 2.0 %copy-start.2 = (f32[1024,256]{1,0:T(8,128)S(1)}, f32[1024,256]{1,0:T(8,128)}, u32[]{:S(2)}) copy-start(f32[1024,256]{1,0:T(8,128)} %fusion.67) | copy-start | bytes 3145732
  118.6 3.7 %collective-permute-start.4 = (f32[1152,256]{1,0:T(8,128)}, f32[1152,256]{1,0:T(8,128)}, u32[]{:S(2)}, u32[]{:S(2)}) collective-permute-start(f32[1152,256]{1,0:T(8,128)} %dynamic-slice_bitcast_fusion), channel_id=1, source_target_pairs={{0,1},{1,0},{2,3},{3,2},{4,5},{5,4},{6,7},{7,6},{8,9},{9,8},{10,11... | collective-permute-start | bytes 3538952 | tf_op jit(solution)/shard_map/ppermute | solution.py:61
  124.4 25.7 %copy-start.22 = (s32[1,4,1024]{2,1,0:T(4,128)S(1)}, s32[1,4,1024]{2,1,0:T(4,128)}, u32[]{:S(2)}) copy-start(s32[1,4,1024]{2,1,0:T(4,128)} %param.17) | copy-start | bytes 49156
  124.4 20.7 %all-to-all-start.2 = ((bf16[16,72,256]{2,1,0:T(8,128)(2,1)}), bf16[16,72,256]{2,1,0:T(8,128)(2,1)S(1)}, u32[]{:S(2)}, u32[]{:S(2)}) async-start(bf16[16,72,256]{2,1,0:T(8,128)(2,1)} %bitcast.23), calls=%async_computation.2 | async-start | bytes 1179648 | tf_op jit(solution)/shard_map/all_to_all | solution.py:62
  146.3 23.8 %all-to-all-start.3 = ((bf16[16,72,256]{2,1,0:T(8,128)(2,1)}), bf16[16,72,256]{2,1,0:T(8,128)(2,1)S(1)}, u32[]{:S(2)}, u32[]{:S(2)}) async-start(bf16[16,72,256]{2,1,0:T(8,128)(2,1)} %broadcast_in_dim.10), calls=%async_computation.3 | async-start | bytes 1179648 | tf_op jit(solution)/shard_map/all_to_all | solution.py:69
  160.1 9.7 %copy-start.9 = (bf16[1024,256]{1,0:T(8,128)(2,1)S(1)}, bf16[1024,256]{1,0:T(8,128)(2,1)}, u32[]{:S(2)}) copy-start(bf16[1024,256]{1,0:T(8,128)(2,1)} %copy-done.8) | copy-start | bytes 1572868
  163.2 10.9 %copy-start.23 = (s32[1,512]{1,0:T(1,128)S(1)}, s32[1,512]{1,0:T(1,128)}, u32[]{:S(2)}) copy-start(s32[1,512]{1,0:T(1,128)} %param.16) | copy-start | bytes 6148
  163.2 7.7 %collective-permute-start.2 = (bf16[256,256]{1,0:T(8,128)(2,1)S(1)}, bf16[256,256]{1,0:T(8,128)(2,1)S(1)}, u32[]{:S(2)}, u32[]{:S(2)}) collective-permute-start(bf16[256,256]{1,0:T(8,128)(2,1)S(1)} %get-tuple-element.22), channel_id=1, source_target_pairs={{0,1},{1,2},{2,3},{3,4},{4,5},{5,6},{6,7},{8,9},{9,10},{10,11},{11... | collective-permute-start | bytes 393224 | tf_op jit(solution)/shard_map/ppermute | solution.py:27
  167.8 6.3 %collective-permute-start.3 = (bf16[256,256]{1,0:T(8,128)(2,1)S(1)}, bf16[256,256]{1,0:T(8,128)(2,1)S(1)}, u32[]{:S(2)}, u32[]{:S(2)}) collective-permute-start(bf16[256,256]{1,0:T(8,128)(2,1)S(1)} %get-tuple-element.23), channel_id=1, source_target_pairs={{1,0},{2,1},{3,2},{4,3},{5,4},{6,5},{7,6},{9,8},{10,9},{11,10},{12... | collective-permute-start | bytes 393224 | tf_op jit(solution)/shard_map/ppermute | solution.py:30
  170.1 5.7 %collective-permute-start.5 = (bf16[1152,256]{1,0:T(8,128)(2,1)S(1)}, bf16[1152,256]{1,0:T(8,128)(2,1)S(1)}, u32[]{:S(2)}, u32[]{:S(2)}) collective-permute-start(bf16[1152,256]{1,0:T(8,128)(2,1)S(1)} %bitcast.90), channel_id=1, source_target_pairs={{0,1},{1,0},{2,3},{3,2},{4,5},{5,4},{6,7},{7,6},{8,9},{9,8},{10,11... | collective-permute-start | bytes 1769480 | tf_op jit(solution)/shard_map/ppermute | solution.py:72

commit v7 on v6

--- a/solution.py
+++ b/solution.py
@@ -39,6 +39,10 @@
 
 def one_hot(index, count):
     return (index[..., None] == jnp.arange(count, dtype=index.dtype)).astype(BF16)
+
+
+def one_hot_rows(index, count):
+    return (jnp.arange(count, dtype=index.dtype)[:, None] == index[..., None, :]).astype(BF16)
 
 
 def split_dot(spec, left, right):
@@ -103,7 +107,9 @@
     gathered = jnp.einsum(
         "ter,rd->ted", src_hot, node_table, preferred_element_type=F32
     ).astype(BF16)
-    edge_in = jnp.einsum("tep,ted->tpd", dst_hot, gathered, preferred_element_type=F32)
+    edge_in = jnp.einsum(
+        "tpe,ted->tpd", one_hot_rows(endpoints, pin_count), gathered, preferred_element_type=F32
+    )
     summed = split_dot("tpk,tkd->pd", edge_in, w_edge)
     degree = jnp.sum(dst_hot.astype(F32), axis=(0, 1))
     inverse = 1.0 / (1.0 + degree)
@@ -127,8 +133,9 @@
     pin_slot = owner_ids * capacity + slot_rank
     slot_hot = one_hot(pin_slot, owners * capacity)
     net_code = (pin_net + 1).astype(BF16)[:, None]
-    slot_nets = jnp.dot(slot_hot.T, net_code, preferred_element_type=F32)[:, 0] - 1.0
-    outbound = jnp.dot(slot_hot.T, hidden, preferred_element_type=F32).astype(BF16)
+    slot_rows = one_hot_rows(pin_slot, owners * capacity)
+    slot_nets = jnp.dot(slot_rows, net_code, preferred_element_type=F32)[:, 0] - 1.0
+    outbound = jnp.dot(slot_rows, hidden, preferred_element_type=F32).astype(BF16)
     id_rows = -(-capacity // (8 * feat_width)) * 8
     id_block = jnp.pad(
         slot_nets.reshape(owners, capacity), ((0, 0), (0, id_rows * feat_width - capacity))
@@ -146,7 +153,9 @@
         packet_in[:, capacity:].reshape(owners, -1)[:, :capacity].astype(F32).astype(jnp.int32)
     ).reshape(-1)
     net_hot = one_hot(slot_nets_in, net_count)
-    pooled = jnp.einsum("sn,sd->nd", net_hot, inbound, preferred_element_type=F32)
+    pooled = jnp.dot(
+        one_hot_rows(slot_nets_in, net_count), inbound, preferred_element_type=F32
+    )
     pooled_b = pooled.astype(BF16)
     head_pre = jnp.dot(pooled_b, w_head, preferred_element_type=F32)
     activated = jax.nn.silu(head_pre).astype(BF16)
@@ -191,7 +200,9 @@
         "tep,pd->ted", dst_hot, agg_grad, preferred_element_type=F32
     ).astype(BF16)
     edge_sum = jnp.einsum("tek,ted->tkd", gathered, edge_rows, preferred_element_type=F32)
-    row_in = jnp.einsum("ter,ted->trd", src_hot, edge_rows, preferred_element_type=F32)
+    row_in = jnp.einsum(
+        "tre,ted->trd", one_hot_rows(sources, table_rows), edge_rows, preferred_element_type=F32
+    )
     table_grad = split_dot("trd,tkd->rk", row_in, w_edge)
     local_grad = (
         jnp.einsum("pd,kd->pk", preact_grad, w_self, preferred_element_type=F32)
@@ -201,7 +212,8 @@
     back_padded = extended(halo_grad, ((DOM, 0),), halo_span)
     received = jnp.concatenate([back_padded[:halo_span], back_padded[3 * halo_span :]], 0)
     grad_feats = (
-        local_grad + jnp.einsum("sp,sd->pd", send_hot, received, preferred_element_type=F32)
+        local_grad
+        + jnp.dot(one_hot_rows(send_list, pin_count), received, preferred_element_type=F32)
     ).astype(BF16)
     pieces = (self_sum, edge_sum.reshape(-1, feat_width), head_sum_t)
     totals = all_sum(jnp.concatenate(pieces, 0), owners)

time: 180 us -> 170 us (0.944)
  matrix products: 46.5 us -> 38.7 us
    dot_general x6, matrix products: 21.4 us -> 13.7 us  [the longest x1 5.88 us: on_device(): jnp.einsum('tre,ted->trd', one_hot_rows(sources, table_rows), edge_rows,...]
    unnamed x53 -> x47, local copies, waits for them, and re-layouts: 4.1 us -> 2.8 us
  transfers between devices with their start and end apart: 10 -> 10, of which waited for: 5 -> 5; matrix products, arithmetic and copies ran while one was open for 14% -> 12% of each run, Pallas kernels for 0% -> 0%
where the time goes in v7:
time: 170 us; the launch traced here: 169 us
  waiting for transfers between devices  79.9 us (47%)
  matrix products  38.7 us (23%)
  starting transfers between devices  32.1 us (19%)
  other arithmetic  10.7 us (6%)
  local copies, waits for them, and re-layouts  6.28 us (4%)
    all_to_all x1, waiting for transfers between devices, on_device(): lax.all_to_all(packet, ALL, split_axis=0, concat_axis=0, tiled=True)  29.7 us
    all_to_all x1, waiting for transfers between devices, on_device(): lax.all_to_all(back_packet, ALL, split_axis=0, concat_axis=0, tiled=True)  28.6 us
    all_to_all x1, waiting for transfers between devices, all_sum(): lax.all_to_all(half.astype(BF16).reshape(chips, -1, width), CHIP, split_a...  17 us
    ppermute x2, starting transfers between devices, extended(): lax.ppermute(lax.slice_in_dim(block, block.shape[dim] - width, None, axis...  9.17 us
    all_to_all x1, starting transfers between devices, on_device(): lax.all_to_all(packet, ALL, split_axis=0, concat_axis=0, tiled=True)  6.14 us
    dot_general x1, matrix products, on_device(): jnp.einsum('tre,ted->trd', one_hot_rows(sources, table_rows), edge_rows,...  5.88 us
    dot_general x2, matrix products, split_dot(): jnp.einsum(spec, left, right.astype(F32), precision=lax.Precision.HIGHEST...  5.18 us
    dot_general x1, matrix products, on_device(): jnp.einsum('ter,rd->ted', src_hot, node_table, preferred_element_type=F32)  4.85 us
  transfers between devices with their start and end apart: 10, of which 5 were waited for; matrix products, arithmetic and copies ran while one was open for 12% of the time, Pallas kernels for 0%

profile of v7, /device:TPU:1, one launch (start us, length us, event | category | flops | bytes accessed | tf_op | source)
XLA Modules:
  0.0 169.0 jit_solution(6650020760471966959)
XLA Ops:
  0.6 0.0 copy-start
  0.7 1.6 fusion.28
  2.3 4.6 %collective-permute-start = (bf16[256,256]{1,0:T(8,128)(2,1)S(1)}, bf16[256,256]{1,0:T(8,128)(2,1)S(1)}, u32[]{:S(2)}, u32[]{:S(2)}) collective-permute-start(bf16[256,256]{1,0:T(8,128)(2,1)S(1)} %get-tuple-element.24), channel_id=1, source_target_pairs={{0,1},{1,2},{2,3},{3,4},{4,5},{5,6},{6,7},{8,9},{9,10},{10,11},{11... | collective-permute-start | bytes 393224 | tf_op jit(solution)/shard_map/ppermute | solution.py:27
  6.9 1.9 %collective-permute-start.1 = (bf16[256,256]{1,0:T(8,128)(2,1)S(1)}, bf16[256,256]{1,0:T(8,128)(2,1)S(1)}, u32[]{:S(2)}, u32[]{:S(2)}) collective-permute-start(bf16[256,256]{1,0:T(8,128)(2,1)S(1)} %get-tuple-element.25), channel_id=1, source_target_pairs={{1,0},{2,1},{3,2},{4,3},{5,4},{6,5},{7,6},{9,8},{10,9},{11,10},{12... | collective-permute-start | bytes 393224 | tf_op jit(solution)/shard_map/ppermute | solution.py:30
  8.8 0.7 add_convert_fusion.1
  9.6 1.3 fusion.32
  10.9 0.0 copy-start.7
  10.9 1.5 fusion.9
  12.4 0.1 sub.16
  12.5 1.9 %convert_reduce_fusion = f32[1024]{0:T(1024)S(1)} fusion(s32[4,1024]{1,0:T(4,128)S(1)} %bitcast.113), kind=kLoop, calls=%fused_computation.4 | loop fusion | flops 16776192 | bytes 20480 | tf_op jit(solution)/shard_map/reduce_sum | solution.py:114
  14.5 0.3 fusion.63
  14.8 4.8 %fusion.20 = bf16[4,1024,256]{2,1,0:T(8,128)(2,1)S(1)} fusion(s32[4,1024]{1,0:T(4,128)S(1)} %bitcast.116, bf16[256,256]{1,0:T(8,128)(2,1)S(1)} %collective-permute-done.1, bf16[256,256]{1,0:T(8,128)(2,1)S(1)} %collective-permute-done, bf16[1024,256]{1,0:T(8,128)(2,1)S(1)} %copy-done.7), kind=kOutput, calls=%fused_computation.35 | convolution fusion | flops 3230924800 | bytes 2899968 | tf_op jit(solution)/shard_map/ter,rd->ted/dot_general | solution.py:107
  19.7 2.8 %fusion.4 = f32[4,1024,256]{2,1,0:T(8,128)S(1)} fusion(bf16[4,1024,256]{2,1,0:T(8,128)(2,1)S(1)} %fusion.20, s32[4,1024]{1,0:T(4,128)S(1)} %bitcast.114), kind=kOutput, calls=%fused_computation.9 | convolution fusion | flops 2151677952 | bytes 6307840 | tf_op jit(solution)/shard_map/tpe,ted->tpd/dot_general | solution.py:110
  22.5 2.1 %fusion.24 = f32[1024,256]{1,0:T(8,128)S(1)} fusion(f32[1024,256]{1,0:T(8,128)S(1)} %fusion.63, f32[4,1024,256]{2,1,0:T(8,128)S(1)} %fusion.4, bf16[4,256,256]{2,1,0:T(8,128)(2,1)S(1)} %copy-done.3, f32[1024]{0:T(1024)S(1)} %add_divide_fusion.2), kind=kOutput, calls=%fused_computation.41 | convolution fusion | flops 3221749760 | bytes 6819840 | tf_op jit(solution)/shard_map/tpk,tkd->pd/dot_general | solution.py:49
  24.6 1.8 %fusion.16 = bf16[2048,256]{1,0:T(8,128)(2,1)S(1)} fusion(s32[1024]{0:T(1024)S(1)} %multiply_add_fusion.1, f32[1024,256]{1,0:T(8,128)S(1)} %fusion.24), kind=kOutput, calls=%fused_computation.25 | convolution fusion | flops 1077673984 | bytes 2101248 | tf_op jit(solution)/shard_map/dot_general | solution.py:138
  26.4 1.1 pad_maximum_fusion.1
  27.6 6.1 %all-to-all-start = ((bf16[32,72,256]{2,1,0:T(8,128)(2,1)}), bf16[32,72,256]{2,1,0:T(8,128)(2,1)S(1)}, u32[]{:S(2)}, u32[]{:S(2)}) async-start(bf16[32,72,256]{2,1,0:T(8,128)(2,1)} %pad_maximum_fusion.1), calls=%async_computation | async-start | bytes 2359296 | tf_op jit(solution)/shard_map/all_to_all | solution.py:150
  33.8 0.1 pad.15.clone
  33.8 29.7 %all-to-all-done = bf16[32,72,256]{2,1,0:T(8,128)(2,1)S(1)} async-done(((bf16[32,72,256]{2,1,0:T(8,128)(2,1)}), bf16[32,72,256]{2,1,0:T(8,128)(2,1)S(1)}, u32[]{:S(2)}, u32[]{:S(2)}) %all-to-all-start) | async-done | bytes 1179680 | tf_op jit(solution)/shard_map/all_to_all | solution.py:150
  63.6 0.1 eq.181
  63.7 0.1 slice.60
  63.8 0.5 fusion.30
  64.3 0.5 multiply_convert_fusion.2
  64.7 0.2 fusion.64
  65.0 0.3 fusion.65
  65.3 0.2 copy-done.14
  65.6 0.4 multiply_convert_fusion.1
  66.0 1.0 convolution_convert_fusion
  67.0 1.5 maximum_maximum_fusion
  68.5 3.1 %all-to-all-start.1 = ((bf16[32,72,256]{2,1,0:T(8,128)(2,1)}), bf16[32,72,256]{2,1,0:T(8,128)(2,1)S(1)}, u32[]{:S(2)}, u32[]{:S(2)}) async-start(bf16[32,72,256]{2,1,0:T(8,128)(2,1)} %maximum_maximum_fusion), calls=%async_computation.1 | async-start | bytes 2359296 | tf_op jit(solution)/shard_map/all_to_all | solution.py:185
  71.7 1.3 fusion.67
  73.0 28.6 %all-to-all-done.1 = bf16[32,72,256]{2,1,0:T(8,128)(2,1)S(1)} async-done(((bf16[32,72,256]{2,1,0:T(8,128)(2,1)}), bf16[32,72,256]{2,1,0:T(8,128)(2,1)S(1)}, u32[]{:S(2)}, u32[]{:S(2)}) %all-to-all-start.1) | async-done | bytes 1179680 | tf_op jit(solution)/shard_map/all_to_all | solution.py:185
  101.6 0.1 slice.61
  101.7 3.3 %fusion.26 = bf16[1024,256]{1,0:T(8,128)(2,1)S(1)} fusion(bf16[2048,256]{1,0:T(8,128)(2,1)S(1)} %bitcast.94, s32[1024]{0:T(1024)S(1)} %bitcast.112, f32[1024,256]{1,0:T(8,128)} %copy-done.10), kind=kOutput, calls=%fused_computation.43 | convolution fusion | flops 1078198272 | bytes 2625536 | tf_op jit(solution)/shard_map/dot_general | solution.py:195
  105.1 0.4 convolution_bitcast_fusion.2
  105.4 3.3 %fusion.21 = bf16[4,1024,256]{2,1,0:T(8,128)(2,1)S(1)} fusion(s32[4,1024]{1,0:T(4,128)S(1)} %bitcast.115, bf16[1024,256]{1,0:T(8,128)(2,1)S(1)} %fusion.26, f32[1024]{0:T(1024)S(1)} %add_divide_fusion.2), kind=kOutput, calls=%fused_computation.36 | convolution fusion | flops 2153512960 | bytes 2641920 | tf_op jit(solution)/shard_map/tep,pd->ted/dot_general | solution.py:199
  108.8 0.9 fusion.66
  109.7 0.4 copy-done.6
  110.1 0.6 copy-done.2
  110.8 0.2 pad_maximum_fusion
  110.9 1.1 dynamic-slice_bitcast_fusion
  112.0 0.8 collective-permute-start.4
  112.9 2.8 %collective-permute-done.4 = f32[1152,256]{1,0:T(8,128)} collective-permute-done((f32[1152,256]{1,0:T(8,128)}, f32[1152,256]{1,0:T(8,128)}, u32[]{:S(2)}, u32[]{:S(2)}) %collective-permute-start.4) | collective-permute-done | bytes 1179680 | tf_op jit(solution)/shard_map/ppermute | solution.py:65
  115.7 2.2 %fusion.29 = bf16[1152,256]{1,0:T(8,128)(2,1)} fusion(f32[1152,256]{1,0:T(8,128)} %collective-permute-done.4, f32[2,1152,256]{2,1,0:T(8,128)S(1)} %bitcast.88, s32[]{:T(128)S(6)} %select_n.27), kind=kLoop, calls=%fused_computation.49 | loop fusion | flops 589824 | bytes 2949124 | tf_op jit(solution)/shard_map/convert_element_type | solution.py:67
  117.9 3.7 %all-to-all-start.2 = ((bf16[16,72,256]{2,1,0:T(8,128)(2,1)}), bf16[16,72,256]{2,1,0:T(8,128)(2,1)S(1)}, u32[]{:S(2)}, u32[]{:S(2)}) async-start(bf16[16,72,256]{2,1,0:T(8,128)(2,1)} %bitcast.23), calls=%async_computation.2 | async-start | bytes 1179648 | tf_op jit(solution)/shard_map/all_to_all | solution.py:66
  121.6 17.0 %all-to-all-done.2 = bf16[16,72,256]{2,1,0:T(8,128)(2,1)S(1)} async-done(((bf16[16,72,256]{2,1,0:T(8,128)(2,1)}), bf16[16,72,256]{2,1,0:T(8,128)(2,1)S(1)}, u32[]{:S(2)}, u32[]{:S(2)}) %all-to-all-start.2) | async-done | bytes 589856 | tf_op jit(solution)/shard_map/all_to_all | solution.py:66
  138.6 0.2 fusion.41
  138.9 0.9 broadcast_in_dim.10
  139.7 3.8 %all-to-all-start.3 = ((bf16[16,72,256]{2,1,0:T(8,128)(2,1)}), bf16[16,72,256]{2,1,0:T(8,128)(2,1)S(1)}, u32[]{:S(2)}, u32[]{:S(2)}) async-start(bf16[16,72,256]{2,1,0:T(8,128)(2,1)} %broadcast_in_dim.10), calls=%async_computation.3 | async-start | bytes 1179648 | tf_op jit(solution)/shard_map/all_to_all | solution.py:73
  143.6 5.9 %fusion.1 = f32[4,1536,256]{2,1,0:T(8,128)S(1)} fusion(bf16[4,1024,256]{2,1,0:T(8,128)(2,1)} %copy-done.6, s32[4,1024]{1,0:T(4,128)S(1)} %bitcast.117), kind=kOutput, calls=%fused_computation.3 | convolution fusion | flops 3227516928 | bytes 8404992 | tf_op jit(solution)/shard_map/tre,ted->trd/dot_general | solution.py:203
  149.5 0.9 slice.65
  150.4 3.1 %fusion.62 = (bf16[1536,256]{1,0:T(8,128)(2,1)S(1)}, f32[1536,256]{1,0:T(8,128)S(1)}) fusion(f32[4,1536,256]{2,1,0:T(8,128)S(1)} %fusion.1, bf16[4,256,256]{2,1,0:T(8,128)(2,1)S(1)} %copy-done.3), kind=kOutput, calls=%fused_computation.106 | convolution fusion | flops 4832231424 | bytes 9175040 | tf_op jit(solution)/shard_map/trd,tkd->rk/dot_general | solution.py:49
  153.5 4.6 %collective-permute-start.2 = (bf16[256,256]{1,0:T(8,128)(2,1)S(1)}, bf16[256,256]{1,0:T(8,128)(2,1)S(1)}, u32[]{:S(2)}, u32[]{:S(2)}) collective-permute-start(bf16[256,256]{1,0:T(8,128)(2,1)S(1)} %get-tuple-element.22), channel_id=1, source_target_pairs={{0,1},{1,2},{2,3},{3,4},{4,5},{5,6},{6,7},{8,9},{9,10},{10,11},{11... | collective-permute-start | bytes 393224 | tf_op jit(solution)/shard_map/ppermute | solution.py:27
  158.1 1.9 %collective-permute-start.3 = (bf16[256,256]{1,0:T(8,128)(2,1)S(1)}, bf16[256,256]{1,0:T(8,128)(2,1)S(1)}, u32[]{:S(2)}, u32[]{:S(2)}) collective-permute-start(bf16[256,256]{1,0:T(8,128)(2,1)S(1)} %get-tuple-element.23), channel_id=1, source_target_pairs={{1,0},{2,1},{3,2},{4,3},{5,4},{6,5},{7,6},{9,8},{10,9},{11,10},{12... | collective-permute-start | bytes 393224 | tf_op jit(solution)/shard_map/ppermute | solution.py:30
  160.1 0.3 convolution_add_fusion
  160.4 1.5 collective-permute-start.5
  161.9 0.1 fusion.52
  162.0 0.6 broadcast_multiply_fusion
  162.6 1.8 %collective-permute-done.3 = bf16[256,256]{1,0:T(8,128)(2,1)S(1)} collective-permute-done((bf16[256,256]{1,0:T(8,128)(2,1)S(1)}, bf16[256,256]{1,0:T(8,128)(2,1)S(1)}, u32[]{:S(2)}, u32[]{:S(2)}) %collective-permute-start.3) | collective-permute-done | bytes 131104 | tf_op jit(solution)/shard_map/ppermute | solution.py:30
  164.4 1.3 fusion.27
  165.7 0.1 broadcast_select_fusion.1
  165.8 0.7 convert_multiply_fusion.1
  166.6 1.2 multiply_bitcast_fusion
  167.7 1.3 copy.20
  (64 shorter events, 0.4 us)
Async XLA Ops:
  0.6 63.6 %copy-start = (bf16[256,1024]{1,0:T(8,128)(2,1)S(1)}, bf16[256,1024]{1,0:T(8,128)(2,1)}, u32[]{:S(2)}) copy-start(bf16[256,1024]{1,0:T(8,128)(2,1)} %param.14) | copy-start | bytes 1572868
  0.6 10.2 %copy-start.12 = (s32[1024,1]{0,1:T(1,128)S(1)}, s32[1024,1]{0,1:T(1,128)}, u32[]{:S(2)}) copy-start(s32[1024,1]{0,1:T(1,128)} %param.19) | copy-start | bytes 12292
  2.3 12.5 %collective-permute-start = (bf16[256,256]{1,0:T(8,128)(2,1)S(1)}, bf16[256,256]{1,0:T(8,128)(2,1)S(1)}, u32[]{:S(2)}, u32[]{:S(2)}) collective-permute-start(bf16[256,256]{1,0:T(8,128)(2,1)S(1)} %get-tuple-element.24), channel_id=1, source_target_pairs={{0,1},{1,2},{2,3},{3,4},{4,5},{5,6},{6,7},{8,9},{9,10},{10,11},{11... | collective-permute-start | bytes 393224 | tf_op jit(solution)/shard_map/ppermute | solution.py:27
  6.9 7.9 %collective-permute-start.1 = (bf16[256,256]{1,0:T(8,128)(2,1)S(1)}, bf16[256,256]{1,0:T(8,128)(2,1)S(1)}, u32[]{:S(2)}, u32[]{:S(2)}) collective-permute-start(bf16[256,256]{1,0:T(8,128)(2,1)S(1)} %get-tuple-element.25), channel_id=1, source_target_pairs={{1,0},{2,1},{3,2},{4,3},{5,4},{6,5},{7,6},{9,8},{10,9},{11,10},{12... | collective-permute-start | bytes 393224 | tf_op jit(solution)/shard_map/ppermute | solution.py:30
  9.6 2.9 %copy-start.16 = (s32[1,4,1024]{2,1,0:T(4,128)S(1)}, s32[1,4,1024]{2,1,0:T(4,128)}, u32[]{:S(2)}) copy-start(s32[1,4,1024]{2,1,0:T(4,128)} %param.18) | copy-start | bytes 49156
  10.9 3.6 %copy-start.7 = (bf16[1024,256]{1,0:T(8,128)(2,1)S(1)}, bf16[1024,256]{1,0:T(8,128)(2,1)}, u32[]{:S(2)}) copy-start(bf16[1024,256]{1,0:T(8,128)(2,1)} %param.11) | copy-start | bytes 1572868
  10.9 3.6 %copy-start.11 = (bf16[256,256]{1,0:T(8,128)(2,1)S(1)}, bf16[256,256]{1,0:T(8,128)(2,1)}, u32[]{:S(2)}) copy-start(bf16[256,256]{1,0:T(8,128)(2,1)} %param.12) | copy-start | bytes 393220
  10.9 3.9 %copy-start.18 = (s32[1,4,1024]{2,1,0:T(4,128)S(1)}, s32[1,4,1024]{2,1,0:T(4,128)}, u32[]{:S(2)}) copy-start(s32[1,4,1024]{2,1,0:T(4,128)} %param.17) | copy-start | bytes 49156
  19.7 2.8 %copy-start.4 = (bf16[4,1024,256]{2,1,0:T(8,128)(2,1)}, bf16[4,1024,256]{2,1,0:T(8,128)(2,1)S(1)}, u32[]{:S(2)}) copy-start(bf16[4,1024,256]{2,1,0:T(8,128)(2,1)S(1)} %fusion.20) | copy-start | bytes 6291460
  19.7 2.8 %copy-start.3 = (bf16[4,256,256]{2,1,0:T(8,128)(2,1)S(1)}, bf16[4,256,256]{2,1,0:T(8,128)(2,1)}, u32[]{:S(2)}) copy-start(bf16[4,256,256]{2,1,0:T(8,128)(2,1)} %param.13) | copy-start | bytes 1572868
  24.6 1.8 %copy-start.10 = (f32[1024,256]{1,0:T(8,128)}, f32[1024,256]{1,0:T(8,128)S(1)}, u32[]{:S(2)}) copy-start(f32[1024,256]{1,0:T(8,128)S(1)} %fusion.24) | copy-start | bytes 3145732
  26.4 7.3 %copy-start.13 = (bf16[1024]{0:T(1024)(128)(2,1)S(1)}, bf16[1024]{0:T(1024)(128)(2,1)}, u32[]{:S(2)}) copy-start(bf16[1024]{0:T(1024)(128)(2,1)} %param.15) | copy-start | bytes 6148
  27.6 36.0 %all-to-all-start = ((bf16[32,72,256]{2,1,0:T(8,128)(2,1)}), bf16[32,72,256]{2,1,0:T(8,128)(2,1)S(1)}, u32[]{:S(2)}, u32[]{:S(2)}) async-start(bf16[32,72,256]{2,1,0:T(8,128)(2,1)} %pad_maximum_fusion.1), calls=%async_computation | async-start | bytes 2359296 | tf_op jit(solution)/shard_map/all_to_all | solution.py:150
  64.3 0.7 copy-start.15
  65.0 0.6 copy-start.14
  68.5 33.1 %all-to-all-start.1 = ((bf16[32,72,256]{2,1,0:T(8,128)(2,1)}), bf16[32,72,256]{2,1,0:T(8,128)(2,1)S(1)}, u32[]{:S(2)}, u32[]{:S(2)}) async-start(bf16[32,72,256]{2,1,0:T(8,128)(2,1)} %maximum_maximum_fusion), calls=%async_computation.1 | async-start | bytes 2359296 | tf_op jit(solution)/shard_map/all_to_all | solution.py:185
  101.6 3.4 %copy-start.1 = (bf16[32,72,256]{2,1,0:T(8,128)(2,1)}, bf16[32,72,256]{2,1,0:T(8,128)(2,1)S(1)}, u32[]{:S(2)}) copy-start(bf16[32,72,256]{2,1,0:T(8,128)(2,1)S(1)} %all-to-all-done.1) | copy-start | bytes 3538948
  101.7 3.7 %copy-start.17 = (s32[1,4,1024]{2,1,0:T(4,128)S(1)}, s32[1,4,1024]{2,1,0:T(4,128)}, u32[]{:S(2)}) copy-start(s32[1,4,1024]{2,1,0:T(4,128)} %param.18) | copy-start | bytes 49156
  105.0 3.7 %copy-start.8 = (bf16[1024,256]{1,0:T(8,128)(2,1)}, bf16[1024,256]{1,0:T(8,128)(2,1)S(1)}, u32[]{:S(2)}) copy-start(bf16[1024,256]{1,0:T(8,128)(2,1)S(1)} %fusion.26) | copy-start | bytes 1572868
  105.4 3.3 %copy-start.5 = (bf16[4,1024,256]{2,1,0:T(8,128)(2,1)S(1)}, bf16[4,1024,256]{2,1,0:T(8,128)(2,1)}, u32[]{:S(2)}) copy-start(bf16[4,1024,256]{2,1,0:T(8,128)(2,1)} %copy-done.4) | copy-start | bytes 6291460
  108.8 1.3 copy-start.6
  108.8 2.0 %copy-start.2 = (f32[1024,256]{1,0:T(8,128)S(1)}, f32[1024,256]{1,0:T(8,128)}, u32[]{:S(2)}) copy-start(f32[1024,256]{1,0:T(8,128)} %fusion.67) | copy-start | bytes 3145732
  112.0 3.7 %collective-permute-start.4 = (f32[1152,256]{1,0:T(8,128)}, f32[1152,256]{1,0:T(8,128)}, u32[]{:S(2)}, u32[]{:S(2)}) collective-permute-start(f32[1152,256]{1,0:T(8,128)} %dynamic-slice_bitcast_fusion), channel_id=1, source_target_pairs={{0,1},{1,0},{2,3},{3,2},{4,5},{5,4},{6,7},{7,6},{8,9},{9,8},{10,11... | collective-permute-start | bytes 3538952 | tf_op jit(solution)/shard_map/ppermute | solution.py:65
  117.9 25.7 %copy-start.19 = (s32[1,4,1024]{2,1,0:T(4,128)S(1)}, s32[1,4,1024]{2,1,0:T(4,128)}, u32[]{:S(2)}) copy-start(s32[1,4,1024]{2,1,0:T(4,128)} %param.17) | copy-start | bytes 49156
  117.9 20.7 %all-to-all-start.2 = ((bf16[16,72,256]{2,1,0:T(8,128)(2,1)}), bf16[16,72,256]{2,1,0:T(8,128)(2,1)S(1)}, u32[]{:S(2)}, u32[]{:S(2)}) async-start(bf16[16,72,256]{2,1,0:T(8,128)(2,1)} %bitcast.23), calls=%async_computation.2 | async-start | bytes 1179648 | tf_op jit(solution)/shard_map/all_to_all | solution.py:66
  139.7 20.7 %all-to-all-start.3 = ((bf16[16,72,256]{2,1,0:T(8,128)(2,1)}), bf16[16,72,256]{2,1,0:T(8,128)(2,1)S(1)}, u32[]{:S(2)}, u32[]{:S(2)}) async-start(bf16[16,72,256]{2,1,0:T(8,128)(2,1)} %broadcast_in_dim.10), calls=%async_computation.3 | async-start | bytes 1179648 | tf_op jit(solution)/shard_map/all_to_all | solution.py:73
  150.4 9.7 %copy-start.9 = (bf16[1024,256]{1,0:T(8,128)(2,1)S(1)}, bf16[1024,256]{1,0:T(8,128)(2,1)}, u32[]{:S(2)}) copy-start(bf16[1024,256]{1,0:T(8,128)(2,1)} %copy-done.8) | copy-start | bytes 1572868
  153.5 10.9 %copy-start.20 = (s32[1,512]{1,0:T(1,128)S(1)}, s32[1,512]{1,0:T(1,128)}, u32[]{:S(2)}) copy-start(s32[1,512]{1,0:T(1,128)} %param.16) | copy-start | bytes 6148
  153.5 9.1 %collective-permute-start.2 = (bf16[256,256]{1,0:T(8,128)(2,1)S(1)}, bf16[256,256]{1,0:T(8,128)(2,1)S(1)}, u32[]{:S(2)}, u32[]{:S(2)}) collective-permute-start(bf16[256,256]{1,0:T(8,128)(2,1)S(1)} %get-tuple-element.22), channel_id=1, source_target_pairs={{0,1},{1,2},{2,3},{3,4},{4,5},{5,6},{6,7},{8,9},{9,10},{10,11},{11... | collective-permute-start | bytes 393224 | tf_op jit(solution)/shard_map/ppermute | solution.py:27
  158.1 6.3 %collective-permute-start.3 = (bf16[256,256]{1,0:T(8,128)(2,1)S(1)}, bf16[256,256]{1,0:T(8,128)(2,1)S(1)}, u32[]{:S(2)}, u32[]{:S(2)}) collective-permute-start(bf16[256,256]{1,0:T(8,128)(2,1)S(1)} %get-tuple-element.23), channel_id=1, source_target_pairs={{1,0},{2,1},{3,2},{4,3},{5,4},{6,5},{7,6},{9,8},{10,9},{11,10},{12... | collective-permute-start | bytes 393224 | tf_op jit(solution)/shard_map/ppermute | solution.py:30
  160.4 5.3 %collective-permute-start.5 = (bf16[1152,256]{1,0:T(8,128)(2,1)S(1)}, bf16[1152,256]{1,0:T(8,128)(2,1)S(1)}, u32[]{:S(2)}, u32[]{:S(2)}) collective-permute-start(bf16[1152,256]{1,0:T(8,128)(2,1)S(1)} %bitcast.90), channel_id=1, source_target_pairs={{0,1},{1,0},{2,3},{3,2},{4,5},{5,4},{6,7},{7,6},{8,9},{9,8},{10,11... | collective-permute-start | bytes 1769480 | tf_op jit(solution)/shard_map/ppermute | solution.py:76

commit v8 on v7

--- a/solution.py
+++ b/solution.py
@@ -62,7 +62,7 @@
     swap = [(i, (i + 1) % cores) for i in range(cores)]
     kept = lax.dynamic_index_in_dim(rows, core, 0, keepdims=False)
     given = lax.dynamic_index_in_dim(rows, (core + 1) % cores, 0, keepdims=False)
-    half = kept + lax.ppermute(given, "core", swap)
+    half = kept + lax.ppermute(given.astype(BF16), "core", swap).astype(F32)
     mine = lax.all_to_all(
         half.astype(BF16).reshape(chips, -1, width), CHIP, split_axis=0, concat_axis=0, tiled=True
     )

time: 170 us -> 169 us (level)
  no operation moved by 1% of the time
where the time goes in v8:
time: 169 us; the launch traced here: 168 us
  waiting for transfers between devices  79 us (47%)
  matrix products  38.7 us (23%)
  starting transfers between devices  32.1 us (19%)
  other arithmetic  10.5 us (6%)
  local copies, waits for them, and re-layouts  6.04 us (4%)
    all_to_all x1, waiting for transfers between devices, on_device(): lax.all_to_all(packet, ALL, split_axis=0, concat_axis=0, tiled=True)  29.7 us
    all_to_all x1, waiting for transfers between devices, on_device(): lax.all_to_all(back_packet, ALL, split_axis=0, concat_axis=0, tiled=True)  28.6 us
    all_to_all x1, waiting for transfers between devices, all_sum(): lax.all_to_all(half.astype(BF16).reshape(chips, -1, width), CHIP, split_a...  17 us
    ppermute x2, starting transfers between devices, extended(): lax.ppermute(lax.slice_in_dim(block, block.shape[dim] - width, None, axis...  9.18 us
    all_to_all x1, starting transfers between devices, on_device(): lax.all_to_all(packet, ALL, split_axis=0, concat_axis=0, tiled=True)  6.14 us
    dot_general x1, matrix products, on_device(): jnp.einsum('tre,ted->trd', one_hot_rows(sources, table_rows), edge_rows,...  5.87 us
    dot_general x2, matrix products, split_dot(): jnp.einsum(spec, left, right.astype(F32), precision=lax.Precision.HIGHEST...  5.18 us
    dot_general x1, matrix products, on_device(): jnp.einsum('ter,rd->ted', src_hot, node_table, preferred_element_type=F32)  4.85 us
  transfers between devices with their start and end apart: 10, of which 5 were waited for; matrix products, arithmetic and copies ran while one was open for 12% of the time, Pallas kernels for 0%

profile of v8, /device:TPU:1, one launch (start us, length us, event | category | flops | bytes accessed | tf_op | source)
XLA Modules:
  0.0 167.8 jit_solution(9193840854295710628)
XLA Ops:
  0.6 0.0 copy-start
  0.6 0.0 copy-start.12
  0.7 1.6 fusion.28
  2.3 4.6 %collective-permute-start = (bf16[256,256]{1,0:T(8,128)(2,1)S(1)}, bf16[256,256]{1,0:T(8,128)(2,1)S(1)}, u32[]{:S(2)}, u32[]{:S(2)}) collective-permute-start(bf16[256,256]{1,0:T(8,128)(2,1)S(1)} %get-tuple-element.24), channel_id=1, source_target_pairs={{0,1},{1,2},{2,3},{3,4},{4,5},{5,6},{6,7},{8,9},{9,10},{10,11},{11... | collective-permute-start | bytes 393224 | tf_op jit(solution)/shard_map/ppermute | solution.py:27
  6.9 1.9 %collective-permute-start.1 = (bf16[256,256]{1,0:T(8,128)(2,1)S(1)}, bf16[256,256]{1,0:T(8,128)(2,1)S(1)}, u32[]{:S(2)}, u32[]{:S(2)}) collective-permute-start(bf16[256,256]{1,0:T(8,128)(2,1)S(1)} %get-tuple-element.25), channel_id=1, source_target_pairs={{1,0},{2,1},{3,2},{4,3},{5,4},{6,5},{7,6},{9,8},{10,9},{11,10},{12... | collective-permute-start | bytes 393224 | tf_op jit(solution)/shard_map/ppermute | solution.py:30
  8.8 0.7 add_convert_fusion.1
  9.6 1.3 fusion.32
  10.9 1.5 fusion.9
  12.4 0.1 sub.16
  12.5 1.9 %convert_reduce_fusion = f32[1024]{0:T(1024)S(1)} fusion(s32[4,1024]{1,0:T(4,128)S(1)} %bitcast.113), kind=kLoop, calls=%fused_computation.4 | loop fusion | flops 16776192 | bytes 20480 | tf_op jit(solution)/shard_map/reduce_sum | solution.py:114
  14.5 0.3 fusion.64
  14.8 4.8 %fusion.20 = bf16[4,1024,256]{2,1,0:T(8,128)(2,1)S(1)} fusion(s32[4,1024]{1,0:T(4,128)S(1)} %bitcast.116, bf16[256,256]{1,0:T(8,128)(2,1)S(1)} %collective-permute-done.1, bf16[256,256]{1,0:T(8,128)(2,1)S(1)} %collective-permute-done, bf16[1024,256]{1,0:T(8,128)(2,1)S(1)} %copy-done.7), kind=kOutput, calls=%fused_computation.35 | convolution fusion | flops 3230924800 | bytes 2899968 | tf_op jit(solution)/shard_map/ter,rd->ted/dot_general | solution.py:107
  19.7 2.8 %fusion.4 = f32[4,1024,256]{2,1,0:T(8,128)S(1)} fusion(bf16[4,1024,256]{2,1,0:T(8,128)(2,1)S(1)} %fusion.20, s32[4,1024]{1,0:T(4,128)S(1)} %bitcast.114), kind=kOutput, calls=%fused_computation.9 | convolution fusion | flops 2151677952 | bytes 6307840 | tf_op jit(solution)/shard_map/tpe,ted->tpd/dot_general | solution.py:110
  22.5 2.1 %fusion.24 = f32[1024,256]{1,0:T(8,128)S(1)} fusion(f32[1024,256]{1,0:T(8,128)S(1)} %fusion.64, f32[4,1024,256]{2,1,0:T(8,128)S(1)} %fusion.4, bf16[4,256,256]{2,1,0:T(8,128)(2,1)S(1)} %copy-done.3, f32[1024]{0:T(1024)S(1)} %add_divide_fusion.2), kind=kOutput, calls=%fused_computation.41 | convolution fusion | flops 3221749760 | bytes 6819840 | tf_op jit(solution)/shard_map/tpk,tkd->pd/dot_general | solution.py:49
  24.6 1.8 %fusion.16 = bf16[2048,256]{1,0:T(8,128)(2,1)S(1)} fusion(s32[1024]{0:T(1024)S(1)} %multiply_add_fusion.1, f32[1024,256]{1,0:T(8,128)S(1)} %fusion.24), kind=kOutput, calls=%fused_computation.25 | convolution fusion | flops 1077673984 | bytes 2101248 | tf_op jit(solution)/shard_map/dot_general | solution.py:138
  26.4 1.1 pad_maximum_fusion.1
  27.6 6.1 %all-to-all-start = ((bf16[32,72,256]{2,1,0:T(8,128)(2,1)}), bf16[32,72,256]{2,1,0:T(8,128)(2,1)S(1)}, u32[]{:S(2)}, u32[]{:S(2)}) async-start(bf16[32,72,256]{2,1,0:T(8,128)(2,1)} %pad_maximum_fusion.1), calls=%async_computation | async-start | bytes 2359296 | tf_op jit(solution)/shard_map/all_to_all | solution.py:150
  33.8 0.1 pad.15.clone
  33.8 29.7 %all-to-all-done = bf16[32,72,256]{2,1,0:T(8,128)(2,1)S(1)} async-done(((bf16[32,72,256]{2,1,0:T(8,128)(2,1)}), bf16[32,72,256]{2,1,0:T(8,128)(2,1)S(1)}, u32[]{:S(2)}, u32[]{:S(2)}) %all-to-all-start) | async-done | bytes 1179680 | tf_op jit(solution)/shard_map/all_to_all | solution.py:150
  63.6 0.1 eq.181
  63.7 0.1 slice.60
  63.8 0.5 fusion.30
  64.3 0.5 multiply_convert_fusion.2
  64.7 0.2 fusion.65
  65.0 0.3 fusion.66
  65.3 0.2 copy-done.14
  65.6 0.4 multiply_convert_fusion.1
  66.0 1.0 convolution_convert_fusion
  67.0 1.5 maximum_maximum_fusion
  68.5 3.1 %all-to-all-start.1 = ((bf16[32,72,256]{2,1,0:T(8,128)(2,1)}), bf16[32,72,256]{2,1,0:T(8,128)(2,1)S(1)}, u32[]{:S(2)}, u32[]{:S(2)}) async-start(bf16[32,72,256]{2,1,0:T(8,128)(2,1)} %maximum_maximum_fusion), calls=%async_computation.1 | async-start | bytes 2359296 | tf_op jit(solution)/shard_map/all_to_all | solution.py:185
  71.7 1.3 fusion.68
  73.0 28.6 %all-to-all-done.1 = bf16[32,72,256]{2,1,0:T(8,128)(2,1)S(1)} async-done(((bf16[32,72,256]{2,1,0:T(8,128)(2,1)}), bf16[32,72,256]{2,1,0:T(8,128)(2,1)S(1)}, u32[]{:S(2)}, u32[]{:S(2)}) %all-to-all-start.1) | async-done | bytes 1179680 | tf_op jit(solution)/shard_map/all_to_all | solution.py:185
  101.6 0.1 slice.61
  101.7 3.3 %fusion.26 = bf16[1024,256]{1,0:T(8,128)(2,1)S(1)} fusion(bf16[2048,256]{1,0:T(8,128)(2,1)S(1)} %bitcast.94, s32[1024]{0:T(1024)S(1)} %bitcast.112, f32[1024,256]{1,0:T(8,128)} %copy-done.10), kind=kOutput, calls=%fused_computation.43 | convolution fusion | flops 1078198272 | bytes 2625536 | tf_op jit(solution)/shard_map/dot_general | solution.py:195
  105.1 0.4 convolution_bitcast_fusion.2
  105.4 3.3 %fusion.21 = bf16[4,1024,256]{2,1,0:T(8,128)(2,1)S(1)} fusion(s32[4,1024]{1,0:T(4,128)S(1)} %bitcast.115, bf16[1024,256]{1,0:T(8,128)(2,1)S(1)} %fusion.26, f32[1024]{0:T(1024)S(1)} %add_divide_fusion.2), kind=kOutput, calls=%fused_computation.36 | convolution fusion | flops 2153512960 | bytes 2641920 | tf_op jit(solution)/shard_map/tep,pd->ted/dot_general | solution.py:199
  108.8 0.9 fusion.67
  109.7 0.4 copy-done.6
  110.1 0.6 copy-done.2
  110.8 0.2 pad_maximum_fusion
  110.9 0.9 fusion.41
  111.8 0.8 collective-permute-start.4
  112.6 2.0 %collective-permute-done.4 = bf16[1152,256]{1,0:T(8,128)(2,1)} collective-permute-done((bf16[1152,256]{1,0:T(8,128)(2,1)}, bf16[1152,256]{1,0:T(8,128)(2,1)}, u32[]{:S(2)}, u32[]{:S(2)}) %collective-permute-start.4) | collective-permute-done | bytes 589856 | tf_op jit(solution)/shard_map/ppermute | solution.py:65
  114.6 2.0 %fusion.29 = bf16[1152,256]{1,0:T(8,128)(2,1)} fusion(bf16[1152,256]{1,0:T(8,128)(2,1)} %collective-permute-done.4, f32[2,1152,256]{2,1,0:T(8,128)S(1)} %bitcast.88, s32[]{:T(128)S(6)} %select_n.27), kind=kLoop, calls=%fused_computation.49 | loop fusion | flops 884736 | bytes 2359300 | tf_op jit(solution)/shard_map/convert_element_type | solution.py:67
  116.6 3.7 %all-to-all-start.2 = ((bf16[16,72,256]{2,1,0:T(8,128)(2,1)}), bf16[16,72,256]{2,1,0:T(8,128)(2,1)S(1)}, u32[]{:S(2)}, u32[]{:S(2)}) async-start(bf16[16,72,256]{2,1,0:T(8,128)(2,1)} %bitcast.23), calls=%async_computation.2 | async-start | bytes 1179648 | tf_op jit(solution)/shard_map/all_to_all | solution.py:66
  120.4 17.0 %all-to-all-done.2 = bf16[16,72,256]{2,1,0:T(8,128)(2,1)S(1)} async-done(((bf16[16,72,256]{2,1,0:T(8,128)(2,1)}), bf16[16,72,256]{2,1,0:T(8,128)(2,1)S(1)}, u32[]{:S(2)}, u32[]{:S(2)}) %all-to-all-start.2) | async-done | bytes 589856 | tf_op jit(solution)/shard_map/all_to_all | solution.py:66
  137.4 0.2 fusion.42
  137.6 0.9 broadcast_in_dim.10
  138.5 3.8 %all-to-all-start.3 = ((bf16[16,72,256]{2,1,0:T(8,128)(2,1)}), bf16[16,72,256]{2,1,0:T(8,128)(2,1)S(1)}, u32[]{:S(2)}, u32[]{:S(2)}) async-start(bf16[16,72,256]{2,1,0:T(8,128)(2,1)} %broadcast_in_dim.10), calls=%async_computation.3 | async-start | bytes 1179648 | tf_op jit(solution)/shard_map/all_to_all | solution.py:73
  142.3 5.9 %fusion.1 = f32[4,1536,256]{2,1,0:T(8,128)S(1)} fusion(bf16[4,1024,256]{2,1,0:T(8,128)(2,1)} %copy-done.6, s32[4,1024]{1,0:T(4,128)S(1)} %bitcast.117), kind=kOutput, calls=%fused_computation.3 | convolution fusion | flops 3227516928 | bytes 8404992 | tf_op jit(solution)/shard_map/tre,ted->trd/dot_general | solution.py:203
  148.2 0.9 slice.65
  149.1 3.1 %fusion.63 = (bf16[1536,256]{1,0:T(8,128)(2,1)S(1)}, f32[1536,256]{1,0:T(8,128)S(1)}) fusion(f32[4,1536,256]{2,1,0:T(8,128)S(1)} %fusion.1, bf16[4,256,256]{2,1,0:T(8,128)(2,1)S(1)} %copy-done.3), kind=kOutput, calls=%fused_computation.107 | convolution fusion | flops 4832231424 | bytes 9175040 | tf_op jit(solution)/shard_map/trd,tkd->rk/dot_general | solution.py:49
  152.3 4.6 %collective-permute-start.2 = (bf16[256,256]{1,0:T(8,128)(2,1)S(1)}, bf16[256,256]{1,0:T(8,128)(2,1)S(1)}, u32[]{:S(2)}, u32[]{:S(2)}) collective-permute-start(bf16[256,256]{1,0:T(8,128)(2,1)S(1)} %get-tuple-element.22), channel_id=1, source_target_pairs={{0,1},{1,2},{2,3},{3,4},{4,5},{5,6},{6,7},{8,9},{9,10},{10,11},{11... | collective-permute-start | bytes 393224 | tf_op jit(solution)/shard_map/ppermute | solution.py:27
  156.9 1.9 %collective-permute-start.3 = (bf16[256,256]{1,0:T(8,128)(2,1)S(1)}, bf16[256,256]{1,0:T(8,128)(2,1)S(1)}, u32[]{:S(2)}, u32[]{:S(2)}) collective-permute-start(bf16[256,256]{1,0:T(8,128)(2,1)S(1)} %get-tuple-element.23), channel_id=1, source_target_pairs={{1,0},{2,1},{3,2},{4,3},{5,4},{6,5},{7,6},{9,8},{10,9},{11,10},{12... | collective-permute-start | bytes 393224 | tf_op jit(solution)/shard_map/ppermute | solution.py:30
  158.8 0.3 convolution_add_fusion
  159.2 1.5 collective-permute-start.5
  160.6 0.1 fusion.53
  160.8 0.6 broadcast_multiply_fusion
  161.4 1.8 %collective-permute-done.3 = bf16[256,256]{1,0:T(8,128)(2,1)S(1)} collective-permute-done((bf16[256,256]{1,0:T(8,128)(2,1)S(1)}, bf16[256,256]{1,0:T(8,128)(2,1)S(1)}, u32[]{:S(2)}, u32[]{:S(2)}) %collective-permute-start.3) | collective-permute-done | bytes 131104 | tf_op jit(solution)/shard_map/ppermute | solution.py:30
  163.2 1.3 fusion.27
  164.5 0.1 broadcast_select_fusion.1
  164.6 0.7 convert_multiply_fusion.1
  165.3 1.2 multiply_bitcast_fusion
  166.5 1.3 copy.20
  (64 shorter events, 0.4 us)
Async XLA Ops:
  0.6 63.6 %copy-start = (bf16[256,1024]{1,0:T(8,128)(2,1)S(1)}, bf16[256,1024]{1,0:T(8,128)(2,1)}, u32[]{:S(2)}) copy-start(bf16[256,1024]{1,0:T(8,128)(2,1)} %param.14) | copy-start | bytes 1572868
  0.6 10.2 %copy-start.12 = (s32[1024,1]{0,1:T(1,128)S(1)}, s32[1024,1]{0,1:T(1,128)}, u32[]{:S(2)}) copy-start(s32[1024,1]{0,1:T(1,128)} %param.19) | copy-start | bytes 12292
  2.3 12.5 %collective-permute-start = (bf16[256,256]{1,0:T(8,128)(2,1)S(1)}, bf16[256,256]{1,0:T(8,128)(2,1)S(1)}, u32[]{:S(2)}, u32[]{:S(2)}) collective-permute-start(bf16[256,256]{1,0:T(8,128)(2,1)S(1)} %get-tuple-element.24), channel_id=1, source_target_pairs={{0,1},{1,2},{2,3},{3,4},{4,5},{5,6},{6,7},{8,9},{9,10},{10,11},{11... | collective-permute-start | bytes 393224 | tf_op jit(solution)/shard_map/ppermute | solution.py:27
  6.9 7.9 %collective-permute-start.1 = (bf16[256,256]{1,0:T(8,128)(2,1)S(1)}, bf16[256,256]{1,0:T(8,128)(2,1)S(1)}, u32[]{:S(2)}, u32[]{:S(2)}) collective-permute-start(bf16[256,256]{1,0:T(8,128)(2,1)S(1)} %get-tuple-element.25), channel_id=1, source_target_pairs={{1,0},{2,1},{3,2},{4,3},{5,4},{6,5},{7,6},{9,8},{10,9},{11,10},{12... | collective-permute-start | bytes 393224 | tf_op jit(solution)/shard_map/ppermute | solution.py:30
  9.6 2.9 %copy-start.16 = (s32[1,4,1024]{2,1,0:T(4,128)S(1)}, s32[1,4,1024]{2,1,0:T(4,128)}, u32[]{:S(2)}) copy-start(s32[1,4,1024]{2,1,0:T(4,128)} %param.18) | copy-start | bytes 49156
  10.9 3.6 %copy-start.7 = (bf16[1024,256]{1,0:T(8,128)(2,1)S(1)}, bf16[1024,256]{1,0:T(8,128)(2,1)}, u32[]{:S(2)}) copy-start(bf16[1024,256]{1,0:T(8,128)(2,1)} %param.11) | copy-start | bytes 1572868
  10.9 3.6 %copy-start.11 = (bf16[256,256]{1,0:T(8,128)(2,1)S(1)}, bf16[256,256]{1,0:T(8,128)(2,1)}, u32[]{:S(2)}) copy-start(bf16[256,256]{1,0:T(8,128)(2,1)} %param.12) | copy-start | bytes 393220
  10.9 3.9 %copy-start.18 = (s32[1,4,1024]{2,1,0:T(4,128)S(1)}, s32[1,4,1024]{2,1,0:T(4,128)}, u32[]{:S(2)}) copy-start(s32[1,4,1024]{2,1,0:T(4,128)} %param.17) | copy-start | bytes 49156
  19.7 2.8 %copy-start.4 = (bf16[4,1024,256]{2,1,0:T(8,128)(2,1)}, bf16[4,1024,256]{2,1,0:T(8,128)(2,1)S(1)}, u32[]{:S(2)}) copy-start(bf16[4,1024,256]{2,1,0:T(8,128)(2,1)S(1)} %fusion.20) | copy-start | bytes 6291460
  19.7 2.8 %copy-start.3 = (bf16[4,256,256]{2,1,0:T(8,128)(2,1)S(1)}, bf16[4,256,256]{2,1,0:T(8,128)(2,1)}, u32[]{:S(2)}) copy-start(bf16[4,256,256]{2,1,0:T(8,128)(2,1)} %param.13) | copy-start | bytes 1572868
  24.6 1.8 %copy-start.10 = (f32[1024,256]{1,0:T(8,128)}, f32[1024,256]{1,0:T(8,128)S(1)}, u32[]{:S(2)}) copy-start(f32[1024,256]{1,0:T(8,128)S(1)} %fusion.24) | copy-start | bytes 3145732
  26.4 7.3 %copy-start.13 = (bf16[1024]{0:T(1024)(128)(2,1)S(1)}, bf16[1024]{0:T(1024)(128)(2,1)}, u32[]{:S(2)}) copy-start(bf16[1024]{0:T(1024)(128)(2,1)} %param.15) | copy-start | bytes 6148
  27.6 36.0 %all-to-all-start = ((bf16[32,72,256]{2,1,0:T(8,128)(2,1)}), bf16[32,72,256]{2,1,0:T(8,128)(2,1)S(1)}, u32[]{:S(2)}, u32[]{:S(2)}) async-start(bf16[32,72,256]{2,1,0:T(8,128)(2,1)} %pad_maximum_fusion.1), calls=%async_computation | async-start | bytes 2359296 | tf_op jit(solution)/shard_map/all_to_all | solution.py:150
  64.3 0.7 copy-start.15
  65.0 0.6 copy-start.14
  68.5 33.1 %all-to-all-start.1 = ((bf16[32,72,256]{2,1,0:T(8,128)(2,1)}), bf16[32,72,256]{2,1,0:T(8,128)(2,1)S(1)}, u32[]{:S(2)}, u32[]{:S(2)}) async-start(bf16[32,72,256]{2,1,0:T(8,128)(2,1)} %maximum_maximum_fusion), calls=%async_computation.1 | async-start | bytes 2359296 | tf_op jit(solution)/shard_map/all_to_all | solution.py:185
  101.6 3.4 %copy-start.1 = (bf16[32,72,256]{2,1,0:T(8,128)(2,1)}, bf16[32,72,256]{2,1,0:T(8,128)(2,1)S(1)}, u32[]{:S(2)}) copy-start(bf16[32,72,256]{2,1,0:T(8,128)(2,1)S(1)} %all-to-all-done.1) | copy-start | bytes 3538948
  101.7 3.7 %copy-start.17 = (s32[1,4,1024]{2,1,0:T(4,128)S(1)}, s32[1,4,1024]{2,1,0:T(4,128)}, u32[]{:S(2)}) copy-start(s32[1,4,1024]{2,1,0:T(4,128)} %param.18) | copy-start | bytes 49156
  105.0 3.7 %copy-start.8 = (bf16[1024,256]{1,0:T(8,128)(2,1)}, bf16[1024,256]{1,0:T(8,128)(2,1)S(1)}, u32[]{:S(2)}) copy-start(bf16[1024,256]{1,0:T(8,128)(2,1)S(1)} %fusion.26) | copy-start | bytes 1572868
  105.4 3.3 %copy-start.5 = (bf16[4,1024,256]{2,1,0:T(8,128)(2,1)S(1)}, bf16[4,1024,256]{2,1,0:T(8,128)(2,1)}, u32[]{:S(2)}) copy-start(bf16[4,1024,256]{2,1,0:T(8,128)(2,1)} %copy-done.4) | copy-start | bytes 6291460
  108.8 1.3 copy-start.6
  108.8 2.0 %copy-start.2 = (f32[1024,256]{1,0:T(8,128)S(1)}, f32[1024,256]{1,0:T(8,128)}, u32[]{:S(2)}) copy-start(f32[1024,256]{1,0:T(8,128)} %fusion.68) | copy-start | bytes 3145732
  111.8 2.8 %collective-permute-start.4 = (bf16[1152,256]{1,0:T(8,128)(2,1)}, bf16[1152,256]{1,0:T(8,128)(2,1)}, u32[]{:S(2)}, u32[]{:S(2)}) collective-permute-start(bf16[1152,256]{1,0:T(8,128)(2,1)} %fusion.41), channel_id=1, source_target_pairs={{0,1},{1,0},{2,3},{3,2},{4,5},{5,4},{6,7},{7,6},{8,9},{9,8},{10,11... | collective-permute-start | bytes 1769480 | tf_op jit(solution)/shard_map/ppermute | solution.py:65
  116.6 25.7 %copy-start.19 = (s32[1,4,1024]{2,1,0:T(4,128)S(1)}, s32[1,4,1024]{2,1,0:T(4,128)}, u32[]{:S(2)}) copy-start(s32[1,4,1024]{2,1,0:T(4,128)} %param.17) | copy-start | bytes 49156
  116.6 20.7 %all-to-all-start.2 = ((bf16[16,72,256]{2,1,0:T(8,128)(2,1)}), bf16[16,72,256]{2,1,0:T(8,128)(2,1)S(1)}, u32[]{:S(2)}, u32[]{:S(2)}) async-start(bf16[16,72,256]{2,1,0:T(8,128)(2,1)} %bitcast.23), calls=%async_computation.2 | async-start | bytes 1179648 | tf_op jit(solution)/shard_map/all_to_all | solution.py:66
  138.5 20.7 %all-to-all-start.3 = ((bf16[16,72,256]{2,1,0:T(8,128)(2,1)}), bf16[16,72,256]{2,1,0:T(8,128)(2,1)S(1)}, u32[]{:S(2)}, u32[]{:S(2)}) async-start(bf16[16,72,256]{2,1,0:T(8,128)(2,1)} %broadcast_in_dim.10), calls=%async_computation.3 | async-start | bytes 1179648 | tf_op jit(solution)/shard_map/all_to_all | solution.py:73
  149.1 9.7 %copy-start.9 = (bf16[1024,256]{1,0:T(8,128)(2,1)S(1)}, bf16[1024,256]{1,0:T(8,128)(2,1)}, u32[]{:S(2)}) copy-start(bf16[1024,256]{1,0:T(8,128)(2,1)} %copy-done.8) | copy-start | bytes 1572868
  152.2 10.9 %copy-start.20 = (s32[1,512]{1,0:T(1,128)S(1)}, s32[1,512]{1,0:T(1,128)}, u32[]{:S(2)}) copy-start(s32[1,512]{1,0:T(1,128)} %param.16) | copy-start | bytes 6148
  152.3 9.1 %collective-permute-start.2 = (bf16[256,256]{1,0:T(8,128)(2,1)S(1)}, bf16[256,256]{1,0:T(8,128)(2,1)S(1)}, u32[]{:S(2)}, u32[]{:S(2)}) collective-permute-start(bf16[256,256]{1,0:T(8,128)(2,1)S(1)} %get-tuple-element.22), channel_id=1, source_target_pairs={{0,1},{1,2},{2,3},{3,4},{4,5},{5,6},{6,7},{8,9},{9,10},{10,11},{11... | collective-permute-start | bytes 393224 | tf_op jit(solution)/shard_map/ppermute | solution.py:27
  156.9 6.3 %collective-permute-start.3 = (bf16[256,256]{1,0:T(8,128)(2,1)S(1)}, bf16[256,256]{1,0:T(8,128)(2,1)S(1)}, u32[]{:S(2)}, u32[]{:S(2)}) collective-permute-start(bf16[256,256]{1,0:T(8,128)(2,1)S(1)} %get-tuple-element.23), channel_id=1, source_target_pairs={{1,0},{2,1},{3,2},{4,3},{5,4},{6,5},{7,6},{9,8},{10,9},{11,10},{12... | collective-permute-start | bytes 393224 | tf_op jit(solution)/shard_map/ppermute | solution.py:30
  159.2 5.3 %collective-permute-start.5 = (bf16[1152,256]{1,0:T(8,128)(2,1)S(1)}, bf16[1152,256]{1,0:T(8,128)(2,1)S(1)}, u32[]{:S(2)}, u32[]{:S(2)}) collective-permute-start(bf16[1152,256]{1,0:T(8,128)(2,1)S(1)} %bitcast.90), channel_id=1, source_target_pairs={{0,1},{1,0},{2,3},{3,2},{4,5},{5,4},{6,7},{7,6},{8,9},{9,8},{10,11... | collective-permute-start | bytes 1769480 | tf_op jit(solution)/shard_map/ppermute | solution.py:76

commit v9 on v8

--- a/solution.py
+++ b/solution.py
@@ -153,6 +153,7 @@
         packet_in[:, capacity:].reshape(owners, -1)[:, :capacity].astype(F32).astype(jnp.int32)
     ).reshape(-1)
     net_hot = one_hot(slot_nets_in, net_count)
+    slot_hot, dst_hot, inbound = lax.optimization_barrier((slot_hot, dst_hot, inbound))
     pooled = jnp.dot(
         one_hot_rows(slot_nets_in, net_count), inbound, preferred_element_type=F32
     )

time: 169 us -> 173 us (1.024)
  other arithmetic: 10.5 us -> 19 us
  waiting for transfers between devices: 79 us -> 71.1 us
    all_to_all x1, waiting for transfers between devices: 29.7 us -> 22.7 us  [on_device(): lax.all_to_all(packet, ALL, split_axis=0, concat_axis=0, tiled=True)]
    convert_element_type x0 -> x2, other arithmetic: none -> 6.97 us  [one_hot(): (index[..., None] == jnp.arange(count, dtype=index.dtype)).astype(BF16)]
  transfers between devices with their start and end apart: 10 -> 10, of which waited for: 5 -> 5; matrix products, arithmetic and copies ran while one was open for 12% -> 15% of each run, Pallas kernels for 0% -> 0%
where the time goes in v9:
time: 173 us; the launch traced here: 172 us
  waiting for transfers between devices  71.1 us (41%)
  matrix products  40.3 us (23%)
  starting transfers between devices  32.3 us (19%)
  other arithmetic  19 us (11%)
  local copies, waits for them, and re-layouts  7.58 us (4%)
    all_to_all x1, waiting for transfers between devices, on_device(): lax.all_to_all(back_packet, ALL, split_axis=0, concat_axis=0, tiled=True)  28.6 us
    all_to_all x1, waiting for transfers between devices, on_device(): lax.all_to_all(packet, ALL, split_axis=0, concat_axis=0, tiled=True)  22.7 us
    all_to_all x1, waiting for transfers between devices, all_sum(): lax.all_to_all(half.astype(BF16).reshape(chips, -1, width), CHIP, split_a...  17 us
    ppermute x2, starting transfers between devices, extended(): lax.ppermute(lax.slice_in_dim(block, block.shape[dim] - width, None, axis...  9.18 us
    convert_element_type x2, other arithmetic, one_hot(): (index[..., None] == jnp.arange(count, dtype=index.dtype)).astype(BF16)  6.97 us
    all_to_all x1, starting transfers between devices, on_device(): lax.all_to_all(packet, ALL, split_axis=0, concat_axis=0, tiled=True)  6.13 us
    dot_general x1, matrix products, on_device(): jnp.einsum('tre,ted->trd', one_hot_rows(sources, table_rows), edge_rows,...  5.87 us
    dot_general x2, matrix products, split_dot(): jnp.einsum(spec, left, right.astype(F32), precision=lax.Precision.HIGHEST...  5.19 us
  transfers between devices with their start and end apart: 10, of which 5 were waited for; matrix products, arithmetic and copies ran while one was open for 15% of the time, Pallas kernels for 0%

profile of v9, /device:TPU:1, one launch (start us, length us, event | category | flops | bytes accessed | tf_op | source)
XLA Modules:
  0.0 171.6 jit_solution(1418416797872430209)
XLA Ops:
  0.7 1.7 fusion.23
  2.4 4.6 %collective-permute-start = (bf16[256,256]{1,0:T(8,128)(2,1)S(1)}, bf16[256,256]{1,0:T(8,128)(2,1)S(1)}, u32[]{:S(2)}, u32[]{:S(2)}) collective-permute-start(bf16[256,256]{1,0:T(8,128)(2,1)S(1)} %get-tuple-element.30), channel_id=1, source_target_pairs={{0,1},{1,2},{2,3},{3,4},{4,5},{5,6},{6,7},{8,9},{9,10},{10,11},{11... | collective-permute-start | bytes 393224 | tf_op jit(solution)/shard_map/ppermute | solution.py:27
  7.0 1.9 %collective-permute-start.1 = (bf16[256,256]{1,0:T(8,128)(2,1)S(1)}, bf16[256,256]{1,0:T(8,128)(2,1)S(1)}, u32[]{:S(2)}, u32[]{:S(2)}) collective-permute-start(bf16[256,256]{1,0:T(8,128)(2,1)S(1)} %get-tuple-element.31), channel_id=1, source_target_pairs={{1,0},{2,1},{3,2},{4,3},{5,4},{6,5},{7,6},{9,8},{10,9},{11,10},{12... | collective-permute-start | bytes 393224 | tf_op jit(solution)/shard_map/ppermute | solution.py:30
  8.9 2.8 %convert_reduce_fusion = f32[1024]{0:T(1024)S(1)} fusion(s32[4,1024]{1,0:T(4,128)} %bitcast.107), kind=kLoop, calls=%fused_computation.4 | loop fusion | flops 16776192 | bytes 20480 | tf_op jit(solution)/shard_map/reduce_sum | solution.py:114
  11.8 0.3 fusion.59
  12.1 0.5 fusion.27
  12.7 1.5 fusion.7
  14.2 0.1 sub.16
  14.3 4.8 %fusion.17 = bf16[4,1024,256]{2,1,0:T(8,128)(2,1)S(1)} fusion(s32[4,1024]{1,0:T(4,128)S(1)} %bitcast.120, bf16[256,256]{1,0:T(8,128)(2,1)S(1)} %collective-permute-done.1, bf16[256,256]{1,0:T(8,128)(2,1)S(1)} %collective-permute-done, bf16[1024,256]{1,0:T(8,128)(2,1)S(1)} %copy-done.7), kind=kOutput, calls=%fused_computation.32 | convolution fusion | flops 3230924800 | bytes 2899968 | tf_op jit(solution)/shard_map/ter,rd->ted/dot_general | solution.py:107
  19.2 2.8 %fusion.2 = f32[4,1024,256]{2,1,0:T(8,128)S(1)} fusion(bf16[4,1024,256]{2,1,0:T(8,128)(2,1)S(1)} %fusion.17, s32[4,1024]{1,0:T(4,128)S(1)} %bitcast.108), kind=kOutput, calls=%fused_computation.7 | convolution fusion | flops 2151677952 | bytes 6307840 | tf_op jit(solution)/shard_map/tpe,ted->tpd/dot_general | solution.py:110
  22.0 2.1 %fusion.19 = f32[1024,256]{1,0:T(8,128)S(1)} fusion(f32[1024,256]{1,0:T(8,128)S(1)} %fusion.59, f32[4,1024,256]{2,1,0:T(8,128)S(1)} %fusion.2, bf16[4,256,256]{2,1,0:T(8,128)(2,1)S(1)} %copy-done.3, f32[1024]{0:T(1024)S(1)} %add_divide_fusion.2), kind=kOutput, calls=%fused_computation.38 | convolution fusion | flops 3221749760 | bytes 6819840 | tf_op jit(solution)/shard_map/tpk,tkd->pd/dot_general | solution.py:49
  24.1 1.8 %fusion.13 = bf16[2048,256]{1,0:T(8,128)(2,1)S(1)} fusion(s32[1024]{0:T(1024)S(1)} %multiply_add_fusion.1, f32[1024,256]{1,0:T(8,128)S(1)} %fusion.19), kind=kOutput, calls=%fused_computation.22 | convolution fusion | flops 1077673984 | bytes 2101248 | tf_op jit(solution)/shard_map/dot_general | solution.py:138
  26.0 1.1 pad_maximum_fusion.1
  27.1 6.1 %all-to-all-start = ((bf16[32,72,256]{2,1,0:T(8,128)(2,1)}), bf16[32,72,256]{2,1,0:T(8,128)(2,1)S(1)}, u32[]{:S(2)}, u32[]{:S(2)}) async-start(bf16[32,72,256]{2,1,0:T(8,128)(2,1)} %pad_maximum_fusion.1), calls=%async_computation | async-start | bytes 2359296 | tf_op jit(solution)/shard_map/all_to_all | solution.py:150
  33.3 0.1 pad.15.clone
  33.4 2.8 %fusion.9 = bf16[1024,2048]{1,0:T(8,128)(2,1)} fusion(s32[1024]{0:T(1024)S(1)} %bitcast.110), kind=kLoop, calls=%fused_computation.16 | loop fusion | flops 4194304 | bytes 4198400 | tf_op jit(solution)/shard_map/convert_element_type | solution.py:41
  36.1 4.2 %fusion.3 = bf16[4,1024,1024]{2,1,0:T(8,128)(2,1)} fusion(s32[4,1024]{1,0:T(4,128)S(1)} %bitcast.109), kind=kLoop, calls=%fused_computation.8 | loop fusion | flops 8388608 | bytes 8404992 | tf_op jit(solution)/shard_map/convert_element_type | solution.py:41
  40.4 22.7 %all-to-all-done = bf16[32,72,256]{2,1,0:T(8,128)(2,1)S(1)} async-done(((bf16[32,72,256]{2,1,0:T(8,128)(2,1)}), bf16[32,72,256]{2,1,0:T(8,128)(2,1)S(1)}, u32[]{:S(2)}, u32[]{:S(2)}) %all-to-all-start) | async-done | bytes 1179680 | tf_op jit(solution)/shard_map/all_to_all | solution.py:150
  63.1 1.1 slice.60
  64.2 0.1 eq.181
  64.3 1.7 fusion.25
  66.0 0.5 multiply_convert_fusion.2
  66.5 0.2 copy-done.12
  66.6 0.2 fusion.60
  66.9 0.4 multiply_convert_fusion.1
  67.3 2.0 %convolution_convert_fusion = bf16[2048,256]{1,0:T(8,128)(2,1)} fusion(bf16[256,1024]{1,0:T(8,128)(2,1)S(1)} %multiply_convert_fusion.1, bf16[256,1024]{1,0:T(8,128)(2,1)S(1)} %copy-done, s32[2048]{0:T(1024)S(1)} %eq.181), kind=kOutput, calls=%fused_computation.23 | convolution fusion | flops 403767296 | bytes 2105344 | tf_op jit(solution)/shard_map/dot_general | solution.py:173
  69.3 0.3 fusion.61
  69.6 2.8 %maximum_maximum_fusion = bf16[32,72,256]{2,1,0:T(8,128)(2,1)} fusion(bf16[32,4,256]{2,1,0:T(4,128)(2,1)S(1)} %broadcast_in_dim.8, bf16[32,64,256]{2,1,0:T(8,128)(2,1)} %bitcast.96, bf16[72]{0:T(256)(128)(2,1)S(1)} %pad.15.clone), kind=kLoop, calls=%fused_computation.44 | loop fusion | flops 3538944 | bytes 2293904 | tf_op jit(solution)/shard_map/concatenate | solution.py:176
  72.4 3.2 %all-to-all-start.1 = ((bf16[32,72,256]{2,1,0:T(8,128)(2,1)}), bf16[32,72,256]{2,1,0:T(8,128)(2,1)S(1)}, u32[]{:S(2)}, u32[]{:S(2)}) async-start(bf16[32,72,256]{2,1,0:T(8,128)(2,1)} %maximum_maximum_fusion), calls=%async_computation.1 | async-start | bytes 2359296 | tf_op jit(solution)/shard_map/all_to_all | solution.py:186
  75.7 1.3 fusion.63
  77.0 28.6 %all-to-all-done.1 = bf16[32,72,256]{2,1,0:T(8,128)(2,1)S(1)} async-done(((bf16[32,72,256]{2,1,0:T(8,128)(2,1)}), bf16[32,72,256]{2,1,0:T(8,128)(2,1)S(1)}, u32[]{:S(2)}, u32[]{:S(2)}) %all-to-all-start.1) | async-done | bytes 1179680 | tf_op jit(solution)/shard_map/all_to_all | solution.py:186
  105.6 0.1 slice.61
  105.8 4.3 %fusion.21 = bf16[1024,256]{1,0:T(8,128)(2,1)S(1)} fusion(bf16[1024,2048]{1,0:T(8,128)(2,1)} %fusion.9, bf16[2048,256]{1,0:T(8,128)(2,1)S(1)} %bitcast.99, f32[1024,256]{1,0:T(8,128)} %copy-done.10), kind=kOutput, calls=%fused_computation.40 | convolution fusion | flops 1076101120 | bytes 6815744 | tf_op jit(solution)/shard_map/dot_general | solution.py:196
  110.1 0.4 convolution_bitcast_fusion.2
  110.5 0.6 slice-done.1
  111.1 2.5 %convolution_convert_fusion.1 = bf16[4,1024,256]{2,1,0:T(8,128)(2,1)S(1)} fusion(bf16[4,1024,1024]{2,1,0:T(8,128)(2,1)S(1)} %bitcast.90, bf16[1024,256]{1,0:T(8,128)(2,1)S(1)} %fusion.21, f32[1024]{0:T(1024)S(1)} %add_divide_fusion.2), kind=kOutput, calls=%fused_computation.33 | convolution fusion | flops 2149318656 | bytes 11014144 | tf_op jit(solution)/shard_map/tep,pd->ted/dot_general | solution.py:200
  113.6 0.9 fusion.62
  114.4 0.5 copy-done.6
  114.9 0.6 copy-done.2
  115.5 0.2 pad_maximum_fusion
  115.7 0.9 fusion.36
  116.6 0.8 collective-permute-start.4
  117.4 2.0 %collective-permute-done.4 = bf16[1152,256]{1,0:T(8,128)(2,1)} collective-permute-done((bf16[1152,256]{1,0:T(8,128)(2,1)}, bf16[1152,256]{1,0:T(8,128)(2,1)}, u32[]{:S(2)}, u32[]{:S(2)}) %collective-permute-start.4) | collective-permute-done | bytes 589856 | tf_op jit(solution)/shard_map/ppermute | solution.py:65
  119.4 2.0 %fusion.24 = bf16[1152,256]{1,0:T(8,128)(2,1)} fusion(bf16[1152,256]{1,0:T(8,128)(2,1)} %collective-permute-done.4, f32[2,1152,256]{2,1,0:T(8,128)S(1)} %bitcast.92, s32[]{:T(128)S(6)} %select_n.27), kind=kLoop, calls=%fused_computation.46 | loop fusion | flops 884736 | bytes 2359300 | tf_op jit(solution)/shard_map/convert_element_type | solution.py:67
  121.4 3.7 %all-to-all-start.2 = ((bf16[16,72,256]{2,1,0:T(8,128)(2,1)}), bf16[16,72,256]{2,1,0:T(8,128)(2,1)S(1)}, u32[]{:S(2)}, u32[]{:S(2)}) async-start(bf16[16,72,256]{2,1,0:T(8,128)(2,1)} %bitcast.23), calls=%async_computation.2 | async-start | bytes 1179648 | tf_op jit(solution)/shard_map/all_to_all | solution.py:66
  125.1 17.0 %all-to-all-done.2 = bf16[16,72,256]{2,1,0:T(8,128)(2,1)S(1)} async-done(((bf16[16,72,256]{2,1,0:T(8,128)(2,1)}), bf16[16,72,256]{2,1,0:T(8,128)(2,1)S(1)}, u32[]{:S(2)}, u32[]{:S(2)}) %all-to-all-start.2) | async-done | bytes 589856 | tf_op jit(solution)/shard_map/all_to_all | solution.py:66
  142.2 0.2 fusion.37
  142.4 0.9 broadcast_in_dim.10
  143.3 3.8 %all-to-all-start.3 = ((bf16[16,72,256]{2,1,0:T(8,128)(2,1)}), bf16[16,72,256]{2,1,0:T(8,128)(2,1)S(1)}, u32[]{:S(2)}, u32[]{:S(2)}) async-start(bf16[16,72,256]{2,1,0:T(8,128)(2,1)} %broadcast_in_dim.10), calls=%async_computation.3 | async-start | bytes 1179648 | tf_op jit(solution)/shard_map/all_to_all | solution.py:73
  147.1 5.9 %fusion.1 = f32[4,1536,256]{2,1,0:T(8,128)S(1)} fusion(bf16[4,1024,256]{2,1,0:T(8,128)(2,1)} %copy-done.6, s32[4,1024]{1,0:T(4,128)S(1)} %bitcast.121), kind=kOutput, calls=%fused_computation.3 | convolution fusion | flops 3227516928 | bytes 8404992 | tf_op jit(solution)/shard_map/tre,ted->trd/dot_general | solution.py:204
  153.0 3.1 %fusion.58 = (bf16[1536,256]{1,0:T(8,128)(2,1)S(1)}, f32[1536,256]{1,0:T(8,128)S(1)}) fusion(f32[4,1536,256]{2,1,0:T(8,128)S(1)} %fusion.1, bf16[4,256,256]{2,1,0:T(8,128)(2,1)S(1)} %copy-done.3), kind=kOutput, calls=%fused_computation.104 | convolution fusion | flops 4832231424 | bytes 9175040 | tf_op jit(solution)/shard_map/trd,tkd->rk/dot_general | solution.py:49
  156.1 4.6 %collective-permute-start.2 = (bf16[256,256]{1,0:T(8,128)(2,1)S(1)}, bf16[256,256]{1,0:T(8,128)(2,1)S(1)}, u32[]{:S(2)}, u32[]{:S(2)}) collective-permute-start(bf16[256,256]{1,0:T(8,128)(2,1)S(1)} %get-tuple-element.28), channel_id=1, source_target_pairs={{0,1},{1,2},{2,3},{3,4},{4,5},{5,6},{6,7},{8,9},{9,10},{10,11},{11... | collective-permute-start | bytes 393224 | tf_op jit(solution)/shard_map/ppermute | solution.py:27
  160.7 1.9 %collective-permute-start.3 = (bf16[256,256]{1,0:T(8,128)(2,1)S(1)}, bf16[256,256]{1,0:T(8,128)(2,1)S(1)}, u32[]{:S(2)}, u32[]{:S(2)}) collective-permute-start(bf16[256,256]{1,0:T(8,128)(2,1)S(1)} %get-tuple-element.29), channel_id=1, source_target_pairs={{1,0},{2,1},{3,2},{4,3},{5,4},{6,5},{7,6},{9,8},{10,9},{11,10},{12... | collective-permute-start | bytes 393224 | tf_op jit(solution)/shard_map/ppermute | solution.py:30
  162.6 0.9 slice.65
  163.6 0.3 convolution_add_fusion
  163.9 1.5 collective-permute-start.5
  165.4 0.1 fusion.48
  165.6 0.6 broadcast_multiply_fusion
  166.2 0.8 collective-permute-done.3
  167.0 1.3 fusion.22
  168.3 0.1 broadcast_select_fusion.1
  168.4 1.2 multiply_bitcast_fusion
  169.6 0.7 convert_multiply_fusion.1
  170.3 1.3 copy.20
  (75 shorter events, 0.4 us)
Async XLA Ops:
  0.6 65.3 %copy-start = (bf16[256,1024]{1,0:T(8,128)(2,1)S(1)}, bf16[256,1024]{1,0:T(8,128)(2,1)}, u32[]{:S(2)}) copy-start(bf16[256,1024]{1,0:T(8,128)(2,1)} %param.14) | copy-start | bytes 1572868
  0.6 11.1 %copy-start.7 = (bf16[1024,256]{1,0:T(8,128)(2,1)S(1)}, bf16[1024,256]{1,0:T(8,128)(2,1)}, u32[]{:S(2)}) copy-start(bf16[1024,256]{1,0:T(8,128)(2,1)} %param.11) | copy-start | bytes 1572868
  0.7 11.1 %copy-start.11 = (bf16[256,256]{1,0:T(8,128)(2,1)S(1)}, bf16[256,256]{1,0:T(8,128)(2,1)}, u32[]{:S(2)}) copy-start(bf16[256,256]{1,0:T(8,128)(2,1)} %param.12) | copy-start | bytes 393220
  0.7 11.4 %copy-start.15 = (s32[1024,1]{0,1:T(1,128)S(1)}, s32[1024,1]{0,1:T(1,128)}, u32[]{:S(2)}) copy-start(s32[1024,1]{0,1:T(1,128)} %param.19) | copy-start | bytes 12292
  0.7 12.0 %copy-start.18 = (s32[1024]{0:T(1024)S(1)}, s32[1024]{0:T(1024)}, u32[]{:S(2)}) copy-start(s32[1024]{0:T(1024)} %param.20) | copy-start | bytes 12292
  2.4 11.9 %collective-permute-start = (bf16[256,256]{1,0:T(8,128)(2,1)S(1)}, bf16[256,256]{1,0:T(8,128)(2,1)S(1)}, u32[]{:S(2)}, u32[]{:S(2)}) collective-permute-start(bf16[256,256]{1,0:T(8,128)(2,1)S(1)} %get-tuple-element.30), channel_id=1, source_target_pairs={{0,1},{1,2},{2,3},{3,4},{4,5},{5,6},{6,7},{8,9},{9,10},{10,11},{11... | collective-permute-start | bytes 393224 | tf_op jit(solution)/shard_map/ppermute | solution.py:27
  7.0 7.3 %collective-permute-start.1 = (bf16[256,256]{1,0:T(8,128)(2,1)S(1)}, bf16[256,256]{1,0:T(8,128)(2,1)S(1)}, u32[]{:S(2)}, u32[]{:S(2)}) collective-permute-start(bf16[256,256]{1,0:T(8,128)(2,1)S(1)} %get-tuple-element.31), channel_id=1, source_target_pairs={{1,0},{2,1},{3,2},{4,3},{5,4},{6,5},{7,6},{9,8},{10,9},{11,10},{12... | collective-permute-start | bytes 393224 | tf_op jit(solution)/shard_map/ppermute | solution.py:30
  12.6 1.7 copy-start.20
  14.3 4.9 %copy-start.14 = (s32[1,4,1024]{2,1,0:T(4,128)S(1)}, s32[1,4,1024]{2,1,0:T(4,128)}, u32[]{:S(2)}) copy-start(s32[1,4,1024]{2,1,0:T(4,128)} %param.18) | copy-start | bytes 49156
  19.2 2.8 %copy-start.4 = (bf16[4,1024,256]{2,1,0:T(8,128)(2,1)}, bf16[4,1024,256]{2,1,0:T(8,128)(2,1)S(1)}, u32[]{:S(2)}) copy-start(bf16[4,1024,256]{2,1,0:T(8,128)(2,1)S(1)} %fusion.17) | copy-start | bytes 6291460
  19.2 2.8 %copy-start.3 = (bf16[4,256,256]{2,1,0:T(8,128)(2,1)S(1)}, bf16[4,256,256]{2,1,0:T(8,128)(2,1)}, u32[]{:S(2)}) copy-start(bf16[4,256,256]{2,1,0:T(8,128)(2,1)} %param.13) | copy-start | bytes 1572868
  24.1 1.8 %copy-start.10 = (f32[1024,256]{1,0:T(8,128)}, f32[1024,256]{1,0:T(8,128)S(1)}, u32[]{:S(2)}) copy-start(f32[1024,256]{1,0:T(8,128)S(1)} %fusion.19) | copy-start | bytes 3145732
  26.0 7.3 %copy-start.16 = (bf16[1024]{0:T(1024)(128)(2,1)S(1)}, bf16[1024]{0:T(1024)(128)(2,1)}, u32[]{:S(2)}) copy-start(bf16[1024]{0:T(1024)(128)(2,1)} %param.15) | copy-start | bytes 6148
  27.1 35.9 %all-to-all-start = ((bf16[32,72,256]{2,1,0:T(8,128)(2,1)}), bf16[32,72,256]{2,1,0:T(8,128)(2,1)S(1)}, u32[]{:S(2)}, u32[]{:S(2)}) async-start(bf16[32,72,256]{2,1,0:T(8,128)(2,1)} %pad_maximum_fusion.1), calls=%async_computation | async-start | bytes 2359296 | tf_op jit(solution)/shard_map/all_to_all | solution.py:150
  66.0 0.7 copy-start.12
  66.0 0.9 copy-start.19
  66.9 5.6 %copy-start.17 = (f32[1,256]{1,0:T(1,128)}, f32[1,256]{1,0:T(1,128)S(1)}, u32[]{:S(2)}) copy-start(f32[1,256]{1,0:T(1,128)S(1)} %fusion.60) | copy-start | bytes 3076
  72.4 3.3 %copy-start.13 = (bf16[256,256]{1,0:T(8,128)(2,1)S(1)}, bf16[256,256]{1,0:T(8,128)(2,1)}, u32[]{:S(2)}) copy-start(bf16[256,256]{1,0:T(8,128)(2,1)} %copy-done.12) | copy-start | bytes 393220
  72.4 33.2 %all-to-all-start.1 = ((bf16[32,72,256]{2,1,0:T(8,128)(2,1)}), bf16[32,72,256]{2,1,0:T(8,128)(2,1)S(1)}, u32[]{:S(2)}, u32[]{:S(2)}) async-start(bf16[32,72,256]{2,1,0:T(8,128)(2,1)} %maximum_maximum_fusion), calls=%async_computation.1 | async-start | bytes 2359296 | tf_op jit(solution)/shard_map/all_to_all | solution.py:186
  105.6 4.5 %copy-start.1 = (bf16[32,72,256]{2,1,0:T(8,128)(2,1)}, bf16[32,72,256]{2,1,0:T(8,128)(2,1)S(1)}, u32[]{:S(2)}) copy-start(bf16[32,72,256]{2,1,0:T(8,128)(2,1)S(1)} %all-to-all-done.1) | copy-start | bytes 3538948
  105.6 4.9 %slice-start = ((s8[8388608]{0:T(1024)(128)(4,1)}), s8[4194304]{0:T(1024)(128)(4,1)S(1)}, s32[]{:S(2)}) async-start(s8[8388608]{0:T(1024)(128)(4,1)} %bitcast.89), calls=%async_computation.4 | async-start | bytes 8388608
  105.7 5.3 %slice-start.1 = ((s8[8388608]{0:T(1024)(128)(4,1)}), s8[4194304]{0:T(1024)(128)(4,1)S(1)}, s32[]{:S(2)}) async-start(s8[8388608]{0:T(1024)(128)(4,1)} %bitcast.89), calls=%async_computation.5 | async-start | bytes 8388608
  110.1 3.4 %copy-start.8 = (bf16[1024,256]{1,0:T(8,128)(2,1)}, bf16[1024,256]{1,0:T(8,128)(2,1)S(1)}, u32[]{:S(2)}) copy-start(bf16[1024,256]{1,0:T(8,128)(2,1)S(1)} %fusion.21) | copy-start | bytes 1572868
  111.1 2.5 %copy-start.5 = (bf16[4,1024,256]{2,1,0:T(8,128)(2,1)S(1)}, bf16[4,1024,256]{2,1,0:T(8,128)(2,1)}, u32[]{:S(2)}) copy-start(bf16[4,1024,256]{2,1,0:T(8,128)(2,1)} %copy-done.4) | copy-start | bytes 6291460
  113.5 1.4 copy-start.6
  113.6 2.0 %copy-start.2 = (f32[1024,256]{1,0:T(8,128)S(1)}, f32[1024,256]{1,0:T(8,128)}, u32[]{:S(2)}) copy-start(f32[1024,256]{1,0:T(8,128)} %fusion.63) | copy-start | bytes 3145732
  116.6 2.8 %collective-permute-start.4 = (bf16[1152,256]{1,0:T(8,128)(2,1)}, bf16[1152,256]{1,0:T(8,128)(2,1)}, u32[]{:S(2)}, u32[]{:S(2)}) collective-permute-start(bf16[1152,256]{1,0:T(8,128)(2,1)} %fusion.36), channel_id=1, source_target_pairs={{0,1},{1,0},{2,3},{3,2},{4,5},{5,4},{6,7},{7,6},{8,9},{9,8},{10,11... | collective-permute-start | bytes 1769480 | tf_op jit(solution)/shard_map/ppermute | solution.py:65
  121.4 25.7 %copy-start.21 = (s32[1,4,1024]{2,1,0:T(4,128)S(1)}, s32[1,4,1024]{2,1,0:T(4,128)}, u32[]{:S(2)}) copy-start(s32[1,4,1024]{2,1,0:T(4,128)} %param.17) | copy-start | bytes 49156
  121.4 20.7 %all-to-all-start.2 = ((bf16[16,72,256]{2,1,0:T(8,128)(2,1)}), bf16[16,72,256]{2,1,0:T(8,128)(2,1)S(1)}, u32[]{:S(2)}, u32[]{:S(2)}) async-start(bf16[16,72,256]{2,1,0:T(8,128)(2,1)} %bitcast.23), calls=%async_computation.2 | async-start | bytes 1179648 | tf_op jit(solution)/shard_map/all_to_all | solution.py:66
  143.3 20.7 %all-to-all-start.3 = ((bf16[16,72,256]{2,1,0:T(8,128)(2,1)}), bf16[16,72,256]{2,1,0:T(8,128)(2,1)S(1)}, u32[]{:S(2)}, u32[]{:S(2)}) async-start(bf16[16,72,256]{2,1,0:T(8,128)(2,1)} %broadcast_in_dim.10), calls=%async_computation.3 | async-start | bytes 1179648 | tf_op jit(solution)/shard_map/all_to_all | solution.py:73
  153.0 10.6 %copy-start.9 = (bf16[1024,256]{1,0:T(8,128)(2,1)S(1)}, bf16[1024,256]{1,0:T(8,128)(2,1)}, u32[]{:S(2)}) copy-start(bf16[1024,256]{1,0:T(8,128)(2,1)} %copy-done.8) | copy-start | bytes 1572868
  156.1 10.9 %copy-start.22 = (s32[1,512]{1,0:T(1,128)S(1)}, s32[1,512]{1,0:T(1,128)}, u32[]{:S(2)}) copy-start(s32[1,512]{1,0:T(1,128)} %param.16) | copy-start | bytes 6148
  156.1 10.0 %collective-permute-start.2 = (bf16[256,256]{1,0:T(8,128)(2,1)S(1)}, bf16[256,256]{1,0:T(8,128)(2,1)S(1)}, u32[]{:S(2)}, u32[]{:S(2)}) collective-permute-start(bf16[256,256]{1,0:T(8,128)(2,1)S(1)} %get-tuple-element.28), channel_id=1, source_target_pairs={{0,1},{1,2},{2,3},{3,4},{4,5},{5,6},{6,7},{8,9},{9,10},{10,11},{11... | collective-permute-start | bytes 393224 | tf_op jit(solution)/shard_map/ppermute | solution.py:27
  160.7 6.3 %collective-permute-start.3 = (bf16[256,256]{1,0:T(8,128)(2,1)S(1)}, bf16[256,256]{1,0:T(8,128)(2,1)S(1)}, u32[]{:S(2)}, u32[]{:S(2)}) collective-permute-start(bf16[256,256]{1,0:T(8,128)(2,1)S(1)} %get-tuple-element.29), channel_id=1, source_target_pairs={{1,0},{2,1},{3,2},{4,3},{5,4},{6,5},{7,6},{9,8},{10,9},{11,10},{12... | collective-permute-start | bytes 393224 | tf_op jit(solution)/shard_map/ppermute | solution.py:30
  163.9 4.4 %collective-permute-start.5 = (bf16[1152,256]{1,0:T(8,128)(2,1)S(1)}, bf16[1152,256]{1,0:T(8,128)(2,1)S(1)}, u32[]{:S(2)}, u32[]{:S(2)}) collective-permute-start(bf16[1152,256]{1,0:T(8,128)(2,1)S(1)} %bitcast.94), channel_id=1, source_target_pairs={{0,1},{1,0},{2,3},{3,2},{4,5},{5,4},{6,7},{7,6},{8,9},{9,8},{10,11... | collective-permute-start | bytes 1769480 | tf_op jit(solution)/shard_map/ppermute | solution.py:76

commit v10 on v8

--- a/solution.py
+++ b/solution.py
@@ -170,7 +170,7 @@
         "nh,dh->nd", head_grad, w_head, preferred_element_type=F32
     ).astype(BF16)
     returned = jnp.dot(net_hot, net_grad, preferred_element_type=F32).astype(BF16)
-    out_rows = out_sum.reshape(-1, feat_width).astype(BF16)
+    out_rows = (out_sum * (1.0 / math.sqrt(pin_count * owners))).reshape(-1, feat_width).astype(BF16)
     back_rows = -(-(capacity + out_rows.shape[0]) // 8) * 8
     back_packet = jnp.concatenate(
         [
@@ -215,13 +215,13 @@
         local_grad
         + jnp.dot(one_hot_rows(send_list, pin_count), received, preferred_element_type=F32)
     ).astype(BF16)
+    grad_scale = 1.0 / math.sqrt(pin_count * owners)
     pieces = (self_sum, edge_sum.reshape(-1, feat_width), head_sum_t)
-    totals = all_sum(jnp.concatenate(pieces, 0), owners)
-    grad_scale = 1.0 / math.sqrt(pin_count * owners)
+    totals = all_sum(jnp.concatenate(pieces, 0) * grad_scale, owners)
     outs = []
     offset = 0
     for piece in pieces:
-        outs.append(totals[offset : offset + piece.shape[0]] * grad_scale)
+        outs.append(totals[offset : offset + piece.shape[0]])
         offset += piece.shape[0]
     return (
         predicted,
@@ -229,7 +229,7 @@
         outs[0],
         outs[1].reshape(edge_sum.shape),
         outs[2].T,
-        out_total * grad_scale,
+        out_total,
     )
 
 

time: 169 us -> 169 us (level)
  matrix products: 38.7 us -> 40.4 us
    ppermute x2, waiting for transfers between devices: 1.78 us -> 0.01 us  [extended(): lax.ppermute(lax.slice_in_dim(block, 0, width, axis=dim), axis, backward)]
where the time goes in v10:
time: 169 us; the launch traced here: 168 us
  waiting for transfers between devices  78.3 us (46%)
  matrix products  40.4 us (24%)
  starting transfers between devices  32.4 us (19%)
  other arithmetic  9.98 us (6%)
  local copies, waits for them, and re-layouts  6.04 us (4%)
    all_to_all x1, waiting for transfers between devices, on_device(): lax.all_to_all(packet, ALL, split_axis=0, concat_axis=0, tiled=True)  29.7 us
    all_to_all x1, waiting for transfers between devices, on_device(): lax.all_to_all(back_packet, ALL, split_axis=0, concat_axis=0, tiled=True)  28.6 us
    all_to_all x1, waiting for transfers between devices, all_sum(): lax.all_to_all(half.astype(BF16).reshape(chips, -1, width), CHIP, split_a...  17 us
    ppermute x2, starting transfers between devices, extended(): lax.ppermute(lax.slice_in_dim(block, block.shape[dim] - width, None, axis...  9.16 us
    all_to_all x1, starting transfers between devices, on_device(): lax.all_to_all(packet, ALL, split_axis=0, concat_axis=0, tiled=True)  6.14 us
    dot_general x1, matrix products, on_device(): jnp.einsum('tre,ted->trd', one_hot_rows(sources, table_rows), edge_rows,...  5.88 us
    dot_general x2, matrix products, split_dot(): jnp.einsum(spec, left, right.astype(F32), precision=lax.Precision.HIGHEST...  5.18 us
    dot_general x1, matrix products, on_device(): jnp.einsum('ter,rd->ted', src_hot, node_table, preferred_element_type=F32)  4.85 us
  transfers between devices with their start and end apart: 10, of which 5 were waited for; matrix products, arithmetic and copies ran while one was open for 12% of the time, Pallas kernels for 0%

profile of v10, /device:TPU:1, one launch (start us, length us, event | category | flops | bytes accessed | tf_op | source)
XLA Modules:
  0.0 168.4 jit_solution(7850528449821611518)
XLA Ops:
  0.6 0.0 copy-start
  0.6 0.0 copy-start.11
  0.7 1.6 fusion.28
  2.3 4.6 %collective-permute-start = (bf16[256,256]{1,0:T(8,128)(2,1)S(1)}, bf16[256,256]{1,0:T(8,128)(2,1)S(1)}, u32[]{:S(2)}, u32[]{:S(2)}) collective-permute-start(bf16[256,256]{1,0:T(8,128)(2,1)S(1)} %get-tuple-element.24), channel_id=1, source_target_pairs={{0,1},{1,2},{2,3},{3,4},{4,5},{5,6},{6,7},{8,9},{9,10},{10,11},{11... | collective-permute-start | bytes 393224 | tf_op jit(solution)/shard_map/ppermute | solution.py:27
  6.9 1.9 %collective-permute-start.1 = (bf16[256,256]{1,0:T(8,128)(2,1)S(1)}, bf16[256,256]{1,0:T(8,128)(2,1)S(1)}, u32[]{:S(2)}, u32[]{:S(2)}) collective-permute-start(bf16[256,256]{1,0:T(8,128)(2,1)S(1)} %get-tuple-element.25), channel_id=1, source_target_pairs={{1,0},{2,1},{3,2},{4,3},{5,4},{6,5},{7,6},{9,8},{10,9},{11,10},{12... | collective-permute-start | bytes 393224 | tf_op jit(solution)/shard_map/ppermute | solution.py:30
  8.8 0.7 add_convert_fusion.1
  9.6 1.3 fusion.32
  10.9 0.0 copy-start.17
  10.9 1.5 fusion.9
  12.4 0.1 sub.16
  12.5 1.9 %convert_reduce_fusion = f32[1024]{0:T(1024)S(1)} fusion(s32[4,1024]{1,0:T(4,128)S(1)} %bitcast.113), kind=kLoop, calls=%fused_computation.4 | loop fusion | flops 16776192 | bytes 20480 | tf_op jit(solution)/shard_map/reduce_sum | solution.py:114
  14.5 0.3 fusion.64
  14.8 4.8 %fusion.20 = bf16[4,1024,256]{2,1,0:T(8,128)(2,1)S(1)} fusion(s32[4,1024]{1,0:T(4,128)S(1)} %bitcast.116, bf16[256,256]{1,0:T(8,128)(2,1)S(1)} %collective-permute-done.1, bf16[256,256]{1,0:T(8,128)(2,1)S(1)} %collective-permute-done, bf16[1024,256]{1,0:T(8,128)(2,1)S(1)} %copy-done.7), kind=kOutput, calls=%fused_computation.35 | convolution fusion | flops 3230924800 | bytes 2899968 | tf_op jit(solution)/shard_map/ter,rd->ted/dot_general | solution.py:107
  19.7 2.8 %fusion.4 = f32[4,1024,256]{2,1,0:T(8,128)S(1)} fusion(bf16[4,1024,256]{2,1,0:T(8,128)(2,1)S(1)} %fusion.20, s32[4,1024]{1,0:T(4,128)S(1)} %bitcast.114), kind=kOutput, calls=%fused_computation.9 | convolution fusion | flops 2151677952 | bytes 6307840 | tf_op jit(solution)/shard_map/tpe,ted->tpd/dot_general | solution.py:110
  22.5 2.1 %fusion.24 = f32[1024,256]{1,0:T(8,128)S(1)} fusion(f32[1024,256]{1,0:T(8,128)S(1)} %fusion.64, f32[4,1024,256]{2,1,0:T(8,128)S(1)} %fusion.4, bf16[4,256,256]{2,1,0:T(8,128)(2,1)S(1)} %copy-done.3, f32[1024]{0:T(1024)S(1)} %add_divide_fusion.2), kind=kOutput, calls=%fused_computation.41 | convolution fusion | flops 3221749760 | bytes 6819840 | tf_op jit(solution)/shard_map/tpk,tkd->pd/dot_general | solution.py:49
  24.6 1.8 %fusion.16 = bf16[2048,256]{1,0:T(8,128)(2,1)S(1)} fusion(s32[1024]{0:T(1024)S(1)} %multiply_add_fusion.1, f32[1024,256]{1,0:T(8,128)S(1)} %fusion.24), kind=kOutput, calls=%fused_computation.25 | convolution fusion | flops 1077673984 | bytes 2101248 | tf_op jit(solution)/shard_map/dot_general | solution.py:138
  26.4 1.1 pad_maximum_fusion
  27.6 6.1 %all-to-all-start = ((bf16[32,72,256]{2,1,0:T(8,128)(2,1)}), bf16[32,72,256]{2,1,0:T(8,128)(2,1)S(1)}, u32[]{:S(2)}, u32[]{:S(2)}) async-start(bf16[32,72,256]{2,1,0:T(8,128)(2,1)} %pad_maximum_fusion), calls=%async_computation | async-start | bytes 2359296 | tf_op jit(solution)/shard_map/all_to_all | solution.py:150
  33.8 0.1 pad.15.clone
  33.9 29.7 %all-to-all-done = bf16[32,72,256]{2,1,0:T(8,128)(2,1)S(1)} async-done(((bf16[32,72,256]{2,1,0:T(8,128)(2,1)}), bf16[32,72,256]{2,1,0:T(8,128)(2,1)S(1)}, u32[]{:S(2)}, u32[]{:S(2)}) %all-to-all-start) | async-done | bytes 1179680 | tf_op jit(solution)/shard_map/all_to_all | solution.py:150
  63.6 0.1 eq.181
  63.7 0.1 slice.60
  63.8 0.5 fusion.30
  64.3 0.5 multiply_convert_fusion.2
  64.7 0.2 fusion.65
  65.0 0.3 fusion.66
  65.3 0.2 copy-done.13
  65.6 0.4 multiply_convert_fusion.1
  66.0 1.0 convolution_convert_fusion
  67.0 1.6 maximum_maximum_fusion
  68.6 3.1 %all-to-all-start.1 = ((bf16[32,72,256]{2,1,0:T(8,128)(2,1)}), bf16[32,72,256]{2,1,0:T(8,128)(2,1)S(1)}, u32[]{:S(2)}, u32[]{:S(2)}) async-start(bf16[32,72,256]{2,1,0:T(8,128)(2,1)} %maximum_maximum_fusion), calls=%async_computation.1 | async-start | bytes 2359296 | tf_op jit(solution)/shard_map/all_to_all | solution.py:185
  71.7 1.3 fusion.68
  73.0 28.6 %all-to-all-done.1 = bf16[32,72,256]{2,1,0:T(8,128)(2,1)S(1)} async-done(((bf16[32,72,256]{2,1,0:T(8,128)(2,1)}), bf16[32,72,256]{2,1,0:T(8,128)(2,1)S(1)}, u32[]{:S(2)}, u32[]{:S(2)}) %all-to-all-start.1) | async-done | bytes 1179680 | tf_op jit(solution)/shard_map/all_to_all | solution.py:185
  101.6 0.1 slice.61
  101.8 3.3 %fusion.26 = bf16[1024,256]{1,0:T(8,128)(2,1)S(1)} fusion(bf16[2048,256]{1,0:T(8,128)(2,1)S(1)} %bitcast.94, s32[1024]{0:T(1024)S(1)} %bitcast.112, f32[1024,256]{1,0:T(8,128)} %copy-done.9), kind=kOutput, calls=%fused_computation.43 | convolution fusion | flops 1078198272 | bytes 2625536 | tf_op jit(solution)/shard_map/dot_general | solution.py:195
  105.1 0.4 convolution_bitcast_fusion.2
  105.5 3.3 %fusion.21 = bf16[4,1024,256]{2,1,0:T(8,128)(2,1)S(1)} fusion(s32[4,1024]{1,0:T(4,128)S(1)} %bitcast.115, bf16[1024,256]{1,0:T(8,128)(2,1)S(1)} %fusion.26, f32[1024]{0:T(1024)S(1)} %add_divide_fusion.2), kind=kOutput, calls=%fused_computation.36 | convolution fusion | flops 2153512960 | bytes 2641920 | tf_op jit(solution)/shard_map/tep,pd->ted/dot_general | solution.py:199
  108.8 0.9 fusion.67
  109.7 0.4 copy-done.6
  110.1 0.6 copy-done.2
  110.8 0.2 maximum_multiply_fusion
  111.0 0.9 fusion.41
  111.9 0.8 collective-permute-start.4
  112.7 2.0 %collective-permute-done.4 = bf16[1152,256]{1,0:T(8,128)(2,1)} collective-permute-done((bf16[1152,256]{1,0:T(8,128)(2,1)}, bf16[1152,256]{1,0:T(8,128)(2,1)}, u32[]{:S(2)}, u32[]{:S(2)}) %collective-permute-start.4) | collective-permute-done | bytes 589856 | tf_op jit(solution)/shard_map/ppermute | solution.py:65
  114.7 2.0 %fusion.29 = bf16[1152,256]{1,0:T(8,128)(2,1)} fusion(bf16[1152,256]{1,0:T(8,128)(2,1)} %collective-permute-done.4, f32[2,1152,256]{2,1,0:T(8,128)S(1)} %bitcast.88, s32[]{:T(128)S(6)} %select_n.27), kind=kLoop, calls=%fused_computation.49 | loop fusion | flops 884736 | bytes 2359300 | tf_op jit(solution)/shard_map/convert_element_type | solution.py:67
  116.7 3.7 %all-to-all-start.2 = ((bf16[16,72,256]{2,1,0:T(8,128)(2,1)}), bf16[16,72,256]{2,1,0:T(8,128)(2,1)S(1)}, u32[]{:S(2)}, u32[]{:S(2)}) async-start(bf16[16,72,256]{2,1,0:T(8,128)(2,1)} %bitcast.23), calls=%async_computation.2 | async-start | bytes 1179648 | tf_op jit(solution)/shard_map/all_to_all | solution.py:66
  120.4 17.0 %all-to-all-done.2 = bf16[16,72,256]{2,1,0:T(8,128)(2,1)S(1)} async-done(((bf16[16,72,256]{2,1,0:T(8,128)(2,1)}), bf16[16,72,256]{2,1,0:T(8,128)(2,1)S(1)}, u32[]{:S(2)}, u32[]{:S(2)}) %all-to-all-start.2) | async-done | bytes 589856 | tf_op jit(solution)/shard_map/all_to_all | solution.py:66
  137.4 0.2 fusion.42
  137.7 0.9 broadcast_in_dim.10
  138.5 3.8 %all-to-all-start.3 = ((bf16[16,72,256]{2,1,0:T(8,128)(2,1)}), bf16[16,72,256]{2,1,0:T(8,128)(2,1)S(1)}, u32[]{:S(2)}, u32[]{:S(2)}) async-start(bf16[16,72,256]{2,1,0:T(8,128)(2,1)} %broadcast_in_dim.10), calls=%async_computation.3 | async-start | bytes 1179648 | tf_op jit(solution)/shard_map/all_to_all | solution.py:73
  142.4 5.9 %fusion.1 = f32[4,1536,256]{2,1,0:T(8,128)S(1)} fusion(bf16[4,1024,256]{2,1,0:T(8,128)(2,1)} %copy-done.6, s32[4,1024]{1,0:T(4,128)S(1)} %bitcast.117), kind=kOutput, calls=%fused_computation.3 | convolution fusion | flops 3227516928 | bytes 8404992 | tf_op jit(solution)/shard_map/tre,ted->trd/dot_general | solution.py:203
  148.3 3.1 %fusion.63 = (bf16[1536,256]{1,0:T(8,128)(2,1)S(1)}, f32[1536,256]{1,0:T(8,128)S(1)}) fusion(f32[4,1536,256]{2,1,0:T(8,128)S(1)} %fusion.1, bf16[4,256,256]{2,1,0:T(8,128)(2,1)S(1)} %copy-done.3), kind=kOutput, calls=%fused_computation.107 | convolution fusion | flops 4832231424 | bytes 9175040 | tf_op jit(solution)/shard_map/trd,tkd->rk/dot_general | solution.py:49
  151.4 4.6 %collective-permute-start.2 = (bf16[256,256]{1,0:T(8,128)(2,1)S(1)}, bf16[256,256]{1,0:T(8,128)(2,1)S(1)}, u32[]{:S(2)}, u32[]{:S(2)}) collective-permute-start(bf16[256,256]{1,0:T(8,128)(2,1)S(1)} %get-tuple-element.22), channel_id=1, source_target_pairs={{0,1},{1,2},{2,3},{3,4},{4,5},{5,6},{6,7},{8,9},{9,10},{10,11},{11... | collective-permute-start | bytes 393224 | tf_op jit(solution)/shard_map/ppermute | solution.py:27
  156.0 1.9 %collective-permute-start.3 = (bf16[256,256]{1,0:T(8,128)(2,1)S(1)}, bf16[256,256]{1,0:T(8,128)(2,1)S(1)}, u32[]{:S(2)}, u32[]{:S(2)}) collective-permute-start(bf16[256,256]{1,0:T(8,128)(2,1)S(1)} %get-tuple-element.23), channel_id=1, source_target_pairs={{1,0},{2,1},{3,2},{4,3},{5,4},{6,5},{7,6},{9,8},{10,9},{11,10},{12... | collective-permute-start | bytes 393224 | tf_op jit(solution)/shard_map/ppermute | solution.py:30
  157.9 1.1 all-to-all-done.3
  159.0 1.8 %collective-permute-start.5 = (bf16[1152,256]{1,0:T(8,128)(2,1)S(1)}, bf16[1152,256]{1,0:T(8,128)(2,1)S(1)}, u32[]{:S(2)}, u32[]{:S(2)}) collective-permute-start(bf16[1152,256]{1,0:T(8,128)(2,1)S(1)} %bitcast.90), channel_id=1, source_target_pairs={{0,1},{1,0},{2,3},{3,2},{4,5},{5,4},{6,7},{7,6},{8,9},{9,8},{10,11... | collective-permute-start | bytes 1769480 | tf_op jit(solution)/shard_map/ppermute | solution.py:76
  160.7 1.4 convolution_add_fusion
  162.1 0.9 slice.65
  163.0 0.7 fusion.53
  163.8 1.3 fusion.27
  165.1 0.1 broadcast_select_fusion.1
  165.2 0.7 maximum_convert_fusion.1
  165.9 1.1 convert_bitcast_fusion
  167.1 1.3 copy.20
  (61 shorter events, 0.4 us)
Async XLA Ops:
  0.6 63.6 %copy-start = (bf16[256,1024]{1,0:T(8,128)(2,1)S(1)}, bf16[256,1024]{1,0:T(8,128)(2,1)}, u32[]{:S(2)}) copy-start(bf16[256,1024]{1,0:T(8,128)(2,1)} %param.14) | copy-start | bytes 1572868
  0.6 10.2 %copy-start.11 = (s32[1024,1]{0,1:T(1,128)S(1)}, s32[1024,1]{0,1:T(1,128)}, u32[]{:S(2)}) copy-start(s32[1024,1]{0,1:T(1,128)} %param.19) | copy-start | bytes 12292
  2.3 12.5 %collective-permute-start = (bf16[256,256]{1,0:T(8,128)(2,1)S(1)}, bf16[256,256]{1,0:T(8,128)(2,1)S(1)}, u32[]{:S(2)}, u32[]{:S(2)}) collective-permute-start(bf16[256,256]{1,0:T(8,128)(2,1)S(1)} %get-tuple-element.24), channel_id=1, source_target_pairs={{0,1},{1,2},{2,3},{3,4},{4,5},{5,6},{6,7},{8,9},{9,10},{10,11},{11... | collective-permute-start | bytes 393224 | tf_op jit(solution)/shard_map/ppermute | solution.py:27
  6.9 7.9 %collective-permute-start.1 = (bf16[256,256]{1,0:T(8,128)(2,1)S(1)}, bf16[256,256]{1,0:T(8,128)(2,1)S(1)}, u32[]{:S(2)}, u32[]{:S(2)}) collective-permute-start(bf16[256,256]{1,0:T(8,128)(2,1)S(1)} %get-tuple-element.25), channel_id=1, source_target_pairs={{1,0},{2,1},{3,2},{4,3},{5,4},{6,5},{7,6},{9,8},{10,9},{11,10},{12... | collective-permute-start | bytes 393224 | tf_op jit(solution)/shard_map/ppermute | solution.py:30
  9.6 2.9 %copy-start.15 = (s32[1,4,1024]{2,1,0:T(4,128)S(1)}, s32[1,4,1024]{2,1,0:T(4,128)}, u32[]{:S(2)}) copy-start(s32[1,4,1024]{2,1,0:T(4,128)} %param.18) | copy-start | bytes 49156
  10.9 3.6 %copy-start.7 = (bf16[1024,256]{1,0:T(8,128)(2,1)S(1)}, bf16[1024,256]{1,0:T(8,128)(2,1)}, u32[]{:S(2)}) copy-start(bf16[1024,256]{1,0:T(8,128)(2,1)} %param.11) | copy-start | bytes 1572868
  10.9 3.6 %copy-start.10 = (bf16[256,256]{1,0:T(8,128)(2,1)S(1)}, bf16[256,256]{1,0:T(8,128)(2,1)}, u32[]{:S(2)}) copy-start(bf16[256,256]{1,0:T(8,128)(2,1)} %param.12) | copy-start | bytes 393220
  10.9 3.9 %copy-start.17 = (s32[1,4,1024]{2,1,0:T(4,128)S(1)}, s32[1,4,1024]{2,1,0:T(4,128)}, u32[]{:S(2)}) copy-start(s32[1,4,1024]{2,1,0:T(4,128)} %param.17) | copy-start | bytes 49156
  19.7 2.8 %copy-start.4 = (bf16[4,1024,256]{2,1,0:T(8,128)(2,1)}, bf16[4,1024,256]{2,1,0:T(8,128)(2,1)S(1)}, u32[]{:S(2)}) copy-start(bf16[4,1024,256]{2,1,0:T(8,128)(2,1)S(1)} %fusion.20) | copy-start | bytes 6291460
  19.7 2.8 %copy-start.3 = (bf16[4,256,256]{2,1,0:T(8,128)(2,1)S(1)}, bf16[4,256,256]{2,1,0:T(8,128)(2,1)}, u32[]{:S(2)}) copy-start(bf16[4,256,256]{2,1,0:T(8,128)(2,1)} %param.13) | copy-start | bytes 1572868
  24.6 1.8 %copy-start.9 = (f32[1024,256]{1,0:T(8,128)}, f32[1024,256]{1,0:T(8,128)S(1)}, u32[]{:S(2)}) copy-start(f32[1024,256]{1,0:T(8,128)S(1)} %fusion.24) | copy-start | bytes 3145732
  26.4 7.3 %copy-start.12 = (bf16[1024]{0:T(1024)(128)(2,1)S(1)}, bf16[1024]{0:T(1024)(128)(2,1)}, u32[]{:S(2)}) copy-start(bf16[1024]{0:T(1024)(128)(2,1)} %param.15) | copy-start | bytes 6148
  27.6 36.0 %all-to-all-start = ((bf16[32,72,256]{2,1,0:T(8,128)(2,1)}), bf16[32,72,256]{2,1,0:T(8,128)(2,1)S(1)}, u32[]{:S(2)}, u32[]{:S(2)}) async-start(bf16[32,72,256]{2,1,0:T(8,128)(2,1)} %pad_maximum_fusion), calls=%async_computation | async-start | bytes 2359296 | tf_op jit(solution)/shard_map/all_to_all | solution.py:150
  64.3 0.7 copy-start.14
  65.0 0.6 copy-start.13
  68.6 33.0 %all-to-all-start.1 = ((bf16[32,72,256]{2,1,0:T(8,128)(2,1)}), bf16[32,72,256]{2,1,0:T(8,128)(2,1)S(1)}, u32[]{:S(2)}, u32[]{:S(2)}) async-start(bf16[32,72,256]{2,1,0:T(8,128)(2,1)} %maximum_maximum_fusion), calls=%async_computation.1 | async-start | bytes 2359296 | tf_op jit(solution)/shard_map/all_to_all | solution.py:185
  101.6 3.4 %copy-start.1 = (bf16[32,72,256]{2,1,0:T(8,128)(2,1)}, bf16[32,72,256]{2,1,0:T(8,128)(2,1)S(1)}, u32[]{:S(2)}) copy-start(bf16[32,72,256]{2,1,0:T(8,128)(2,1)S(1)} %all-to-all-done.1) | copy-start | bytes 3538948
  101.7 3.7 %copy-start.16 = (s32[1,4,1024]{2,1,0:T(4,128)S(1)}, s32[1,4,1024]{2,1,0:T(4,128)}, u32[]{:S(2)}) copy-start(s32[1,4,1024]{2,1,0:T(4,128)} %param.18) | copy-start | bytes 49156
  105.1 3.7 %copy-start.8 = (bf16[1024,256]{1,0:T(8,128)(2,1)}, bf16[1024,256]{1,0:T(8,128)(2,1)S(1)}, u32[]{:S(2)}) copy-start(bf16[1024,256]{1,0:T(8,128)(2,1)S(1)} %fusion.26) | copy-start | bytes 1572868
  105.4 3.3 %copy-start.5 = (bf16[4,1024,256]{2,1,0:T(8,128)(2,1)S(1)}, bf16[4,1024,256]{2,1,0:T(8,128)(2,1)}, u32[]{:S(2)}) copy-start(bf16[4,1024,256]{2,1,0:T(8,128)(2,1)} %copy-done.4) | copy-start | bytes 6291460
  108.8 1.4 copy-start.6
  108.8 2.0 %copy-start.2 = (f32[1024,256]{1,0:T(8,128)S(1)}, f32[1024,256]{1,0:T(8,128)}, u32[]{:S(2)}) copy-start(f32[1024,256]{1,0:T(8,128)} %fusion.68) | copy-start | bytes 3145732
  111.9 2.8 %collective-permute-start.4 = (bf16[1152,256]{1,0:T(8,128)(2,1)}, bf16[1152,256]{1,0:T(8,128)(2,1)}, u32[]{:S(2)}, u32[]{:S(2)}) collective-permute-start(bf16[1152,256]{1,0:T(8,128)(2,1)} %fusion.41), channel_id=1, source_target_pairs={{0,1},{1,0},{2,3},{3,2},{4,5},{5,4},{6,7},{7,6},{8,9},{9,8},{10,11... | collective-permute-start | bytes 1769480 | tf_op jit(solution)/shard_map/ppermute | solution.py:65
  116.7 25.7 %copy-start.18 = (s32[1,4,1024]{2,1,0:T(4,128)S(1)}, s32[1,4,1024]{2,1,0:T(4,128)}, u32[]{:S(2)}) copy-start(s32[1,4,1024]{2,1,0:T(4,128)} %param.17) | copy-start | bytes 49156
  116.7 20.7 %all-to-all-start.2 = ((bf16[16,72,256]{2,1,0:T(8,128)(2,1)}), bf16[16,72,256]{2,1,0:T(8,128)(2,1)S(1)}, u32[]{:S(2)}, u32[]{:S(2)}) async-start(bf16[16,72,256]{2,1,0:T(8,128)(2,1)} %bitcast.23), calls=%async_computation.2 | async-start | bytes 1179648 | tf_op jit(solution)/shard_map/all_to_all | solution.py:66
  138.5 20.4 %all-to-all-start.3 = ((bf16[16,72,256]{2,1,0:T(8,128)(2,1)}), bf16[16,72,256]{2,1,0:T(8,128)(2,1)S(1)}, u32[]{:S(2)}, u32[]{:S(2)}) async-start(bf16[16,72,256]{2,1,0:T(8,128)(2,1)} %broadcast_in_dim.10), calls=%async_computation.3 | async-start | bytes 1179648 | tf_op jit(solution)/shard_map/all_to_all | solution.py:73
  151.4 12.4 %copy-start.19 = (s32[1,512]{1,0:T(1,128)S(1)}, s32[1,512]{1,0:T(1,128)}, u32[]{:S(2)}) copy-start(s32[1,512]{1,0:T(1,128)} %param.16) | copy-start | bytes 6148
  151.4 12.4 %collective-permute-start.2 = (bf16[256,256]{1,0:T(8,128)(2,1)S(1)}, bf16[256,256]{1,0:T(8,128)(2,1)S(1)}, u32[]{:S(2)}, u32[]{:S(2)}) collective-permute-start(bf16[256,256]{1,0:T(8,128)(2,1)S(1)} %get-tuple-element.22), channel_id=1, source_target_pairs={{0,1},{1,2},{2,3},{3,4},{4,5},{5,6},{6,7},{8,9},{9,10},{10,11},{11... | collective-permute-start | bytes 393224 | tf_op jit(solution)/shard_map/ppermute | solution.py:27
  156.0 7.8 %collective-permute-start.3 = (bf16[256,256]{1,0:T(8,128)(2,1)S(1)}, bf16[256,256]{1,0:T(8,128)(2,1)S(1)}, u32[]{:S(2)}, u32[]{:S(2)}) collective-permute-start(bf16[256,256]{1,0:T(8,128)(2,1)S(1)} %get-tuple-element.23), channel_id=1, source_target_pairs={{1,0},{2,1},{3,2},{4,3},{5,4},{6,5},{7,6},{9,8},{10,9},{11,10},{12... | collective-permute-start | bytes 393224 | tf_op jit(solution)/shard_map/ppermute | solution.py:30
  159.0 6.1 %collective-permute-start.5 = (bf16[1152,256]{1,0:T(8,128)(2,1)S(1)}, bf16[1152,256]{1,0:T(8,128)(2,1)S(1)}, u32[]{:S(2)}, u32[]{:S(2)}) collective-permute-start(bf16[1152,256]{1,0:T(8,128)(2,1)S(1)} %bitcast.90), channel_id=1, source_target_pairs={{0,1},{1,0},{2,3},{3,2},{4,5},{5,4},{6,7},{7,6},{8,9},{9,8},{10,11... | collective-permute-start | bytes 1769480 | tf_op jit(solution)/shard_map/ppermute | solution.py:76

commit v11 on v8

--- a/solution.py
+++ b/solution.py
@@ -132,10 +132,13 @@
     slot_rank = jnp.sum(before * owner_hot.astype(F32), axis=1).astype(jnp.int32)
     pin_slot = owner_ids * capacity + slot_rank
     slot_hot = one_hot(pin_slot, owners * capacity)
-    net_code = (pin_net + 1).astype(BF16)[:, None]
+    net_code = jnp.pad((pin_net + 1).astype(BF16)[:, None], ((0, 0), (0, 127)))
     slot_rows = one_hot_rows(pin_slot, owners * capacity)
-    slot_nets = jnp.dot(slot_rows, net_code, preferred_element_type=F32)[:, 0] - 1.0
-    outbound = jnp.dot(slot_rows, hidden, preferred_element_type=F32).astype(BF16)
+    routed = jnp.dot(
+        slot_rows, jnp.concatenate([hidden, net_code], 1), preferred_element_type=F32
+    )
+    slot_nets = routed[:, feat_width] - 1.0
+    outbound = routed[:, :feat_width].astype(BF16)
     id_rows = -(-capacity // (8 * feat_width)) * 8
     id_block = jnp.pad(
         slot_nets.reshape(owners, capacity), ((0, 0), (0, id_rows * feat_width - capacity))

time: 169 us -> 170 us (level)
  transfers between devices with their start and end apart: 10 -> 10, of which waited for: 5 -> 6; matrix products, arithmetic and copies ran while one was open for 12% -> 10% of each run, Pallas kernels for 0% -> 0%
where the time goes in v11:
time: 170 us; the launch traced here: 169 us
  waiting for transfers between devices  78.6 us (46%)
  matrix products  39.7 us (23%)
  starting transfers between devices  32.4 us (19%)
  other arithmetic  11 us (6%)
  local copies, waits for them, and re-layouts  5.9 us (3%)
    all_to_all x1, waiting for transfers between devices, on_device(): lax.all_to_all(packet, ALL, split_axis=0, concat_axis=0, tiled=True)  29.7 us
    all_to_all x1, waiting for transfers between devices, on_device(): lax.all_to_all(back_packet, ALL, split_axis=0, concat_axis=0, tiled=True)  28.6 us
    all_to_all x1, waiting for transfers between devices, all_sum(): lax.all_to_all(half.astype(BF16).reshape(chips, -1, width), CHIP, split_a...  17 us
    ppermute x2, starting transfers between devices, extended(): lax.ppermute(lax.slice_in_dim(block, block.shape[dim] - width, None, axis...  9.17 us
    dot_general x2, matrix products, split_dot(): jnp.einsum(spec, left, right.astype(F32), precision=lax.Precision.HIGHEST...  6.47 us
    all_to_all x1, starting transfers between devices, on_device(): lax.all_to_all(packet, ALL, split_axis=0, concat_axis=0, tiled=True)  6.15 us
    dot_general x1, matrix products, on_device(): jnp.einsum('ter,rd->ted', src_hot, node_table, preferred_element_type=F32)  4.85 us
    dot_general x1, matrix products, on_device(): jnp.einsum('tre,ted->trd', one_hot_rows(sources, table_rows), edge_rows,...  4.61 us
  transfers between devices with their start and end apart: 10, of which 6 were waited for; matrix products, arithmetic and copies ran while one was open for 10% of the time, Pallas kernels for 0%

profile of v11, /device:TPU:1, one launch (start us, length us, event | category | flops | bytes accessed | tf_op | source)
XLA Modules:
  0.0 168.9 jit_solution(14918834141011039332)
XLA Ops:
  0.6 0.0 copy-start
  0.7 1.7 fusion.26
  2.4 4.6 %collective-permute-start = (bf16[256,256]{1,0:T(8,128)(2,1)S(1)}, bf16[256,256]{1,0:T(8,128)(2,1)S(1)}, u32[]{:S(2)}, u32[]{:S(2)}) collective-permute-start(bf16[256,256]{1,0:T(8,128)(2,1)S(1)} %get-tuple-element.24), channel_id=1, source_target_pairs={{0,1},{1,2},{2,3},{3,4},{4,5},{5,6},{6,7},{8,9},{9,10},{10,11},{11... | collective-permute-start | bytes 393224 | tf_op jit(solution)/shard_map/ppermute | solution.py:27
  7.0 1.9 %collective-permute-start.1 = (bf16[256,256]{1,0:T(8,128)(2,1)S(1)}, bf16[256,256]{1,0:T(8,128)(2,1)S(1)}, u32[]{:S(2)}, u32[]{:S(2)}) collective-permute-start(bf16[256,256]{1,0:T(8,128)(2,1)S(1)} %get-tuple-element.25), channel_id=1, source_target_pairs={{1,0},{2,1},{3,2},{4,3},{5,4},{6,5},{7,6},{9,8},{10,9},{11,10},{12... | collective-permute-start | bytes 393224 | tf_op jit(solution)/shard_map/ppermute | solution.py:30
  8.9 0.7 add_convert_fusion
  9.6 1.3 fusion.30
  11.0 1.9 %convert_reduce_fusion = f32[1024]{0:T(1024)S(1)} fusion(s32[4,1024]{1,0:T(4,128)S(1)} %bitcast.110), kind=kLoop, calls=%fused_computation.4 | loop fusion | flops 16776192 | bytes 20480 | tf_op jit(solution)/shard_map/reduce_sum | solution.py:114
  12.9 0.3 fusion.71
  13.3 4.8 %fusion.17 = bf16[4,1024,256]{2,1,0:T(8,128)(2,1)S(1)} fusion(s32[4,1024]{1,0:T(4,128)S(1)} %bitcast.113, bf16[256,256]{1,0:T(8,128)(2,1)S(1)} %collective-permute-done.1, bf16[256,256]{1,0:T(8,128)(2,1)S(1)} %collective-permute-done, bf16[1024,256]{1,0:T(8,128)(2,1)S(1)} %copy-done.7), kind=kOutput, calls=%fused_computation.33 | convolution fusion | flops 3230924800 | bytes 2899968 | tf_op jit(solution)/shard_map/ter,rd->ted/dot_general | solution.py:107
  18.2 2.8 %fusion.4 = f32[4,1024,256]{2,1,0:T(8,128)S(1)} fusion(bf16[4,1024,256]{2,1,0:T(8,128)(2,1)S(1)} %fusion.17, s32[4,1024]{1,0:T(4,128)S(1)} %bitcast.111), kind=kOutput, calls=%fused_computation.9 | convolution fusion | flops 2151677952 | bytes 6307840 | tf_op jit(solution)/shard_map/tpe,ted->tpd/dot_general | solution.py:110
  21.0 3.4 %multiply_convert_fusion.3 = (bf16[1024,256]{0,1:T(8,128)(2,1)S(1)}, f32[1024,256]{0,1:T(8,128)}) fusion(f32[1024,256]{0,1:T(8,128)S(1)} %fusion.71, f32[1024]{0:T(1024)S(1)} %add_divide_fusion.2, f32[4,1024,256]{2,1,0:T(8,128)S(1)} %fusion.4, bf16[4,256,256]{2,1,0:T(8,128)(2,1)S(1)} %copy-done), kind=kOutput, calls=%fused_computation.67 | convolution fusion | flops 3223060480 | bytes 7344128 | tf_op jit(solution)/shard_map/tpk,tkd->pd/dot_general | solution.py:49
  24.4 2.4 %fusion.9 = f32[2048,384]{1,0:T(8,128)S(1)} fusion(s32[1024]{0:T(1024)S(1)} %multiply_add_fusion.1, bf16[1024,1]{0,1:T(2,128)(2,1)S(1)} %broadcast_in_dim.10, bf16[1024,256]{0,1:T(8,128)(2,1)S(1)} %get-tuple-element.26), kind=kOutput, calls=%fused_computation.16 | convolution fusion | flops 1615069184 | bytes 3676160 | tf_op jit(solution)/shard_map/dot_general | solution.py:137
  26.7 0.3 fusion.50
  27.1 0.1 slice.85
  27.2 0.1 sub.16
  27.3 1.1 pad_maximum_fusion.1
  28.4 6.1 %all-to-all-start = ((bf16[32,72,256]{2,1,0:T(8,128)(2,1)}), bf16[32,72,256]{2,1,0:T(8,128)(2,1)S(1)}, u32[]{:S(2)}, u32[]{:S(2)}) async-start(bf16[32,72,256]{2,1,0:T(8,128)(2,1)} %pad_maximum_fusion.1), calls=%async_computation | async-start | bytes 2359296 | tf_op jit(solution)/shard_map/all_to_all | solution.py:153
  34.7 0.1 pad.20.clone
  34.7 29.7 %all-to-all-done = bf16[32,72,256]{2,1,0:T(8,128)(2,1)S(1)} async-done(((bf16[32,72,256]{2,1,0:T(8,128)(2,1)}), bf16[32,72,256]{2,1,0:T(8,128)(2,1)S(1)}, u32[]{:S(2)}, u32[]{:S(2)}) %all-to-all-start) | async-done | bytes 1179680 | tf_op jit(solution)/shard_map/all_to_all | solution.py:153
  64.5 0.1 eq.181
  64.5 0.1 slice.71
  64.7 0.5 fusion.28
  65.2 1.3 multiply_convert_fusion.2
  66.5 0.2 fusion.72
  66.8 0.3 fusion.73
  67.1 1.6 multiply_convert_fusion.1
  68.7 1.0 convolution_convert_fusion
  69.8 1.5 maximum_maximum_fusion
  71.3 3.1 %all-to-all-start.1 = ((bf16[32,72,256]{2,1,0:T(8,128)(2,1)}), bf16[32,72,256]{2,1,0:T(8,128)(2,1)S(1)}, u32[]{:S(2)}, u32[]{:S(2)}) async-start(bf16[32,72,256]{2,1,0:T(8,128)(2,1)} %maximum_maximum_fusion), calls=%async_computation.1 | async-start | bytes 2359296 | tf_op jit(solution)/shard_map/all_to_all | solution.py:188
  74.5 1.3 fusion.75
  75.8 28.6 %all-to-all-done.1 = bf16[32,72,256]{2,1,0:T(8,128)(2,1)S(1)} async-done(((bf16[32,72,256]{2,1,0:T(8,128)(2,1)}), bf16[32,72,256]{2,1,0:T(8,128)(2,1)S(1)}, u32[]{:S(2)}, u32[]{:S(2)}) %all-to-all-start.1) | async-done | bytes 1179680 | tf_op jit(solution)/shard_map/all_to_all | solution.py:188
  104.3 0.1 slice.72
  104.5 3.8 %fusion.24 = bf16[1024,256]{0,1:T(8,128)(2,1)S(1)} fusion(bf16[2048,256]{1,0:T(8,128)(2,1)S(1)} %bitcast.92, s32[1024]{0:T(1024)S(1)} %bitcast.109, f32[1024,256]{0,1:T(8,128)} %get-tuple-element.27), kind=kOutput, calls=%fused_computation.43 | convolution fusion | flops 1078198272 | bytes 2625536 | tf_op jit(solution)/shard_map/dot_general | solution.py:198
  108.3 0.4 convolution_bitcast_fusion.2
  108.7 3.6 %fusion.18 = bf16[4,1024,256]{2,1,0:T(8,128)(2,1)S(1)} fusion(s32[4,1024]{1,0:T(4,128)S(1)} %bitcast.112, bf16[1024,256]{0,1:T(8,128)(2,1)S(1)} %fusion.24, f32[1024]{0:T(1024)S(1)} %add_divide_fusion.2), kind=kOutput, calls=%fused_computation.34 | convolution fusion | flops 2153512960 | bytes 2641920 | tf_op jit(solution)/shard_map/tep,pd->ted/dot_general | solution.py:202
  112.3 0.9 fusion.74
  113.3 0.4 copy-done.5
  113.7 0.6 copy-done.2
  114.3 0.2 pad_maximum_fusion
  114.5 0.9 fusion.45
  115.4 0.8 collective-permute-start.4
  116.2 1.8 %collective-permute-done.4 = bf16[1152,256]{1,0:T(8,128)(2,1)S(1)} collective-permute-done((bf16[1152,256]{1,0:T(8,128)(2,1)}, bf16[1152,256]{1,0:T(8,128)(2,1)S(1)}, u32[]{:S(2)}, u32[]{:S(2)}) %collective-permute-start.4) | collective-permute-done | bytes 589856 | tf_op jit(solution)/shard_map/ppermute | solution.py:65
  118.1 0.9 fusion.27
  119.0 3.7 %all-to-all-start.2 = ((bf16[16,72,256]{2,1,0:T(8,128)(2,1)}), bf16[16,72,256]{2,1,0:T(8,128)(2,1)S(1)}, u32[]{:S(2)}, u32[]{:S(2)}) async-start(bf16[16,72,256]{2,1,0:T(8,128)(2,1)} %bitcast.22), calls=%async_computation.2 | async-start | bytes 1179648 | tf_op jit(solution)/shard_map/all_to_all | solution.py:66
  122.7 17.0 %all-to-all-done.2 = bf16[16,72,256]{2,1,0:T(8,128)(2,1)S(1)} async-done(((bf16[16,72,256]{2,1,0:T(8,128)(2,1)}), bf16[16,72,256]{2,1,0:T(8,128)(2,1)S(1)}, u32[]{:S(2)}, u32[]{:S(2)}) %all-to-all-start.2) | async-done | bytes 589856 | tf_op jit(solution)/shard_map/all_to_all | solution.py:66
  139.7 0.2 fusion.46
  140.0 0.9 broadcast_in_dim.13
  140.8 3.8 %all-to-all-start.3 = ((bf16[16,72,256]{2,1,0:T(8,128)(2,1)}), bf16[16,72,256]{2,1,0:T(8,128)(2,1)S(1)}, u32[]{:S(2)}, u32[]{:S(2)}) async-start(bf16[16,72,256]{2,1,0:T(8,128)(2,1)} %broadcast_in_dim.13), calls=%async_computation.3 | async-start | bytes 1179648 | tf_op jit(solution)/shard_map/all_to_all | solution.py:73
  144.7 4.6 %fusion.1 = f32[4,1536,256]{2,1,0:T(8,128)S(1)} fusion(bf16[4,1024,256]{2,1,0:T(8,128)(2,1)S(1)} %copy-done.6, s32[4,1024]{1,0:T(4,128)S(1)} %bitcast.114), kind=kOutput, calls=%fused_computation.3 | convolution fusion | flops 3227516928 | bytes 8404992 | tf_op jit(solution)/shard_map/tre,ted->trd/dot_general | solution.py:206
  149.3 0.9 slice.76
  150.3 3.1 %fusion.70 = (bf16[1536,256]{1,0:T(8,128)(2,1)S(1)}, f32[1536,256]{1,0:T(8,128)S(1)}) fusion(f32[4,1536,256]{2,1,0:T(8,128)S(1)} %fusion.1, bf16[4,256,256]{2,1,0:T(8,128)(2,1)S(1)} %copy-done), kind=kOutput, calls=%fused_computation.115 | convolution fusion | flops 4832231424 | bytes 9175040 | tf_op jit(solution)/shard_map/trd,tkd->rk/dot_general | solution.py:49
  153.4 4.6 %collective-permute-start.2 = (bf16[256,256]{1,0:T(8,128)(2,1)S(1)}, bf16[256,256]{1,0:T(8,128)(2,1)S(1)}, u32[]{:S(2)}, u32[]{:S(2)}) collective-permute-start(bf16[256,256]{1,0:T(8,128)(2,1)S(1)} %get-tuple-element.22), channel_id=1, source_target_pairs={{0,1},{1,2},{2,3},{3,4},{4,5},{5,6},{6,7},{8,9},{9,10},{10,11},{11... | collective-permute-start | bytes 393224 | tf_op jit(solution)/shard_map/ppermute | solution.py:27
  158.0 1.9 %collective-permute-start.3 = (bf16[256,256]{1,0:T(8,128)(2,1)S(1)}, bf16[256,256]{1,0:T(8,128)(2,1)S(1)}, u32[]{:S(2)}, u32[]{:S(2)}) collective-permute-start(bf16[256,256]{1,0:T(8,128)(2,1)S(1)} %get-tuple-element.23), channel_id=1, source_target_pairs={{1,0},{2,1},{3,2},{4,3},{5,4},{6,5},{7,6},{9,8},{10,9},{11,10},{12... | collective-permute-start | bytes 393224 | tf_op jit(solution)/shard_map/ppermute | solution.py:30
  159.9 0.4 convolution_add_fusion
  160.3 1.0 all-to-all-done.3
  161.3 1.8 %collective-permute-start.5 = (bf16[1152,256]{1,0:T(8,128)(2,1)S(1)}, bf16[1152,256]{1,0:T(8,128)(2,1)S(1)}, u32[]{:S(2)}, u32[]{:S(2)}) collective-permute-start(bf16[1152,256]{1,0:T(8,128)(2,1)S(1)} %bitcast.89), channel_id=1, source_target_pairs={{0,1},{1,0},{2,3},{3,2},{4,5},{5,4},{6,7},{7,6},{8,9},{9,8},{10,11... | collective-permute-start | bytes 1769480 | tf_op jit(solution)/shard_map/ppermute | solution.py:76
  163.0 0.1 fusion.58
  163.1 0.6 broadcast_multiply_fusion
  163.7 0.5 collective-permute-done.3
  164.3 1.3 fusion.25
  165.6 0.1 broadcast_select_fusion.1
  165.7 0.7 convert_multiply_fusion.1
  166.4 1.2 multiply_bitcast_fusion
  167.6 1.3 copy.26
  (62 shorter events, 0.4 us)
Async XLA Ops:
  0.6 20.3 %copy-start = (bf16[4,256,256]{2,1,0:T(8,128)(2,1)S(1)}, bf16[4,256,256]{2,1,0:T(8,128)(2,1)}, u32[]{:S(2)}) copy-start(bf16[4,256,256]{2,1,0:T(8,128)(2,1)} %param.13) | copy-start | bytes 1572868
  0.6 12.3 %copy-start.7 = (bf16[1024,256]{1,0:T(8,128)(2,1)S(1)}, bf16[1024,256]{1,0:T(8,128)(2,1)}, u32[]{:S(2)}) copy-start(bf16[1024,256]{1,0:T(8,128)(2,1)} %param.11) | copy-start | bytes 1572868
  0.7 10.3 %copy-start.12 = (s32[1024,1]{0,1:T(1,128)S(1)}, s32[1024,1]{0,1:T(1,128)}, u32[]{:S(2)}) copy-start(s32[1024,1]{0,1:T(1,128)} %param.19) | copy-start | bytes 12292
  0.7 10.3 %copy-start.17 = (s32[1,4,1024]{2,1,0:T(4,128)S(1)}, s32[1,4,1024]{2,1,0:T(4,128)}, u32[]{:S(2)}) copy-start(s32[1,4,1024]{2,1,0:T(4,128)} %param.18) | copy-start | bytes 49156
  0.7 12.2 %copy-start.10 = (bf16[256,256]{1,0:T(8,128)(2,1)S(1)}, bf16[256,256]{1,0:T(8,128)(2,1)}, u32[]{:S(2)}) copy-start(bf16[256,256]{1,0:T(8,128)(2,1)} %param.12) | copy-start | bytes 393220
  0.7 12.6 %copy-start.18 = (s32[1,4,1024]{2,1,0:T(4,128)S(1)}, s32[1,4,1024]{2,1,0:T(4,128)}, u32[]{:S(2)}) copy-start(s32[1,4,1024]{2,1,0:T(4,128)} %param.17) | copy-start | bytes 49156
  2.4 10.9 %collective-permute-start = (bf16[256,256]{1,0:T(8,128)(2,1)S(1)}, bf16[256,256]{1,0:T(8,128)(2,1)S(1)}, u32[]{:S(2)}, u32[]{:S(2)}) collective-permute-start(bf16[256,256]{1,0:T(8,128)(2,1)S(1)} %get-tuple-element.24), channel_id=1, source_target_pairs={{0,1},{1,2},{2,3},{3,4},{4,5},{5,6},{6,7},{8,9},{9,10},{10,11},{11... | collective-permute-start | bytes 393224 | tf_op jit(solution)/shard_map/ppermute | solution.py:27
  7.0 6.3 %collective-permute-start.1 = (bf16[256,256]{1,0:T(8,128)(2,1)S(1)}, bf16[256,256]{1,0:T(8,128)(2,1)S(1)}, u32[]{:S(2)}, u32[]{:S(2)}) collective-permute-start(bf16[256,256]{1,0:T(8,128)(2,1)S(1)} %get-tuple-element.25), channel_id=1, source_target_pairs={{1,0},{2,1},{3,2},{4,3},{5,4},{6,5},{7,6},{9,8},{10,9},{11,10},{12... | collective-permute-start | bytes 393224 | tf_op jit(solution)/shard_map/ppermute | solution.py:30
  18.2 2.8 %copy-start.3 = (bf16[4,1024,256]{2,1,0:T(8,128)(2,1)}, bf16[4,1024,256]{2,1,0:T(8,128)(2,1)S(1)}, u32[]{:S(2)}) copy-start(bf16[4,1024,256]{2,1,0:T(8,128)(2,1)S(1)} %fusion.17) | copy-start | bytes 6291460
  27.3 7.3 %copy-start.13 = (bf16[1024]{0:T(1024)(128)(2,1)S(1)}, bf16[1024]{0:T(1024)(128)(2,1)}, u32[]{:S(2)}) copy-start(bf16[1024]{0:T(1024)(128)(2,1)} %param.15) | copy-start | bytes 6148
  28.4 36.0 %all-to-all-start = ((bf16[32,72,256]{2,1,0:T(8,128)(2,1)}), bf16[32,72,256]{2,1,0:T(8,128)(2,1)S(1)}, u32[]{:S(2)}, u32[]{:S(2)}) async-start(bf16[32,72,256]{2,1,0:T(8,128)(2,1)} %pad_maximum_fusion.1), calls=%async_computation | async-start | bytes 2359296 | tf_op jit(solution)/shard_map/all_to_all | solution.py:153
  34.6 30.5 %copy-start.16 = (bf16[256,1024]{1,0:T(8,128)(2,1)S(1)}, bf16[256,1024]{1,0:T(8,128)(2,1)}, u32[]{:S(2)}) copy-start(bf16[256,1024]{1,0:T(8,128)(2,1)} %param.14) | copy-start | bytes 1572868
  65.1 1.6 copy-start.15
  66.7 4.6 %copy-start.14 = (f32[1,256]{1,0:T(1,128)}, f32[1,256]{1,0:T(1,128)S(1)}, u32[]{:S(2)}) copy-start(f32[1,256]{1,0:T(1,128)S(1)} %fusion.72) | copy-start | bytes 3076
  71.3 33.0 %all-to-all-start.1 = ((bf16[32,72,256]{2,1,0:T(8,128)(2,1)}), bf16[32,72,256]{2,1,0:T(8,128)(2,1)S(1)}, u32[]{:S(2)}, u32[]{:S(2)}) async-start(bf16[32,72,256]{2,1,0:T(8,128)(2,1)} %maximum_maximum_fusion), calls=%async_computation.1 | async-start | bytes 2359296 | tf_op jit(solution)/shard_map/all_to_all | solution.py:188
  104.3 3.9 %copy-start.1 = (bf16[32,72,256]{2,1,0:T(8,128)(2,1)}, bf16[32,72,256]{2,1,0:T(8,128)(2,1)S(1)}, u32[]{:S(2)}) copy-start(bf16[32,72,256]{2,1,0:T(8,128)(2,1)S(1)} %all-to-all-done.1) | copy-start | bytes 3538948
  108.3 4.0 %copy-start.8 = (bf16[1024,256]{0,1:T(8,128)(2,1)}, bf16[1024,256]{0,1:T(8,128)(2,1)S(1)}, u32[]{:S(2)}) copy-start(bf16[1024,256]{0,1:T(8,128)(2,1)S(1)} %fusion.24) | copy-start | bytes 1572868
  108.7 3.7 %copy-start.4 = (bf16[4,1024,256]{2,1,0:T(8,128)(2,1)S(1)}, bf16[4,1024,256]{2,1,0:T(8,128)(2,1)}, u32[]{:S(2)}) copy-start(bf16[4,1024,256]{2,1,0:T(8,128)(2,1)} %copy-done.3) | copy-start | bytes 6291460
  112.3 1.4 copy-start.5
  112.3 2.0 %copy-start.2 = (f32[1024,256]{1,0:T(8,128)S(1)}, f32[1024,256]{1,0:T(8,128)}, u32[]{:S(2)}) copy-start(f32[1024,256]{1,0:T(8,128)} %fusion.75) | copy-start | bytes 3145732
  115.4 2.7 %collective-permute-start.4 = (bf16[1152,256]{1,0:T(8,128)(2,1)}, bf16[1152,256]{1,0:T(8,128)(2,1)S(1)}, u32[]{:S(2)}, u32[]{:S(2)}) collective-permute-start(bf16[1152,256]{1,0:T(8,128)(2,1)} %fusion.45), channel_id=1, source_target_pairs={{0,1},{1,0},{2,3},{3,2},{4,5},{5,4},{6,7},{7,6},{8,9},{9,8},{10,11... | collective-permute-start | bytes 1769480 | tf_op jit(solution)/shard_map/ppermute | solution.py:65
  119.0 25.7 %copy-start.6 = (bf16[4,1024,256]{2,1,0:T(8,128)(2,1)S(1)}, bf16[4,1024,256]{2,1,0:T(8,128)(2,1)}, u32[]{:S(2)}) copy-start(bf16[4,1024,256]{2,1,0:T(8,128)(2,1)} %copy-done.5) | copy-start | bytes 6291460
  119.0 20.7 %all-to-all-start.2 = ((bf16[16,72,256]{2,1,0:T(8,128)(2,1)}), bf16[16,72,256]{2,1,0:T(8,128)(2,1)S(1)}, u32[]{:S(2)}, u32[]{:S(2)}) async-start(bf16[16,72,256]{2,1,0:T(8,128)(2,1)} %bitcast.22), calls=%async_computation.2 | async-start | bytes 1179648 | tf_op jit(solution)/shard_map/all_to_all | solution.py:66
  140.8 20.4 %all-to-all-start.3 = ((bf16[16,72,256]{2,1,0:T(8,128)(2,1)}), bf16[16,72,256]{2,1,0:T(8,128)(2,1)S(1)}, u32[]{:S(2)}, u32[]{:S(2)}) async-start(bf16[16,72,256]{2,1,0:T(8,128)(2,1)} %broadcast_in_dim.13), calls=%async_computation.3 | async-start | bytes 1179648 | tf_op jit(solution)/shard_map/all_to_all | solution.py:73
  150.2 9.7 %copy-start.9 = (bf16[1024,256]{0,1:T(8,128)(2,1)S(1)}, bf16[1024,256]{0,1:T(8,128)(2,1)}, u32[]{:S(2)}) copy-start(bf16[1024,256]{0,1:T(8,128)(2,1)} %copy-done.8) | copy-start | bytes 1572868
  150.3 9.7 %copy-start.11 = (bf16[256,256]{1,0:T(8,128)(2,1)S(1)}, bf16[256,256]{1,0:T(8,128)(2,1)}, u32[]{:S(2)}) copy-start(bf16[256,256]{1,0:T(8,128)(2,1)} %param.12) | copy-start | bytes 393220
  153.4 10.9 %copy-start.19 = (s32[1,512]{1,0:T(1,128)S(1)}, s32[1,512]{1,0:T(1,128)}, u32[]{:S(2)}) copy-start(s32[1,512]{1,0:T(1,128)} %param.16) | copy-start | bytes 6148
  153.4 10.3 %collective-permute-start.2 = (bf16[256,256]{1,0:T(8,128)(2,1)S(1)}, bf16[256,256]{1,0:T(8,128)(2,1)S(1)}, u32[]{:S(2)}, u32[]{:S(2)}) collective-permute-start(bf16[256,256]{1,0:T(8,128)(2,1)S(1)} %get-tuple-element.22), channel_id=1, source_target_pairs={{0,1},{1,2},{2,3},{3,4},{4,5},{5,6},{6,7},{8,9},{9,10},{10,11},{11... | collective-permute-start | bytes 393224 | tf_op jit(solution)/shard_map/ppermute | solution.py:27
  158.0 6.3 %collective-permute-start.3 = (bf16[256,256]{1,0:T(8,128)(2,1)S(1)}, bf16[256,256]{1,0:T(8,128)(2,1)S(1)}, u32[]{:S(2)}, u32[]{:S(2)}) collective-permute-start(bf16[256,256]{1,0:T(8,128)(2,1)S(1)} %get-tuple-element.23), channel_id=1, source_target_pairs={{1,0},{2,1},{3,2},{4,3},{5,4},{6,5},{7,6},{9,8},{10,9},{11,10},{12... | collective-permute-start | bytes 393224 | tf_op jit(solution)/shard_map/ppermute | solution.py:30
  161.3 4.3 %collective-permute-start.5 = (bf16[1152,256]{1,0:T(8,128)(2,1)S(1)}, bf16[1152,256]{1,0:T(8,128)(2,1)S(1)}, u32[]{:S(2)}, u32[]{:S(2)}) collective-permute-start(bf16[1152,256]{1,0:T(8,128)(2,1)S(1)} %bitcast.89), channel_id=1, source_target_pairs={{0,1},{1,0},{2,3},{3,2},{4,5},{5,4},{6,7},{7,6},{8,9},{9,8},{10,11... | collective-permute-start | bytes 1769480 | tf_op jit(solution)/shard_map/ppermute | solution.py:76

commit v12 on v8

--- a/solution.py
+++ b/solution.py
@@ -60,8 +60,8 @@
     rows = jnp.pad(rows, ((0, length - count), (0, 0))).reshape(cores, length // cores, width)
     core = lax.axis_index("core")
     swap = [(i, (i + 1) % cores) for i in range(cores)]
-    kept = lax.dynamic_index_in_dim(rows, core, 0, keepdims=False)
-    given = lax.dynamic_index_in_dim(rows, (core + 1) % cores, 0, keepdims=False)
+    kept = jnp.where(core == 0, rows[0], rows[1])
+    given = jnp.where(core == 0, rows[1], rows[0])
     half = kept + lax.ppermute(given.astype(BF16), "core", swap).astype(F32)
     mine = lax.all_to_all(
         half.astype(BF16).reshape(chips, -1, width), CHIP, split_axis=0, concat_axis=0, tiled=True

time: 169 us -> 161 us (0.953)
  blocking collectives: 0 us -> 19.5 us
  waiting for transfers between devices: 79 us -> 61.4 us
  starting transfers between devices: 32.1 us -> 29 us
  other arithmetic: 10.5 us -> 8.21 us
  matrix products: 38.7 us -> 36.5 us
    all_to_all x0 -> x1, blocking collectives: none -> 19.5 us  [all_sum(): lax.all_to_all(half.astype(BF16).reshape(chips, -1, width), CHIP, split_a...]
    all_to_all x1 -> x0, waiting for transfers between devices: 17 us -> none  [all_sum(): lax.all_to_all(half.astype(BF16).reshape(chips, -1, width), CHIP, split_a...]
    all_to_all x1 -> x0, starting transfers between devices: 3.72 us -> none  [all_sum(): lax.all_to_all(half.astype(BF16).reshape(chips, -1, width), CHIP, split_a...]
    convert_element_type x1, other arithmetic: 2.01 us -> 0.28 us  [all_sum(): half.astype(BF16).reshape(chips, -1, width)]
  transfers between devices with their start and end apart: 10 -> 9, of which waited for: 5 -> 5; matrix products, arithmetic and copies ran while one was open for 12% -> 11% of each run, Pallas kernels for 0% -> 0%
where the time goes in v12:
time: 161 us; the launch traced here: 160 us
  waiting for transfers between devices  61.4 us (38%)
  matrix products  36.5 us (23%)
  starting transfers between devices  29 us (18%)
  blocking collectives  19.5 us (12%)
  other arithmetic  8.21 us (5%)
  local copies, waits for them, and re-layouts  4.49 us (3%)
    all_to_all x1, waiting for transfers between devices, on_device(): lax.all_to_all(packet, ALL, split_axis=0, concat_axis=0, tiled=True)  29.7 us
    all_to_all x1, waiting for transfers between devices, on_device(): lax.all_to_all(back_packet, ALL, split_axis=0, concat_axis=0, tiled=True)  28.5 us
    all_to_all x1, blocking collectives, all_sum(): lax.all_to_all(half.astype(BF16).reshape(chips, -1, width), CHIP, split_a...  19.5 us
    ppermute x2, starting transfers between devices, extended(): lax.ppermute(lax.slice_in_dim(block, block.shape[dim] - width, None, axis...  9.39 us
    all_to_all x1, starting transfers between devices, on_device(): lax.all_to_all(packet, ALL, split_axis=0, concat_axis=0, tiled=True)  6.14 us
    dot_general x1, matrix products, on_device(): jnp.einsum('tre,ted->trd', one_hot_rows(sources, table_rows), edge_rows,...  5.87 us
    dot_general x2, matrix products, split_dot(): jnp.einsum(spec, left, right.astype(F32), precision=lax.Precision.HIGHEST...  5.18 us
    dot_general x1, matrix products, on_device(): jnp.einsum('ter,rd->ted', src_hot, node_table, preferred_element_type=F32)  4.85 us
  transfers between devices with their start and end apart: 9, of which 5 were waited for; matrix products, arithmetic and copies ran while one was open for 11% of the time, Pallas kernels for 0%

profile of v12, /device:TPU:1, one launch (start us, length us, event | category | flops | bytes accessed | tf_op | source)
XLA Modules:
  0.0 160.3 jit_solution(8105019486650355930)
XLA Ops:
  0.6 0.0 copy-start
  0.7 1.6 %fusion.28 = bf16[512,256]{1,0:T(8,128)(2,1)S(1)} fusion(bf16[1024,256]{1,0:T(8,128)(2,1)} %param.11, s32[512]{0:T(512)} %bitcast.111), kind=kOutput, calls=%fused_computation.44 | convolution fusion | flops 269090816 | bytes 788480 | tf_op jit(solution)/shard_map/dot_general | solution.py:99
  2.3 4.6 %collective-permute-start = (bf16[256,256]{1,0:T(8,128)(2,1)S(1)}, bf16[256,256]{1,0:T(8,128)(2,1)S(1)}, u32[]{:S(2)}, u32[]{:S(2)}) collective-permute-start(bf16[256,256]{1,0:T(8,128)(2,1)S(1)} %get-tuple-element.18), channel_id=1, source_target_pairs={{0,1},{1,2},{2,3},{3,4},{4,5},{5,6},{6,7},{8,9},{9,10},{10,11},{11... | collective-permute-start | bytes 393224 | tf_op jit(solution)/shard_map/ppermute | solution.py:27
  6.9 1.9 %collective-permute-start.1 = (bf16[256,256]{1,0:T(8,128)(2,1)S(1)}, bf16[256,256]{1,0:T(8,128)(2,1)S(1)}, u32[]{:S(2)}, u32[]{:S(2)}) collective-permute-start(bf16[256,256]{1,0:T(8,128)(2,1)S(1)} %get-tuple-element.19), channel_id=1, source_target_pairs={{1,0},{2,1},{3,2},{4,3},{5,4},{6,5},{7,6},{9,8},{10,9},{11,10},{12... | collective-permute-start | bytes 393224 | tf_op jit(solution)/shard_map/ppermute | solution.py:30
  8.9 0.5 fusion.31
  9.4 0.0 copy-start.18
  9.5 0.0 copy-start.12
  9.5 0.0 copy-start.20
  9.5 1.5 fusion.9
  11.0 0.1 sub.16
  11.1 1.9 %convert_reduce_fusion = f32[1024]{0:T(1024)S(1)} fusion(s32[4,1024]{1,0:T(4,128)S(1)} %bitcast.106), kind=kLoop, calls=%fused_computation.4 | loop fusion | flops 16776192 | bytes 20480 | tf_op jit(solution)/shard_map/reduce_sum | solution.py:114
  13.1 0.3 fusion.62
  13.4 4.8 %fusion.20 = bf16[4,1024,256]{2,1,0:T(8,128)(2,1)S(1)} fusion(s32[4,1024]{1,0:T(4,128)S(1)} %bitcast.109, bf16[256,256]{1,0:T(8,128)(2,1)S(1)} %collective-permute-done.1, bf16[256,256]{1,0:T(8,128)(2,1)S(1)} %collective-permute-done, bf16[1024,256]{1,0:T(8,128)(2,1)S(1)} %copy-done.5), kind=kOutput, calls=%fused_computation.34 | convolution fusion | flops 3230924800 | bytes 2899968 | tf_op jit(solution)/shard_map/ter,rd->ted/dot_general | solution.py:107
  18.3 0.0 copy-start.1
  18.3 2.8 %fusion.4 = f32[4,1024,256]{2,1,0:T(8,128)S(1)} fusion(bf16[4,1024,256]{2,1,0:T(8,128)(2,1)S(1)} %fusion.20, s32[4,1024]{1,0:T(4,128)S(1)} %bitcast.107), kind=kOutput, calls=%fused_computation.9 | convolution fusion | flops 2151677952 | bytes 6307840 | tf_op jit(solution)/shard_map/tpe,ted->tpd/dot_general | solution.py:110
  21.1 2.1 %fusion.24 = f32[1024,256]{1,0:T(8,128)S(1)} fusion(f32[1024,256]{1,0:T(8,128)S(1)} %fusion.62, f32[4,1024,256]{2,1,0:T(8,128)S(1)} %fusion.4, bf16[4,256,256]{2,1,0:T(8,128)(2,1)S(1)} %copy-done.1, f32[1024]{0:T(1024)S(1)} %add_divide_fusion.2), kind=kOutput, calls=%fused_computation.40 | convolution fusion | flops 3221749760 | bytes 6819840 | tf_op jit(solution)/shard_map/tpk,tkd->pd/dot_general | solution.py:49
  23.2 1.8 %fusion.16 = bf16[2048,256]{1,0:T(8,128)(2,1)S(1)} fusion(s32[1024]{0:T(1024)S(1)} %multiply_add_fusion.1, f32[1024,256]{1,0:T(8,128)S(1)} %fusion.24), kind=kOutput, calls=%fused_computation.25 | convolution fusion | flops 1077673984 | bytes 2101248 | tf_op jit(solution)/shard_map/dot_general | solution.py:138
  25.0 1.1 pad_maximum_fusion.2
  26.2 6.1 %all-to-all-start = ((bf16[32,72,256]{2,1,0:T(8,128)(2,1)}), bf16[32,72,256]{2,1,0:T(8,128)(2,1)S(1)}, u32[]{:S(2)}, u32[]{:S(2)}) async-start(bf16[32,72,256]{2,1,0:T(8,128)(2,1)} %pad_maximum_fusion.2), calls=%async_computation | async-start | bytes 2359296 | tf_op jit(solution)/shard_map/all_to_all | solution.py:150
  32.3 0.1 pad.16.clone
  32.4 29.7 %all-to-all-done = bf16[32,72,256]{2,1,0:T(8,128)(2,1)S(1)} async-done(((bf16[32,72,256]{2,1,0:T(8,128)(2,1)}), bf16[32,72,256]{2,1,0:T(8,128)(2,1)S(1)}, u32[]{:S(2)}, u32[]{:S(2)}) %all-to-all-start) | async-done | bytes 1179680 | tf_op jit(solution)/shard_map/all_to_all | solution.py:150
  62.2 0.1 eq.181
  62.2 0.1 slice.74
  62.4 0.4 fusion.29
  62.8 0.4 multiply_convert_fusion.2
  63.3 0.2 fusion.63
  63.6 0.3 fusion.64
  63.9 0.4 multiply_convert_fusion.1
  64.3 1.0 convolution_convert_fusion
  65.4 1.5 maximum_maximum_fusion
  66.9 3.1 %all-to-all-start.1 = ((bf16[32,72,256]{2,1,0:T(8,128)(2,1)}), bf16[32,72,256]{2,1,0:T(8,128)(2,1)S(1)}, u32[]{:S(2)}, u32[]{:S(2)}) async-start(bf16[32,72,256]{2,1,0:T(8,128)(2,1)} %maximum_maximum_fusion), calls=%async_computation.1 | async-start | bytes 2359296 | tf_op jit(solution)/shard_map/all_to_all | solution.py:185
  70.1 1.4 fusion.66
  71.5 28.5 %all-to-all-done.1 = bf16[32,72,256]{2,1,0:T(8,128)(2,1)S(1)} async-done(((bf16[32,72,256]{2,1,0:T(8,128)(2,1)}), bf16[32,72,256]{2,1,0:T(8,128)(2,1)S(1)}, u32[]{:S(2)}, u32[]{:S(2)}) %all-to-all-start.1) | async-done | bytes 1179680 | tf_op jit(solution)/shard_map/all_to_all | solution.py:185
  100.0 0.1 slice.75
  100.1 1.1 copy-done.11
  101.2 1.8 %fusion.26 = bf16[1024,256]{1,0:T(8,128)(2,1)S(1)} fusion(bf16[2048,256]{1,0:T(8,128)(2,1)S(1)} %bitcast.87, s32[1024]{0:T(1024)S(1)} %bitcast.105, f32[1024,256]{1,0:T(8,128)S(1)} %copy-done.11), kind=kOutput, calls=%fused_computation.42 | convolution fusion | flops 1078198272 | bytes 2625536 | tf_op jit(solution)/shard_map/dot_general | solution.py:195
  103.0 0.3 convolution_bitcast_fusion.2
  103.4 3.3 %fusion.21 = bf16[4,1024,256]{2,1,0:T(8,128)(2,1)S(1)} fusion(s32[4,1024]{1,0:T(4,128)S(1)} %bitcast.108, bf16[1024,256]{1,0:T(8,128)(2,1)S(1)} %fusion.26, f32[1024]{0:T(1024)S(1)} %add_divide_fusion.2), kind=kOutput, calls=%fused_computation.35 | convolution fusion | flops 2153512960 | bytes 2641920 | tf_op jit(solution)/shard_map/tep,pd->ted/dot_general | solution.py:199
  106.7 0.9 fusion.65
  107.6 0.4 copy-done.4
  108.0 0.2 select_convert_fusion
  108.3 0.9 collective-permute-start.4
  109.2 1.6 %collective-permute-done.4 = bf16[1152,256]{1,0:T(8,128)(2,1)S(1)} collective-permute-done((bf16[1152,256]{1,0:T(8,128)(2,1)S(1)}, bf16[1152,256]{1,0:T(8,128)(2,1)S(1)}, u32[]{:S(2)}, u32[]{:S(2)}) %collective-permute-start.4) | collective-permute-done | bytes 589856 | tf_op jit(solution)/shard_map/ppermute | solution.py:65
  110.8 0.3 add_convert_fusion
  111.1 19.5 %all_to_all.20 = bf16[16,72,256]{2,1,0:T(8,128)(2,1)S(1)} all-to-all(bf16[16,72,256]{2,1,0:T(8,128)(2,1)S(1)} %bitcast.83), channel_id=1, replica_groups=mesh['group'=4,'zdom'=4,'core'=2] {'group','zdom'}, dimensions={0} | all-to-all | bytes 1179648 | tf_op jit(solution)/shard_map/all_to_all | solution.py:66
  130.6 0.2 fusion.40
  130.9 0.9 broadcast_in_dim.10
  131.7 3.8 %all-to-all-start.3 = ((bf16[16,72,256]{2,1,0:T(8,128)(2,1)}), bf16[16,72,256]{2,1,0:T(8,128)(2,1)S(1)}, u32[]{:S(2)}, u32[]{:S(2)}) async-start(bf16[16,72,256]{2,1,0:T(8,128)(2,1)} %broadcast_in_dim.10), calls=%async_computation.3 | async-start | bytes 1179648 | tf_op jit(solution)/shard_map/all_to_all | solution.py:73
  135.5 5.9 %fusion.1 = f32[4,1536,256]{2,1,0:T(8,128)S(1)} fusion(bf16[4,1024,256]{2,1,0:T(8,128)(2,1)} %copy-done.4, s32[4,1024]{1,0:T(4,128)S(1)} %bitcast.110), kind=kOutput, calls=%fused_computation.3 | convolution fusion | flops 3227516928 | bytes 8404992 | tf_op jit(solution)/shard_map/tre,ted->trd/dot_general | solution.py:203
  141.5 0.0 copy-start.8
  141.5 3.1 %fusion.61 = (bf16[1536,256]{1,0:T(8,128)(2,1)S(1)}, f32[1536,256]{1,0:T(8,128)S(1)}) fusion(f32[4,1536,256]{2,1,0:T(8,128)S(1)} %fusion.1, bf16[4,256,256]{2,1,0:T(8,128)(2,1)S(1)} %copy-done.1), kind=kOutput, calls=%fused_computation.106 | convolution fusion | flops 4832231424 | bytes 9175040 | tf_op jit(solution)/shard_map/trd,tkd->rk/dot_general | solution.py:49
  144.6 4.8 %collective-permute-start.2 = (bf16[256,256]{1,0:T(8,128)(2,1)S(1)}, bf16[256,256]{1,0:T(8,128)(2,1)S(1)}, u32[]{:S(2)}, u32[]{:S(2)}) collective-permute-start(bf16[256,256]{1,0:T(8,128)(2,1)S(1)} %get-tuple-element.16), channel_id=1, source_target_pairs={{0,1},{1,2},{2,3},{3,4},{4,5},{5,6},{6,7},{8,9},{9,10},{10,11},{11... | collective-permute-start | bytes 393224 | tf_op jit(solution)/shard_map/ppermute | solution.py:27
  149.4 1.9 %collective-permute-start.3 = (bf16[256,256]{1,0:T(8,128)(2,1)S(1)}, bf16[256,256]{1,0:T(8,128)(2,1)S(1)}, u32[]{:S(2)}, u32[]{:S(2)}) collective-permute-start(bf16[256,256]{1,0:T(8,128)(2,1)S(1)} %get-tuple-element.17), channel_id=1, source_target_pairs={{1,0},{2,1},{3,2},{4,3},{5,4},{6,5},{7,6},{9,8},{10,9},{11,10},{12... | collective-permute-start | bytes 393224 | tf_op jit(solution)/shard_map/ppermute | solution.py:30
  151.4 0.3 convolution_add_fusion
  151.7 0.4 all-to-all-done.3
  152.1 1.8 %collective-permute-start.5 = (bf16[1152,256]{1,0:T(8,128)(2,1)S(1)}, bf16[1152,256]{1,0:T(8,128)(2,1)S(1)}, u32[]{:S(2)}, u32[]{:S(2)}) collective-permute-start(bf16[1152,256]{1,0:T(8,128)(2,1)S(1)} %bitcast.82), channel_id=1, source_target_pairs={{0,1},{1,0},{2,3},{3,2},{4,5},{5,4},{6,7},{7,6},{8,9},{9,8},{10,11... | collective-permute-start | bytes 1769480 | tf_op jit(solution)/shard_map/ppermute | solution.py:76
  153.8 0.1 fusion.51
  153.9 0.6 broadcast_multiply_fusion
  154.5 1.2 collective-permute-done.3
  155.7 1.3 fusion.27
  157.0 0.1 broadcast_select_fusion.1
  157.1 0.7 convert_multiply_fusion.1
  157.9 1.2 multiply_bitcast_fusion
  159.0 1.3 copy.18
  (66 shorter events, 0.4 us)
Async XLA Ops:
  0.6 62.2 %copy-start = (bf16[256,1024]{1,0:T(8,128)(2,1)S(1)}, bf16[256,1024]{1,0:T(8,128)(2,1)}, u32[]{:S(2)}) copy-start(bf16[256,1024]{1,0:T(8,128)(2,1)} %param.14) | copy-start | bytes 1572868
  0.6 8.2 %copy-start.16 = (s32[1024]{0:T(1024)S(1)}, s32[1024]{0:T(1024)}, u32[]{:S(2)}) copy-start(s32[1024]{0:T(1024)} %param.20) | copy-start | bytes 12292
  0.7 8.2 %copy-start.13 = (s32[1024,1]{0,1:T(1,128)S(1)}, s32[1024,1]{0,1:T(1,128)}, u32[]{:S(2)}) copy-start(s32[1024,1]{0,1:T(1,128)} %param.19) | copy-start | bytes 12292
  2.3 11.1 %collective-permute-start = (bf16[256,256]{1,0:T(8,128)(2,1)S(1)}, bf16[256,256]{1,0:T(8,128)(2,1)S(1)}, u32[]{:S(2)}, u32[]{:S(2)}) collective-permute-start(bf16[256,256]{1,0:T(8,128)(2,1)S(1)} %get-tuple-element.18), channel_id=1, source_target_pairs={{0,1},{1,2},{2,3},{3,4},{4,5},{5,6},{6,7},{8,9},{9,10},{10,11},{11... | collective-permute-start | bytes 393224 | tf_op jit(solution)/shard_map/ppermute | solution.py:27
  6.9 6.5 %collective-permute-start.1 = (bf16[256,256]{1,0:T(8,128)(2,1)S(1)}, bf16[256,256]{1,0:T(8,128)(2,1)S(1)}, u32[]{:S(2)}, u32[]{:S(2)}) collective-permute-start(bf16[256,256]{1,0:T(8,128)(2,1)S(1)} %get-tuple-element.19), channel_id=1, source_target_pairs={{1,0},{2,1},{3,2},{4,3},{5,4},{6,5},{7,6},{9,8},{10,9},{11,10},{12... | collective-permute-start | bytes 393224 | tf_op jit(solution)/shard_map/ppermute | solution.py:30
  9.4 1.6 %copy-start.18 = (s32[1,4,1024]{2,1,0:T(4,128)S(1)}, s32[1,4,1024]{2,1,0:T(4,128)}, u32[]{:S(2)}) copy-start(s32[1,4,1024]{2,1,0:T(4,128)} %param.18) | copy-start | bytes 49156
  9.4 3.6 %copy-start.5 = (bf16[1024,256]{1,0:T(8,128)(2,1)S(1)}, bf16[1024,256]{1,0:T(8,128)(2,1)}, u32[]{:S(2)}) copy-start(bf16[1024,256]{1,0:T(8,128)(2,1)} %param.11) | copy-start | bytes 1572868
  9.5 3.6 %copy-start.12 = (bf16[256,256]{1,0:T(8,128)(2,1)S(1)}, bf16[256,256]{1,0:T(8,128)(2,1)}, u32[]{:S(2)}) copy-start(bf16[256,256]{1,0:T(8,128)(2,1)} %param.12) | copy-start | bytes 393220
  9.5 3.9 %copy-start.20 = (s32[1,4,1024]{2,1,0:T(4,128)S(1)}, s32[1,4,1024]{2,1,0:T(4,128)}, u32[]{:S(2)}) copy-start(s32[1,4,1024]{2,1,0:T(4,128)} %param.17) | copy-start | bytes 49156
  18.3 2.8 %copy-start.2 = (bf16[4,1024,256]{2,1,0:T(8,128)(2,1)}, bf16[4,1024,256]{2,1,0:T(8,128)(2,1)S(1)}, u32[]{:S(2)}) copy-start(bf16[4,1024,256]{2,1,0:T(8,128)(2,1)S(1)} %fusion.20) | copy-start | bytes 6291460
  18.3 2.8 %copy-start.1 = (bf16[4,256,256]{2,1,0:T(8,128)(2,1)S(1)}, bf16[4,256,256]{2,1,0:T(8,128)(2,1)}, u32[]{:S(2)}) copy-start(bf16[4,256,256]{2,1,0:T(8,128)(2,1)} %param.13) | copy-start | bytes 1572868
  23.2 1.8 %copy-start.10 = (f32[1024,256]{1,0:T(8,128)}, f32[1024,256]{1,0:T(8,128)S(1)}, u32[]{:S(2)}) copy-start(f32[1024,256]{1,0:T(8,128)S(1)} %fusion.24) | copy-start | bytes 3145732
  25.0 7.3 %copy-start.14 = (bf16[1024]{0:T(1024)(128)(2,1)S(1)}, bf16[1024]{0:T(1024)(128)(2,1)}, u32[]{:S(2)}) copy-start(bf16[1024]{0:T(1024)(128)(2,1)} %param.15) | copy-start | bytes 6148
  26.2 36.0 %all-to-all-start = ((bf16[32,72,256]{2,1,0:T(8,128)(2,1)}), bf16[32,72,256]{2,1,0:T(8,128)(2,1)S(1)}, u32[]{:S(2)}, u32[]{:S(2)}) async-start(bf16[32,72,256]{2,1,0:T(8,128)(2,1)} %pad_maximum_fusion.2), calls=%async_computation | async-start | bytes 2359296 | tf_op jit(solution)/shard_map/all_to_all | solution.py:150
  62.8 0.7 copy-start.17
  63.5 1.8 %copy-start.15 = (f32[1,256]{1,0:T(1,128)}, f32[1,256]{1,0:T(1,128)S(1)}, u32[]{:S(2)}) copy-start(f32[1,256]{1,0:T(1,128)S(1)} %fusion.63) | copy-start | bytes 3076
  64.3 2.6 %copy-start.9 = (bf16[256,1024]{1,0:T(8,128)(2,1)}, bf16[256,1024]{1,0:T(8,128)(2,1)S(1)}, u32[]{:S(2)}) copy-start(bf16[256,1024]{1,0:T(8,128)(2,1)S(1)} %multiply_convert_fusion.1) | copy-start | bytes 1572868
  66.9 33.1 %all-to-all-start.1 = ((bf16[32,72,256]{2,1,0:T(8,128)(2,1)}), bf16[32,72,256]{2,1,0:T(8,128)(2,1)S(1)}, u32[]{:S(2)}, u32[]{:S(2)}) async-start(bf16[32,72,256]{2,1,0:T(8,128)(2,1)} %maximum_maximum_fusion), calls=%async_computation.1 | async-start | bytes 2359296 | tf_op jit(solution)/shard_map/all_to_all | solution.py:185
  100.0 1.2 copy-start.11
  101.2 1.8 %copy-start.6 = (bf16[1024,256]{1,0:T(8,128)(2,1)S(1)}, bf16[1024,256]{1,0:T(8,128)(2,1)}, u32[]{:S(2)}) copy-start(bf16[1024,256]{1,0:T(8,128)(2,1)} %param.11) | copy-start | bytes 1572868
  101.2 2.2 %copy-start.19 = (s32[1,4,1024]{2,1,0:T(4,128)S(1)}, s32[1,4,1024]{2,1,0:T(4,128)}, u32[]{:S(2)}) copy-start(s32[1,4,1024]{2,1,0:T(4,128)} %param.18) | copy-start | bytes 49156
  103.0 3.7 %copy-start.7 = (bf16[1024,256]{1,0:T(8,128)(2,1)}, bf16[1024,256]{1,0:T(8,128)(2,1)S(1)}, u32[]{:S(2)}) copy-start(bf16[1024,256]{1,0:T(8,128)(2,1)S(1)} %fusion.26) | copy-start | bytes 1572868
  103.4 3.3 %copy-start.3 = (bf16[4,1024,256]{2,1,0:T(8,128)(2,1)S(1)}, bf16[4,1024,256]{2,1,0:T(8,128)(2,1)}, u32[]{:S(2)}) copy-start(bf16[4,1024,256]{2,1,0:T(8,128)(2,1)} %copy-done.2) | copy-start | bytes 6291460
  106.7 1.3 copy-start.4
  108.3 2.5 %collective-permute-start.4 = (bf16[1152,256]{1,0:T(8,128)(2,1)S(1)}, bf16[1152,256]{1,0:T(8,128)(2,1)S(1)}, u32[]{:S(2)}, u32[]{:S(2)}) collective-permute-start(bf16[1152,256]{1,0:T(8,128)(2,1)S(1)} %select_convert_fusion), channel_id=1, source_target_pairs={{0,1},{1,0},{2,3},{3,2},{4,5},{5,4},{6,7},{7,6},{8,9},{9,8},{10,11... | collective-permute-start | bytes 1769480 | tf_op jit(solution)/shard_map/ppermute | solution.py:65
  111.1 24.4 %copy-start.21 = (s32[1,4,1024]{2,1,0:T(4,128)S(1)}, s32[1,4,1024]{2,1,0:T(4,128)}, u32[]{:S(2)}) copy-start(s32[1,4,1024]{2,1,0:T(4,128)} %param.17) | copy-start | bytes 49156
  131.7 20.3 %all-to-all-start.3 = ((bf16[16,72,256]{2,1,0:T(8,128)(2,1)}), bf16[16,72,256]{2,1,0:T(8,128)(2,1)S(1)}, u32[]{:S(2)}, u32[]{:S(2)}) async-start(bf16[16,72,256]{2,1,0:T(8,128)(2,1)} %broadcast_in_dim.10), calls=%async_computation.3 | async-start | bytes 1179648 | tf_op jit(solution)/shard_map/all_to_all | solution.py:73
  141.5 9.9 %copy-start.8 = (bf16[1024,256]{1,0:T(8,128)(2,1)S(1)}, bf16[1024,256]{1,0:T(8,128)(2,1)}, u32[]{:S(2)}) copy-start(bf16[1024,256]{1,0:T(8,128)(2,1)} %copy-done.7) | copy-start | bytes 1572868
  144.6 11.1 %copy-start.22 = (s32[1,512]{1,0:T(1,128)S(1)}, s32[1,512]{1,0:T(1,128)}, u32[]{:S(2)}) copy-start(s32[1,512]{1,0:T(1,128)} %param.16) | copy-start | bytes 6148
  144.6 9.9 %collective-permute-start.2 = (bf16[256,256]{1,0:T(8,128)(2,1)S(1)}, bf16[256,256]{1,0:T(8,128)(2,1)S(1)}, u32[]{:S(2)}, u32[]{:S(2)}) collective-permute-start(bf16[256,256]{1,0:T(8,128)(2,1)S(1)} %get-tuple-element.16), channel_id=1, source_target_pairs={{0,1},{1,2},{2,3},{3,4},{4,5},{5,6},{6,7},{8,9},{9,10},{10,11},{11... | collective-permute-start | bytes 393224 | tf_op jit(solution)/shard_map/ppermute | solution.py:27
  149.4 6.3 %collective-permute-start.3 = (bf16[256,256]{1,0:T(8,128)(2,1)S(1)}, bf16[256,256]{1,0:T(8,128)(2,1)S(1)}, u32[]{:S(2)}, u32[]{:S(2)}) collective-permute-start(bf16[256,256]{1,0:T(8,128)(2,1)S(1)} %get-tuple-element.17), channel_id=1, source_target_pairs={{1,0},{2,1},{3,2},{4,3},{5,4},{6,5},{7,6},{9,8},{10,9},{11,10},{12... | collective-permute-start | bytes 393224 | tf_op jit(solution)/shard_map/ppermute | solution.py:30
  152.1 5.0 %collective-permute-start.5 = (bf16[1152,256]{1,0:T(8,128)(2,1)S(1)}, bf16[1152,256]{1,0:T(8,128)(2,1)S(1)}, u32[]{:S(2)}, u32[]{:S(2)}) collective-permute-start(bf16[1152,256]{1,0:T(8,128)(2,1)S(1)} %bitcast.82), channel_id=1, source_target_pairs={{0,1},{1,0},{2,3},{3,2},{4,5},{5,4},{6,7},{7,6},{8,9},{9,8},{10,11... | collective-permute-start | bytes 1769480 | tf_op jit(solution)/shard_map/ppermute | solution.py:76

commit v13 on v12

--- a/solution.py
+++ b/solution.py
@@ -107,11 +107,10 @@
     gathered = jnp.einsum(
         "ter,rd->ted", src_hot, node_table, preferred_element_type=F32
     ).astype(BF16)
-    edge_in = jnp.einsum(
-        "tpe,ted->tpd", one_hot_rows(endpoints, pin_count), gathered, preferred_element_type=F32
-    )
+    dst_rows = one_hot_rows(endpoints, pin_count)
+    edge_in = jnp.einsum("tpe,ted->tpd", dst_rows, gathered, preferred_element_type=F32)
     summed = split_dot("tpk,tkd->pd", edge_in, w_edge)
-    degree = jnp.sum(dst_hot.astype(F32), axis=(0, 1))
+    degree = jnp.sum(dst_rows.astype(F32), axis=(0, 2))
     inverse = 1.0 / (1.0 + degree)
     preact = (
         jnp.dot(pin_feats, w_self, preferred_element_type=F32) + summed * inverse[:, None]

time: 161 us -> 161 us (level)
  no operation moved by 1% of the time
where the time goes in v13:
time: 161 us; the launch traced here: 160 us
  waiting for transfers between devices  61.4 us (38%)
  matrix products  36.6 us (23%)
  starting transfers between devices  29 us (18%)
  blocking collectives  19.5 us (12%)
  other arithmetic  7.99 us (5%)
  local copies, waits for them, and re-layouts  4.49 us (3%)
    all_to_all x1, waiting for transfers between devices, on_device(): lax.all_to_all(packet, ALL, split_axis=0, concat_axis=0, tiled=True)  29.7 us
    all_to_all x1, waiting for transfers between devices, on_device(): lax.all_to_all(back_packet, ALL, split_axis=0, concat_axis=0, tiled=True)  28.5 us
    all_to_all x1, blocking collectives, all_sum(): lax.all_to_all(half.astype(BF16).reshape(chips, -1, width), CHIP, split_a...  19.5 us
    ppermute x2, starting transfers between devices, extended(): lax.ppermute(lax.slice_in_dim(block, block.shape[dim] - width, None, axis...  9.35 us
    all_to_all x1, starting transfers between devices, on_device(): lax.all_to_all(packet, ALL, split_axis=0, concat_axis=0, tiled=True)  6.15 us
    dot_general x1, matrix products, on_device(): jnp.einsum('tre,ted->trd', one_hot_rows(sources, table_rows), edge_rows,...  5.87 us
    dot_general x2, matrix products, split_dot(): jnp.einsum(spec, left, right.astype(F32), precision=lax.Precision.HIGHEST...  5.18 us
    dot_general x1, matrix products, on_device(): jnp.einsum('ter,rd->ted', src_hot, node_table, preferred_element_type=F32)  5.01 us
  transfers between devices with their start and end apart: 9, of which 5 were waited for; matrix products, arithmetic and copies ran while one was open for 11% of the time, Pallas kernels for 0%

profile of v13, /device:TPU:1, one launch (start us, length us, event | category | flops | bytes accessed | tf_op | source)
XLA Modules:
  0.0 160.3 jit_solution(14753796396974378476)
XLA Ops:
  0.6 0.0 copy-start
  0.7 1.6 %fusion.28 = bf16[512,256]{1,0:T(8,128)(2,1)S(1)} fusion(bf16[1024,256]{1,0:T(8,128)(2,1)} %param.11, s32[512]{0:T(512)} %bitcast.111), kind=kOutput, calls=%fused_computation.44 | convolution fusion | flops 269090816 | bytes 788480 | tf_op jit(solution)/shard_map/dot_general | solution.py:99
  2.3 4.6 %collective-permute-start = (bf16[256,256]{1,0:T(8,128)(2,1)S(1)}, bf16[256,256]{1,0:T(8,128)(2,1)S(1)}, u32[]{:S(2)}, u32[]{:S(2)}) collective-permute-start(bf16[256,256]{1,0:T(8,128)(2,1)S(1)} %get-tuple-element.24), channel_id=1, source_target_pairs={{0,1},{1,2},{2,3},{3,4},{4,5},{5,6},{6,7},{8,9},{9,10},{10,11},{11... | collective-permute-start | bytes 393224 | tf_op jit(solution)/shard_map/ppermute | solution.py:27
  6.9 1.9 %collective-permute-start.1 = (bf16[256,256]{1,0:T(8,128)(2,1)S(1)}, bf16[256,256]{1,0:T(8,128)(2,1)S(1)}, u32[]{:S(2)}, u32[]{:S(2)}) collective-permute-start(bf16[256,256]{1,0:T(8,128)(2,1)S(1)} %get-tuple-element.25), channel_id=1, source_target_pairs={{1,0},{2,1},{3,2},{4,3},{5,4},{6,5},{7,6},{9,8},{10,9},{11,10},{12... | collective-permute-start | bytes 393224 | tf_op jit(solution)/shard_map/ppermute | solution.py:30
  8.9 0.5 fusion.31
  9.4 0.0 copy-start.5
  9.5 0.0 copy-start.12
  9.5 1.5 fusion.9
  11.0 0.1 sub.16
  11.1 1.7 %convert_reduce_fusion = f32[1024]{0:T(1024)S(1)} fusion(s32[4,1024]{1,0:T(4,128)S(1)} %bitcast.106), kind=kLoop, calls=%fused_computation.5 | loop fusion | flops 16776192 | bytes 20480 | tf_op jit(solution)/shard_map/reduce_sum | solution.py:113
  12.8 0.3 fusion.62
  13.2 0.0 collective-permute-done.1
  13.2 5.0 %fusion.20 = bf16[4,1024,256]{2,1,0:T(8,128)(2,1)S(1)} fusion(s32[4,1024]{1,0:T(4,128)S(1)} %bitcast.109, bf16[256,256]{1,0:T(8,128)(2,1)S(1)} %collective-permute-done.1, bf16[256,256]{1,0:T(8,128)(2,1)S(1)} %collective-permute-done, bf16[1024,256]{1,0:T(8,128)(2,1)S(1)} %copy-done.5), kind=kOutput, calls=%fused_computation.34 | convolution fusion | flops 3230924800 | bytes 2899968 | tf_op jit(solution)/shard_map/ter,rd->ted/dot_general | solution.py:107
  18.2 0.0 copy-start.1
  18.3 2.8 %fusion.3 = f32[4,1024,256]{2,1,0:T(8,128)S(1)} fusion(bf16[4,1024,256]{2,1,0:T(8,128)(2,1)S(1)} %fusion.20, s32[4,1024]{1,0:T(4,128)S(1)} %bitcast.107), kind=kOutput, calls=%fused_computation.8 | convolution fusion | flops 2151677952 | bytes 6307840 | tf_op jit(solution)/shard_map/tpe,ted->tpd/dot_general | solution.py:111
  21.0 2.1 %fusion.24 = f32[1024,256]{1,0:T(8,128)S(1)} fusion(f32[1024,256]{1,0:T(8,128)S(1)} %fusion.62, f32[4,1024,256]{2,1,0:T(8,128)S(1)} %fusion.3, bf16[4,256,256]{2,1,0:T(8,128)(2,1)S(1)} %copy-done.1, f32[1024]{0:T(1024)S(1)} %add_divide_fusion.2), kind=kOutput, calls=%fused_computation.40 | convolution fusion | flops 3221749760 | bytes 6819840 | tf_op jit(solution)/shard_map/tpk,tkd->pd/dot_general | solution.py:49
  23.1 1.8 %fusion.16 = bf16[2048,256]{1,0:T(8,128)(2,1)S(1)} fusion(s32[1024]{0:T(1024)S(1)} %multiply_add_fusion.1, f32[1024,256]{1,0:T(8,128)S(1)} %fusion.24), kind=kOutput, calls=%fused_computation.25 | convolution fusion | flops 1077673984 | bytes 2101248 | tf_op jit(solution)/shard_map/dot_general | solution.py:137
  25.0 0.0 copy-start.14
  25.0 1.1 pad_maximum_fusion.2
  26.1 6.1 %all-to-all-start = ((bf16[32,72,256]{2,1,0:T(8,128)(2,1)}), bf16[32,72,256]{2,1,0:T(8,128)(2,1)S(1)}, u32[]{:S(2)}, u32[]{:S(2)}) async-start(bf16[32,72,256]{2,1,0:T(8,128)(2,1)} %pad_maximum_fusion.2), calls=%async_computation | async-start | bytes 2359296 | tf_op jit(solution)/shard_map/all_to_all | solution.py:149
  32.3 0.1 pad.16.clone
  32.4 29.7 %all-to-all-done = bf16[32,72,256]{2,1,0:T(8,128)(2,1)S(1)} async-done(((bf16[32,72,256]{2,1,0:T(8,128)(2,1)}), bf16[32,72,256]{2,1,0:T(8,128)(2,1)S(1)}, u32[]{:S(2)}, u32[]{:S(2)}) %all-to-all-start) | async-done | bytes 1179680 | tf_op jit(solution)/shard_map/all_to_all | solution.py:149
  62.1 0.1 eq.178
  62.2 0.1 slice.74
  62.3 0.4 fusion.29
  62.8 0.4 multiply_convert_fusion.2
  63.3 0.2 fusion.63
  63.5 0.3 fusion.64
  63.9 0.4 multiply_convert_fusion.1
  64.3 1.0 convolution_convert_fusion
  65.3 1.5 maximum_maximum_fusion
  66.9 3.1 %all-to-all-start.1 = ((bf16[32,72,256]{2,1,0:T(8,128)(2,1)}), bf16[32,72,256]{2,1,0:T(8,128)(2,1)S(1)}, u32[]{:S(2)}, u32[]{:S(2)}) async-start(bf16[32,72,256]{2,1,0:T(8,128)(2,1)} %maximum_maximum_fusion), calls=%async_computation.1 | async-start | bytes 2359296 | tf_op jit(solution)/shard_map/all_to_all | solution.py:184
  70.0 1.4 fusion.66
  71.4 28.5 %all-to-all-done.1 = bf16[32,72,256]{2,1,0:T(8,128)(2,1)S(1)} async-done(((bf16[32,72,256]{2,1,0:T(8,128)(2,1)}), bf16[32,72,256]{2,1,0:T(8,128)(2,1)S(1)}, u32[]{:S(2)}, u32[]{:S(2)}) %all-to-all-start.1) | async-done | bytes 1179680 | tf_op jit(solution)/shard_map/all_to_all | solution.py:184
  99.9 0.1 slice.75
  100.0 1.1 copy-done.11
  101.1 1.8 %fusion.26 = bf16[1024,256]{1,0:T(8,128)(2,1)S(1)} fusion(bf16[2048,256]{1,0:T(8,128)(2,1)S(1)} %bitcast.87, s32[1024]{0:T(1024)S(1)} %bitcast.105, f32[1024,256]{1,0:T(8,128)S(1)} %copy-done.11), kind=kOutput, calls=%fused_computation.42 | convolution fusion | flops 1078198272 | bytes 2625536 | tf_op jit(solution)/shard_map/dot_general | solution.py:194
  102.9 0.3 convolution_bitcast_fusion.2
  103.3 3.3 %fusion.21 = bf16[4,1024,256]{2,1,0:T(8,128)(2,1)S(1)} fusion(s32[4,1024]{1,0:T(4,128)S(1)} %bitcast.108, bf16[1024,256]{1,0:T(8,128)(2,1)S(1)} %fusion.26, f32[1024]{0:T(1024)S(1)} %add_divide_fusion.2), kind=kOutput, calls=%fused_computation.35 | convolution fusion | flops 2153512960 | bytes 2641920 | tf_op jit(solution)/shard_map/tep,pd->ted/dot_general | solution.py:198
  106.7 0.9 fusion.65
  107.5 0.4 copy-done.4
  108.0 0.2 select_convert_fusion
  108.2 0.9 collective-permute-start.4
  109.1 1.6 %collective-permute-done.4 = bf16[1152,256]{1,0:T(8,128)(2,1)S(1)} collective-permute-done((bf16[1152,256]{1,0:T(8,128)(2,1)S(1)}, bf16[1152,256]{1,0:T(8,128)(2,1)S(1)}, u32[]{:S(2)}, u32[]{:S(2)}) %collective-permute-start.4) | collective-permute-done | bytes 589856 | tf_op jit(solution)/shard_map/ppermute | solution.py:65
  110.8 0.3 add_convert_fusion
  111.1 19.5 %all_to_all.20 = bf16[16,72,256]{2,1,0:T(8,128)(2,1)S(1)} all-to-all(bf16[16,72,256]{2,1,0:T(8,128)(2,1)S(1)} %bitcast.83), channel_id=1, replica_groups=mesh['group'=4,'zdom'=4,'core'=2] {'group','zdom'}, dimensions={0} | all-to-all | bytes 1179648 | tf_op jit(solution)/shard_map/all_to_all | solution.py:66
  130.6 0.2 fusion.40
  130.8 0.9 broadcast_in_dim.10
  131.7 3.8 %all-to-all-start.3 = ((bf16[16,72,256]{2,1,0:T(8,128)(2,1)}), bf16[16,72,256]{2,1,0:T(8,128)(2,1)S(1)}, u32[]{:S(2)}, u32[]{:S(2)}) async-start(bf16[16,72,256]{2,1,0:T(8,128)(2,1)} %broadcast_in_dim.10), calls=%async_computation.3 | async-start | bytes 1179648 | tf_op jit(solution)/shard_map/all_to_all | solution.py:73
  135.5 5.9 %fusion.1 = f32[4,1536,256]{2,1,0:T(8,128)S(1)} fusion(bf16[4,1024,256]{2,1,0:T(8,128)(2,1)} %copy-done.4, s32[4,1024]{1,0:T(4,128)S(1)} %bitcast.110), kind=kOutput, calls=%fused_computation.3 | convolution fusion | flops 3227516928 | bytes 8404992 | tf_op jit(solution)/shard_map/tre,ted->trd/dot_general | solution.py:202
  141.5 3.1 %fusion.61 = (bf16[1536,256]{1,0:T(8,128)(2,1)S(1)}, f32[1536,256]{1,0:T(8,128)S(1)}) fusion(f32[4,1536,256]{2,1,0:T(8,128)S(1)} %fusion.1, bf16[4,256,256]{2,1,0:T(8,128)(2,1)S(1)} %copy-done.1), kind=kOutput, calls=%fused_computation.106 | convolution fusion | flops 4832231424 | bytes 9175040 | tf_op jit(solution)/shard_map/trd,tkd->rk/dot_general | solution.py:49
  144.6 4.8 %collective-permute-start.2 = (bf16[256,256]{1,0:T(8,128)(2,1)S(1)}, bf16[256,256]{1,0:T(8,128)(2,1)S(1)}, u32[]{:S(2)}, u32[]{:S(2)}) collective-permute-start(bf16[256,256]{1,0:T(8,128)(2,1)S(1)} %get-tuple-element.22), channel_id=1, source_target_pairs={{0,1},{1,2},{2,3},{3,4},{4,5},{5,6},{6,7},{8,9},{9,10},{10,11},{11... | collective-permute-start | bytes 393224 | tf_op jit(solution)/shard_map/ppermute | solution.py:27
  149.4 1.9 %collective-permute-start.3 = (bf16[256,256]{1,0:T(8,128)(2,1)S(1)}, bf16[256,256]{1,0:T(8,128)(2,1)S(1)}, u32[]{:S(2)}, u32[]{:S(2)}) collective-permute-start(bf16[256,256]{1,0:T(8,128)(2,1)S(1)} %get-tuple-element.23), channel_id=1, source_target_pairs={{1,0},{2,1},{3,2},{4,3},{5,4},{6,5},{7,6},{9,8},{10,9},{11,10},{12... | collective-permute-start | bytes 393224 | tf_op jit(solution)/shard_map/ppermute | solution.py:30
  151.3 0.3 convolution_add_fusion
  151.6 0.4 all-to-all-done.3
  152.0 1.8 %collective-permute-start.5 = (bf16[1152,256]{1,0:T(8,128)(2,1)S(1)}, bf16[1152,256]{1,0:T(8,128)(2,1)S(1)}, u32[]{:S(2)}, u32[]{:S(2)}) collective-permute-start(bf16[1152,256]{1,0:T(8,128)(2,1)S(1)} %bitcast.82), channel_id=1, source_target_pairs={{0,1},{1,0},{2,3},{3,2},{4,5},{5,4},{6,7},{7,6},{8,9},{9,8},{10,11... | collective-permute-start | bytes 1769480 | tf_op jit(solution)/shard_map/ppermute | solution.py:76
  153.8 0.1 fusion.51
  153.9 0.6 broadcast_multiply_fusion
  154.5 1.2 collective-permute-done.3
  155.7 1.3 fusion.27
  157.0 0.1 broadcast_select_fusion.1
  157.1 0.7 convert_multiply_fusion.1
  157.8 1.2 multiply_bitcast_fusion
  159.0 1.3 copy.20
  (66 shorter events, 0.4 us)
Async XLA Ops:
  0.6 62.1 %copy-start = (bf16[256,1024]{1,0:T(8,128)(2,1)S(1)}, bf16[256,1024]{1,0:T(8,128)(2,1)}, u32[]{:S(2)}) copy-start(bf16[256,1024]{1,0:T(8,128)(2,1)} %param.14) | copy-start | bytes 1572868
  0.6 8.2 %copy-start.16 = (s32[1024]{0:T(1024)S(1)}, s32[1024]{0:T(1024)}, u32[]{:S(2)}) copy-start(s32[1024]{0:T(1024)} %param.20) | copy-start | bytes 12292
  0.7 8.2 %copy-start.13 = (s32[1024,1]{0,1:T(1,128)S(1)}, s32[1024,1]{0,1:T(1,128)}, u32[]{:S(2)}) copy-start(s32[1024,1]{0,1:T(1,128)} %param.19) | copy-start | bytes 12292
  2.3 10.8 %collective-permute-start = (bf16[256,256]{1,0:T(8,128)(2,1)S(1)}, bf16[256,256]{1,0:T(8,128)(2,1)S(1)}, u32[]{:S(2)}, u32[]{:S(2)}) collective-permute-start(bf16[256,256]{1,0:T(8,128)(2,1)S(1)} %get-tuple-element.24), channel_id=1, source_target_pairs={{0,1},{1,2},{2,3},{3,4},{4,5},{5,6},{6,7},{8,9},{9,10},{10,11},{11... | collective-permute-start | bytes 393224 | tf_op jit(solution)/shard_map/ppermute | solution.py:27
  6.9 6.3 %collective-permute-start.1 = (bf16[256,256]{1,0:T(8,128)(2,1)S(1)}, bf16[256,256]{1,0:T(8,128)(2,1)S(1)}, u32[]{:S(2)}, u32[]{:S(2)}) collective-permute-start(bf16[256,256]{1,0:T(8,128)(2,1)S(1)} %get-tuple-element.25), channel_id=1, source_target_pairs={{1,0},{2,1},{3,2},{4,3},{5,4},{6,5},{7,6},{9,8},{10,9},{11,10},{12... | collective-permute-start | bytes 393224 | tf_op jit(solution)/shard_map/ppermute | solution.py:30
  9.4 1.6 %copy-start.18 = (s32[1,4,1024]{2,1,0:T(4,128)S(1)}, s32[1,4,1024]{2,1,0:T(4,128)}, u32[]{:S(2)}) copy-start(s32[1,4,1024]{2,1,0:T(4,128)} %param.18) | copy-start | bytes 49156
  9.4 3.4 %copy-start.5 = (bf16[1024,256]{1,0:T(8,128)(2,1)S(1)}, bf16[1024,256]{1,0:T(8,128)(2,1)}, u32[]{:S(2)}) copy-start(bf16[1024,256]{1,0:T(8,128)(2,1)} %param.11) | copy-start | bytes 1572868
  9.5 3.4 %copy-start.12 = (bf16[256,256]{1,0:T(8,128)(2,1)S(1)}, bf16[256,256]{1,0:T(8,128)(2,1)}, u32[]{:S(2)}) copy-start(bf16[256,256]{1,0:T(8,128)(2,1)} %param.12) | copy-start | bytes 393220
  9.5 3.7 %copy-start.20 = (s32[1,4,1024]{2,1,0:T(4,128)S(1)}, s32[1,4,1024]{2,1,0:T(4,128)}, u32[]{:S(2)}) copy-start(s32[1,4,1024]{2,1,0:T(4,128)} %param.17) | copy-start | bytes 49156
  18.2 2.8 %copy-start.2 = (bf16[4,1024,256]{2,1,0:T(8,128)(2,1)}, bf16[4,1024,256]{2,1,0:T(8,128)(2,1)S(1)}, u32[]{:S(2)}) copy-start(bf16[4,1024,256]{2,1,0:T(8,128)(2,1)S(1)} %fusion.20) | copy-start | bytes 6291460
  18.2 2.8 %copy-start.1 = (bf16[4,256,256]{2,1,0:T(8,128)(2,1)S(1)}, bf16[4,256,256]{2,1,0:T(8,128)(2,1)}, u32[]{:S(2)}) copy-start(bf16[4,256,256]{2,1,0:T(8,128)(2,1)} %param.13) | copy-start | bytes 1572868
  23.1 1.8 %copy-start.10 = (f32[1024,256]{1,0:T(8,128)}, f32[1024,256]{1,0:T(8,128)S(1)}, u32[]{:S(2)}) copy-start(f32[1024,256]{1,0:T(8,128)S(1)} %fusion.24) | copy-start | bytes 3145732
  25.0 7.3 %copy-start.14 = (bf16[1024]{0:T(1024)(128)(2,1)S(1)}, bf16[1024]{0:T(1024)(128)(2,1)}, u32[]{:S(2)}) copy-start(bf16[1024]{0:T(1024)(128)(2,1)} %param.15) | copy-start | bytes 6148
  26.1 36.0 %all-to-all-start = ((bf16[32,72,256]{2,1,0:T(8,128)(2,1)}), bf16[32,72,256]{2,1,0:T(8,128)(2,1)S(1)}, u32[]{:S(2)}, u32[]{:S(2)}) async-start(bf16[32,72,256]{2,1,0:T(8,128)(2,1)} %pad_maximum_fusion.2), calls=%async_computation | async-start | bytes 2359296 | tf_op jit(solution)/shard_map/all_to_all | solution.py:149
  62.8 0.7 copy-start.17
  63.5 1.8 %copy-start.15 = (f32[1,256]{1,0:T(1,128)}, f32[1,256]{1,0:T(1,128)S(1)}, u32[]{:S(2)}) copy-start(f32[1,256]{1,0:T(1,128)S(1)} %fusion.63) | copy-start | bytes 3076
  64.3 2.6 %copy-start.9 = (bf16[256,1024]{1,0:T(8,128)(2,1)}, bf16[256,1024]{1,0:T(8,128)(2,1)S(1)}, u32[]{:S(2)}) copy-start(bf16[256,1024]{1,0:T(8,128)(2,1)S(1)} %multiply_convert_fusion.1) | copy-start | bytes 1572868
  66.9 33.1 %all-to-all-start.1 = ((bf16[32,72,256]{2,1,0:T(8,128)(2,1)}), bf16[32,72,256]{2,1,0:T(8,128)(2,1)S(1)}, u32[]{:S(2)}, u32[]{:S(2)}) async-start(bf16[32,72,256]{2,1,0:T(8,128)(2,1)} %maximum_maximum_fusion), calls=%async_computation.1 | async-start | bytes 2359296 | tf_op jit(solution)/shard_map/all_to_all | solution.py:184
  99.9 1.2 copy-start.11
  101.1 1.8 %copy-start.6 = (bf16[1024,256]{1,0:T(8,128)(2,1)S(1)}, bf16[1024,256]{1,0:T(8,128)(2,1)}, u32[]{:S(2)}) copy-start(bf16[1024,256]{1,0:T(8,128)(2,1)} %param.11) | copy-start | bytes 1572868
  101.1 2.2 %copy-start.19 = (s32[1,4,1024]{2,1,0:T(4,128)S(1)}, s32[1,4,1024]{2,1,0:T(4,128)}, u32[]{:S(2)}) copy-start(s32[1,4,1024]{2,1,0:T(4,128)} %param.18) | copy-start | bytes 49156
  102.9 3.7 %copy-start.7 = (bf16[1024,256]{1,0:T(8,128)(2,1)}, bf16[1024,256]{1,0:T(8,128)(2,1)S(1)}, u32[]{:S(2)}) copy-start(bf16[1024,256]{1,0:T(8,128)(2,1)S(1)} %fusion.26) | copy-start | bytes 1572868
  103.3 3.3 %copy-start.3 = (bf16[4,1024,256]{2,1,0:T(8,128)(2,1)S(1)}, bf16[4,1024,256]{2,1,0:T(8,128)(2,1)}, u32[]{:S(2)}) copy-start(bf16[4,1024,256]{2,1,0:T(8,128)(2,1)} %copy-done.2) | copy-start | bytes 6291460
  106.6 1.3 copy-start.4
  108.2 2.5 %collective-permute-start.4 = (bf16[1152,256]{1,0:T(8,128)(2,1)S(1)}, bf16[1152,256]{1,0:T(8,128)(2,1)S(1)}, u32[]{:S(2)}, u32[]{:S(2)}) collective-permute-start(bf16[1152,256]{1,0:T(8,128)(2,1)S(1)} %select_convert_fusion), channel_id=1, source_target_pairs={{0,1},{1,0},{2,3},{3,2},{4,5},{5,4},{6,7},{7,6},{8,9},{9,8},{10,11... | collective-permute-start | bytes 1769480 | tf_op jit(solution)/shard_map/ppermute | solution.py:65
  111.1 24.5 %copy-start.21 = (s32[1,4,1024]{2,1,0:T(4,128)S(1)}, s32[1,4,1024]{2,1,0:T(4,128)}, u32[]{:S(2)}) copy-start(s32[1,4,1024]{2,1,0:T(4,128)} %param.17) | copy-start | bytes 49156
  131.7 20.3 %all-to-all-start.3 = ((bf16[16,72,256]{2,1,0:T(8,128)(2,1)}), bf16[16,72,256]{2,1,0:T(8,128)(2,1)S(1)}, u32[]{:S(2)}, u32[]{:S(2)}) async-start(bf16[16,72,256]{2,1,0:T(8,128)(2,1)} %broadcast_in_dim.10), calls=%async_computation.3 | async-start | bytes 1179648 | tf_op jit(solution)/shard_map/all_to_all | solution.py:73
  141.5 9.8 %copy-start.8 = (bf16[1024,256]{1,0:T(8,128)(2,1)S(1)}, bf16[1024,256]{1,0:T(8,128)(2,1)}, u32[]{:S(2)}) copy-start(bf16[1024,256]{1,0:T(8,128)(2,1)} %copy-done.7) | copy-start | bytes 1572868
  144.6 11.1 %copy-start.22 = (s32[1,512]{1,0:T(1,128)S(1)}, s32[1,512]{1,0:T(1,128)}, u32[]{:S(2)}) copy-start(s32[1,512]{1,0:T(1,128)} %param.16) | copy-start | bytes 6148
  144.6 9.9 %collective-permute-start.2 = (bf16[256,256]{1,0:T(8,128)(2,1)S(1)}, bf16[256,256]{1,0:T(8,128)(2,1)S(1)}, u32[]{:S(2)}, u32[]{:S(2)}) collective-permute-start(bf16[256,256]{1,0:T(8,128)(2,1)S(1)} %get-tuple-element.22), channel_id=1, source_target_pairs={{0,1},{1,2},{2,3},{3,4},{4,5},{5,6},{6,7},{8,9},{9,10},{10,11},{11... | collective-permute-start | bytes 393224 | tf_op jit(solution)/shard_map/ppermute | solution.py:27
  149.4 6.3 %collective-permute-start.3 = (bf16[256,256]{1,0:T(8,128)(2,1)S(1)}, bf16[256,256]{1,0:T(8,128)(2,1)S(1)}, u32[]{:S(2)}, u32[]{:S(2)}) collective-permute-start(bf16[256,256]{1,0:T(8,128)(2,1)S(1)} %get-tuple-element.23), channel_id=1, source_target_pairs={{1,0},{2,1},{3,2},{4,3},{5,4},{6,5},{7,6},{9,8},{10,9},{11,10},{12... | collective-permute-start | bytes 393224 | tf_op jit(solution)/shard_map/ppermute | solution.py:30
  152.0 5.0 %collective-permute-start.5 = (bf16[1152,256]{1,0:T(8,128)(2,1)S(1)}, bf16[1152,256]{1,0:T(8,128)(2,1)S(1)}, u32[]{:S(2)}, u32[]{:S(2)}) collective-permute-start(bf16[1152,256]{1,0:T(8,128)(2,1)S(1)} %bitcast.82), channel_id=1, source_target_pairs={{0,1},{1,0},{2,3},{3,2},{4,5},{5,4},{6,7},{7,6},{8,9},{9,8},{10,11... | collective-permute-start | bytes 1769480 | tf_op jit(solution)/shard_map/ppermute | solution.py:76
